TPU v7x, 32 devices: a whole 2x2x4 slice. The times are simulated.
32 devices in a mesh: az: 8 (over z, y), ax: 4 (over x, core).
Axes of the slice: x: 2, y: 2, z: 4, core: 2. Of those that a mesh axis runs over, the one named last changes fastest.
Arguments:
- acoustic: float32 [4, 64, 64, 128], P(None, 'az', 'ax'), may hold values from -6 to 6
- mean_flow: float32 [4, 64, 64, 128], P(None, 'az', 'ax'), may hold values from -0.4 to 2, as said below
- adjoint_in: float32 [4, 64, 64, 128], P(None, 'az', 'ax'), may hold values from -6 to 6
- admittance: float32 [64], replicated, may hold values from 0.2 to 2
- segment_id: int32 [64, 64], P('az', 'ax'), may hold values from 0 to 63, as said below
- noise_code: int32 [64, 64], P('az', 'ax'), may hold values from 0 to 63
- noise_table: float32 [64], replicated, may hold values from -4 to 4
- mic_az: int32 [512], replicated, may hold values from 0 to 63, as said below
- mic_ax: int32 [512], replicated, may hold values from 0 to 63
- measured: float32 [512], replicated, may hold values from -17 to 17
Outputs:
- adjoint_out: float32 [4, 64, 64, 128], P(None, 'az', 'ax')
- liner_grad: float32 [64], replicated
- misfit: float32 [], replicated
Inputs may be any that keep to these rules, and one draw needn't show every extreme that they name: `mean_flow`: component 0 lies in 0.2 to 0.6, component 1 in -0.4 to 0.4, component 2 in 0.5 to 2, component 3 in 0.7 to 1.4. segment_id = sector * 4 + band, where the 16 sectors are runs of contiguous azimuthal cells (wrapping) and the 4 bands runs of contiguous axial cells; every segment has cells. `mic_az`: microphones sit on casing cells; several may share a cell.
All inputs are finite; a program needn't handle non-finite values.
Results may differ from a plain program's by a relative error of at most 0.000086.
Values sent between devices are 32-bit elements; how exact they have to be, the bound alone decides.
No kernel may reach another device: no remote copies, remote signals or barrier semaphores. Data moves between devices by JAX's collectives and lax.ppermute only.
A program may use at most 128 MiB of HBM per device.

v0:
```python
import jax
import jax.numpy as jnp
from jax import lax
from jax.sharding import PartitionSpec as P

step_dt = 0.25
epsilon = 1e-06
highest = lax.Precision.HIGHEST


def with_halo(array, sides, width, wrap):
    for axis, dim in sides:
        size, length = (lax.axis_size(axis), array.shape[dim])
        up = [(i, (i + 1) % size) for i in range(size if wrap else size - 1)]
        down = [(j, i) for i, j in up]
        last = lax.slice_in_dim(array, length - width, length, axis=dim)
        initial = lax.slice_in_dim(array, 0, width, axis=dim)
        before = lax.ppermute(last, axis, up)
        after = lax.ppermute(initial, axis, down)
        array = jnp.concatenate([before, array, after], axis=dim)
    return array


def center(values):
    return values[..., 1:-1, 1:-1, :]


def az_next(values):
    return values[..., 2:, 1:-1, :]


def az_prev(values):
    return values[..., :-2, 1:-1, :]


def ax_next(values):
    return values[..., 1:-1, 2:, :]


def ax_prev(values):
    return values[..., 1:-1, :-2, :]


def shrink(values, margin):
    return values[..., margin : values.shape[-3] - margin, margin : values.shape[-2] - margin, :]


def rad_next(values):
    return jnp.concatenate([values[..., 1:], jnp.zeros_like(values[..., :1])], axis=-1)


def rad_prev(values):
    return jnp.concatenate([jnp.zeros_like(values[..., :1]), values[..., :-1]], axis=-1)


def casing_mask(values):
    return lax.broadcasted_iota(jnp.int32, values.shape, values.ndim - 1) == values.shape[-1] - 1


def advect(values, axial_flow, swirl_flow):
    return (
        center(axial_flow) * (ax_next(values) - ax_prev(values)) * 0.5
        + center(swirl_flow) * (az_next(values) - az_prev(values)) * 0.5
    )


def advect_back(values, axial_flow, swirl_flow):
    carried_ax = axial_flow * values
    carried_az = swirl_flow * values
    return 0.5 * (ax_prev(carried_ax) - ax_next(carried_ax)) + 0.5 * (
        az_prev(carried_az) - az_next(carried_az)
    )


def exchange_rims(fields, rim_width):
    widened = with_halo(fields, (("ax", 2),), rim_width, False)
    return with_halo(widened, (("az", 1),), rim_width, True)


def forward_pressure(padded, wall_admit, source):
    pressure, vel_az, vel_ax, vel_rad = (padded[0], padded[1], padded[2], padded[3])
    axial_flow, swirl_flow, buoyancy, stiffness = (padded[4], padded[5], padded[6], padded[7])
    new_az = center(vel_az) - step_dt * (
        advect(vel_az, axial_flow, swirl_flow)
        + center(buoyancy) * (az_next(pressure) - center(pressure))
    )
    new_ax = center(vel_ax) - step_dt * (
        advect(vel_ax, axial_flow, swirl_flow)
        + center(buoyancy) * (ax_next(pressure) - center(pressure))
    )
    press_in = shrink(pressure, 1)
    rad_in = shrink(vel_rad, 1)
    axial_in = shrink(axial_flow, 1)
    swirl_in = shrink(swirl_flow, 1)
    buoy_in = shrink(buoyancy, 1)
    stiff_in = shrink(stiffness, 1)
    press_own = center(press_in)
    new_rad = jnp.where(
        casing_mask(press_own),
        wall_admit[:, :, None] * press_own,
        center(rad_in)
        - step_dt
        * (
            advect(rad_in, axial_in, swirl_in) + center(buoy_in) * (rad_next(press_own) - press_own)
        ),
    )
    spread = (
        center(new_az)
        - az_prev(new_az)
        + (center(new_ax) - ax_prev(new_ax))
        + (new_rad - rad_prev(new_rad))
    )
    return (
        press_own
        - step_dt * (advect(press_in, axial_in, swirl_in) + center(stiff_in) * spread)
        + step_dt * source
    )


def first_half(press_pad, vel_pad, coef_pad):
    pushed = step_dt * coef_pad[3] * press_pad
    pushed_own = center(pushed)
    head_az = vel_pad[0] - (pushed_own - az_next(pushed))
    head_ax = vel_pad[1] - (pushed_own - ax_next(pushed))
    head_rad = vel_pad[2] - (pushed_own - rad_next(pushed_own))
    return jnp.stack([head_az, head_ax, head_rad])


def second_half(press_pad, head_stack, coef_pad, wall_admit):
    axial_flow, swirl_flow, buoyancy = (coef_pad[0], coef_pad[1], coef_pad[2])
    head_az, head_ax = (head_stack[0], head_stack[1])
    head_masked = jnp.where(casing_mask(head_stack[2]), 0.0, head_stack[2])
    back_az = center(head_az) - step_dt * advect_back(head_az, axial_flow, swirl_flow)
    back_ax = center(head_ax) - step_dt * advect_back(head_ax, axial_flow, swirl_flow)
    back_rad = center(head_masked) - step_dt * advect_back(head_masked, axial_flow, swirl_flow)
    push_az = step_dt * buoyancy * head_az
    push_ax = step_dt * buoyancy * head_ax
    push_rad = step_dt * center(buoyancy) * center(head_masked)
    rad_own = center(head_stack[2])
    back_press = center(press_pad) - step_dt * advect_back(press_pad, axial_flow, swirl_flow)
    back_press = (
        back_press
        + (center(push_az) - az_prev(push_az))
        + (center(push_ax) - ax_prev(push_ax))
        + (push_rad - rad_prev(push_rad))
    )
    back_press = back_press + jnp.where(casing_mask(rad_own), wall_admit[:, :, None] * rad_own, 0.0)
    return (jnp.stack([back_press, back_az, back_ax, back_rad]), rad_own[..., -1])


def adjoint_step(seed_list, velocity_list, coef_wide, wall_admit, rim_width):
    joined = exchange_rims(jnp.stack(seed_list), rim_width)
    coef_first = shrink(coef_wide, 2 - rim_width)
    coef_second = shrink(coef_wide, 1)
    member = 0
    head_list = first_half(joined[member], velocity_list[member], coef_first)
    widened = exchange_rims(head_list, 1)
    member = 0
    results = [second_half(joined[member], widened, coef_second, wall_admit)]
    return results


def shards(
    acoustic,
    mean_flow,
    adjoint_in,
    admittance,
    segment_id,
    noise_code,
    noise_table,
    mic_az,
    mic_ax,
    measured,
):
    az_cells, ax_cells, rad_cells = (acoustic.shape[1], acoustic.shape[2], acoustic.shape[3])
    buoyancy = 1.0 / mean_flow[2]
    stiffness = mean_flow[2] * mean_flow[3] * mean_flow[3]
    segment_hot = (
        segment_id[:, :, None] == lax.broadcasted_iota(jnp.int32, (1, 1, admittance.shape[0]), 2)
    ).astype(jnp.float32)
    wall_admit = jnp.dot(segment_hot, admittance, precision=highest)
    noise_hot = (
        noise_code[:, :, None] == lax.broadcasted_iota(jnp.int32, (1, 1, noise_table.shape[0]), 2)
    ).astype(jnp.float32)
    profile = (lax.broadcasted_iota(jnp.float32, (rad_cells,), 0) + 0.5) / rad_cells
    source = jnp.dot(noise_hot, noise_table, precision=highest)[:, :, None] * profile
    coefficients = jnp.stack([mean_flow[0], mean_flow[1], buoyancy, stiffness])
    rim_width = 1
    padded = exchange_rims(jnp.concatenate([acoustic, coefficients], axis=0), 2)
    velocities = adjoint_in[1:]
    coef_wide = padded[4:8]
    new_press = forward_pressure(padded, wall_admit, source)
    first_az = lax.axis_index("az") * az_cells
    first_ax = lax.axis_index("ax") * ax_cells
    local_az = mic_az - first_az
    local_ax = mic_ax - first_ax
    owned = (local_az >= 0) & (local_az < az_cells) & (local_ax >= 0) & (local_ax < ax_cells)
    flat_cell = jnp.clip(local_az, 0, az_cells - 1) * ax_cells + jnp.clip(local_ax, 0, ax_cells - 1)
    heard = new_press[:, :, rad_cells - 1].reshape(az_cells * ax_cells)[flat_cell]
    misses = jnp.where(owned, heard - measured, 0.0)
    square_sum = jnp.sum(misses * misses)
    mic_count = mic_az.shape[0]
    casing_own = acoustic[0][:, :, rad_cells - 1]
    grad_scale = (
        az_cells * lax.axis_size("az") * ax_cells * lax.axis_size("ax") / admittance.shape[0]
    ) ** (-0.5)
    total_sq = lax.psum(square_sum, ("az", "ax"))
    mean_sq = total_sq / mic_count + epsilon
    placed = (
        jnp.zeros((az_cells * ax_cells,), jnp.float32)
        .at[flat_cell]
        .add(jnp.where(owned, misses / mean_sq, 0.0))
        .reshape(az_cells, ax_cells)
    )
    seed_press = adjoint_in[0] + jnp.where(casing_mask(adjoint_in[0]), placed[:, :, None], 0.0)
    outcome = adjoint_step([seed_press], [velocities], coef_wide, wall_admit, rim_width)
    adjoint_out, rad_top = outcome[0]
    segment_sums = jnp.einsum("acs,ac->s", segment_hot, rad_top * casing_own, precision=highest)
    liner_grad = lax.psum(segment_sums, ("az", "ax")) * grad_scale
    misfit = 0.5 * jnp.log(mean_sq)
    return (adjoint_out, liner_grad, misfit)


def solution(mesh):
    placed = (
        P(None, "az", "ax", None),
        P(None, "az", "ax", None),
        P(None, "az", "ax", None),
        P(),
        P("az", "ax"),
        P("az", "ax"),
        P(),
        P(),
        P(),
        P(),
    )
    return jax.shard_map(
        shards,
        mesh=mesh,
        in_specs=placed,
        out_specs=(P(None, "az", "ax", None), P(), P()),
        check_vma=False,
    )
```

profile of v0, /device:TPU:0, one launch (start us, length us, event | category | flops | bytes accessed | tf_op | source)
XLA Modules:
  0.0 222.2 jit_solution(4559688916384890473)
XLA Ops:
  5.0 3.0 %collective-permute-start = (f32[8,8,2,128]{3,1,2,0:T(8,128)S(1)}, f32[8,8,2,128]{3,1,2,0:T(8,128)S(1)}, u32[]{:S(2)}, u32[]{:S(2)}) collective-permute-start(f32[8,8,2,128]{3,1,2,0:T(8,128)S(1)} %copy.107), channel_id=1, source_target_pairs={{0,1},{1,2},{2,3},{4,5},{5,6},{6,7},{8,9},{9,10},{10,11},{12,13},{... | collective-permute-start | bytes 196616 | tf_op jit(solution)/shard_map/ppermute | solution.py:18
  8.0 2.7 %copy.81 = f32[8,8,16,128]{2,1,3,0:T(8,128)} copy(f32[8,8,16,128]{3,2,1,0:T(8,128)S(1)} %pad_maximum_fusion.6) | data formatting | bytes 1048576 | tf_op jit(solution)/shard_map/concatenate | solution.py:189
  11.6 2.7 %copy.82 = f32[8,8,2,128]{2,1,3,0:T(8,128)} copy(f32[8,8,2,128]{3,1,2,0:T(8,128)S(1)} %collective-permute-done.1) | data formatting | bytes 131072 | tf_op jit(solution)/shard_map/ppermute | solution.py:19
  17.0 12.7 %pad_maximum_fusion.5 = (f32[8,2,20,128]{2,1,3,0:T(2,128)S(1)}, f32[8,2,20,128]{2,1,3,0:T(2,128)S(1)}) fusion(f32[8,8,2,128]{2,1,3,0:T(8,128)} %copy.82, f32[8,8,16,128]{2,1,3,0:T(8,128)} %copy.81, f32[8,8,2,128]{2,1,3,0:T(8,128)} %copy.80), kind=kLoop, calls=%fused_computation.47 | loop fusion | flops 163840 | bytes 983040 | tf_op jit(solution)/shard_map/slice | solution.py:16
  30.1 6.1 %collective-permute-start.3 = (f32[8,2,20,128]{3,0,2,1:T(8,128)S(1)}, f32[8,2,20,128]{3,0,2,1:T(8,128)S(1)}, u32[]{:S(2)}, u32[]{:S(2)}) collective-permute-start(f32[8,2,20,128]{3,0,2,1:T(8,128)S(1)} %copy.84), channel_id=1, source_target_pairs={{4,0},{8,4},{12,8},{16,12},{20,16},{24,20},{28,24},{0,28},{5,1},{9... | collective-permute-start | bytes 491528 | tf_op jit(solution)/shard_map/ppermute | solution.py:19
  37.3 3.2 %collective-permute-done.3 = f32[8,2,20,128]{3,0,2,1:T(8,128)S(1)} collective-permute-done((f32[8,2,20,128]{3,0,2,1:T(8,128)S(1)}, f32[8,2,20,128]{3,0,2,1:T(8,128)S(1)}, u32[]{:S(2)}, u32[]{:S(2)}) %collective-permute-start.3) | collective-permute-done | bytes 163872 | tf_op jit(solution)/shard_map/ppermute | solution.py:19
  41.1 5.3 %collective-permute-done.2 = f32[8,2,20,128]{3,0,2,1:T(8,128)S(1)} collective-permute-done((f32[8,2,20,128]{3,0,2,1:T(8,128)S(1)}, f32[8,2,20,128]{3,0,2,1:T(8,128)S(1)}, u32[]{:S(2)}, u32[]{:S(2)}) %collective-permute-start.2) | collective-permute-done | bytes 163872 | tf_op jit(solution)/shard_map/ppermute | solution.py:18
  46.8 7.7 %pad_maximum_fusion = f32[8,12,20,128]{2,1,3,0:T(8,128)S(1)} fusion(f32[8,2,20,128]{2,1,3,0:T(2,128)S(1)} %copy.86, f32[8,8,2,128]{2,1,3,0:T(8,128)} %copy.82, f32[8,8,16,128]{2,1,3,0:T(8,128)} %copy.81, f32[8,8,2,128]{2,1,3,0:T(8,128)} %copy.80, f32[8,2,20,128]{2,1,3,0:T(2,128)S(1)} %copy.85), kind=kLoop, calls=%fused_computation.2 | loop fusion | flops 983040 | bytes 1966080 | tf_op jit(solution)/shard_map/concatenate | solution.py:20
  55.1 2.7 %copy-done.2 = f32[8,12,20,128]{2,1,3,0:T(8,128)} copy-done((f32[8,12,20,128]{2,1,3,0:T(8,128)}, f32[8,12,20,128]{2,1,3,0:T(8,128)S(1)}, u32[]{:S(2)}) %copy-start.2) | copy-done | bytes 983064
  66.4 3.3 %gather_fusion = f32[512]{0:T(512)S(1)} fusion(f32[128]{0:T(128)S(1)} %reshape_squeeze.3, s32[1024]{0:T(1024)S(1)} %pad_clamp_fusion), kind=kCustom, calls=%fused_computation | custom fusion | bytes 6144 | tf_op jit(solution)/shard_map/gather | solution.py:199
  70.4 37.3 %psum.14 = f32[]{:T(128)} all-reduce(f32[]{:T(128)} %get-tuple-element.11), channel_id=1, replica_groups=mesh['az'=8,'ax'=4] {'az','ax'}, use_global_device_ids=true, to_apply=%region_1.2 | all-reduce | flops 1 | bytes 8 | tf_op jit(solution)/shard_map/psum | solution.py:207
  108.4 4.1 %scatter_custom_fusion = f32[128]{0:T(128)S(1)} fusion(s32[512]{0:T(512)S(1)} %compare_select_fusion, f32[512]{0:T(512)S(1)} %divide_select_fusion, f32[]{:T(128)} %constant.19.clone.1), kind=kCustom, calls=%fused_computation.159 | custom fusion | flops 512 | bytes 516 | tf_op jit(solution)/shard_map/scatter-add | solution.py:212
  114.0 3.0 %collective-permute-start.4 = (f32[1,8,1,128]{3,1,2,0:T(8,128)S(1)}, f32[1,8,1,128]{3,1,2,0:T(8,128)S(1)}, u32[]{:S(2)}, u32[]{:S(2)}) collective-permute-start(f32[1,8,1,128]{3,1,2,0:T(8,128)S(1)} %get-tuple-element.60), channel_id=1, source_target_pairs={{0,1},{1,2},{2,3},{4,5},{5,6},{6,7},{8,9},{9,10},{10,11},{12,13},{... | collective-permute-start | bytes 12296 | tf_op jit(solution)/shard_map/ppermute | solution.py:18
  118.0 4.3 %collective-permute-start.7 = (f32[1,1,18,128]{2,1,3,0:T(1,128)S(1)}, f32[1,1,18,128]{2,1,3,0:T(1,128)S(1)}, u32[]{:S(2)}, u32[]{:S(2)}) collective-permute-start(f32[1,1,18,128]{2,1,3,0:T(1,128)S(1)} %copy.89), channel_id=1, source_target_pairs={{4,0},{8,4},{12,8},{16,12},{20,16},{24,20},{28,24},{0,28},{5,1},{9... | collective-permute-start | bytes 27656 | tf_op jit(solution)/shard_map/ppermute | solution.py:19
  124.4 4.9 %collective-permute-done.6 = f32[1,1,18,128]{2,1,3,0:T(1,128)S(1)} collective-permute-done((f32[1,1,18,128]{2,1,3,0:T(1,128)S(1)}, f32[1,1,18,128]{2,1,3,0:T(1,128)S(1)}, u32[]{:S(2)}, u32[]{:S(2)}) %collective-permute-start.6) | collective-permute-done | bytes 9248 | tf_op jit(solution)/shard_map/ppermute | solution.py:18
  129.4 4.2 %fusion.21 = (f32[10,18,128]{1,0,2:T(8,128)}, f32[10,18,128]{1,0,2:T(8,128)S(1)}, f32[10,18,128]{1,0,2:T(8,128)}) fusion(f32[8,12,20,128]{2,1,3,0:T(8,128)} %copy-done.2, f32[1,1,18,128]{2,1,3,0:T(1,128)S(1)} %collective-permute-done.7, f32[1,8,18,128]{2,1,3,0:T(8,128)S(1)} %copy.90, f32[1,1,18,128]{2,1,3,0:T(1,128)S(1)} %collective-permute-done.6), kind=kLoop, calls=%fused_computation.54 | loop fusion | flops 138240 | bytes 645120 | tf_op jit(solution)/shard_map/mul | solution.py:68
  137.7 3.0 %collective-permute-start.8 = (f32[3,8,1,128]{3,1,2,0:T(8,128)S(1)}, f32[3,8,1,128]{3,1,2,0:T(8,128)S(1)}, u32[]{:S(2)}, u32[]{:S(2)}) collective-permute-start(f32[3,8,1,128]{3,1,2,0:T(8,128)S(1)} %copy.94), channel_id=1, source_target_pairs={{0,1},{1,2},{2,3},{4,5},{5,6},{6,7},{8,9},{9,10},{10,11},{12,13},{... | collective-permute-start | bytes 36872 | tf_op jit(solution)/shard_map/ppermute | solution.py:18
  144.6 3.8 %pad_maximum_fusion.12 = (f32[3,1,18,128]{2,1,3,0:T(1,128)S(1)}, f32[3,1,18,128]{2,1,3,0:T(1,128)S(1)}) fusion(f32[3,8,1,128]{2,1,3,0:T(8,128)S(1)} %copy.97, f32[3,8,1,128]{2,1,3,0:T(8,128)S(1)} %copy.96, f32[1,8,16,128]{2,1,3,0:T(8,128)} %copy-done.7, f32[1,8,16,128]{2,1,3,0:T(8,128)} %copy-done.5, f32[1,8,16,128]{2,1,3,0:T(8,128)} %copy-done.3), kind=kLoop, calls=%fused_computation.127 | loop fusion | flops 55296 | bytes 276480 | tf_op jit(solution)/shard_map/slice | solution.py:16
  151.7 3.3 %collective-permute-done.11 = f32[3,1,18,128]{2,1,3,0:T(1,128)S(1)} collective-permute-done((f32[3,1,18,128]{2,1,3,0:T(1,128)S(1)}, f32[3,1,18,128]{2,1,3,0:T(1,128)S(1)}, u32[]{:S(2)}, u32[]{:S(2)}) %collective-permute-start.11) | collective-permute-done | bytes 27680 | tf_op jit(solution)/shard_map/ppermute | solution.py:19
  155.0 3.1 %collective-permute-done.10 = f32[3,1,18,128]{2,1,3,0:T(1,128)S(1)} collective-permute-done((f32[3,1,18,128]{2,1,3,0:T(1,128)S(1)}, f32[3,1,18,128]{2,1,3,0:T(1,128)S(1)}, u32[]{:S(2)}, u32[]{:S(2)}) %collective-permute-start.10) | collective-permute-done | bytes 27680 | tf_op jit(solution)/shard_map/ppermute | solution.py:18
  159.9 4.9 %multiply_multiply_fusion.1 = (f32[10,18,128]{1,0,2:T(8,128)}, f32[10,18,128]{1,0,2:T(8,128)}, f32[10,18,128]{1,0,2:T(8,128)S(1)}, f32[10,18,128]{1,0,2:T(8,128)...) fusion(f32[8,12,20,128]{2,1,3,0:T(8,128)} %copy-done.2, ...), kind=kLoop, calls=%fused_computation.50 | loop fusion | flops 207360 | bytes 1290368 | tf_op jit(solution)/shard_map/mul | solution.py:136
  169.2 3.1 %fusion.33 = f32[1,8,16,128]{2,1,3,0:T(8,128)S(1)} fusion(f32[10,18,128]{1,0,2:T(8,128)} %get-tuple-element.18, f32[10,18,128]{1,0,2:T(8,128)} %get-tuple-element.20, f32[10,18,128]{1,0,2:T(8,128)} %get-tuple-element.37), kind=kLoop, calls=%fused_computation.69 | loop fusion | flops 81920 | bytes 393216 | tf_op jit(solution)/shard_map/stack | solution.py:148
  174.6 5.0 %fusion.40 = f32[1,8,16,128]{2,1,3,0:T(8,128)S(1)} fusion(f32[10,18,128]{1,0,2:T(8,128)} %get-tuple-element.36, f32[10,18,128]{1,0,2:T(8,128)} %get-tuple-element.16, f32[10,18,128]{1,0,2:T(8,128)} %get-tuple-element.15, f32[10,18,128]{1,0,2:T(8,128)} %get-tuple-element.25, f32[10,18,128]{1,0,2:T(8,128)} %get-tuple-element.23, ...), kind=kLoop, calls=%fused_computation.80 | loop fusion | flops 229376 | bytes 852096 | tf_op jit(solution)/shard_map/stack | solution.py:148
  180.8 39.0 %psum.15 = f32[64]{0:T(128)S(1)} all-reduce(f32[64]{0:T(128)S(1)} %convolution_bitcast_fusion), channel_id=1, replica_groups=mesh['az'=8,'ax'=4] {'az','ax'}, use_global_device_ids=true, to_apply=%region_3.4 | all-reduce | flops 64 | bytes 512 | tf_op jit(solution)/shard_map/psum | solution.py:219
  (121 shorter events, 46.7 us)
Async XLA Ops:
  0.6 10.1 %copy-start = (f32[64]{0:T(128)S(1)}, f32[64]{0:T(128)}, u32[]{:S(2)}) copy-start(f32[64]{0:T(128)} %param.13) | copy-start | bytes 772
  2.5 8.2 %copy-start.12 = (f32[4,8,16,128]{3,2,1,0:T(8,128)S(1)}, f32[4,8,16,128]{3,2,1,0:T(8,128)}, u32[]{:S(2)}) copy-start(f32[4,8,16,128]{3,2,1,0:T(8,128)} %param.12) | copy-start | bytes 786436
  3.5 7.6 %copy-start.16 = (s32[8,16]{1,0:T(8,128)S(1)}, s32[8,16]{1,0:T(8,128)}, u32[]{:S(2)}) copy-start(s32[8,16]{1,0:T(8,128)} %param.15) | copy-start | bytes 1540
  3.5 7.6 %copy-start.18 = (f32[64]{0:T(128)S(1)}, f32[64]{0:T(128)}, u32[]{:S(2)}) copy-start(f32[64]{0:T(128)} %param.16) | copy-start | bytes 772
  3.6 8.0 %copy-start.13 = (s32[512]{0:T(512)S(1)}, s32[512]{0:T(512)}, u32[]{:S(2)}) copy-start(s32[512]{0:T(512)} %param.18) | copy-start | bytes 6148
  3.6 8.0 %copy-start.14 = (s32[512]{0:T(512)S(1)}, s32[512]{0:T(512)}, u32[]{:S(2)}) copy-start(s32[512]{0:T(512)} %param.17) | copy-start | bytes 6148
  3.7 8.0 %collective-permute-start.1 = (f32[8,8,2,128]{3,1,2,0:T(8,128)S(1)}, f32[8,8,2,128]{3,1,2,0:T(8,128)S(1)}, u32[]{:S(2)}, u32[]{:S(2)}) collective-permute-start(f32[8,8,2,128]{3,1,2,0:T(8,128)S(1)} %copy.108), channel_id=1, source_target_pairs={{1,0},{2,1},{3,2},{5,4},{6,5},{7,6},{9,8},{10,9},{11,10},{13,12},{... | collective-permute-start | bytes 196616 | tf_op jit(solution)/shard_map/ppermute | solution.py:19
  5.0 9.3 %collective-permute-start = (f32[8,8,2,128]{3,1,2,0:T(8,128)S(1)}, f32[8,8,2,128]{3,1,2,0:T(8,128)S(1)}, u32[]{:S(2)}, u32[]{:S(2)}) collective-permute-start(f32[8,8,2,128]{3,1,2,0:T(8,128)S(1)} %copy.107), channel_id=1, source_target_pairs={{0,1},{1,2},{2,3},{4,5},{5,6},{6,7},{8,9},{9,10},{10,11},{12,13},{... | collective-permute-start | bytes 196616 | tf_op jit(solution)/shard_map/ppermute | solution.py:18
  30.1 10.5 %collective-permute-start.3 = (f32[8,2,20,128]{3,0,2,1:T(8,128)S(1)}, f32[8,2,20,128]{3,0,2,1:T(8,128)S(1)}, u32[]{:S(2)}, u32[]{:S(2)}) collective-permute-start(f32[8,2,20,128]{3,0,2,1:T(8,128)S(1)} %copy.84), channel_id=1, source_target_pairs={{4,0},{8,4},{12,8},{16,12},{20,16},{24,20},{28,24},{0,28},{5,1},{9... | collective-permute-start | bytes 491528 | tf_op jit(solution)/shard_map/ppermute | solution.py:19
  36.5 9.9 %collective-permute-start.2 = (f32[8,2,20,128]{3,0,2,1:T(8,128)S(1)}, f32[8,2,20,128]{3,0,2,1:T(8,128)S(1)}, u32[]{:S(2)}, u32[]{:S(2)}) collective-permute-start(f32[8,2,20,128]{3,0,2,1:T(8,128)S(1)} %copy.83), channel_id=1, source_target_pairs={{0,4},{4,8},{8,12},{12,16},{16,20},{20,24},{24,28},{28,0},{1,5},{5... | collective-permute-start | bytes 491528 | tf_op jit(solution)/shard_map/ppermute | solution.py:18
  65.7 57.5 %slice-start = ((f32[4,8,16,128]{3,2,1,0:T(8,128)}), f32[1,8,16,128]{3,2,1,0:T(8,128)S(1)}, s32[]{:S(2)}) async-start(f32[4,8,16,128]{3,2,1,0:T(8,128)} %param.10), calls=%async_computation | async-start | bytes 131072 | tf_op jit(solution)/shard_map/slice | solution.py:203
  112.7 4.3 %collective-permute-start.5 = (f32[1,8,1,128]{3,1,2,0:T(8,128)S(1)}, f32[1,8,1,128]{3,1,2,0:T(8,128)S(1)}, u32[]{:S(2)}, u32[]{:S(2)}) collective-permute-start(f32[1,8,1,128]{3,1,2,0:T(8,128)S(1)} %get-tuple-element.61), channel_id=1, source_target_pairs={{1,0},{2,1},{3,2},{5,4},{6,5},{7,6},{9,8},{10,9},{11,10},{13,12},{... | collective-permute-start | bytes 12296 | tf_op jit(solution)/shard_map/ppermute | solution.py:19
  114.0 3.8 %collective-permute-start.4 = (f32[1,8,1,128]{3,1,2,0:T(8,128)S(1)}, f32[1,8,1,128]{3,1,2,0:T(8,128)S(1)}, u32[]{:S(2)}, u32[]{:S(2)}) collective-permute-start(f32[1,8,1,128]{3,1,2,0:T(8,128)S(1)} %get-tuple-element.60), channel_id=1, source_target_pairs={{0,1},{1,2},{2,3},{4,5},{5,6},{6,7},{8,9},{9,10},{10,11},{12,13},{... | collective-permute-start | bytes 12296 | tf_op jit(solution)/shard_map/ppermute | solution.py:18
  118.0 6.4 %collective-permute-start.7 = (f32[1,1,18,128]{2,1,3,0:T(1,128)S(1)}, f32[1,1,18,128]{2,1,3,0:T(1,128)S(1)}, u32[]{:S(2)}, u32[]{:S(2)}) collective-permute-start(f32[1,1,18,128]{2,1,3,0:T(1,128)S(1)} %copy.89), channel_id=1, source_target_pairs={{4,0},{8,4},{12,8},{16,12},{20,16},{24,20},{28,24},{0,28},{5,1},{9... | collective-permute-start | bytes 27656 | tf_op jit(solution)/shard_map/ppermute | solution.py:19
  122.4 7.0 %collective-permute-start.6 = (f32[1,1,18,128]{2,1,3,0:T(1,128)S(1)}, f32[1,1,18,128]{2,1,3,0:T(1,128)S(1)}, u32[]{:S(2)}, u32[]{:S(2)}) collective-permute-start(f32[1,1,18,128]{2,1,3,0:T(1,128)S(1)} %copy.88), channel_id=1, source_target_pairs={{0,4},{4,8},{8,12},{12,16},{16,20},{20,24},{24,28},{28,0},{1,5},{5... | collective-permute-start | bytes 27656 | tf_op jit(solution)/shard_map/ppermute | solution.py:18
  124.4 9.1 %copy-start.9 = (f32[1,8,18,128]{2,1,3,0:T(8,128)}, f32[1,8,18,128]{2,1,3,0:T(8,128)S(1)}, u32[]{:S(2)}) copy-start(f32[1,8,18,128]{2,1,3,0:T(8,128)S(1)} %copy.90) | copy-start | bytes 221188
  135.9 7.5 %collective-permute-start.9 = (f32[3,8,1,128]{3,1,2,0:T(8,128)S(1)}, f32[3,8,1,128]{3,1,2,0:T(8,128)S(1)}, u32[]{:S(2)}, u32[]{:S(2)}) collective-permute-start(f32[3,8,1,128]{3,1,2,0:T(8,128)S(1)} %copy.95), channel_id=1, source_target_pairs={{1,0},{2,1},{3,2},{5,4},{6,5},{7,6},{9,8},{10,9},{11,10},{13,12},{... | collective-permute-start | bytes 36872 | tf_op jit(solution)/shard_map/ppermute | solution.py:19
  137.7 6.3 %collective-permute-start.8 = (f32[3,8,1,128]{3,1,2,0:T(8,128)S(1)}, f32[3,8,1,128]{3,1,2,0:T(8,128)S(1)}, u32[]{:S(2)}, u32[]{:S(2)}) collective-permute-start(f32[3,8,1,128]{3,1,2,0:T(8,128)S(1)} %copy.94), channel_id=1, source_target_pairs={{0,1},{1,2},{2,3},{4,5},{5,6},{6,7},{8,9},{9,10},{10,11},{12,13},{... | collective-permute-start | bytes 36872 | tf_op jit(solution)/shard_map/ppermute | solution.py:18
  144.6 13.6 %copy-start.4 = (f32[1,8,16,128]{2,1,3,0:T(8,128)S(1)}, f32[1,8,16,128]{2,1,3,0:T(8,128)}, u32[]{:S(2)}) copy-start(f32[1,8,16,128]{2,1,3,0:T(8,128)} %copy-done.3) | copy-start | bytes 196612
  144.6 13.6 %copy-start.6 = (f32[1,8,16,128]{2,1,3,0:T(8,128)S(1)}, f32[1,8,16,128]{2,1,3,0:T(8,128)}, u32[]{:S(2)}) copy-start(f32[1,8,16,128]{2,1,3,0:T(8,128)} %copy-done.5) | copy-start | bytes 196612
  144.6 13.6 %copy-start.8 = (f32[1,8,16,128]{2,1,3,0:T(8,128)S(1)}, f32[1,8,16,128]{2,1,3,0:T(8,128)}, u32[]{:S(2)}) copy-start(f32[1,8,16,128]{2,1,3,0:T(8,128)} %copy-done.7) | copy-start | bytes 196612
  148.4 6.6 %collective-permute-start.11 = (f32[3,1,18,128]{2,1,3,0:T(1,128)S(1)}, f32[3,1,18,128]{2,1,3,0:T(1,128)S(1)}, u32[]{:S(2)}, u32[]{:S(2)}) collective-permute-start(f32[3,1,18,128]{2,1,3,0:T(1,128)S(1)} %get-tuple-element.35), channel_id=1, source_target_pairs={{4,0},{8,4},{12,8},{16,12},{20,16},{24,20},{28,24},{0,28},{5,1},{9... | collective-permute-start | bytes 82952 | tf_op jit(solution)/shard_map/ppermute | solution.py:19
  148.8 9.4 %collective-permute-start.10 = (f32[3,1,18,128]{2,1,3,0:T(1,128)S(1)}, f32[3,1,18,128]{2,1,3,0:T(1,128)S(1)}, u32[]{:S(2)}, u32[]{:S(2)}) collective-permute-start(f32[3,1,18,128]{2,1,3,0:T(1,128)S(1)} %get-tuple-element.34), channel_id=1, source_target_pairs={{0,4},{4,8},{8,12},{12,16},{16,20},{20,24},{24,28},{28,0},{1,5},{5... | collective-permute-start | bytes 82952 | tf_op jit(solution)/shard_map/ppermute | solution.py:18
  174.6 46.4 %copy-start.1 = (f32[64]{0:T(128)S(1)}, f32[64]{0:T(128)}, u32[]{:S(2)}) copy-start(f32[64]{0:T(128)} %param.13) | copy-start | bytes 772
  (8 other events, 25.6 us)
where the time goes:
time: 223 us; the launch traced here: 222 us
  blocking collectives  76.2 us (34%)
  other arithmetic  66.1 us (30%)
  local copies, waits for them, and re-layouts  29.3 us (13%)
  starting transfers between devices  25.7 us (12%)
  waiting for transfers between devices  20.7 us (9%)
  between operations  3.07 us (1%)
    psum x1, blocking collectives, shards(): liner_grad = lax.psum(segment_sums, ('az', 'ax')) * grad_scale  39 us
    psum x1, blocking collectives, shards(): total_sq = lax.psum(square_sum, ('az', 'ax'))  37.3 us
    slice x2, other arithmetic, with_halo(): last = lax.slice_in_dim(array, length - width, length, axis=dim)  16.5 us
    ppermute x6, starting transfers between devices, with_halo(): after = lax.ppermute(initial, axis, down)  14.6 us
    ppermute x6, waiting for transfers between devices, with_halo(): before = lax.ppermute(last, axis, up)  14.1 us
    ppermute x6, starting transfers between devices, with_halo(): before = lax.ppermute(last, axis, up)  11.1 us
    another operation x4, other arithmetic, second_half(): jnp.stack([back_press, back_az, back_ax, back_rad])  10.7 us
    concatenate x3, other arithmetic, with_halo(): array = jnp.concatenate([before, array, after], axis=dim)  9.38 us
  transfers between devices with their start and end apart: 12, of which 6 were waited for; matrix products, arithmetic and copies ran while one was open for 7% of the time, Pallas kernels for 0%

commit v1 on v0

v1 whole, which is shorter than its diff:
```python
import jax
import jax.numpy as jnp
from jax import lax
from jax.sharding import PartitionSpec as P

step_dt = 0.25
epsilon = 1e-06


def with_halo(array, axis, dim, before, after, wrap):
    size, length = (lax.axis_size(axis), array.shape[dim])
    up = [(i, (i + 1) % size) for i in range(size if wrap else size - 1)]
    down = [(j, i) for i, j in up]
    parts = []
    if before:
        parts.append(lax.ppermute(lax.slice_in_dim(array, length - before, length, axis=dim), axis, up))
    parts.append(array)
    if after:
        parts.append(lax.ppermute(lax.slice_in_dim(array, 0, after, axis=dim), axis, down))
    return jnp.concatenate(parts, axis=dim)


def exchange(array, before, after):
    widened = with_halo(array, "ax", 2, before, after, False)
    return with_halo(widened, "az", 1, before, after, True)


def win(values, origin, da, dx, na, nx):
    a0, x0 = origin[0] + da, origin[1] + dx
    return values[a0 : a0 + na, x0 : x0 + nx]


def rad_next(values):
    return jnp.concatenate([values[..., 1:], jnp.zeros_like(values[..., :1])], axis=-1)


def rad_prev(values):
    return jnp.concatenate([jnp.zeros_like(values[..., :1]), values[..., :-1]], axis=-1)


def casing_mask(shape):
    return lax.broadcasted_iota(jnp.int32, shape, len(shape) - 1) == shape[-1] - 1


def advect_back(carried_ax, carried_az, na, nx):
    return 0.5 * (carried_ax[..., 1 : 1 + na, 0:nx] - carried_ax[..., 1 : 1 + na, 2 : 2 + nx]) + 0.5 * (
        carried_az[..., 0:na, 1 : 1 + nx] - carried_az[..., 2 : 2 + na, 1 : 1 + nx]
    )


def advect_back4(carried_ax, carried_az, na, nx):
    return 0.5 * (carried_ax[:, 1 : 1 + na, 0:nx, :] - carried_ax[:, 1 : 1 + na, 2 : 2 + nx, :]) + 0.5 * (
        carried_az[:, 0:na, 1 : 1 + nx, :] - carried_az[:, 2 : 2 + na, 1 : 1 + nx, :]
    )


def butterfly_sum(values, axes):
    for axis in axes:
        size = lax.axis_size(axis)
        if size & (size - 1):
            values = lax.psum(values, axis)
            continue
        step = 1
        while step < size:
            values = values + lax.ppermute(values, axis, [(i, i ^ step) for i in range(size)])
            step *= 2
    return values


def shards(
    acoustic,
    mean_flow,
    adjoint_in,
    admittance,
    segment_id,
    noise_code,
    noise_table,
    mic_az,
    mic_ax,
    measured,
):
    na, nx, nr = (acoustic.shape[1], acoustic.shape[2], acoustic.shape[3])
    nseg = admittance.shape[0]
    buoyancy = 1.0 / mean_flow[2]
    stiffness = mean_flow[2] * mean_flow[3] * mean_flow[3]
    axial_flow, swirl_flow = (mean_flow[0], mean_flow[1])

    segment_hot = segment_id[:, :, None] == lax.broadcasted_iota(jnp.int32, (1, 1, nseg), 2)
    wall = jnp.sum(jnp.where(segment_hot, admittance, 0.0), axis=2)
    noise_hot = noise_code[:, :, None] == lax.broadcasted_iota(jnp.int32, (1, 1, noise_table.shape[0]), 2)
    top_profile = (nr - 1 + 0.5) / nr
    source_top = jnp.sum(jnp.where(noise_hot, noise_table, 0.0), axis=2) * top_profile

    a0 = adjoint_in[0]
    push = -step_dt * stiffness * a0
    stack_f = jnp.stack([a0, adjoint_in[1], adjoint_in[2], adjoint_in[3], axial_flow, swirl_flow, buoyancy, push])
    top, below = nr - 1, nr - 2
    planes = [
        acoustic[0, :, :, top],
        acoustic[0, :, :, below],
        acoustic[1, :, :, top],
        acoustic[2, :, :, top],
        acoustic[3, :, :, below],
        axial_flow[:, :, top],
        axial_flow[:, :, below],
        swirl_flow[:, :, top],
        swirl_flow[:, :, below],
        buoyancy[:, :, top],
        buoyancy[:, :, below],
        stiffness[:, :, top],
        wall,
        source_top,
    ]
    stack_c = jnp.stack(planes)

    wide_f = exchange(stack_f, 1, 2)
    wide_c = exchange(stack_c, 3, 3)

    oc = (3, 3)
    p_t, p_b, va_t, vx_t, vr_b, u_t, u_b, w_t, w_b, b_t, b_b, s_t, wall_c, src_c = [wide_c[i] for i in range(14)]
    ea, ex = na + 3, nx + 3

    def c(f, da, dx, la, lx):
        return win(f, oc, da, dx, la, lx)

    def advect_c(f, u, w, da, dx, la, lx):
        return c(u, da, dx, la, lx) * (c(f, da, dx + 1, la, lx) - c(f, da, dx - 1, la, lx)) * 0.5 + c(
            w, da, dx, la, lx
        ) * (c(f, da + 1, dx, la, lx) - c(f, da - 1, dx, la, lx)) * 0.5

    new_az = c(va_t, -2, -1, ea + 1, ex) - step_dt * (
        advect_c(va_t, u_t, w_t, -2, -1, ea + 1, ex)
        + c(b_t, -2, -1, ea + 1, ex) * (c(p_t, -1, -1, ea + 1, ex) - c(p_t, -2, -1, ea + 1, ex))
    )
    new_ax = c(vx_t, -1, -2, ea, ex + 1) - step_dt * (
        advect_c(vx_t, u_t, w_t, -1, -2, ea, ex + 1)
        + c(b_t, -1, -2, ea, ex + 1) * (c(p_t, -1, -1, ea, ex + 1) - c(p_t, -1, -2, ea, ex + 1))
    )
    rad_top = c(wall_c, -1, -1, ea, ex) * c(p_t, -1, -1, ea, ex)
    rad_below = c(vr_b, -1, -1, ea, ex) - step_dt * (
        advect_c(vr_b, u_b, w_b, -1, -1, ea, ex)
        + c(b_b, -1, -1, ea, ex) * (c(p_t, -1, -1, ea, ex) - c(p_b, -1, -1, ea, ex))
    )
    spread = (new_az[1:] - new_az[:-1]) + (new_ax[:, 1:] - new_ax[:, :-1]) + (rad_top - rad_below)
    press_ring = (
        c(p_t, -1, -1, ea, ex)
        - step_dt * (advect_c(p_t, u_t, w_t, -1, -1, ea, ex) + c(s_t, -1, -1, ea, ex) * spread)
        + step_dt * c(src_c, -1, -1, ea, ex)
    )

    total_az = na * lax.axis_size("az")
    first_az = lax.axis_index("az") * na
    first_ax = lax.axis_index("ax") * nx
    ring_az = jnp.remainder(mic_az - first_az + 1, total_az)
    ring_ax = mic_ax - first_ax + 1
    on_ring = (ring_az < ea) & (ring_ax >= 0) & (ring_ax < ex)
    owned = (ring_az >= 1) & (ring_az <= na) & (ring_ax >= 1) & (ring_ax <= nx)
    ring_cell = jnp.where(on_ring, ring_az * ex + ring_ax, -1)
    cell_hot = ring_cell[:, None] == lax.broadcasted_iota(jnp.int32, (1, ea * ex), 1)
    heard = jnp.sum(jnp.where(cell_hot, press_ring.reshape(1, ea * ex), 0.0), axis=1)
    misses = heard - measured
    square_sum = jnp.sum(jnp.where(owned, misses * misses, 0.0))
    placed = jnp.sum(jnp.where(cell_hot, misses[:, None], 0.0), axis=0).reshape(ea, ex)

    push_e = -step_dt * c(s_t, -1, -1, ea, ex) * placed
    r1a, r1x = na + 2, nx + 2
    head_az_e = push_e[:r1a, :r1x] - push_e[1 : 1 + r1a, :r1x]
    head_ax_e = push_e[:r1a, :r1x] - push_e[:r1a, 1 : 1 + r1x]
    head_rad_e = -push_e[:r1a, :r1x]
    u_t1, w_t1 = c(u_t, -1, -1, r1a, r1x), c(w_t, -1, -1, r1a, r1x)
    u_b1, w_b1 = c(u_b, -1, -1, r1a, r1x), c(w_b, -1, -1, r1a, r1x)
    b_t1 = c(b_t, -1, -1, r1a, r1x)
    own_e = (slice(1, 1 + na), slice(1, 1 + nx))
    back_press_t = (
        placed[1 : 1 + na, 1 : 1 + nx]
        - step_dt * advect_back(u_t1 * placed[:r1a, :r1x], w_t1 * placed[:r1a, :r1x], na, nx)
    )
    shove_az = step_dt * b_t1 * head_az_e
    shove_ax = step_dt * b_t1 * head_ax_e
    b_b0, wall_0, push_0 = c(b_b, 0, 0, na, nx), c(wall_c, 0, 0, na, nx), push_e[own_e]
    back_press_t = (
        back_press_t
        + (shove_az[own_e] - shove_az[0:na, 1 : 1 + nx])
        + (shove_ax[own_e] - shove_ax[1 : 1 + na, 0:nx])
        + step_dt * b_b0 * push_0
        + wall_0 * push_0
    )
    back_press_b = -step_dt * b_b0 * push_0
    back_az_t = head_az_e[own_e] - step_dt * advect_back(u_t1 * head_az_e, w_t1 * head_az_e, na, nx)
    back_ax_t = head_ax_e[own_e] - step_dt * advect_back(u_t1 * head_ax_e, w_t1 * head_ax_e, na, nx)
    back_rad_b = head_rad_e[own_e] - step_dt * advect_back(u_b1 * head_rad_e, w_b1 * head_rad_e, na, nx)
    zero = jnp.zeros_like(back_press_b)
    extra = jnp.stack(
        [
            jnp.stack([back_press_b, back_press_t], axis=-1),
            jnp.stack([zero, back_az_t], axis=-1),
            jnp.stack([zero, back_ax_t], axis=-1),
            jnp.stack([back_rad_b, zero], axis=-1),
        ]
    )

    of = (1, 1)
    g_a0, g_a1, g_a2, g_a3, g_u, g_w, g_b, g_push = [wide_f[i] for i in range(8)]
    head_az = win(g_a1, of, -1, -1, r1a, r1x) + win(g_push, of, -1, -1, r1a, r1x) - win(g_push, of, 0, -1, r1a, r1x)
    head_ax = win(g_a2, of, -1, -1, r1a, r1x) + win(g_push, of, -1, -1, r1a, r1x) - win(g_push, of, -1, 0, r1a, r1x)
    push_1 = win(g_push, of, -1, -1, r1a, r1x)
    head_rad = win(g_a3, of, -1, -1, r1a, r1x) + push_1 - rad_next(push_1)
    casing = casing_mask(head_rad.shape)
    head_masked = jnp.where(casing, 0.0, head_rad)
    heads = jnp.stack([head_az, head_ax, head_masked])
    u1, w1, b1 = win(g_u, of, -1, -1, r1a, r1x), win(g_w, of, -1, -1, r1a, r1x), win(g_b, of, -1, -1, r1a, r1x)
    backs = heads[:, 1 : 1 + na, 1 : 1 + nx, :] - step_dt * advect_back4(u1 * heads, w1 * heads, na, nx)
    seed_1 = win(g_a0, of, -1, -1, r1a, r1x)
    back_press = (
        seed_1[1 : 1 + na, 1 : 1 + nx]
        - step_dt * advect_back4((u1 * seed_1)[None], (w1 * seed_1)[None], na, nx)[0]
    )
    shoves = step_dt * b1 * heads
    own = (slice(1, 1 + na), slice(1, 1 + nx))
    shove_r = shoves[2][own]
    back_press = (
        back_press
        + (shoves[0][own] - shoves[0][0:na, 1 : 1 + nx])
        + (shoves[1][own] - shoves[1][1 : 1 + na, 0:nx])
        + (shove_r - rad_prev(shove_r))
    )
    head_rad_own = head_rad[own]
    back_press = back_press + jnp.where(casing_mask(head_rad_own.shape), wall[:, :, None] * head_rad_own, 0.0)
    base = jnp.concatenate([back_press[None], backs], axis=0)

    press_top = acoustic[0, :, :, top]
    sens_base = press_top * head_rad_own[:, :, top]
    sens_placed = press_top * push_0
    seg_base = jnp.sum(jnp.where(segment_hot, sens_base[:, :, None], 0.0), axis=(0, 1))
    seg_placed = jnp.sum(jnp.where(segment_hot, sens_placed[:, :, None], 0.0), axis=(0, 1))

    totals = butterfly_sum(jnp.concatenate([square_sum[None], seg_base, seg_placed]), ("ax", "az"))
    mean_sq = totals[0] / mic_az.shape[0] + epsilon
    grad_scale = (na * lax.axis_size("az") * nx * lax.axis_size("ax") / nseg) ** (-0.5)
    liner_grad = (totals[1 : 1 + nseg] + totals[1 + nseg :] / mean_sq) * grad_scale
    misfit = 0.5 * jnp.log(mean_sq)
    adjoint_out = jnp.concatenate([base[..., : nr - 2], base[..., nr - 2 :] + extra / mean_sq], axis=-1)
    return (adjoint_out, liner_grad, misfit)


def solution(mesh):
    placed = (
        P(None, "az", "ax", None),
        P(None, "az", "ax", None),
        P(None, "az", "ax", None),
        P(),
        P("az", "ax"),
        P("az", "ax"),
        P(),
        P(),
        P(),
        P(),
    )
    return jax.shard_map(
        shards,
        mesh=mesh,
        in_specs=placed,
        out_specs=(P(None, "az", "ax", None), P(), P()),
        check_vma=False,
    )
```

time: 223 us -> 128 us (0.57)
  blocking collectives: 76.2 us -> 0 us
  other arithmetic: 66.1 us -> 48.3 us
  starting transfers between devices: 25.7 us -> 21.1 us
  waiting for transfers between devices: 20.7 us -> 24.5 us
    psum x2 -> x0, blocking collectives: 76.2 us -> none  [the longest x1 39 us: shards(): liner_grad = lax.psum(segment_sums, ('az', 'ax')) * grad_scale]
    slice x16 -> x13, local copies, waits for them, and re-layouts: 4.22 us -> 17.7 us  [the longest x4 8.9 us: with_halo(): lax.slice_in_dim(array, length - before, length, axis=dim)]
    mul x7 -> x5, other arithmetic: 14.8 us -> 4.41 us  [the longest x1 3.58 us: shards(): shoves = step_dt * b1 * heads]
    slice x2, other arithmetic: 16.5 us -> 6.75 us  [the longest x1 6.57 us: with_halo(): lax.slice_in_dim(array, length - before, length, axis=dim)]
    concatenate x4 -> x7, other arithmetic: 10.4 us -> 19.1 us  [the longest x4 16 us: with_halo(): return jnp.concatenate(parts, axis=dim)]
    another operation x6 -> x7, other arithmetic: 11.3 us -> 6.49 us  [the longest x1 3.47 us: shards(): jnp.stack([a0, adjoint_in[1], adjoint_in[2], adjoint_in[3], axial_flow, s...]
    ppermute x12 -> x13, starting transfers between devices: 25.7 us -> 21.1 us  [the longest x4 10.8 us: with_halo(): lax.ppermute(lax.slice_in_dim(array, 0, after, axis=dim), axis, down)]
    squeeze x3, local copies, waits for them, and re-layouts: 4.93 us -> 0.76 us  [the longest x1 0.54 us: shards(): wide_f[i]]
  transfers between devices with their start and end apart: 12 -> 13, of which waited for: 6 -> 6; matrix products, arithmetic and copies ran while one was open for 7% -> 36% of each run, Pallas kernels for 0% -> 0%
where the time goes in v1:
time: 128 us; the launch traced here: 127 us
  other arithmetic  48.3 us (38%)
  local copies, waits for them, and re-layouts  30.5 us (24%)
  waiting for transfers between devices  24.5 us (19%)
  starting transfers between devices  21.1 us (16%)
  between operations  3 us (2%)
    ppermute x4, waiting for transfers between devices, with_halo(): lax.ppermute(lax.slice_in_dim(array, length - before, length, axis=dim),...  16.6 us
    concatenate x4, other arithmetic, with_halo(): return jnp.concatenate(parts, axis=dim)  16 us
    ppermute x4, starting transfers between devices, with_halo(): lax.ppermute(lax.slice_in_dim(array, 0, after, axis=dim), axis, down)  10.8 us
    ppermute x4, starting transfers between devices, with_halo(): lax.ppermute(lax.slice_in_dim(array, length - before, length, axis=dim),...  10.3 us
    slice x4, local copies, waits for them, and re-layouts, with_halo(): lax.slice_in_dim(array, length - before, length, axis=dim)  8.9 us
    ppermute x5, waiting for transfers between devices, butterfly_sum(): lax.ppermute(values, axis, [(i, i ^ step) for i in range(size)])  7.94 us
    slice x1, other arithmetic, with_halo(): lax.slice_in_dim(array, length - before, length, axis=dim)  6.57 us
    slice x2, local copies, waits for them, and re-layouts, with_halo(): lax.slice_in_dim(array, 0, after, axis=dim)  4.41 us
  transfers between devices with their start and end apart: 13, of which 6 were waited for; matrix products, arithmetic and copies ran while one was open for 36% of the time, Pallas kernels for 0%

profile of v1, /device:TPU:0, one launch (start us, length us, event | category | flops | bytes accessed | tf_op | source)
XLA Modules:
  0.0 127.4 jit_solution(9963920087095430910)
XLA Ops:
  6.4 2.3 %collective-permute-start.4 = (f32[14,8,3]{2,1,0:T(8,128)}, f32[14,8,3]{2,1,0:T(8,128)S(1)}, u32[]{:S(2)}, u32[]{:S(2)}) collective-permute-start(f32[14,8,3]{2,1,0:T(8,128)} %get-tuple-element.68), channel_id=1, source_target_pairs={{0,1},{1,2},{2,3},{4,5},{5,6},{6,7},{8,9},{9,10},{10,11},{12,13},{... | collective-permute-start | bytes 4040 | tf_op jit(solution)/shard_map/ppermute | solution.py:16
  13.3 3.5 %pad_maximum_fusion.1 = f32[8,8,16,128]{2,1,3,0:T(8,128)} fusion(f32[1,8,16,128]{2,1,3,0:T(8,128)} %copy.103, f32[1,8,16,128]{2,1,3,0:T(8,128)} %copy.102, f32[2,8,16,128]{2,1,3,0:T(8,128)S(1)} %copy.101, f32[4,8,16,128]{2,1,3,0:T(8,128)S(1)} %copy.100), kind=kLoop, calls=%fused_computation.1 | loop fusion | flops 393216 | bytes 1048576 | tf_op jit(solution)/shard_map/stack | solution.py:96
  16.7 2.8 %copy.105 = f32[8,8,2,128]{3,1,2,0:T(8,128)S(1)} copy(f32[8,8,2,128]{2,1,3,0:T(8,128)} %bitcast.139) | data formatting | bytes 131072 | tf_op jit(solution)/shard_map/slice | solution.py:19
  20.9 5.3 %slice.677 = f32[8,8,1,128]{2,1,3,0:T(8,128)} slice(f32[8,8,16,128]{2,1,3,0:T(8,128)} %pad_maximum_fusion.1), slice={[0:8], [0:8], [15:16], [0:128]} | slice | bytes 65536 | tf_op jit(solution)/shard_map/slice | solution.py:16
  26.2 2.9 %copy.104 = f32[8,8,1,128]{3,1,2,0:T(8,128)S(1)} copy(f32[8,8,1,128]{2,1,3,0:T(8,128)} %slice.677) | data formatting | bytes 65536 | tf_op jit(solution)/shard_map/slice | solution.py:16
  29.0 6.4 %collective-permute-start = (f32[8,8,1,128]{3,1,2,0:T(8,128)S(1)}, f32[8,8,1,128]{3,1,2,0:T(8,128)}, u32[]{:S(2)}, u32[]{:S(2)}) collective-permute-start(f32[8,8,1,128]{3,1,2,0:T(8,128)S(1)} %copy.104), channel_id=1, source_target_pairs={{0,1},{1,2},{2,3},{4,5},{5,6},{6,7},{8,9},{9,10},{10,11},{12,13},{... | collective-permute-start | bytes 98312 | tf_op jit(solution)/shard_map/ppermute | solution.py:16
  36.3 1.6 %collective-permute-start.6 = (f32[14,3,22]{2,1,0:T(4,128)S(1)}, f32[14,3,22]{2,1,0:T(4,128)S(1)}, u32[]{:S(2)}, u32[]{:S(2)}) collective-permute-start(f32[14,3,22]{2,1,0:T(4,128)S(1)} %get-tuple-element.66), channel_id=1, source_target_pairs={{0,4},{4,8},{8,12},{12,16},{16,20},{20,24},{24,28},{28,0},{1,5},{5... | collective-permute-start | bytes 11096 | tf_op jit(solution)/shard_map/ppermute | solution.py:16
  37.8 3.2 %collective-permute-start.7 = (f32[14,3,22]{2,1,0:T(4,128)S(1)}, f32[14,3,22]{2,1,0:T(4,128)S(1)}, u32[]{:S(2)}, u32[]{:S(2)}) collective-permute-start(f32[14,3,22]{2,1,0:T(4,128)S(1)} %get-tuple-element.67), channel_id=1, source_target_pairs={{4,0},{8,4},{12,8},{16,12},{20,16},{24,20},{28,24},{0,28},{5,1},{9... | collective-permute-start | bytes 11096 | tf_op jit(solution)/shard_map/ppermute | solution.py:19
  46.2 3.3 %copy.106 = f32[8,8,1,128]{2,1,3,0:T(8,128)} copy(f32[8,8,1,128]{3,1,2,0:T(8,128)} %collective-permute-done) | data formatting | bytes 65536 | tf_op jit(solution)/shard_map/ppermute | solution.py:16
  49.6 2.7 %copy.107 = f32[8,8,2,128]{2,1,3,0:T(8,128)} copy(f32[8,8,2,128]{3,1,2,0:T(8,128)S(1)} %collective-permute-done.1) | data formatting | bytes 131072 | tf_op jit(solution)/shard_map/ppermute | solution.py:19
  52.2 6.6 %pad_maximum_fusion.3 = f32[8,2,19,128]{2,1,3,0:T(2,128)} fusion(f32[8,8,2,128]{2,1,3,0:T(8,128)} %copy.107, f32[8,8,1,128]{2,1,3,0:T(8,128)} %copy.106, f32[1,8,16,128]{2,1,3,0:T(8,128)} %copy.103, f32[1,8,16,128]{2,1,3,0:T(8,128)} %copy.102, f32[2,8,16,128]{2,1,3,0:T(8,128)S(1)} %copy.101, f32[4,8,16,128]{2,1,3,0:T(8,128)S(1)} %copy.100), kind=kLoop, calls=%fused_computation.34 | loop fusion | flops 194560 | bytes 778240 | tf_op jit(solution)/shard_map/concatenate | solution.py:20
  58.9 1.6 %copy.108 = f32[8,2,19,128]{3,0,2,1:T(8,128)S(1)} copy(f32[8,2,19,128]{2,1,3,0:T(2,128)} %pad_maximum_fusion.3) | data formatting | bytes 311296 | tf_op jit(solution)/shard_map/slice | solution.py:19
  60.4 5.0 %collective-permute-start.3 = (f32[8,2,19,128]{3,0,2,1:T(8,128)S(1)}, f32[8,2,19,128]{3,0,2,1:T(8,128)S(1)}, u32[]{:S(2)}, u32[]{:S(2)}) collective-permute-start(f32[8,2,19,128]{3,0,2,1:T(8,128)S(1)} %copy.108), channel_id=1, source_target_pairs={{4,0},{8,4},{12,8},{16,12},{20,16},{24,20},{28,24},{0,28},{5,1},{9... | collective-permute-start | bytes 466952 | tf_op jit(solution)/shard_map/ppermute | solution.py:19
  65.4 6.6 %pad_maximum_fusion.8 = f32[8,1,19,128]{2,1,3,0:T(1,128)} fusion(f32[8,8,2,128]{2,1,3,0:T(8,128)} %copy.107, f32[8,8,1,128]{2,1,3,0:T(8,128)} %copy.106, f32[1,8,16,128]{2,1,3,0:T(8,128)} %copy.103, f32[1,8,16,128]{2,1,3,0:T(8,128)} %copy.102, f32[2,8,16,128]{2,1,3,0:T(8,128)S(1)} %copy.101, f32[4,8,16,128]{2,1,3,0:T(8,128)S(1)} %copy.100), kind=kLoop, calls=%fused_computation.58 | loop fusion | flops 97280 | bytes 700416 | tf_op jit(solution)/shard_map/slice | solution.py:16
  73.5 15.2 %collective-permute-done.2 = f32[8,1,19,128]{2,1,3,0:T(1,128)} collective-permute-done((f32[8,1,19,128]{2,1,3,0:T(1,128)}, f32[8,1,19,128]{2,1,3,0:T(1,128)}, u32[]{:S(2)}, u32[]{:S(2)}) %collective-permute-start.2) | collective-permute-done | bytes 77856 | tf_op jit(solution)/shard_map/ppermute | solution.py:16
  88.7 9.2 %pad_maximum_fusion = f32[8,11,19,128]{2,1,3,0:T(8,128)S(1)} fusion(f32[8,2,19,128]{2,1,3,0:T(2,128)} %copy.109, f32[8,8,2,128]{2,1,3,0:T(8,128)} %copy.107, f32[1,8,16,128]{2,1,3,0:T(8,128)} %copy.103, f32[1,8,16,128]{2,1,3,0:T(8,128)} %copy.102, f32[2,8,16,128]{2,1,3,0:T(8,128)S(1)} %copy.101, f32[4,8,16,128]{2,1,3,0:T(8,128)S(1)} %copy.100, ...), kind=kLoop, calls=%fused_computation | loop fusion | flops 1498112 | bytes 1712128 | tf_op jit(solution)/shard_map/concatenate | solution.py:20
  98.5 2.2 %fusion.6 = (f32[1,10,18,128]{2,1,3,0:T(8,128)S(1)}, f32[1,10,18,128]{2,1,3,0:T(8,128)}, f32[1,10,18,128]{2,1,3,0:T(8,128)}, f32[10,18,128]{1,0,2:T(8,128)S(1)}, f32[10,18,128]{1,0,2:T(8,128)}) fusion(f32[11,19,128]{1,0,2:T(8,128)S(1)} %get-tuple-element.21, f32[11,19,128]{1,0,2:T(8,128)S(1)} %get-tuple-element.22, f32[11,19,128]{1,0,2:T(8,128)S(1)} %get-tuple-element.20, ...), kind=kLoop, calls=%fused_computation.25 | loop fusion | flops 184320 | bytes 1197488 | tf_op jit(solution)/shard_map/stack | solution.py:210
  101.7 2.1 %multiply_bitcast_fusion.1 = (f32[1,10,18,128]{2,1,3,0:T(8,128)}, f32[10,18,128]{1,0,2:T(8,128)}, f32[1,10,18,128]{2,1,3,0:T(8,128)}, f32[10,18,128]{1,0,2:T(8,128)}) fusion(f32[11,19,128]{1,0,2:T(8,128)S(1)} %get-tuple-element.18, f32[11,19,128]{1,0,2:T(8,128)S(1)} %get-tuple-element.25, f32[11,19,128]{1,0,2:T(8,128)S(1)} %get-tuple-element.24), kind=kLoop, calls=%fused_computation.41 | loop fusion | flops 46080 | bytes 645120 | tf_op jit(solution)/shard_map/broadcast_in_dim | solution.py:216
  103.8 3.6 %broadcast_multiply_fusion.2 = (f32[3,10,18,128]{2,1,3,0:T(8,128)S(1)}, f32[3,10,18,128]{2,1,3,0:T(8,128)S(1)}, f32[3,10,18,128]{2,1,3,0:T(8,128)S(1)}, f32[3,10,18,128]{2,1,3,0:T(8,128)S(1)}) fusion(f32[10,18,128]{1,0,2:T(8,128)} %get-tuple-element.84, f32[1,10,18,128]{2,1,3,0:T(8,128)} %get-tuple-element.39, f32[1,10,18,128]{2,1,3,0:T(8,128)} %get-tuple-element.38, ...), kind=kLoop, calls=%fused_computation.13 | loop fusion | flops 345600 | bytes 1658880 | tf_op jit(solution)/shard_map/mul | solution.py:218
  108.2 1.7 %fusion.3 = f32[3,8,16,128]{2,1,3,0:T(8,128)S(1)} fusion(f32[3,10,18,128]{2,1,3,0:T(8,128)S(1)} %get-tuple-element.31, f32[3,10,18,128]{2,1,3,0:T(8,128)S(1)} %get-tuple-element.30, f32[3,10,18,128]{2,1,3,0:T(8,128)S(1)} %get-tuple-element.32), kind=kLoop, calls=%fused_computation.9 | loop fusion | flops 245760 | bytes 1179648 | tf_op jit(solution)/shard_map/sub | solution.py:212
  109.9 1.9 %collective-permute-done.9 = f32[129]{0:T(256)S(1)} collective-permute-done((f32[129]{0:T(256)S(1)}, f32[129]{0:T(256)S(1)}, u32[]{:S(2)}, u32[]{:S(2)}) %collective-permute-start.9) | collective-permute-done | bytes 548 | tf_op jit(solution)/shard_map/ppermute | solution.py:65
  112.2 3.1 %collective-permute-done.10 = f32[129]{0:T(256)S(1)} collective-permute-done((f32[129]{0:T(256)S(1)}, f32[129]{0:T(256)S(1)}, u32[]{:S(2)}, u32[]{:S(2)}) %collective-permute-start.10) | collective-permute-done | bytes 548 | tf_op jit(solution)/shard_map/ppermute | solution.py:65
  116.8 2.1 %collective-permute-done.11 = f32[129]{0:T(256)S(1)} collective-permute-done((f32[129]{0:T(256)S(1)}, f32[129]{0:T(256)S(1)}, u32[]{:S(2)}, u32[]{:S(2)}) %collective-permute-start.11) | collective-permute-done | bytes 548 | tf_op jit(solution)/shard_map/ppermute | solution.py:65
  120.4 2.2 %copy.117 = f32[4,8,16,126]{3,2,1,0:T(8,128)S(1)} copy(f32[4,8,16,126]{2,1,3,0:T(8,128)} %fusion) | data formatting | bytes 516096 | tf_op jit(solution)/shard_map/slice | solution.py:242
  (121 shorter events, 27.4 us)
Async XLA Ops:
  0.6 9.5 %copy-start.4 = (f32[4,8,16,128]{3,2,1,0:T(8,128)S(1)}, f32[4,8,16,128]{3,2,1,0:T(8,128)}, u32[]{:S(2)}) copy-start(f32[4,8,16,128]{3,2,1,0:T(8,128)} %param.12) | copy-start | bytes 786436
  0.6 4.5 %copy-start.6 = (s32[8,16]{1,0:T(8,128)S(1)}, s32[8,16]{1,0:T(8,128)}, u32[]{:S(2)}) copy-start(s32[8,16]{1,0:T(8,128)} %param.14) | copy-start | bytes 1540
  0.7 4.5 %copy-start.11 = (f32[64]{0:T(128)S(1)}, f32[64]{0:T(128)}, u32[]{:S(2)}) copy-start(f32[64]{0:T(128)} %param.13) | copy-start | bytes 772
  0.7 4.6 %copy-start.12 = (f32[64]{0:T(128)S(1)}, f32[64]{0:T(128)}, u32[]{:S(2)}) copy-start(f32[64]{0:T(128)} %param.16) | copy-start | bytes 772
  0.7 4.6 %copy-start.9 = (s32[8,16]{1,0:T(8,128)S(1)}, s32[8,16]{1,0:T(8,128)}, u32[]{:S(2)}) copy-start(s32[8,16]{1,0:T(8,128)} %param.15) | copy-start | bytes 1540
  3.4 9.5 %slice-start = ((f32[4,8,16,128]{3,2,1,0:T(8,128)}), f32[2,8,16,128]{3,2,1,0:T(8,128)S(1)}, s32[]{:S(2)}) async-start(f32[4,8,16,128]{3,2,1,0:T(8,128)} %param.11), calls=%async_computation | async-start | bytes 262144 | tf_op jit(solution)/shard_map/slice | solution.py:86
  6.4 29.7 %collective-permute-start.4 = (f32[14,8,3]{2,1,0:T(8,128)}, f32[14,8,3]{2,1,0:T(8,128)S(1)}, u32[]{:S(2)}, u32[]{:S(2)}) collective-permute-start(f32[14,8,3]{2,1,0:T(8,128)} %get-tuple-element.68), channel_id=1, source_target_pairs={{0,1},{1,2},{2,3},{4,5},{5,6},{6,7},{8,9},{9,10},{10,11},{12,13},{... | collective-permute-start | bytes 4040 | tf_op jit(solution)/shard_map/ppermute | solution.py:16
  8.8 27.3 %collective-permute-start.5 = (f32[14,8,3]{2,1,0:T(8,128)S(1)}, f32[14,8,3]{2,1,0:T(8,128)S(1)}, u32[]{:S(2)}, u32[]{:S(2)}) collective-permute-start(f32[14,8,3]{2,1,0:T(8,128)S(1)} %get-tuple-element.69), channel_id=1, source_target_pairs={{1,0},{2,1},{3,2},{5,4},{6,5},{7,6},{9,8},{10,9},{11,10},{13,12},{... | collective-permute-start | bytes 4040 | tf_op jit(solution)/shard_map/ppermute | solution.py:19
  19.6 30.0 %collective-permute-start.1 = (f32[8,8,2,128]{3,1,2,0:T(8,128)S(1)}, f32[8,8,2,128]{3,1,2,0:T(8,128)S(1)}, u32[]{:S(2)}, u32[]{:S(2)}) collective-permute-start(f32[8,8,2,128]{3,1,2,0:T(8,128)S(1)} %copy.105), channel_id=1, source_target_pairs={{1,0},{2,1},{3,2},{5,4},{6,5},{7,6},{9,8},{10,9},{11,10},{13,12},{... | collective-permute-start | bytes 196616 | tf_op jit(solution)/shard_map/ppermute | solution.py:19
  26.2 9.2 %copy-start.8 = (s32[512]{0:T(512)S(1)}, s32[512]{0:T(512)}, u32[]{:S(2)}) copy-start(s32[512]{0:T(512)} %param.18) | copy-start | bytes 6148
  29.0 17.1 %collective-permute-start = (f32[8,8,1,128]{3,1,2,0:T(8,128)S(1)}, f32[8,8,1,128]{3,1,2,0:T(8,128)}, u32[]{:S(2)}, u32[]{:S(2)}) collective-permute-start(f32[8,8,1,128]{3,1,2,0:T(8,128)S(1)} %copy.104), channel_id=1, source_target_pairs={{0,1},{1,2},{2,3},{4,5},{5,6},{6,7},{8,9},{9,10},{10,11},{12,13},{... | collective-permute-start | bytes 98312 | tf_op jit(solution)/shard_map/ppermute | solution.py:16
  36.3 6.6 %collective-permute-start.6 = (f32[14,3,22]{2,1,0:T(4,128)S(1)}, f32[14,3,22]{2,1,0:T(4,128)S(1)}, u32[]{:S(2)}, u32[]{:S(2)}) collective-permute-start(f32[14,3,22]{2,1,0:T(4,128)S(1)} %get-tuple-element.66), channel_id=1, source_target_pairs={{0,4},{4,8},{8,12},{12,16},{16,20},{20,24},{24,28},{28,0},{1,5},{5... | collective-permute-start | bytes 11096 | tf_op jit(solution)/shard_map/ppermute | solution.py:16
  37.8 5.1 %collective-permute-start.7 = (f32[14,3,22]{2,1,0:T(4,128)S(1)}, f32[14,3,22]{2,1,0:T(4,128)S(1)}, u32[]{:S(2)}, u32[]{:S(2)}) collective-permute-start(f32[14,3,22]{2,1,0:T(4,128)S(1)} %get-tuple-element.67), channel_id=1, source_target_pairs={{4,0},{8,4},{12,8},{16,12},{20,16},{24,20},{28,24},{0,28},{5,1},{9... | collective-permute-start | bytes 11096 | tf_op jit(solution)/shard_map/ppermute | solution.py:19
  60.4 11.6 %collective-permute-start.3 = (f32[8,2,19,128]{3,0,2,1:T(8,128)S(1)}, f32[8,2,19,128]{3,0,2,1:T(8,128)S(1)}, u32[]{:S(2)}, u32[]{:S(2)}) collective-permute-start(f32[8,2,19,128]{3,0,2,1:T(8,128)S(1)} %copy.108), channel_id=1, source_target_pairs={{4,0},{8,4},{12,8},{16,12},{20,16},{24,20},{28,24},{0,28},{5,1},{9... | collective-permute-start | bytes 466952 | tf_op jit(solution)/shard_map/ppermute | solution.py:19
  72.0 16.7 %collective-permute-start.2 = (f32[8,1,19,128]{2,1,3,0:T(1,128)}, f32[8,1,19,128]{2,1,3,0:T(1,128)}, u32[]{:S(2)}, u32[]{:S(2)}) collective-permute-start(f32[8,1,19,128]{2,1,3,0:T(1,128)} %pad_maximum_fusion.8), channel_id=1, source_target_pairs={{0,4},{4,8},{8,12},{12,16},{16,20},{20,24},{24,28},{28,0},{1,5},{5... | collective-permute-start | bytes 233480 | tf_op jit(solution)/shard_map/ppermute | solution.py:16
  100.7 3.1 %copy-start.2 = (f32[10,18,128]{1,0,2:T(8,128)}, f32[10,18,128]{1,0,2:T(8,128)S(1)}, u32[]{:S(2)}) copy-start(f32[10,18,128]{1,0,2:T(8,128)S(1)} %get-tuple-element.40) | copy-start | bytes 276484
  101.7 5.8 %collective-permute-start.8 = (f32[129]{0:T(256)S(1)}, f32[129]{0:T(256)S(1)}, u32[]{:S(2)}, u32[]{:S(2)}) collective-permute-start(f32[129]{0:T(256)S(1)} %pad_maximum_fusion.13), channel_id=1, source_target_pairs={{0,1},{1,0},{2,3},{3,2},{4,5},{5,4},{6,7},{7,6},{8,9},{9,8},{10,11... | collective-permute-start | bytes 1556 | tf_op jit(solution)/shard_map/ppermute | solution.py:65
  108.2 3.6 %collective-permute-start.9 = (f32[129]{0:T(256)S(1)}, f32[129]{0:T(256)S(1)}, u32[]{:S(2)}, u32[]{:S(2)}) collective-permute-start(f32[129]{0:T(256)S(1)} %fusion.86), channel_id=1, source_target_pairs={{0,2},{1,3},{2,0},{3,1},{4,6},{5,7},{6,4},{7,5},{8,10},{9,11},{10,... | collective-permute-start | bytes 1556 | tf_op jit(solution)/shard_map/ppermute | solution.py:65
  111.7 3.6 %collective-permute-start.10 = (f32[129]{0:T(256)S(1)}, f32[129]{0:T(256)S(1)}, u32[]{:S(2)}, u32[]{:S(2)}) collective-permute-start(f32[129]{0:T(256)S(1)} %add.161), channel_id=1, source_target_pairs={{0,4},{4,0},{8,12},{12,8},{16,20},{20,16},{24,28},{28,24},{1,5},{5... | collective-permute-start | bytes 1556 | tf_op jit(solution)/shard_map/ppermute | solution.py:65
  111.7 3.6 %copy-start = (f32[1,10,18,128]{2,1,3,0:T(8,128)S(1)}, f32[1,10,18,128]{2,1,3,0:T(8,128)}, u32[]{:S(2)}) copy-start(f32[1,10,18,128]{2,1,3,0:T(8,128)} %get-tuple-element.33) | copy-start | bytes 276484
  111.8 3.6 %copy-start.1 = (f32[1,10,18,128]{2,1,3,0:T(8,128)S(1)}, f32[1,10,18,128]{2,1,3,0:T(8,128)}, u32[]{:S(2)}) copy-start(f32[1,10,18,128]{2,1,3,0:T(8,128)} %get-tuple-element.35) | copy-start | bytes 276484
  111.8 3.6 %copy-start.3 = (f32[10,18,128]{1,0,2:T(8,128)S(1)}, f32[10,18,128]{1,0,2:T(8,128)}, u32[]{:S(2)}) copy-start(f32[10,18,128]{1,0,2:T(8,128)} %copy-done.2) | copy-start | bytes 276484
  115.3 3.6 %collective-permute-start.11 = (f32[129]{0:T(256)S(1)}, f32[129]{0:T(256)S(1)}, u32[]{:S(2)}, u32[]{:S(2)}) collective-permute-start(f32[129]{0:T(256)S(1)} %add.162), channel_id=1, source_target_pairs={{0,8},{4,12},{8,0},{12,4},{16,24},{20,28},{24,16},{28,20},{1,9},{5... | collective-permute-start | bytes 1556 | tf_op jit(solution)/shard_map/ppermute | solution.py:65
  118.9 4.5 %collective-permute-start.12 = (f32[129]{0:T(256)S(1)}, f32[129]{0:T(256)S(1)}, u32[]{:S(2)}, u32[]{:S(2)}) collective-permute-start(f32[129]{0:T(256)S(1)} %add.163), channel_id=1, source_target_pairs={{0,16},{4,20},{8,24},{12,28},{16,0},{20,4},{24,8},{28,12},{1,17},{... | collective-permute-start | bytes 1556 | tf_op jit(solution)/shard_map/ppermute | solution.py:65
  (3 other events, 5.2 us)

commit v2 on v1

--- a/solution.py
+++ b/solution.py
@@ -20,8 +20,10 @@
     return jnp.concatenate(parts, axis=dim)
 
 
-def exchange(array, before, after):
-    widened = with_halo(array, "ax", 2, before, after, False)
+def exchange(array, before, after, ax_before=None, ax_after=None):
+    ax_before = before if ax_before is None else ax_before
+    ax_after = after if ax_after is None else ax_after
+    widened = with_halo(array, "ax", 2, ax_before, ax_after, False)
     return with_halo(widened, "az", 1, before, after, True)
 
 
@@ -113,7 +115,8 @@
     ]
     stack_c = jnp.stack(planes)
 
-    wide_f = exchange(stack_f, 1, 2)
+    tile = 8
+    wide_f = exchange(stack_f, 1, 2, tile, tile)
     wide_c = exchange(stack_c, 3, 3)
 
     oc = (3, 3)
@@ -199,7 +202,7 @@
         ]
     )
 
-    of = (1, 1)
+    of = (1, tile)
     g_a0, g_a1, g_a2, g_a3, g_u, g_w, g_b, g_push = [wide_f[i] for i in range(8)]
     head_az = win(g_a1, of, -1, -1, r1a, r1x) + win(g_push, of, -1, -1, r1a, r1x) - win(g_push, of, 0, -1, r1a, r1x)
     head_ax = win(g_a2, of, -1, -1, r1a, r1x) + win(g_push, of, -1, -1, r1a, r1x) - win(g_push, of, -1, 0, r1a, r1x)

time: 128 us -> 82.1 us (0.64)
  other arithmetic: 48.3 us -> 22 us
  local copies, waits for them, and re-layouts: 30.5 us -> 17.2 us
  waiting for transfers between devices: 24.5 us -> 16.9 us
  starting transfers between devices: 21.1 us -> 22.6 us
    concatenate x4, other arithmetic: 16 us -> 0.4 us  [with_halo(): return jnp.concatenate(parts, axis=dim)]
    slice x4 -> x3, local copies, waits for them, and re-layouts: 8.9 us -> 0.14 us  [with_halo(): lax.slice_in_dim(array, length - before, length, axis=dim)]
    ppermute x3 -> x0, local copies, waits for them, and re-layouts: 7.47 us -> none  [the longest x2 4.12 us: with_halo(): lax.ppermute(lax.slice_in_dim(array, 0, after, axis=dim), axis, down)]
    unnamed x47 -> x53, local copies, waits for them, and re-layouts: 1.88 us -> 9.23 us
    slice x1, other arithmetic: 6.57 us -> 0.01 us  [with_halo(): lax.slice_in_dim(array, length - before, length, axis=dim)]
    ppermute x4, waiting for transfers between devices: 16.6 us -> 10.8 us  [with_halo(): lax.ppermute(lax.slice_in_dim(array, length - before, length, axis=dim),...]
    slice x2 -> x1, local copies, waits for them, and re-layouts: 4.41 us -> 0.11 us  [shards(): wide_f[i]]
    another operation x1, other arithmetic: 2.17 us -> 6.17 us  [shards(): heads = jnp.stack([head_az, head_ax, head_masked])]
  transfers between devices with their start and end apart: 13 -> 13, of which waited for: 6 -> 5; matrix products, arithmetic and copies ran while one was open for 36% -> 16% of each run, Pallas kernels for 0% -> 0%
where the time goes in v2:
time: 82.1 us; the launch traced here: 81.7 us
  starting transfers between devices  22.6 us (28%)
  other arithmetic  22 us (27%)
  local copies, waits for them, and re-layouts  17.2 us (21%)
  waiting for transfers between devices  16.9 us (21%)
  between operations  3.14 us (4%)
    ppermute x4, waiting for transfers between devices, with_halo(): lax.ppermute(lax.slice_in_dim(array, length - before, length, axis=dim),...  10.8 us
    ppermute x4, starting transfers between devices, with_halo(): lax.ppermute(lax.slice_in_dim(array, 0, after, axis=dim), axis, down)  10.5 us
    ppermute x4, starting transfers between devices, with_halo(): lax.ppermute(lax.slice_in_dim(array, length - before, length, axis=dim),...  9.32 us
    unnamed x53, local copies, waits for them, and re-layouts  9.23 us
    another operation x1, other arithmetic, shards(): heads = jnp.stack([head_az, head_ax, head_masked])  6.17 us
    ppermute x5, waiting for transfers between devices, butterfly_sum(): lax.ppermute(values, axis, [(i, i ^ step) for i in range(size)])  6.05 us
    mul x2, other arithmetic, shards(): shoves = step_dt * b1 * heads  3.58 us
    ppermute x5, starting transfers between devices, butterfly_sum(): lax.ppermute(values, axis, [(i, i ^ step) for i in range(size)])  2.81 us
  transfers between devices with their start and end apart: 13, of which 5 were waited for; matrix products, arithmetic and copies ran while one was open for 16% of the time, Pallas kernels for 0%

profile of v2, /device:TPU:0, one launch (start us, length us, event | category | flops | bytes accessed | tf_op | source)
XLA Modules:
  0.0 81.7 jit_solution(1492515549198164728)
XLA Ops:
  5.8 2.4 %collective-permute-start.4 = (f32[14,8,3]{2,1,0:T(8,128)S(1)}, f32[14,8,3]{2,1,0:T(8,128)S(1)}, u32[]{:S(2)}, u32[]{:S(2)}) collective-permute-start(f32[14,8,3]{2,1,0:T(8,128)S(1)} %get-tuple-element.70), channel_id=1, source_target_pairs={{0,1},{1,2},{2,3},{4,5},{5,6},{6,7},{8,9},{9,10},{10,11},{12,13},{... | collective-permute-start | bytes 4040 | tf_op jit(solution)/shard_map/ppermute | solution.py:16
  9.6 5.2 %collective-permute-start = (f32[8,8,8,128]{3,2,1,0:T(8,128)S(1)}, f32[8,8,8,128]{3,2,1,0:T(8,128)S(1)}, u32[]{:S(2)}, u32[]{:S(2)}) collective-permute-start(f32[8,8,8,128]{3,2,1,0:T(8,128)S(1)} %get-tuple-element.41), channel_id=1, source_target_pairs={{0,1},{1,2},{2,3},{4,5},{5,6},{6,7},{8,9},{9,10},{10,11},{12,13},{... | collective-permute-start | bytes 786440 | tf_op jit(solution)/shard_map/ppermute | solution.py:16
  14.8 1.3 %collective-permute-start.1 = (f32[8,8,8,128]{3,2,1,0:T(8,128)S(1)}, f32[8,8,8,128]{3,2,1,0:T(8,128)S(1)}, u32[]{:S(2)}, u32[]{:S(2)}) collective-permute-start(f32[8,8,8,128]{3,2,1,0:T(8,128)S(1)} %get-tuple-element.42), channel_id=1, source_target_pairs={{1,0},{2,1},{3,2},{5,4},{6,5},{7,6},{9,8},{10,9},{11,10},{13,12},{... | collective-permute-start | bytes 786440 | tf_op jit(solution)/shard_map/ppermute | solution.py:19
  16.3 1.6 %collective-permute-start.6 = (f32[14,3,22]{2,1,0:T(4,128)S(1)}, f32[14,3,22]{2,1,0:T(4,128)S(1)}, u32[]{:S(2)}, u32[]{:S(2)}) collective-permute-start(f32[14,3,22]{2,1,0:T(4,128)S(1)} %get-tuple-element.68), channel_id=1, source_target_pairs={{0,4},{4,8},{8,12},{12,16},{16,20},{20,24},{24,28},{28,0},{1,5},{5... | collective-permute-start | bytes 11096 | tf_op jit(solution)/shard_map/ppermute | solution.py:16
  17.9 3.2 %collective-permute-start.7 = (f32[14,3,22]{2,1,0:T(4,128)S(1)}, f32[14,3,22]{2,1,0:T(4,128)S(1)}, u32[]{:S(2)}, u32[]{:S(2)}) collective-permute-start(f32[14,3,22]{2,1,0:T(4,128)S(1)} %get-tuple-element.69), channel_id=1, source_target_pairs={{4,0},{8,4},{12,8},{16,12},{20,16},{24,20},{28,24},{0,28},{5,1},{9... | collective-permute-start | bytes 11096 | tf_op jit(solution)/shard_map/ppermute | solution.py:19
  21.1 1.9 %collective-permute-done.6 = f32[14,3,22]{2,1,0:T(4,128)S(1)} collective-permute-done((f32[14,3,22]{2,1,0:T(4,128)S(1)}, f32[14,3,22]{2,1,0:T(4,128)S(1)}, u32[]{:S(2)}, u32[]{:S(2)}) %collective-permute-start.6) | collective-permute-done | bytes 3728 | tf_op jit(solution)/shard_map/ppermute | solution.py:16
  25.1 4.7 %collective-permute-start.3 = (f32[8,2,32,128]{3,2,1,0:T(8,128)S(1)}, f32[8,2,32,128]{3,2,1,0:T(8,128)S(1)}, u32[]{:S(2)}, u32[]{:S(2)}) collective-permute-start(f32[8,2,32,128]{3,2,1,0:T(8,128)S(1)} %pad_maximum_fusion.3), channel_id=1, source_target_pairs={{4,0},{8,4},{12,8},{16,12},{20,16},{24,20},{28,24},{0,28},{5,1},{9... | collective-permute-start | bytes 786440 | tf_op jit(solution)/shard_map/ppermute | solution.py:19
  30.0 8.9 %collective-permute-done.2 = f32[8,1,32,128]{3,2,1,0:T(8,128)S(1)} collective-permute-done((f32[8,1,32,128]{3,2,1,0:T(8,128)S(1)}, f32[8,1,32,128]{3,2,1,0:T(8,128)S(1)}, u32[]{:S(2)}, u32[]{:S(2)}) %collective-permute-start.2) | collective-permute-done | bytes 131104 | tf_op jit(solution)/shard_map/ppermute | solution.py:16
  39.7 1.4 %copy.97 = f32[10,18,128]{1,0,2:T(8,128)} copy(f32[10,18,128]{2,1,0:T(8,128)S(1)} %slice_multiply_fusion.1) | data formatting | bytes 184320 | tf_op jit(solution)/shard_map/mul | solution.py:221
  41.1 1.5 %copy.116 = f32[1,11,32,128]{2,1,3,0:T(8,128)} copy(f32[1,11,32,128]{3,2,1,0:T(8,128)S(1)} %get-tuple-element.26) | data formatting | bytes 360448
  43.1 1.4 %slice.702 = f32[10,18,127]{1,0,2:T(8,128)} slice(f32[11,32,128]{1,0,2:T(8,128)S(1)} %bitcast.131), slice={[0:10], [7:25], [1:128]} | slice | bytes 182880 | tf_op jit(solution)/shard_map/slice | solution.py:36
  44.5 1.4 %copy.114 = f32[1,11,32,128]{2,1,3,0:T(8,128)} copy(f32[1,11,32,128]{3,2,1,0:T(8,128)S(1)} %get-tuple-element.28) | data formatting | bytes 360448
  45.9 1.4 %copy.113 = f32[1,11,32,128]{2,1,3,0:T(8,128)} copy(f32[1,11,32,128]{3,2,1,0:T(8,128)S(1)} %get-tuple-element.29) | data formatting | bytes 360448
  47.3 1.4 %copy.112 = f32[1,11,32,128]{2,1,3,0:T(8,128)} copy(f32[1,11,32,128]{3,2,1,0:T(8,128)S(1)} %get-tuple-element.30) | data formatting | bytes 360448
  48.7 1.4 %copy.117 = f32[1,11,32,128]{2,1,3,0:T(8,128)} copy(f32[1,11,32,128]{3,2,1,0:T(8,128)S(1)} %get-tuple-element.32) | data formatting | bytes 360448
  50.1 6.2 %fusion.6 = (f32[1,10,18,128]{2,1,3,0:T(8,128)S(1)}, f32[1,10,18,128]{2,1,3,0:T(8,128)}, f32[1,10,18,128]{2,1,3,0:T(8,128)}, f32[10,18,128]{1,0,2:T(8,128)S(1)},...) fusion(f32[11,32,128]{1,0,2:T(8,128)S(1)} %bitcast.132, ...), kind=kLoop, calls=%fused_computation.22 | loop fusion | flops 207360 | bytes 1658288 | tf_op jit(solution)/shard_map/stack | solution.py:213
  57.3 3.6 %broadcast_multiply_fusion.2 = (f32[3,10,18,128]{2,1,3,0:T(8,128)S(1)}, f32[3,10,18,128]{2,1,3,0:T(8,128)S(1)}, f32[3,10,18,128]{2,1,3,0:T(8,128)S(1)}, f32[3,10,18,128]{2,1,3,0:T(8,128)S(1)}) fusion(f32[10,18,128]{1,0,2:T(8,128)} %copy.97, f32[1,10,18,128]{2,1,3,0:T(8,128)} %get-tuple-element.39, f32[1,10,18,128]{2,1,3,0:T(8,128)} %get-tuple-element.38, ...), kind=kLoop, calls=%fused_computation.11 | loop fusion | flops 345600 | bytes 1658880 | tf_op jit(solution)/shard_map/mul | solution.py:221
  61.6 2.7 %collective-permute-start.9 = (f32[129]{0:T(256)S(1)}, f32[129]{0:T(256)S(1)}, u32[]{:S(2)}, u32[]{:S(2)}) collective-permute-start(f32[129]{0:T(256)S(1)} %fusion.88), channel_id=1, source_target_pairs={{0,2},{1,3},{2,0},{3,1},{4,6},{5,7},{6,4},{7,5},{8,10},{9,11},{10,... | collective-permute-start | bytes 1556 | tf_op jit(solution)/shard_map/ppermute | solution.py:67
  64.3 1.7 %fusion.3 = f32[3,8,16,128]{2,1,3,0:T(8,128)S(1)} fusion(f32[3,10,18,128]{2,1,3,0:T(8,128)S(1)} %get-tuple-element.23, f32[3,10,18,128]{2,1,3,0:T(8,128)S(1)} %get-tuple-element.22, f32[3,10,18,128]{2,1,3,0:T(8,128)S(1)} %get-tuple-element.24), kind=kLoop, calls=%fused_computation.7 | loop fusion | flops 245760 | bytes 1179648 | tf_op jit(solution)/shard_map/sub | solution.py:215
  66.5 3.1 %collective-permute-done.10 = f32[129]{0:T(256)S(1)} collective-permute-done((f32[129]{0:T(256)S(1)}, f32[129]{0:T(256)S(1)}, u32[]{:S(2)}, u32[]{:S(2)}) %collective-permute-start.10) | collective-permute-done | bytes 548 | tf_op jit(solution)/shard_map/ppermute | solution.py:67
  69.7 1.4 %fusion.9 = f32[1,8,16,128]{2,1,3,0:T(8,128)S(1)} fusion(f32[10,18,128]{1,0,2:T(8,128)S(1)} %copy-done.4, f32[10,18,128]{1,0,2:T(8,128)S(1)} %get-tuple-element.19, f32[10,18,128]{1,0,2:T(8,128)S(1)} %get-tuple-element.20, f32[10,18,128]{1,0,2:T(8,128)S(1)} %get-tuple-element.18, f32[1,10,18,128]{2,1,3,0:T(8,128)S(1)} %copy-done.1, ...), kind=kLoop, calls=%fused_computation.30 | loop fusion | flops 229376 | bytes 852096 | tf_op jit(solution)/shard_map/broadcast_in_dim | solution.py:232
  71.1 2.1 %collective-permute-done.11 = f32[129]{0:T(256)S(1)} collective-permute-done((f32[129]{0:T(256)S(1)}, f32[129]{0:T(256)S(1)}, u32[]{:S(2)}, u32[]{:S(2)}) %collective-permute-start.11) | collective-permute-done | bytes 548 | tf_op jit(solution)/shard_map/ppermute | solution.py:67
  73.2 1.5 %fusion = f32[4,8,16,126]{2,1,3,0:T(8,128)} fusion(f32[1,8,16,128]{2,1,3,0:T(8,128)S(1)} %fusion.9, f32[3,8,16,128]{2,1,3,0:T(8,128)S(1)} %fusion.3), kind=kLoop, calls=%fused_computation.3 | loop fusion | flops 64512 | bytes 520192 | tf_op jit(solution)/shard_map/concatenate | solution.py:232
  74.7 2.2 %copy.109 = f32[4,8,16,126]{3,2,1,0:T(8,128)S(1)} copy(f32[4,8,16,126]{2,1,3,0:T(8,128)} %fusion) | data formatting | bytes 516096 | tf_op jit(solution)/shard_map/slice | solution.py:245
  (118 shorter events, 15.3 us)
Async XLA Ops:
  1.5 3.6 %copy-start.6 = (s32[8,16]{1,0:T(8,128)S(1)}, s32[8,16]{1,0:T(8,128)}, u32[]{:S(2)}) copy-start(s32[8,16]{1,0:T(8,128)} %param.14) | copy-start | bytes 1540
  1.5 3.6 %copy-start.11 = (f32[64]{0:T(128)S(1)}, f32[64]{0:T(128)}, u32[]{:S(2)}) copy-start(f32[64]{0:T(128)} %param.13) | copy-start | bytes 772
  1.5 3.8 %copy-start.9 = (s32[8,16]{1,0:T(8,128)S(1)}, s32[8,16]{1,0:T(8,128)}, u32[]{:S(2)}) copy-start(s32[8,16]{1,0:T(8,128)} %param.15) | copy-start | bytes 1540
  1.5 3.8 %copy-start.12 = (f32[64]{0:T(128)S(1)}, f32[64]{0:T(128)}, u32[]{:S(2)}) copy-start(f32[64]{0:T(128)} %param.16) | copy-start | bytes 772
  1.7 7.8 %copy-start.5 = (f32[4,8,16,128]{3,2,1,0:T(8,128)S(1)}, f32[4,8,16,128]{3,2,1,0:T(8,128)}, u32[]{:S(2)}) copy-start(f32[4,8,16,128]{3,2,1,0:T(8,128)} %param.11) | copy-start | bytes 786436
  2.9 6.6 %copy-start = (f32[4,8,16,128]{3,2,1,0:T(8,128)S(1)}, f32[4,8,16,128]{3,2,1,0:T(8,128)}, u32[]{:S(2)}) copy-start(f32[4,8,16,128]{3,2,1,0:T(8,128)} %param.12) | copy-start | bytes 786436
  4.8 11.3 %copy-start.7 = (s32[512]{0:T(512)S(1)}, s32[512]{0:T(512)}, u32[]{:S(2)}) copy-start(s32[512]{0:T(512)} %param.18) | copy-start | bytes 6148
  4.9 11.3 %copy-start.8 = (s32[512]{0:T(512)S(1)}, s32[512]{0:T(512)}, u32[]{:S(2)}) copy-start(s32[512]{0:T(512)} %param.17) | copy-start | bytes 6148
  5.8 10.3 %collective-permute-start.4 = (f32[14,8,3]{2,1,0:T(8,128)S(1)}, f32[14,8,3]{2,1,0:T(8,128)S(1)}, u32[]{:S(2)}, u32[]{:S(2)}) collective-permute-start(f32[14,8,3]{2,1,0:T(8,128)S(1)} %get-tuple-element.70), channel_id=1, source_target_pairs={{0,1},{1,2},{2,3},{4,5},{5,6},{6,7},{8,9},{9,10},{10,11},{12,13},{... | collective-permute-start | bytes 4040 | tf_op jit(solution)/shard_map/ppermute | solution.py:16
  8.2 8.0 %collective-permute-start.5 = (f32[14,8,3]{2,1,0:T(8,128)S(1)}, f32[14,8,3]{2,1,0:T(8,128)S(1)}, u32[]{:S(2)}, u32[]{:S(2)}) collective-permute-start(f32[14,8,3]{2,1,0:T(8,128)S(1)} %get-tuple-element.71), channel_id=1, source_target_pairs={{1,0},{2,1},{3,2},{5,4},{6,5},{7,6},{9,8},{10,9},{11,10},{13,12},{... | collective-permute-start | bytes 4040 | tf_op jit(solution)/shard_map/ppermute | solution.py:19
  9.5 14.2 %copy-start.10 = (f32[512]{0:T(512)S(1)}, f32[512]{0:T(512)}, u32[]{:S(2)}) copy-start(f32[512]{0:T(512)} %param.19) | copy-start | bytes 6148
  9.6 15.4 %collective-permute-start = (f32[8,8,8,128]{3,2,1,0:T(8,128)S(1)}, f32[8,8,8,128]{3,2,1,0:T(8,128)S(1)}, u32[]{:S(2)}, u32[]{:S(2)}) collective-permute-start(f32[8,8,8,128]{3,2,1,0:T(8,128)S(1)} %get-tuple-element.41), channel_id=1, source_target_pairs={{0,1},{1,2},{2,3},{4,5},{5,6},{6,7},{8,9},{9,10},{10,11},{12,13},{... | collective-permute-start | bytes 786440 | tf_op jit(solution)/shard_map/ppermute | solution.py:16
  14.8 10.2 %collective-permute-start.1 = (f32[8,8,8,128]{3,2,1,0:T(8,128)S(1)}, f32[8,8,8,128]{3,2,1,0:T(8,128)S(1)}, u32[]{:S(2)}, u32[]{:S(2)}) collective-permute-start(f32[8,8,8,128]{3,2,1,0:T(8,128)S(1)} %get-tuple-element.42), channel_id=1, source_target_pairs={{1,0},{2,1},{3,2},{5,4},{6,5},{7,6},{9,8},{10,9},{11,10},{13,12},{... | collective-permute-start | bytes 786440 | tf_op jit(solution)/shard_map/ppermute | solution.py:19
  16.3 6.7 %collective-permute-start.6 = (f32[14,3,22]{2,1,0:T(4,128)S(1)}, f32[14,3,22]{2,1,0:T(4,128)S(1)}, u32[]{:S(2)}, u32[]{:S(2)}) collective-permute-start(f32[14,3,22]{2,1,0:T(4,128)S(1)} %get-tuple-element.68), channel_id=1, source_target_pairs={{0,4},{4,8},{8,12},{12,16},{16,20},{20,24},{24,28},{28,0},{1,5},{5... | collective-permute-start | bytes 11096 | tf_op jit(solution)/shard_map/ppermute | solution.py:16
  17.9 5.2 %collective-permute-start.7 = (f32[14,3,22]{2,1,0:T(4,128)S(1)}, f32[14,3,22]{2,1,0:T(4,128)S(1)}, u32[]{:S(2)}, u32[]{:S(2)}) collective-permute-start(f32[14,3,22]{2,1,0:T(4,128)S(1)} %get-tuple-element.69), channel_id=1, source_target_pairs={{4,0},{8,4},{12,8},{16,12},{20,16},{24,20},{28,24},{0,28},{5,1},{9... | collective-permute-start | bytes 11096 | tf_op jit(solution)/shard_map/ppermute | solution.py:19
  25.1 13.8 %collective-permute-start.3 = (f32[8,2,32,128]{3,2,1,0:T(8,128)S(1)}, f32[8,2,32,128]{3,2,1,0:T(8,128)S(1)}, u32[]{:S(2)}, u32[]{:S(2)}) collective-permute-start(f32[8,2,32,128]{3,2,1,0:T(8,128)S(1)} %pad_maximum_fusion.3), channel_id=1, source_target_pairs={{4,0},{8,4},{12,8},{16,12},{20,16},{24,20},{28,24},{0,28},{5,1},{9... | collective-permute-start | bytes 786440 | tf_op jit(solution)/shard_map/ppermute | solution.py:19
  29.8 9.2 %collective-permute-start.2 = (f32[8,1,32,128]{3,2,1,0:T(8,128)S(1)}, f32[8,1,32,128]{3,2,1,0:T(8,128)S(1)}, u32[]{:S(2)}, u32[]{:S(2)}) collective-permute-start(f32[8,1,32,128]{3,2,1,0:T(8,128)S(1)} %pad_maximum_fusion.9), channel_id=1, source_target_pairs={{0,4},{4,8},{8,12},{12,16},{16,20},{20,24},{24,28},{28,0},{1,5},{5... | collective-permute-start | bytes 393224 | tf_op jit(solution)/shard_map/ppermute | solution.py:16
  57.2 3.6 %collective-permute-start.8 = (f32[129]{0:T(256)S(1)}, f32[129]{0:T(256)S(1)}, u32[]{:S(2)}, u32[]{:S(2)}) collective-permute-start(f32[129]{0:T(256)S(1)} %pad_maximum_fusion.13), channel_id=1, source_target_pairs={{0,1},{1,0},{2,3},{3,2},{4,5},{5,4},{6,7},{7,6},{8,9},{9,8},{10,11... | collective-permute-start | bytes 1556 | tf_op jit(solution)/shard_map/ppermute | solution.py:67
  61.6 4.4 %collective-permute-start.9 = (f32[129]{0:T(256)S(1)}, f32[129]{0:T(256)S(1)}, u32[]{:S(2)}, u32[]{:S(2)}) collective-permute-start(f32[129]{0:T(256)S(1)} %fusion.88), channel_id=1, source_target_pairs={{0,2},{1,3},{2,0},{3,1},{4,6},{5,7},{6,4},{7,5},{8,10},{9,11},{10,... | collective-permute-start | bytes 1556 | tf_op jit(solution)/shard_map/ppermute | solution.py:67
  66.0 3.6 %collective-permute-start.10 = (f32[129]{0:T(256)S(1)}, f32[129]{0:T(256)S(1)}, u32[]{:S(2)}, u32[]{:S(2)}) collective-permute-start(f32[129]{0:T(256)S(1)} %add.161), channel_id=1, source_target_pairs={{0,4},{4,0},{8,12},{12,8},{16,20},{20,16},{24,28},{28,24},{1,5},{5... | collective-permute-start | bytes 1556 | tf_op jit(solution)/shard_map/ppermute | solution.py:67
  66.1 3.6 %copy-start.2 = (f32[1,10,18,128]{2,1,3,0:T(8,128)S(1)}, f32[1,10,18,128]{2,1,3,0:T(8,128)}, u32[]{:S(2)}) copy-start(f32[1,10,18,128]{2,1,3,0:T(8,128)} %get-tuple-element.89) | copy-start | bytes 276484
  66.1 3.6 %copy-start.4 = (f32[10,18,128]{1,0,2:T(8,128)S(1)}, f32[10,18,128]{1,0,2:T(8,128)}, u32[]{:S(2)}) copy-start(f32[10,18,128]{1,0,2:T(8,128)} %copy-done.3) | copy-start | bytes 276484
  69.7 3.6 %collective-permute-start.11 = (f32[129]{0:T(256)S(1)}, f32[129]{0:T(256)S(1)}, u32[]{:S(2)}, u32[]{:S(2)}) collective-permute-start(f32[129]{0:T(256)S(1)} %add.162), channel_id=1, source_target_pairs={{0,8},{4,12},{8,0},{12,4},{16,24},{20,28},{24,16},{28,20},{1,9},{5... | collective-permute-start | bytes 1556 | tf_op jit(solution)/shard_map/ppermute | solution.py:67
  73.2 4.5 %collective-permute-start.12 = (f32[129]{0:T(256)S(1)}, f32[129]{0:T(256)S(1)}, u32[]{:S(2)}, u32[]{:S(2)}) collective-permute-start(f32[129]{0:T(256)S(1)} %add.163), channel_id=1, source_target_pairs={{0,16},{4,20},{8,24},{12,28},{16,0},{20,4},{24,8},{28,12},{1,17},{... | collective-permute-start | bytes 1556 | tf_op jit(solution)/shard_map/ppermute | solution.py:67
  (2 other events, 4.4 us)

commit v3 on v2

--- a/solution.py
+++ b/solution.py
@@ -25,6 +25,37 @@
     ax_after = after if ax_after is None else ax_after
     widened = with_halo(array, "ax", 2, ax_before, ax_after, False)
     return with_halo(widened, "az", 1, before, after, True)
+
+
+def exchange_once(array, a_lo, a_hi, x_lo, x_hi):
+    n_az, n_ax = (lax.axis_size("az"), lax.axis_size("ax"))
+    length_a, length_x = (array.shape[1], array.shape[2])
+
+    def pairs(da, dx):
+        found = []
+        for az in range(n_az):
+            for ax in range(n_ax):
+                to_ax = ax - dx
+                if 0 <= to_ax < n_ax:
+                    found.append((az * n_ax + ax, ((az - da) % n_az) * n_ax + to_ax))
+        return found
+
+    rows = {-1: (length_a - a_lo, length_a), 0: (0, length_a), 1: (0, a_hi)}
+    cols = {-1: (length_x - x_lo, length_x), 0: (0, length_x), 1: (0, x_hi)}
+    bands = []
+    for da in (-1, 0, 1):
+        if (da == -1 and not a_lo) or (da == 1 and not a_hi):
+            continue
+        pieces = []
+        for dx in (-1, 0, 1):
+            if (dx == -1 and not x_lo) or (dx == 1 and not x_hi):
+                continue
+            piece = lax.slice_in_dim(lax.slice_in_dim(array, *rows[da], axis=1), *cols[dx], axis=2)
+            if da or dx:
+                piece = lax.ppermute(piece, ("az", "ax"), pairs(da, dx))
+            pieces.append(piece)
+        bands.append(jnp.concatenate(pieces, axis=2))
+    return jnp.concatenate(bands, axis=1)
 
 
 def win(values, origin, da, dx, na, nx):
@@ -116,8 +147,8 @@
     stack_c = jnp.stack(planes)
 
     tile = 8
-    wide_f = exchange(stack_f, 1, 2, tile, tile)
-    wide_c = exchange(stack_c, 3, 3)
+    wide_f = exchange_once(stack_f, 1, 2, tile, tile)
+    wide_c = exchange_once(stack_c, 3, 3, 3, 3)
 
     oc = (3, 3)
     p_t, p_b, va_t, vx_t, vr_b, u_t, u_b, w_t, w_b, b_t, b_b, s_t, wall_c, src_c = [wide_c[i] for i in range(14)]

time: 82.1 us -> 107 us (1.30)
  starting transfers between devices: 22.6 us -> 51.5 us
  waiting for transfers between devices: 16.9 us -> 12 us
    ppermute x8 -> x16, starting transfers between devices: 19.8 us -> 44.4 us  [exchange_once(): piece = lax.ppermute(piece, ('az', 'ax'), pairs(da, dx))]
    ppermute x5, starting transfers between devices: 2.81 us -> 7.09 us  [butterfly_sum(): lax.ppermute(values, axis, [(i, i ^ step) for i in range(size)])]
    ppermute x8 -> x16, waiting for transfers between devices: 10.8 us -> 6.57 us  [exchange_once(): piece = lax.ppermute(piece, ('az', 'ax'), pairs(da, dx))]
  transfers between devices with their start and end apart: 13 -> 21, of which waited for: 5 -> 6; matrix products, arithmetic and copies ran while one was open for 16% -> 12% of each run, Pallas kernels for 0% -> 0%
where the time goes in v3:
time: 107 us; the launch traced here: 106 us
  starting transfers between devices  51.5 us (48%)
  other arithmetic  21.9 us (20%)
  local copies, waits for them, and re-layouts  17.8 us (17%)
  waiting for transfers between devices  12 us (11%)
  between operations  3.19 us (3%)
    ppermute x16, starting transfers between devices, exchange_once(): piece = lax.ppermute(piece, ('az', 'ax'), pairs(da, dx))  44.4 us
    unnamed x53, local copies, waits for them, and re-layouts  9.76 us
    ppermute x5, starting transfers between devices, butterfly_sum(): lax.ppermute(values, axis, [(i, i ^ step) for i in range(size)])  7.09 us
    ppermute x16, waiting for transfers between devices, exchange_once(): piece = lax.ppermute(piece, ('az', 'ax'), pairs(da, dx))  6.57 us
    another operation x1, other arithmetic, shards(): heads = jnp.stack([head_az, head_ax, head_masked])  6.13 us
    ppermute x5, waiting for transfers between devices, butterfly_sum(): lax.ppermute(values, axis, [(i, i ^ step) for i in range(size)])  5.47 us
    mul x2, other arithmetic, shards(): shoves = step_dt * b1 * heads  3.58 us
    slice x1, local copies, waits for them, and re-layouts, shards(): base[..., :nr - 2]  2.16 us
  transfers between devices with their start and end apart: 21, of which 6 were waited for; matrix products, arithmetic and copies ran while one was open for 12% of the time, Pallas kernels for 0%

profile of v3, /device:TPU:0, one launch (start us, length us, event | category | flops | bytes accessed | tf_op | source)
XLA Modules:
  0.0 106.4 jit_solution(7754587592816645625)
XLA Ops:
  5.7 3.0 %collective-permute-start.9 = (f32[14,3,16]{2,1,0:T(4,128)S(1)}, f32[14,3,16]{2,1,0:T(4,128)S(1)}, u32[]{:S(2)}, u32[]{:S(2)}) collective-permute-start(f32[14,3,16]{2,1,0:T(4,128)S(1)} %get-tuple-element.76), channel_id=1, source_target_pairs={{0,4},{1,5},{2,6},{3,7},{4,8},{5,9},{6,10},{7,11},{8,12},{9,13},{1... | collective-permute-start | bytes 8072 | tf_op jit(solution)/shard_map/ppermute | solution.py:55
  8.7 3.1 %collective-permute-start.14 = (f32[14,3,16]{2,1,0:T(4,128)S(1)}, f32[14,3,16]{2,1,0:T(4,128)S(1)}, u32[]{:S(2)}, u32[]{:S(2)}) collective-permute-start(f32[14,3,16]{2,1,0:T(4,128)S(1)} %get-tuple-element.77), channel_id=1, source_target_pairs={{0,28},{1,29},{2,30},{3,31},{4,0},{5,1},{6,2},{7,3},{8,4},{9,5},{1... | collective-permute-start | bytes 8072 | tf_op jit(solution)/shard_map/ppermute | solution.py:55
  14.5 8.6 %collective-permute-start.13 = (f32[14,3,3]{2,1,0:T(4,128)S(1)}, f32[14,3,3]{2,1,0:T(4,128)S(1)}, u32[]{:S(2)}, u32[]{:S(2)}) collective-permute-start(f32[14,3,3]{2,1,0:T(4,128)S(1)} %get-tuple-element.74), channel_id=1, source_target_pairs={{0,29},{1,30},{2,31},{4,1},{5,2},{6,3},{8,5},{9,6},{10,7},{12,9},{... | collective-permute-start | bytes 1520 | tf_op jit(solution)/shard_map/ppermute | solution.py:55
  25.3 2.8 %collective-permute-start.11 = (f32[14,8,3]{2,1,0:T(8,128)S(1)}, f32[14,8,3]{2,1,0:T(8,128)S(1)}, u32[]{:S(2)}, u32[]{:S(2)}) collective-permute-start(f32[14,8,3]{2,1,0:T(8,128)S(1)} %get-tuple-element.78), channel_id=1, source_target_pairs={{0,1},{1,2},{2,3},{4,5},{5,6},{6,7},{8,9},{9,10},{10,11},{12,13},{... | collective-permute-start | bytes 4040 | tf_op jit(solution)/shard_map/ppermute | solution.py:55
  29.4 2.4 %collective-permute-done.10 = f32[14,3,3]{2,1,0:T(4,128)S(1)} collective-permute-done((f32[14,3,3]{2,1,0:T(4,128)S(1)}, f32[14,3,3]{2,1,0:T(4,128)S(1)}, u32[]{:S(2)}, u32[]{:S(2)}) %collective-permute-start.10) | collective-permute-done | bytes 536 | tf_op jit(solution)/shard_map/ppermute | solution.py:55
  31.8 3.0 %collective-permute-start = (f32[8,1,8,128]{3,2,1,0:T(8,128)S(1)}, f32[8,1,8,128]{3,2,1,0:T(8,128)S(1)}, u32[]{:S(2)}, u32[]{:S(2)}) collective-permute-start(f32[8,1,8,128]{3,2,1,0:T(8,128)S(1)} %get-tuple-element.41), channel_id=1, source_target_pairs={{0,5},{1,6},{2,7},{4,9},{5,10},{6,11},{8,13},{9,14},{10,15},{12,17... | collective-permute-start | bytes 98312 | tf_op jit(solution)/shard_map/ppermute | solution.py:55
  36.3 3.8 %collective-permute-start.3 = (f32[8,8,8,128]{3,2,1,0:T(8,128)S(1)}, f32[8,8,8,128]{3,2,1,0:T(8,128)S(1)}, u32[]{:S(2)}, u32[]{:S(2)}) collective-permute-start(f32[8,8,8,128]{3,2,1,0:T(8,128)S(1)} %get-tuple-element.43), channel_id=1, source_target_pairs={{0,1},{1,2},{2,3},{4,5},{5,6},{6,7},{8,9},{9,10},{10,11},{12,13},{... | collective-permute-start | bytes 786440 | tf_op jit(solution)/shard_map/ppermute | solution.py:55
  43.6 5.6 %collective-permute-start.6 = (f32[8,2,16,128]{3,2,1,0:T(8,128)S(1)}, f32[8,2,16,128]{3,2,1,0:T(8,128)S(1)}, u32[]{:S(2)}, u32[]{:S(2)}) collective-permute-start(f32[8,2,16,128]{3,2,1,0:T(8,128)S(1)} %slice.727), channel_id=1, source_target_pairs={{0,28},{1,29},{2,30},{3,31},{4,0},{5,1},{6,2},{7,3},{8,4},{9,5},{1... | collective-permute-start | bytes 393224 | tf_op jit(solution)/shard_map/ppermute | solution.py:55
  49.2 5.0 %collective-permute-start.5 = (f32[8,2,8,128]{3,2,1,0:T(8,128)S(1)}, f32[8,2,8,128]{3,2,1,0:T(8,128)S(1)}, u32[]{:S(2)}, u32[]{:S(2)}) collective-permute-start(f32[8,2,8,128]{3,2,1,0:T(8,128)S(1)} %get-tuple-element.45), channel_id=1, source_target_pairs={{0,29},{1,30},{2,31},{4,1},{5,2},{6,3},{8,5},{9,6},{10,7},{12,9},{... | collective-permute-start | bytes 196616 | tf_op jit(solution)/shard_map/ppermute | solution.py:55
  54.3 1.5 %collective-permute-start.7 = (f32[8,2,8,128]{3,2,1,0:T(8,128)S(1)}, f32[8,2,8,128]{3,2,1,0:T(8,128)S(1)}, u32[]{:S(2)}, u32[]{:S(2)}) collective-permute-start(f32[8,2,8,128]{3,2,1,0:T(8,128)S(1)} %get-tuple-element.46), channel_id=1, source_target_pairs={{1,28},{2,29},{3,30},{5,0},{6,1},{7,2},{9,4},{10,5},{11,6},{13,8},... | collective-permute-start | bytes 196616 | tf_op jit(solution)/shard_map/ppermute | solution.py:55
  56.1 3.7 %collective-permute-done.7 = f32[8,2,8,128]{3,2,1,0:T(8,128)S(1)} collective-permute-done((f32[8,2,8,128]{3,2,1,0:T(8,128)S(1)}, f32[8,2,8,128]{3,2,1,0:T(8,128)S(1)}, u32[]{:S(2)}, u32[]{:S(2)}) %collective-permute-start.7) | collective-permute-done | bytes 65568 | tf_op jit(solution)/shard_map/ppermute | solution.py:55
  60.6 1.4 %copy.97 = f32[10,18,128]{1,0,2:T(8,128)} copy(f32[10,18,128]{2,1,0:T(8,128)S(1)} %slice_multiply_fusion.1) | data formatting | bytes 184320 | tf_op jit(solution)/shard_map/mul | solution.py:252
  62.1 1.5 %copy.116 = f32[1,11,32,128]{2,1,3,0:T(8,128)} copy(f32[1,11,32,128]{3,2,1,0:T(8,128)S(1)} %get-tuple-element.26) | data formatting | bytes 360448
  65.4 1.5 %copy.114 = f32[1,11,32,128]{2,1,3,0:T(8,128)} copy(f32[1,11,32,128]{3,2,1,0:T(8,128)S(1)} %get-tuple-element.28) | data formatting | bytes 360448
  71.1 6.1 %fusion.6 = (f32[1,10,18,128]{2,1,3,0:T(8,128)S(1)}, f32[1,10,18,128]{2,1,3,0:T(8,128)}, f32[1,10,18,128]{2,1,3,0:T(8,128)}, f32[10,18,128]{1,0,2:T(8,128)S(1)},...) fusion(f32[11,32,128]{1,0,2:T(8,128)S(1)} %bitcast.132, ...), kind=kLoop, calls=%fused_computation.22 | loop fusion | flops 207360 | bytes 1658288 | tf_op jit(solution)/shard_map/stack | solution.py:244
  78.2 2.8 %collective-permute-start.16 = (f32[129]{0:T(256)S(1)}, f32[129]{0:T(256)S(1)}, u32[]{:S(2)}, u32[]{:S(2)}) collective-permute-start(f32[129]{0:T(256)S(1)} %pad_maximum_fusion.9), channel_id=1, source_target_pairs={{0,1},{1,0},{2,3},{3,2},{4,5},{5,4},{6,7},{7,6},{8,9},{9,8},{10,11... | collective-permute-start | bytes 1556 | tf_op jit(solution)/shard_map/ppermute | solution.py:98
  81.0 3.6 %broadcast_multiply_fusion.2 = (f32[3,10,18,128]{2,1,3,0:T(8,128)S(1)}, f32[3,10,18,128]{2,1,3,0:T(8,128)S(1)}, f32[3,10,18,128]{2,1,3,0:T(8,128)S(1)}, f32[3,10,18,128]{2,1,3,0:T(8,128)S(1)}) fusion(f32[10,18,128]{1,0,2:T(8,128)} %copy.97, f32[1,10,18,128]{2,1,3,0:T(8,128)} %get-tuple-element.39, f32[1,10,18,128]{2,1,3,0:T(8,128)} %get-tuple-element.38, ...), kind=kLoop, calls=%fused_computation.11 | loop fusion | flops 345600 | bytes 1658880 | tf_op jit(solution)/shard_map/mul | solution.py:252
  86.6 1.7 %fusion.3 = f32[3,8,16,128]{2,1,3,0:T(8,128)S(1)} fusion(f32[3,10,18,128]{2,1,3,0:T(8,128)S(1)} %get-tuple-element.23, f32[3,10,18,128]{2,1,3,0:T(8,128)S(1)} %get-tuple-element.22, f32[3,10,18,128]{2,1,3,0:T(8,128)S(1)} %get-tuple-element.24), kind=kLoop, calls=%fused_computation.7 | loop fusion | flops 245760 | bytes 1179648 | tf_op jit(solution)/shard_map/sub | solution.py:246
  89.6 2.8 %collective-permute-done.18 = f32[129]{0:T(256)S(1)} collective-permute-done((f32[129]{0:T(256)S(1)}, f32[129]{0:T(256)S(1)}, u32[]{:S(2)}, u32[]{:S(2)}) %collective-permute-start.18) | collective-permute-done | bytes 548 | tf_op jit(solution)/shard_map/ppermute | solution.py:98
  92.5 1.4 %fusion.9 = f32[1,8,16,128]{2,1,3,0:T(8,128)S(1)} fusion(f32[10,18,128]{1,0,2:T(8,128)S(1)} %copy-done.4, f32[10,18,128]{1,0,2:T(8,128)S(1)} %get-tuple-element.19, f32[10,18,128]{1,0,2:T(8,128)S(1)} %get-tuple-element.20, f32[10,18,128]{1,0,2:T(8,128)S(1)} %get-tuple-element.18, f32[1,10,18,128]{2,1,3,0:T(8,128)S(1)} %copy-done.1, ...), kind=kLoop, calls=%fused_computation.30 | loop fusion | flops 229376 | bytes 852096 | tf_op jit(solution)/shard_map/broadcast_in_dim | solution.py:263
  93.9 2.1 %collective-permute-done.19 = f32[129]{0:T(256)S(1)} collective-permute-done((f32[129]{0:T(256)S(1)}, f32[129]{0:T(256)S(1)}, u32[]{:S(2)}, u32[]{:S(2)}) %collective-permute-start.19) | collective-permute-done | bytes 548 | tf_op jit(solution)/shard_map/ppermute | solution.py:98
  96.0 2.7 %collective-permute-start.20 = (f32[129]{0:T(256)S(1)}, f32[129]{0:T(256)S(1)}, u32[]{:S(2)}, u32[]{:S(2)}) collective-permute-start(f32[129]{0:T(256)S(1)} %add.163), channel_id=1, source_target_pairs={{0,16},{4,20},{8,24},{12,28},{16,0},{20,4},{24,8},{28,12},{1,17},{... | collective-permute-start | bytes 1556 | tf_op jit(solution)/shard_map/ppermute | solution.py:98
  98.7 1.5 %fusion = f32[4,8,16,126]{2,1,3,0:T(8,128)} fusion(f32[1,8,16,128]{2,1,3,0:T(8,128)S(1)} %fusion.9, f32[3,8,16,128]{2,1,3,0:T(8,128)S(1)} %fusion.3), kind=kLoop, calls=%fused_computation.3 | loop fusion | flops 64512 | bytes 520192 | tf_op jit(solution)/shard_map/concatenate | solution.py:263
  100.1 2.2 %copy.109 = f32[4,8,16,126]{3,2,1,0:T(8,128)S(1)} copy(f32[4,8,16,126]{2,1,3,0:T(8,128)} %fusion) | data formatting | bytes 516096 | tf_op jit(solution)/shard_map/slice | solution.py:276
  (136 shorter events, 29.4 us)
Async XLA Ops:
  2.9 20.3 %copy-start.5 = (f32[4,8,16,128]{3,2,1,0:T(8,128)S(1)}, f32[4,8,16,128]{3,2,1,0:T(8,128)}, u32[]{:S(2)}) copy-start(f32[4,8,16,128]{3,2,1,0:T(8,128)} %param.11) | copy-start | bytes 786436
  2.9 20.3 %copy-start = (f32[4,8,16,128]{3,2,1,0:T(8,128)S(1)}, f32[4,8,16,128]{3,2,1,0:T(8,128)}, u32[]{:S(2)}) copy-start(f32[4,8,16,128]{3,2,1,0:T(8,128)} %param.12) | copy-start | bytes 786436
  5.7 30.6 %collective-permute-start.9 = (f32[14,3,16]{2,1,0:T(4,128)S(1)}, f32[14,3,16]{2,1,0:T(4,128)S(1)}, u32[]{:S(2)}, u32[]{:S(2)}) collective-permute-start(f32[14,3,16]{2,1,0:T(4,128)S(1)} %get-tuple-element.76), channel_id=1, source_target_pairs={{0,4},{1,5},{2,6},{3,7},{4,8},{5,9},{6,10},{7,11},{8,12},{9,13},{1... | collective-permute-start | bytes 8072 | tf_op jit(solution)/shard_map/ppermute | solution.py:55
  8.7 31.4 %collective-permute-start.14 = (f32[14,3,16]{2,1,0:T(4,128)S(1)}, f32[14,3,16]{2,1,0:T(4,128)S(1)}, u32[]{:S(2)}, u32[]{:S(2)}) collective-permute-start(f32[14,3,16]{2,1,0:T(4,128)S(1)} %get-tuple-element.77), channel_id=1, source_target_pairs={{0,28},{1,29},{2,30},{3,31},{4,0},{5,1},{6,2},{7,3},{8,4},{9,5},{1... | collective-permute-start | bytes 8072 | tf_op jit(solution)/shard_map/ppermute | solution.py:55
  11.9 12.0 %collective-permute-start.8 = (f32[14,3,3]{2,1,0:T(4,128)S(1)}, f32[14,3,3]{2,1,0:T(4,128)S(1)}, u32[]{:S(2)}, u32[]{:S(2)}) collective-permute-start(f32[14,3,3]{2,1,0:T(4,128)S(1)} %get-tuple-element.72), channel_id=1, source_target_pairs={{0,5},{1,6},{2,7},{4,9},{5,10},{6,11},{8,13},{9,14},{10,15},{12,17... | collective-permute-start | bytes 1520 | tf_op jit(solution)/shard_map/ppermute | solution.py:55
  13.2 12.0 %collective-permute-start.15 = (f32[14,3,3]{2,1,0:T(4,128)S(1)}, f32[14,3,3]{2,1,0:T(4,128)S(1)}, u32[]{:S(2)}, u32[]{:S(2)}) collective-permute-start(f32[14,3,3]{2,1,0:T(4,128)S(1)} %get-tuple-element.73), channel_id=1, source_target_pairs={{1,28},{2,29},{3,30},{5,0},{6,1},{7,2},{9,4},{10,5},{11,6},{13,8},... | collective-permute-start | bytes 1520 | tf_op jit(solution)/shard_map/ppermute | solution.py:55
  14.5 13.5 %collective-permute-start.13 = (f32[14,3,3]{2,1,0:T(4,128)S(1)}, f32[14,3,3]{2,1,0:T(4,128)S(1)}, u32[]{:S(2)}, u32[]{:S(2)}) collective-permute-start(f32[14,3,3]{2,1,0:T(4,128)S(1)} %get-tuple-element.74), channel_id=1, source_target_pairs={{0,29},{1,30},{2,31},{4,1},{5,2},{6,3},{8,5},{9,6},{10,7},{12,9},{... | collective-permute-start | bytes 1520 | tf_op jit(solution)/shard_map/ppermute | solution.py:55
  23.4 18.8 %copy-start.10 = (f32[512]{0:T(512)S(1)}, f32[512]{0:T(512)}, u32[]{:S(2)}) copy-start(f32[512]{0:T(512)} %param.19) | copy-start | bytes 6148
  23.9 7.9 %collective-permute-start.10 = (f32[14,3,3]{2,1,0:T(4,128)S(1)}, f32[14,3,3]{2,1,0:T(4,128)S(1)}, u32[]{:S(2)}, u32[]{:S(2)}) collective-permute-start(f32[14,3,3]{2,1,0:T(4,128)S(1)} %get-tuple-element.75), channel_id=1, source_target_pairs={{1,4},{2,5},{3,6},{5,8},{6,9},{7,10},{9,12},{10,13},{11,14},{13,16... | collective-permute-start | bytes 1520 | tf_op jit(solution)/shard_map/ppermute | solution.py:55
  25.3 9.6 %collective-permute-start.11 = (f32[14,8,3]{2,1,0:T(8,128)S(1)}, f32[14,8,3]{2,1,0:T(8,128)S(1)}, u32[]{:S(2)}, u32[]{:S(2)}) collective-permute-start(f32[14,8,3]{2,1,0:T(8,128)S(1)} %get-tuple-element.78), channel_id=1, source_target_pairs={{0,1},{1,2},{2,3},{4,5},{5,6},{6,7},{8,9},{9,10},{10,11},{12,13},{... | collective-permute-start | bytes 4040 | tf_op jit(solution)/shard_map/ppermute | solution.py:55
  28.1 8.1 %collective-permute-start.12 = (f32[14,8,3]{2,1,0:T(8,128)S(1)}, f32[14,8,3]{2,1,0:T(8,128)S(1)}, u32[]{:S(2)}, u32[]{:S(2)}) collective-permute-start(f32[14,8,3]{2,1,0:T(8,128)S(1)} %get-tuple-element.79), channel_id=1, source_target_pairs={{1,0},{2,1},{3,2},{5,4},{6,5},{7,6},{9,8},{10,9},{11,10},{13,12},{... | collective-permute-start | bytes 4040 | tf_op jit(solution)/shard_map/ppermute | solution.py:55
  31.8 11.7 %collective-permute-start = (f32[8,1,8,128]{3,2,1,0:T(8,128)S(1)}, f32[8,1,8,128]{3,2,1,0:T(8,128)S(1)}, u32[]{:S(2)}, u32[]{:S(2)}) collective-permute-start(f32[8,1,8,128]{3,2,1,0:T(8,128)S(1)} %get-tuple-element.41), channel_id=1, source_target_pairs={{0,5},{1,6},{2,7},{4,9},{5,10},{6,11},{8,13},{9,14},{10,15},{12,17... | collective-permute-start | bytes 98312 | tf_op jit(solution)/shard_map/ppermute | solution.py:55
  34.8 14.4 %collective-permute-start.2 = (f32[8,1,8,128]{3,2,1,0:T(8,128)S(1)}, f32[8,1,8,128]{3,2,1,0:T(8,128)S(1)}, u32[]{:S(2)}, u32[]{:S(2)}) collective-permute-start(f32[8,1,8,128]{3,2,1,0:T(8,128)S(1)} %get-tuple-element.42), channel_id=1, source_target_pairs={{1,4},{2,5},{3,6},{5,8},{6,9},{7,10},{9,12},{10,13},{11,14},{13,16... | collective-permute-start | bytes 98312 | tf_op jit(solution)/shard_map/ppermute | solution.py:55
  36.2 18.1 %collective-permute-start.1 = (f32[8,1,16,128]{3,2,1,0:T(8,128)S(1)}, f32[8,1,16,128]{3,2,1,0:T(8,128)S(1)}, u32[]{:S(2)}, u32[]{:S(2)}) collective-permute-start(f32[8,1,16,128]{3,2,1,0:T(8,128)S(1)} %pad_maximum_fusion.5), channel_id=1, source_target_pairs={{0,4},{1,5},{2,6},{3,7},{4,8},{5,9},{6,10},{7,11},{8,12},{9,13},{1... | collective-permute-start | bytes 196616 | tf_op jit(solution)/shard_map/ppermute | solution.py:55
  36.3 23.5 %collective-permute-start.3 = (f32[8,8,8,128]{3,2,1,0:T(8,128)S(1)}, f32[8,8,8,128]{3,2,1,0:T(8,128)S(1)}, u32[]{:S(2)}, u32[]{:S(2)}) collective-permute-start(f32[8,8,8,128]{3,2,1,0:T(8,128)S(1)} %get-tuple-element.43), channel_id=1, source_target_pairs={{0,1},{1,2},{2,3},{4,5},{5,6},{6,7},{8,9},{9,10},{10,11},{12,13},{... | collective-permute-start | bytes 786440 | tf_op jit(solution)/shard_map/ppermute | solution.py:55
  40.2 19.7 %collective-permute-start.4 = (f32[8,8,8,128]{3,2,1,0:T(8,128)S(1)}, f32[8,8,8,128]{3,2,1,0:T(8,128)S(1)}, u32[]{:S(2)}, u32[]{:S(2)}) collective-permute-start(f32[8,8,8,128]{3,2,1,0:T(8,128)S(1)} %get-tuple-element.44), channel_id=1, source_target_pairs={{1,0},{2,1},{3,2},{5,4},{6,5},{7,6},{9,8},{10,9},{11,10},{13,12},{... | collective-permute-start | bytes 786440 | tf_op jit(solution)/shard_map/ppermute | solution.py:55
  43.6 16.3 %collective-permute-start.6 = (f32[8,2,16,128]{3,2,1,0:T(8,128)S(1)}, f32[8,2,16,128]{3,2,1,0:T(8,128)S(1)}, u32[]{:S(2)}, u32[]{:S(2)}) collective-permute-start(f32[8,2,16,128]{3,2,1,0:T(8,128)S(1)} %slice.727), channel_id=1, source_target_pairs={{0,28},{1,29},{2,30},{3,31},{4,0},{5,1},{6,2},{7,3},{8,4},{9,5},{1... | collective-permute-start | bytes 393224 | tf_op jit(solution)/shard_map/ppermute | solution.py:55
  49.2 6.9 %collective-permute-start.5 = (f32[8,2,8,128]{3,2,1,0:T(8,128)S(1)}, f32[8,2,8,128]{3,2,1,0:T(8,128)S(1)}, u32[]{:S(2)}, u32[]{:S(2)}) collective-permute-start(f32[8,2,8,128]{3,2,1,0:T(8,128)S(1)} %get-tuple-element.45), channel_id=1, source_target_pairs={{0,29},{1,30},{2,31},{4,1},{5,2},{6,3},{8,5},{9,6},{10,7},{12,9},{... | collective-permute-start | bytes 196616 | tf_op jit(solution)/shard_map/ppermute | solution.py:55
  54.3 5.6 %collective-permute-start.7 = (f32[8,2,8,128]{3,2,1,0:T(8,128)S(1)}, f32[8,2,8,128]{3,2,1,0:T(8,128)S(1)}, u32[]{:S(2)}, u32[]{:S(2)}) collective-permute-start(f32[8,2,8,128]{3,2,1,0:T(8,128)S(1)} %get-tuple-element.46), channel_id=1, source_target_pairs={{1,28},{2,29},{3,30},{5,0},{6,1},{7,2},{9,4},{10,5},{11,6},{13,8},... | collective-permute-start | bytes 196616 | tf_op jit(solution)/shard_map/ppermute | solution.py:55
  78.2 6.3 %collective-permute-start.16 = (f32[129]{0:T(256)S(1)}, f32[129]{0:T(256)S(1)}, u32[]{:S(2)}, u32[]{:S(2)}) collective-permute-start(f32[129]{0:T(256)S(1)} %pad_maximum_fusion.9), channel_id=1, source_target_pairs={{0,1},{1,0},{2,3},{3,2},{4,5},{5,4},{6,7},{7,6},{8,9},{9,8},{10,11... | collective-permute-start | bytes 1556 | tf_op jit(solution)/shard_map/ppermute | solution.py:98
  85.3 3.6 %collective-permute-start.17 = (f32[129]{0:T(256)S(1)}, f32[129]{0:T(256)S(1)}, u32[]{:S(2)}, u32[]{:S(2)}) collective-permute-start(f32[129]{0:T(256)S(1)} %fusion.89), channel_id=1, source_target_pairs={{0,2},{1,3},{2,0},{3,1},{4,6},{5,7},{6,4},{7,5},{8,10},{9,11},{10,... | collective-permute-start | bytes 1556 | tf_op jit(solution)/shard_map/ppermute | solution.py:98
  88.9 3.6 %collective-permute-start.18 = (f32[129]{0:T(256)S(1)}, f32[129]{0:T(256)S(1)}, u32[]{:S(2)}, u32[]{:S(2)}) collective-permute-start(f32[129]{0:T(256)S(1)} %add.161), channel_id=1, source_target_pairs={{0,4},{4,0},{8,12},{12,8},{16,20},{20,16},{24,28},{28,24},{1,5},{5... | collective-permute-start | bytes 1556 | tf_op jit(solution)/shard_map/ppermute | solution.py:98
  92.4 3.6 %collective-permute-start.19 = (f32[129]{0:T(256)S(1)}, f32[129]{0:T(256)S(1)}, u32[]{:S(2)}, u32[]{:S(2)}) collective-permute-start(f32[129]{0:T(256)S(1)} %add.162), channel_id=1, source_target_pairs={{0,8},{4,12},{8,0},{12,4},{16,24},{20,28},{24,16},{28,20},{1,9},{5... | collective-permute-start | bytes 1556 | tf_op jit(solution)/shard_map/ppermute | solution.py:98
  96.0 6.3 %collective-permute-start.20 = (f32[129]{0:T(256)S(1)}, f32[129]{0:T(256)S(1)}, u32[]{:S(2)}, u32[]{:S(2)}) collective-permute-start(f32[129]{0:T(256)S(1)} %add.163), channel_id=1, source_target_pairs={{0,16},{4,20},{8,24},{12,28},{16,0},{20,4},{24,8},{28,12},{1,17},{... | collective-permute-start | bytes 1556 | tf_op jit(solution)/shard_map/ppermute | solution.py:98
  (10 other events, 29.4 us)

commit v4 on v2

--- a/solution.py
+++ b/solution.py
@@ -204,35 +204,48 @@
 
     of = (1, tile)
     g_a0, g_a1, g_a2, g_a3, g_u, g_w, g_b, g_push = [wide_f[i] for i in range(8)]
-    head_az = win(g_a1, of, -1, -1, r1a, r1x) + win(g_push, of, -1, -1, r1a, r1x) - win(g_push, of, 0, -1, r1a, r1x)
-    head_ax = win(g_a2, of, -1, -1, r1a, r1x) + win(g_push, of, -1, -1, r1a, r1x) - win(g_push, of, -1, 0, r1a, r1x)
-    push_1 = win(g_push, of, -1, -1, r1a, r1x)
-    head_rad = win(g_a3, of, -1, -1, r1a, r1x) + push_1 - rad_next(push_1)
-    casing = casing_mask(head_rad.shape)
-    head_masked = jnp.where(casing, 0.0, head_rad)
-    heads = jnp.stack([head_az, head_ax, head_masked])
-    u1, w1, b1 = win(g_u, of, -1, -1, r1a, r1x), win(g_w, of, -1, -1, r1a, r1x), win(g_b, of, -1, -1, r1a, r1x)
-    backs = heads[:, 1 : 1 + na, 1 : 1 + nx, :] - step_dt * advect_back4(u1 * heads, w1 * heads, na, nx)
-    seed_1 = win(g_a0, of, -1, -1, r1a, r1x)
+
+    def at(field, da, dx):
+        return win(field, of, da, dx, na, nx)
+
+    def head_az(da, dx):
+        return at(g_a1, da, dx) + at(g_push, da, dx) - at(g_push, da + 1, dx)
+
+    def head_ax(da, dx):
+        return at(g_a2, da, dx) + at(g_push, da, dx) - at(g_push, da, dx + 1)
+
+    casing = casing_mask((na, nx, nr))
+
+    def head_rad(da, dx):
+        push_here = at(g_push, da, dx)
+        return at(g_a3, da, dx) + push_here - rad_next(push_here)
+
+    def head_masked(da, dx):
+        return jnp.where(casing, 0.0, head_rad(da, dx))
+
+    def back_advect(head):
+        return 0.5 * (at(g_u, 0, -1) * head(0, -1) - at(g_u, 0, 1) * head(0, 1)) + 0.5 * (
+            at(g_w, -1, 0) * head(-1, 0) - at(g_w, 1, 0) * head(1, 0)
+        )
+
+    def seed(da, dx):
+        return at(g_a0, da, dx)
+
+    backs = [head(0, 0) - step_dt * back_advect(head) for head in (head_az, head_ax, head_masked)]
+    shove_r = step_dt * at(g_b, 0, 0) * head_masked(0, 0)
+    head_rad_own = head_rad(0, 0)
     back_press = (
-        seed_1[1 : 1 + na, 1 : 1 + nx]
-        - step_dt * advect_back4((u1 * seed_1)[None], (w1 * seed_1)[None], na, nx)[0]
-    )
-    shoves = step_dt * b1 * heads
-    own = (slice(1, 1 + na), slice(1, 1 + nx))
-    shove_r = shoves[2][own]
-    back_press = (
-        back_press
-        + (shoves[0][own] - shoves[0][0:na, 1 : 1 + nx])
-        + (shoves[1][own] - shoves[1][1 : 1 + na, 0:nx])
+        seed(0, 0)
+        - step_dt * back_advect(seed)
+        + (step_dt * at(g_b, 0, 0) * head_az(0, 0) - step_dt * at(g_b, -1, 0) * head_az(-1, 0))
+        + (step_dt * at(g_b, 0, 0) * head_ax(0, 0) - step_dt * at(g_b, 0, -1) * head_ax(0, -1))
         + (shove_r - rad_prev(shove_r))
-    )
-    head_rad_own = head_rad[own]
-    back_press = back_press + jnp.where(casing_mask(head_rad_own.shape), wall[:, :, None] * head_rad_own, 0.0)
-    base = jnp.concatenate([back_press[None], backs], axis=0)
+        + jnp.where(casing, wall[:, :, None] * head_rad_own, 0.0)
+    )
+    base = jnp.stack([back_press] + backs)
 
     press_top = acoustic[0, :, :, top]
-    sens_base = press_top * head_rad_own[:, :, top]
+    sens_base = press_top * (adjoint_in[3, :, :, top] + push[:, :, top])
     sens_placed = press_top * push_0
     seg_base = jnp.sum(jnp.where(segment_hot, sens_base[:, :, None], 0.0), axis=(0, 1))
     seg_placed = jnp.sum(jnp.where(segment_hot, sens_placed[:, :, None], 0.0), axis=(0, 1))
@@ -242,7 +255,7 @@
     grad_scale = (na * lax.axis_size("az") * nx * lax.axis_size("ax") / nseg) ** (-0.5)
     liner_grad = (totals[1 : 1 + nseg] + totals[1 + nseg :] / mean_sq) * grad_scale
     misfit = 0.5 * jnp.log(mean_sq)
-    adjoint_out = jnp.concatenate([base[..., : nr - 2], base[..., nr - 2 :] + extra / mean_sq], axis=-1)
+    adjoint_out = base + jnp.pad(extra / mean_sq, ((0, 0), (0, 0), (0, 0), (nr - 2, 0)))
     return (adjoint_out, liner_grad, misfit)
 
 

time: 82.1 us -> 63.8 us (0.78)
  other arithmetic: 22 us -> 8.58 us
  local copies, waits for them, and re-layouts: 17.2 us -> 8.46 us
  starting transfers between devices: 22.6 us -> 27.7 us
  waiting for transfers between devices: 16.9 us -> 15.5 us
    ppermute x4, waiting for transfers between devices: 10.8 us -> 4.26 us  [with_halo(): lax.ppermute(lax.slice_in_dim(array, length - before, length, axis=dim),...]
    another operation x1 -> x5, other arithmetic: 6.17 us -> 0.37 us  [shards(): base = jnp.stack([back_press] + backs)]
    ppermute x5, starting transfers between devices: 2.81 us -> 8.03 us  [butterfly_sum(): lax.ppermute(values, axis, [(i, i ^ step) for i in range(size)])]
    unnamed x53 -> x40, local copies, waits for them, and re-layouts: 9.23 us -> 4.16 us
    ppermute x5, waiting for transfers between devices: 6.05 us -> 9.97 us  [butterfly_sum(): lax.ppermute(values, axis, [(i, i ^ step) for i in range(size)])]
    mul x2 -> x3, other arithmetic: 3.58 us -> 1.11 us  [the longest x1 0.89 us: shards(): stiffness = mean_flow[2] * mean_flow[3] * mean_flow[3]]
    concatenate x2 -> x0, other arithmetic: 2.3 us -> none  [the longest x1 1.46 us: shards(): base = jnp.concatenate([back_press[None], backs], axis=0)]
    sub x1 -> x0, other arithmetic: 1.68 us -> none  [shards(): heads[:, 1:1 + na, 1:1 + nx, :]]
  transfers between devices with their start and end apart: 13 -> 13, of which waited for: 5 -> 8; matrix products, arithmetic and copies ran while one was open for 16% -> 8% of each run, Pallas kernels for 0% -> 0%
where the time goes in v4:
time: 63.8 us; the launch traced here: 63.4 us
  starting transfers between devices  27.7 us (43%)
  waiting for transfers between devices  15.5 us (24%)
  other arithmetic  8.58 us (13%)
  local copies, waits for them, and re-layouts  8.46 us (13%)
  between operations  3.04 us (5%)
    ppermute x4, starting transfers between devices, with_halo(): lax.ppermute(lax.slice_in_dim(array, length - before, length, axis=dim),...  10.4 us
    ppermute x5, waiting for transfers between devices, butterfly_sum(): lax.ppermute(values, axis, [(i, i ^ step) for i in range(size)])  9.97 us
    ppermute x4, starting transfers between devices, with_halo(): lax.ppermute(lax.slice_in_dim(array, 0, after, axis=dim), axis, down)  9.35 us
    ppermute x5, starting transfers between devices, butterfly_sum(): lax.ppermute(values, axis, [(i, i ^ step) for i in range(size)])  8.03 us
    ppermute x4, waiting for transfers between devices, with_halo(): lax.ppermute(lax.slice_in_dim(array, length - before, length, axis=dim),...  4.26 us
    unnamed x40, local copies, waits for them, and re-layouts  4.16 us
    add x1, other arithmetic, shards(): base + jnp.pad(extra / mean_sq, ((0, 0), (0, 0), (0, 0), (nr - 2, 0)))  1.48 us
    ppermute x4, waiting for transfers between devices, with_halo(): lax.ppermute(lax.slice_in_dim(array, 0, after, axis=dim), axis, down)  1.32 us
  transfers between devices with their start and end apart: 13, of which 8 were waited for; matrix products, arithmetic and copies ran while one was open for 8% of the time, Pallas kernels for 0%

profile of v4, /device:TPU:0, one launch (start us, length us, event | category | flops | bytes accessed | tf_op | source)
XLA Modules:
  0.0 63.4 jit_solution(6784739413804941559)
XLA Ops:
  1.5 1.0 %slice_bitcast_fusion.8 = (f32[8,16,128]{2,1,0:T(8,128)S(1)}, f32[1,8,16,128]{3,2,1,0:T(8,128)S(1)}, f32[1,8,16,128]{3,2,1,0:T(8,128)S(1)}, f32[1,8,16,128]{3,2,1,0:T(8,128)S(1)}, f32[1,8,16,128]{3,2,1,0:T(8,128)S(1)}) fusion(f32[4,8,16,128]{3,2,1,0:T(8,128)} %param.12, f32[4,8,16,128]{3,2,1,0:T(8,128)} %param.11), kind=kLoop, calls=%fused_computation.124 | loop fusion | flops 81920 | bytes 655360 | tf_op jit(solution)/shard_map/squeeze | solution.py:96
  2.5 0.9 %slice.760 = f32[1,8,16,1]{3,2,1,0:T(8,128)S(1)} slice(f32[4,8,16,128]{3,2,1,0:T(8,128)} %param.12), slice={[3:4], [0:8], [0:16], [127:128]} | slice | bytes 1024 | tf_op jit(solution)/shard_map/slice | solution.py:248
  3.5 1.2 %fusion.124 = (f32[1,8,16,1]{3,2,1,0:T(8,128)S(1)}, f32[1,8,16,1]{3,2,1,0:T(8,128)S(1)}, f32[1,8,16,1]{3,2,1,0:T(8,128)S(1)}, f32[1,8,16,1]{3,2,1,0:T(8,128)S(1)}, f32[1,8,16,1]{3,2,1,0:T(8,128)S(1)}) fusion(f32[4,8,16,128]{3,2,1,0:T(8,128)} %param.10), kind=kLoop, calls=%fused_computation.275 | loop fusion | bytes 5120 | tf_op jit(solution)/shard_map/slice | solution.py:105
  7.2 2.4 %collective-permute-start.4 = (f32[14,8,3]{2,1,0:T(8,128)S(1)}, f32[14,8,3]{2,1,0:T(8,128)S(1)}, u32[]{:S(2)}, u32[]{:S(2)}) collective-permute-start(f32[14,8,3]{2,1,0:T(8,128)S(1)} %get-tuple-element.75), channel_id=1, source_target_pairs={{0,1},{1,2},{2,3},{4,5},{5,6},{6,7},{8,9},{9,10},{10,11},{12,13},{... | collective-permute-start | bytes 4040 | tf_op jit(solution)/shard_map/ppermute | solution.py:16
  9.5 1.3 %collective-permute-start.5 = (f32[14,8,3]{2,1,0:T(8,128)S(1)}, f32[14,8,3]{2,1,0:T(8,128)S(1)}, u32[]{:S(2)}, u32[]{:S(2)}) collective-permute-start(f32[14,8,3]{2,1,0:T(8,128)S(1)} %get-tuple-element.76), channel_id=1, source_target_pairs={{1,0},{2,1},{3,2},{5,4},{6,5},{7,6},{9,8},{10,9},{11,10},{13,12},{... | collective-permute-start | bytes 4040 | tf_op jit(solution)/shard_map/ppermute | solution.py:19
  11.0 5.2 %collective-permute-start = (f32[8,8,8,128]{3,2,1,0:T(8,128)S(1)}, f32[8,8,8,128]{3,2,1,0:T(8,128)S(1)}, u32[]{:S(2)}, u32[]{:S(2)}) collective-permute-start(f32[8,8,8,128]{3,2,1,0:T(8,128)S(1)} %get-tuple-element.40), channel_id=1, source_target_pairs={{0,1},{1,2},{2,3},{4,5},{5,6},{6,7},{8,9},{9,10},{10,11},{12,13},{... | collective-permute-start | bytes 786440 | tf_op jit(solution)/shard_map/ppermute | solution.py:16
  16.1 1.3 %collective-permute-start.1 = (f32[8,8,8,128]{3,2,1,0:T(8,128)S(1)}, f32[8,8,8,128]{3,2,1,0:T(8,128)S(1)}, u32[]{:S(2)}, u32[]{:S(2)}) collective-permute-start(f32[8,8,8,128]{3,2,1,0:T(8,128)S(1)} %get-tuple-element.41), channel_id=1, source_target_pairs={{1,0},{2,1},{3,2},{5,4},{6,5},{7,6},{9,8},{10,9},{11,10},{13,12},{... | collective-permute-start | bytes 786440 | tf_op jit(solution)/shard_map/ppermute | solution.py:19
  17.6 1.6 %collective-permute-start.6 = (f32[14,3,22]{2,1,0:T(4,128)S(1)}, f32[14,3,22]{2,1,0:T(4,128)S(1)}, u32[]{:S(2)}, u32[]{:S(2)}) collective-permute-start(f32[14,3,22]{2,1,0:T(4,128)S(1)} %get-tuple-element.73), channel_id=1, source_target_pairs={{0,4},{4,8},{8,12},{12,16},{16,20},{20,24},{24,28},{28,0},{1,5},{5... | collective-permute-start | bytes 11096 | tf_op jit(solution)/shard_map/ppermute | solution.py:16
  19.2 3.2 %collective-permute-start.7 = (f32[14,3,22]{2,1,0:T(4,128)S(1)}, f32[14,3,22]{2,1,0:T(4,128)S(1)}, u32[]{:S(2)}, u32[]{:S(2)}) collective-permute-start(f32[14,3,22]{2,1,0:T(4,128)S(1)} %get-tuple-element.74), channel_id=1, source_target_pairs={{4,0},{8,4},{12,8},{16,12},{20,16},{24,20},{28,24},{0,28},{5,1},{9... | collective-permute-start | bytes 11096 | tf_op jit(solution)/shard_map/ppermute | solution.py:19
  22.4 1.9 %collective-permute-done.6 = f32[14,3,22]{2,1,0:T(4,128)S(1)} collective-permute-done((f32[14,3,22]{2,1,0:T(4,128)S(1)}, f32[14,3,22]{2,1,0:T(4,128)S(1)}, u32[]{:S(2)}, u32[]{:S(2)}) %collective-permute-start.6) | collective-permute-done | bytes 3728 | tf_op jit(solution)/shard_map/ppermute | solution.py:16
  27.1 1.2 %collective-permute-start.8 = (f32[129]{0:T(256)S(1)}, f32[129]{0:T(256)S(1)}, u32[]{:S(2)}, u32[]{:S(2)}) collective-permute-start(f32[129]{0:T(256)S(1)} %pad_maximum_fusion.11), channel_id=1, source_target_pairs={{0,1},{1,0},{2,3},{3,2},{4,5},{5,4},{6,7},{7,6},{8,9},{9,8},{10,11... | collective-permute-start | bytes 1556 | tf_op jit(solution)/shard_map/ppermute | solution.py:67
  29.8 3.0 %collective-permute-start.9 = (f32[129]{0:T(256)S(1)}, f32[129]{0:T(256)S(1)}, u32[]{:S(2)}, u32[]{:S(2)}) collective-permute-start(f32[129]{0:T(256)S(1)} %fusion.128), channel_id=1, source_target_pairs={{0,2},{1,3},{2,0},{3,1},{4,6},{5,7},{6,4},{7,5},{8,10},{9,11},{10,... | collective-permute-start | bytes 1556 | tf_op jit(solution)/shard_map/ppermute | solution.py:67
  32.9 1.5 %collective-permute-done.9 = f32[129]{0:T(256)S(1)} collective-permute-done((f32[129]{0:T(256)S(1)}, f32[129]{0:T(256)S(1)}, u32[]{:S(2)}, u32[]{:S(2)}) %collective-permute-start.9) | collective-permute-done | bytes 548 | tf_op jit(solution)/shard_map/ppermute | solution.py:67
  34.4 1.2 %collective-permute-start.10 = (f32[129]{0:T(256)S(1)}, f32[129]{0:T(256)S(1)}, u32[]{:S(2)}, u32[]{:S(2)}) collective-permute-start(f32[129]{0:T(256)S(1)} %add.234), channel_id=1, source_target_pairs={{0,4},{4,0},{8,12},{12,8},{16,20},{20,16},{24,28},{28,24},{1,5},{5... | collective-permute-start | bytes 1556 | tf_op jit(solution)/shard_map/ppermute | solution.py:67
  35.6 2.3 %collective-permute-done.10 = f32[129]{0:T(256)S(1)} collective-permute-done((f32[129]{0:T(256)S(1)}, f32[129]{0:T(256)S(1)}, u32[]{:S(2)}, u32[]{:S(2)}) %collective-permute-start.10) | collective-permute-done | bytes 548 | tf_op jit(solution)/shard_map/ppermute | solution.py:67
  38.7 2.8 %collective-permute-done.11 = f32[129]{0:T(256)S(1)} collective-permute-done((f32[129]{0:T(256)S(1)}, f32[129]{0:T(256)S(1)}, u32[]{:S(2)}, u32[]{:S(2)}) %collective-permute-start.11) | collective-permute-done | bytes 548 | tf_op jit(solution)/shard_map/ppermute | solution.py:67
  41.5 1.8 %collective-permute-start.12 = (f32[129]{0:T(256)S(1)}, f32[129]{0:T(256)S(1)}, u32[]{:S(2)}, u32[]{:S(2)}) collective-permute-start(f32[129]{0:T(256)S(1)} %add.236), channel_id=1, source_target_pairs={{0,16},{4,20},{8,24},{12,28},{16,0},{20,4},{24,8},{28,12},{1,17},{... | collective-permute-start | bytes 1556 | tf_op jit(solution)/shard_map/ppermute | solution.py:67
  43.3 2.7 %collective-permute-done.12 = f32[129]{0:T(256)S(1)} collective-permute-done((f32[129]{0:T(256)S(1)}, f32[129]{0:T(256)S(1)}, u32[]{:S(2)}, u32[]{:S(2)}) %collective-permute-start.12) | collective-permute-done | bytes 548 | tf_op jit(solution)/shard_map/ppermute | solution.py:67
  47.2 1.3 %collective-permute-start.2 = (f32[8,1,32,128]{3,2,1,0:T(8,128)S(1)}, f32[8,1,32,128]{3,2,1,0:T(8,128)S(1)}, u32[]{:S(2)}, u32[]{:S(2)}) collective-permute-start(f32[8,1,32,128]{3,2,1,0:T(8,128)S(1)} %pad_maximum_fusion.8), channel_id=1, source_target_pairs={{0,4},{4,8},{8,12},{12,16},{16,20},{20,24},{24,28},{28,0},{1,5},{5... | collective-permute-start | bytes 393224 | tf_op jit(solution)/shard_map/ppermute | solution.py:16
  48.5 3.6 %collective-permute-start.3 = (f32[8,2,32,128]{3,2,1,0:T(8,128)S(1)}, f32[8,2,32,128]{3,2,1,0:T(8,128)S(1)}, u32[]{:S(2)}, u32[]{:S(2)}) collective-permute-start(f32[8,2,32,128]{3,2,1,0:T(8,128)S(1)} %pad_maximum_fusion.2), channel_id=1, source_target_pairs={{4,0},{8,4},{12,8},{16,12},{20,16},{24,20},{28,24},{0,28},{5,1},{9... | collective-permute-start | bytes 786440 | tf_op jit(solution)/shard_map/ppermute | solution.py:19
  52.7 2.3 %collective-permute-done.2 = f32[8,1,32,128]{3,2,1,0:T(8,128)S(1)} collective-permute-done((f32[8,1,32,128]{3,2,1,0:T(8,128)S(1)}, f32[8,1,32,128]{3,2,1,0:T(8,128)S(1)}, u32[]{:S(2)}, u32[]{:S(2)}) %collective-permute-start.2) | collective-permute-done | bytes 131104 | tf_op jit(solution)/shard_map/ppermute | solution.py:16
  55.0 1.3 %collective-permute-done.3 = f32[8,2,32,128]{3,2,1,0:T(8,128)S(1)} collective-permute-done((f32[8,2,32,128]{3,2,1,0:T(8,128)S(1)}, f32[8,2,32,128]{3,2,1,0:T(8,128)S(1)}, u32[]{:S(2)}, u32[]{:S(2)}) %collective-permute-start.3) | collective-permute-done | bytes 262176 | tf_op jit(solution)/shard_map/ppermute | solution.py:19
  57.9 1.5 %pad_add_fusion = f32[4,8,16,128]{2,1,3,0:T(8,128)} fusion(f32[4,8,16,128]{2,1,3,0:T(8,128)S(1)} %copy.79, f32[4,8,16,2]{2,1,3,0:T(8,128)S(1)} %maximum_divide_fusion), kind=kLoop, calls=%fused_computation | loop fusion | flops 65536 | bytes 528384 | tf_op jit(solution)/shard_map/add | solution.py:258
  59.4 2.9 %copy.80 = f32[4,8,16,128]{3,2,1,0:T(8,128)} copy(f32[4,8,16,128]{2,1,3,0:T(8,128)} %pad_add_fusion) | data formatting | bytes 524288
  (103 shorter events, 11.2 us)
Async XLA Ops:
  3.4 3.2 %copy-start.2 = (s32[8,16]{1,0:T(8,128)S(1)}, s32[8,16]{1,0:T(8,128)}, u32[]{:S(2)}) copy-start(s32[8,16]{1,0:T(8,128)} %param.14) | copy-start | bytes 1540
  3.5 3.2 %copy-start.7 = (f32[64]{0:T(128)S(1)}, f32[64]{0:T(128)}, u32[]{:S(2)}) copy-start(f32[64]{0:T(128)} %param.13) | copy-start | bytes 772
  3.5 3.4 %copy-start.5 = (s32[8,16]{1,0:T(8,128)S(1)}, s32[8,16]{1,0:T(8,128)}, u32[]{:S(2)}) copy-start(s32[8,16]{1,0:T(8,128)} %param.15) | copy-start | bytes 1540
  3.5 3.4 %copy-start.8 = (f32[64]{0:T(128)S(1)}, f32[64]{0:T(128)}, u32[]{:S(2)}) copy-start(f32[64]{0:T(128)} %param.16) | copy-start | bytes 772
  3.5 7.3 %copy-start.1 = (f32[4,8,16,128]{3,2,1,0:T(8,128)S(1)}, f32[4,8,16,128]{3,2,1,0:T(8,128)}, u32[]{:S(2)}) copy-start(f32[4,8,16,128]{3,2,1,0:T(8,128)} %param.11) | copy-start | bytes 786436
  4.7 6.2 %copy-start = (f32[4,8,16,128]{3,2,1,0:T(8,128)S(1)}, f32[4,8,16,128]{3,2,1,0:T(8,128)}, u32[]{:S(2)}) copy-start(f32[4,8,16,128]{3,2,1,0:T(8,128)} %param.12) | copy-start | bytes 786436
  6.4 11.0 %copy-start.3 = (s32[512]{0:T(512)S(1)}, s32[512]{0:T(512)}, u32[]{:S(2)}) copy-start(s32[512]{0:T(512)} %param.18) | copy-start | bytes 6148
  6.5 11.0 %copy-start.4 = (s32[512]{0:T(512)S(1)}, s32[512]{0:T(512)}, u32[]{:S(2)}) copy-start(s32[512]{0:T(512)} %param.17) | copy-start | bytes 6148
  7.2 10.3 %collective-permute-start.4 = (f32[14,8,3]{2,1,0:T(8,128)S(1)}, f32[14,8,3]{2,1,0:T(8,128)S(1)}, u32[]{:S(2)}, u32[]{:S(2)}) collective-permute-start(f32[14,8,3]{2,1,0:T(8,128)S(1)} %get-tuple-element.75), channel_id=1, source_target_pairs={{0,1},{1,2},{2,3},{4,5},{5,6},{6,7},{8,9},{9,10},{10,11},{12,13},{... | collective-permute-start | bytes 4040 | tf_op jit(solution)/shard_map/ppermute | solution.py:16
  9.5 8.0 %collective-permute-start.5 = (f32[14,8,3]{2,1,0:T(8,128)S(1)}, f32[14,8,3]{2,1,0:T(8,128)S(1)}, u32[]{:S(2)}, u32[]{:S(2)}) collective-permute-start(f32[14,8,3]{2,1,0:T(8,128)S(1)} %get-tuple-element.76), channel_id=1, source_target_pairs={{1,0},{2,1},{3,2},{5,4},{6,5},{7,6},{9,8},{10,9},{11,10},{13,12},{... | collective-permute-start | bytes 4040 | tf_op jit(solution)/shard_map/ppermute | solution.py:19
  10.9 14.1 %copy-start.6 = (f32[512]{0:T(512)S(1)}, f32[512]{0:T(512)}, u32[]{:S(2)}) copy-start(f32[512]{0:T(512)} %param.19) | copy-start | bytes 6148
  11.0 36.2 %collective-permute-start = (f32[8,8,8,128]{3,2,1,0:T(8,128)S(1)}, f32[8,8,8,128]{3,2,1,0:T(8,128)S(1)}, u32[]{:S(2)}, u32[]{:S(2)}) collective-permute-start(f32[8,8,8,128]{3,2,1,0:T(8,128)S(1)} %get-tuple-element.40), channel_id=1, source_target_pairs={{0,1},{1,2},{2,3},{4,5},{5,6},{6,7},{8,9},{9,10},{10,11},{12,13},{... | collective-permute-start | bytes 786440 | tf_op jit(solution)/shard_map/ppermute | solution.py:16
  16.1 31.0 %collective-permute-start.1 = (f32[8,8,8,128]{3,2,1,0:T(8,128)S(1)}, f32[8,8,8,128]{3,2,1,0:T(8,128)S(1)}, u32[]{:S(2)}, u32[]{:S(2)}) collective-permute-start(f32[8,8,8,128]{3,2,1,0:T(8,128)S(1)} %get-tuple-element.41), channel_id=1, source_target_pairs={{1,0},{2,1},{3,2},{5,4},{6,5},{7,6},{9,8},{10,9},{11,10},{13,12},{... | collective-permute-start | bytes 786440 | tf_op jit(solution)/shard_map/ppermute | solution.py:19
  17.6 6.7 %collective-permute-start.6 = (f32[14,3,22]{2,1,0:T(4,128)S(1)}, f32[14,3,22]{2,1,0:T(4,128)S(1)}, u32[]{:S(2)}, u32[]{:S(2)}) collective-permute-start(f32[14,3,22]{2,1,0:T(4,128)S(1)} %get-tuple-element.73), channel_id=1, source_target_pairs={{0,4},{4,8},{8,12},{12,16},{16,20},{20,24},{24,28},{28,0},{1,5},{5... | collective-permute-start | bytes 11096 | tf_op jit(solution)/shard_map/ppermute | solution.py:16
  19.2 5.2 %collective-permute-start.7 = (f32[14,3,22]{2,1,0:T(4,128)S(1)}, f32[14,3,22]{2,1,0:T(4,128)S(1)}, u32[]{:S(2)}, u32[]{:S(2)}) collective-permute-start(f32[14,3,22]{2,1,0:T(4,128)S(1)} %get-tuple-element.74), channel_id=1, source_target_pairs={{4,0},{8,4},{12,8},{16,12},{20,16},{24,20},{28,24},{0,28},{5,1},{9... | collective-permute-start | bytes 11096 | tf_op jit(solution)/shard_map/ppermute | solution.py:19
  27.1 2.0 %collective-permute-start.8 = (f32[129]{0:T(256)S(1)}, f32[129]{0:T(256)S(1)}, u32[]{:S(2)}, u32[]{:S(2)}) collective-permute-start(f32[129]{0:T(256)S(1)} %pad_maximum_fusion.11), channel_id=1, source_target_pairs={{0,1},{1,0},{2,3},{3,2},{4,5},{5,4},{6,7},{7,6},{8,9},{9,8},{10,11... | collective-permute-start | bytes 1556 | tf_op jit(solution)/shard_map/ppermute | solution.py:67
  29.8 4.5 %collective-permute-start.9 = (f32[129]{0:T(256)S(1)}, f32[129]{0:T(256)S(1)}, u32[]{:S(2)}, u32[]{:S(2)}) collective-permute-start(f32[129]{0:T(256)S(1)} %fusion.128), channel_id=1, source_target_pairs={{0,2},{1,3},{2,0},{3,1},{4,6},{5,7},{6,4},{7,5},{8,10},{9,11},{10,... | collective-permute-start | bytes 1556 | tf_op jit(solution)/shard_map/ppermute | solution.py:67
  34.4 3.6 %collective-permute-start.10 = (f32[129]{0:T(256)S(1)}, f32[129]{0:T(256)S(1)}, u32[]{:S(2)}, u32[]{:S(2)}) collective-permute-start(f32[129]{0:T(256)S(1)} %add.234), channel_id=1, source_target_pairs={{0,4},{4,0},{8,12},{12,8},{16,20},{20,16},{24,28},{28,24},{1,5},{5... | collective-permute-start | bytes 1556 | tf_op jit(solution)/shard_map/ppermute | solution.py:67
  37.9 3.6 %collective-permute-start.11 = (f32[129]{0:T(256)S(1)}, f32[129]{0:T(256)S(1)}, u32[]{:S(2)}, u32[]{:S(2)}) collective-permute-start(f32[129]{0:T(256)S(1)} %add.235), channel_id=1, source_target_pairs={{0,8},{4,12},{8,0},{12,4},{16,24},{20,28},{24,16},{28,20},{1,9},{5... | collective-permute-start | bytes 1556 | tf_op jit(solution)/shard_map/ppermute | solution.py:67
  41.5 4.5 %collective-permute-start.12 = (f32[129]{0:T(256)S(1)}, f32[129]{0:T(256)S(1)}, u32[]{:S(2)}, u32[]{:S(2)}) collective-permute-start(f32[129]{0:T(256)S(1)} %add.236), channel_id=1, source_target_pairs={{0,16},{4,20},{8,24},{12,28},{16,0},{20,4},{24,8},{28,12},{1,17},{... | collective-permute-start | bytes 1556 | tf_op jit(solution)/shard_map/ppermute | solution.py:67
  47.2 7.8 %collective-permute-start.2 = (f32[8,1,32,128]{3,2,1,0:T(8,128)S(1)}, f32[8,1,32,128]{3,2,1,0:T(8,128)S(1)}, u32[]{:S(2)}, u32[]{:S(2)}) collective-permute-start(f32[8,1,32,128]{3,2,1,0:T(8,128)S(1)} %pad_maximum_fusion.8), channel_id=1, source_target_pairs={{0,4},{4,8},{8,12},{12,16},{16,20},{20,24},{24,28},{28,0},{1,5},{5... | collective-permute-start | bytes 393224 | tf_op jit(solution)/shard_map/ppermute | solution.py:16
  48.5 7.8 %collective-permute-start.3 = (f32[8,2,32,128]{3,2,1,0:T(8,128)S(1)}, f32[8,2,32,128]{3,2,1,0:T(8,128)S(1)}, u32[]{:S(2)}, u32[]{:S(2)}) collective-permute-start(f32[8,2,32,128]{3,2,1,0:T(8,128)S(1)} %pad_maximum_fusion.2), channel_id=1, source_target_pairs={{4,0},{8,4},{12,8},{16,12},{20,16},{24,20},{28,24},{0,28},{5,1},{9... | collective-permute-start | bytes 786440 | tf_op jit(solution)/shard_map/ppermute | solution.py:19

commit v5 on v4

--- a/solution.py
+++ b/solution.py
@@ -114,12 +114,38 @@
         source_top,
     ]
     stack_c = jnp.stack(planes)
-
+    n_planes = len(planes)
     tile = 8
-    wide_f = exchange(stack_f, 1, 2, tile, tile)
-    wide_c = exchange(stack_c, 3, 3)
-
-    oc = (3, 3)
+    reach = 3
+    packed = jnp.pad(jnp.transpose(stack_c, (1, 2, 0)), ((0, 0), (0, 0), (0, nr - n_planes)))
+    stack_all = jnp.concatenate([stack_f, packed[None]], axis=0)
+    n_f = stack_f.shape[0]
+    widened = with_halo(stack_all, "ax", 2, tile, tile, False)
+    size_az, length_a = (lax.axis_size("az"), widened.shape[1])
+    up = [(i, (i + 1) % size_az) for i in range(size_az)]
+    down = [(j, i) for i, j in up]
+    row_shape = (1,) + widened.shape[2:]
+    sent_up = jnp.concatenate(
+        [widened[:n_f, length_a - 1 :], widened[n_f, length_a - reach :].reshape((reach,) + row_shape)], axis=0
+    )
+    sent_down = jnp.concatenate(
+        [
+            widened[:n_f, :2].reshape((2 * n_f,) + row_shape),
+            widened[n_f, :reach].reshape((reach,) + row_shape),
+        ],
+        axis=0,
+    )
+    from_below = lax.ppermute(sent_up, "az", up)
+    from_above = lax.ppermute(sent_down, "az", down)
+    wide_f = jnp.concatenate(
+        [from_below[:n_f], widened[:n_f], from_above[: 2 * n_f].reshape((n_f, 2) + widened.shape[2:])], axis=1
+    )
+    wide_packed = jnp.concatenate(
+        [from_below[n_f:, 0], widened[n_f], from_above[2 * n_f :, 0]], axis=0
+    )
+    wide_c = jnp.transpose(wide_packed[:, :, :n_planes], (2, 0, 1))
+
+    oc = (reach, tile)
     p_t, p_b, va_t, vx_t, vr_b, u_t, u_b, w_t, w_b, b_t, b_b, s_t, wall_c, src_c = [wide_c[i] for i in range(14)]
     ea, ex = na + 3, nx + 3
 
@@ -255,7 +281,14 @@
     grad_scale = (na * lax.axis_size("az") * nx * lax.axis_size("ax") / nseg) ** (-0.5)
     liner_grad = (totals[1 : 1 + nseg] + totals[1 + nseg :] / mean_sq) * grad_scale
     misfit = 0.5 * jnp.log(mean_sq)
-    adjoint_out = base + jnp.pad(extra / mean_sq, ((0, 0), (0, 0), (0, 0), (nr - 2, 0)))
+    lane = lax.broadcasted_iota(jnp.int32, (1, 1, 1, nr), 3)
+    extra_scaled = extra / mean_sq
+    correction = jnp.where(
+        lane == nr - 1,
+        extra_scaled[..., 1:2],
+        jnp.where(lane == nr - 2, extra_scaled[..., 0:1], 0.0),
+    )
+    adjoint_out = base + correction
     return (adjoint_out, liner_grad, misfit)
 
 

time: 63.8 us -> 56.4 us (0.88)
  starting transfers between devices: 27.7 us -> 13.8 us
  waiting for transfers between devices: 15.5 us -> 23.6 us
  other arithmetic: 8.58 us -> 7.08 us
    ppermute x4 -> x1, starting transfers between devices: 9.35 us -> 1.29 us  [with_halo(): lax.ppermute(lax.slice_in_dim(array, 0, after, axis=dim), axis, down)]
    ppermute x4 -> x1, starting transfers between devices: 10.4 us -> 2.37 us  [with_halo(): lax.ppermute(lax.slice_in_dim(array, length - before, length, axis=dim),...]
    ppermute x0 -> x2, waiting for transfers between devices: none -> 7.49 us  [the longest x1 5.16 us: shards(): from_above = lax.ppermute(sent_down, 'az', down)]
    ppermute x0 -> x2, starting transfers between devices: none -> 4.83 us  [the longest x1 3.26 us: shards(): from_above = lax.ppermute(sent_down, 'az', down)]
    ppermute x4 -> x1, waiting for transfers between devices: 4.26 us -> 0.01 us  [with_halo(): lax.ppermute(lax.slice_in_dim(array, length - before, length, axis=dim),...]
    ppermute x4 -> x1, waiting for transfers between devices: 1.32 us -> 4.19 us  [with_halo(): lax.ppermute(lax.slice_in_dim(array, 0, after, axis=dim), axis, down)]
    ppermute x5, starting transfers between devices: 8.03 us -> 5.32 us  [butterfly_sum(): lax.ppermute(values, axis, [(i, i ^ step) for i in range(size)])]
    ppermute x5, waiting for transfers between devices: 9.97 us -> 11.9 us  [butterfly_sum(): lax.ppermute(values, axis, [(i, i ^ step) for i in range(size)])]
  transfers between devices with their start and end apart: 13 -> 9, of which waited for: 8 -> 7; matrix products, arithmetic and copies ran while one was open for 8% -> 2% of each run, Pallas kernels for 0% -> 0%
where the time goes in v5:
time: 56.4 us; the launch traced here: 56.1 us
  waiting for transfers between devices  23.6 us (42%)
  starting transfers between devices  13.8 us (24%)
  local copies, waits for them, and re-layouts  8.56 us (15%)
  other arithmetic  7.08 us (13%)
  between operations  3.05 us (5%)
    ppermute x5, waiting for transfers between devices, butterfly_sum(): lax.ppermute(values, axis, [(i, i ^ step) for i in range(size)])  11.9 us
    ppermute x5, starting transfers between devices, butterfly_sum(): lax.ppermute(values, axis, [(i, i ^ step) for i in range(size)])  5.32 us
    ppermute x1, waiting for transfers between devices, shards(): from_above = lax.ppermute(sent_down, 'az', down)  5.16 us
    ppermute x1, waiting for transfers between devices, with_halo(): lax.ppermute(lax.slice_in_dim(array, 0, after, axis=dim), axis, down)  4.19 us
    unnamed x41, local copies, waits for them, and re-layouts  3.28 us
    ppermute x1, starting transfers between devices, shards(): from_above = lax.ppermute(sent_down, 'az', down)  3.26 us
    ppermute x1, starting transfers between devices, with_halo(): lax.ppermute(lax.slice_in_dim(array, length - before, length, axis=dim),...  2.37 us
    ppermute x1, waiting for transfers between devices, shards(): from_below = lax.ppermute(sent_up, 'az', up)  2.33 us
  transfers between devices with their start and end apart: 9, of which 7 were waited for; matrix products, arithmetic and copies ran while one was open for 2% of the time, Pallas kernels for 0%

profile of v5, /device:TPU:0, one launch (start us, length us, event | category | flops | bytes accessed | tf_op | source)
XLA Modules:
  0.0 56.1 jit_solution(18199252610443049018)
XLA Ops:
  0.6 1.0 %constant_dynamic-update-slice_fusion.15 = f32[9,8,16,128]{3,2,1,0:T(8,128)S(1)} fusion(f32[4,8,16,128]{3,2,1,0:T(8,128)} %param.12), kind=kLoop, calls=%fused_computation.163 | loop fusion | bytes 524288
  1.7 0.9 %slice.786 = f32[1,8,16,1]{3,2,1,0:T(8,128)S(1)} slice(f32[4,8,16,128]{3,2,1,0:T(8,128)} %param.12), slice={[3:4], [0:8], [0:16], [127:128]} | slice | bytes 1024 | tf_op jit(solution)/shard_map/slice | solution.py:274
  2.6 1.1 %fusion.126 = (f32[1,8,16,1]{3,2,1,0:T(8,128)S(1)}, f32[1,8,16,1]{3,2,1,0:T(8,128)S(1)}, f32[1,8,16,1]{3,2,1,0:T(8,128)S(1)}, f32[1,8,16,1]{3,2,1,0:T(8,128)S(1)}, f32[1,8,16,1]{3,2,1,0:T(8,128)S(1)}) fusion(f32[4,8,16,128]{3,2,1,0:T(8,128)} %param.10), kind=kLoop, calls=%fused_computation.287 | loop fusion | bytes 5120 | tf_op jit(solution)/shard_map/slice | solution.py:105
  4.4 0.9 %slice_bitcast_fusion.9 = (f32[8,16,128]{2,1,0:T(8,128)S(1)}, f32[9,8,16,128]{3,2,1,0:T(8,128)S(1)}, f32[1,8,16,128]{3,2,1,0:T(8,128)S(1)}, f32[1,8,16,128]{3,2,1,0:T(8,128)S(1)}) fusion(f32[4,8,16,128]{3,2,1,0:T(8,128)} %param.12, f32[9,8,16,128]{3,2,1,0:T(8,128)S(1)} %divide_dynamic-update-slice_fusion, f32[4,8,16,128]{3,2,1,0:T(8,128)S(1)} %copy-done.1), kind=kLoop, calls=%fused_computation.143 | loop fusion | flops 65536 | bytes 589824 | tf_op jit(solution)/shard_map/squeeze | solution.py:96
  7.3 2.4 %collective-permute-start = (f32[9,8,8,128]{3,2,1,0:T(8,128)S(1)}, f32[9,8,8,128]{3,2,1,0:T(8,128)S(1)}, u32[]{:S(2)}, u32[]{:S(2)}) collective-permute-start(f32[9,8,8,128]{3,2,1,0:T(8,128)S(1)} %get-tuple-element.44), channel_id=1, source_target_pairs={{0,1},{1,2},{2,3},{4,5},{5,6},{6,7},{8,9},{9,10},{10,11},{12,13},{... | collective-permute-start | bytes 884744 | tf_op jit(solution)/shard_map/ppermute | solution.py:16
  9.7 1.3 %collective-permute-start.1 = (f32[9,8,8,128]{3,2,1,0:T(8,128)S(1)}, f32[9,8,8,128]{3,2,1,0:T(8,128)S(1)}, u32[]{:S(2)}, u32[]{:S(2)}) collective-permute-start(f32[9,8,8,128]{3,2,1,0:T(8,128)S(1)} %get-tuple-element.45), channel_id=1, source_target_pairs={{1,0},{2,1},{3,2},{5,4},{6,5},{7,6},{9,8},{10,9},{11,10},{13,12},{... | collective-permute-start | bytes 884744 | tf_op jit(solution)/shard_map/ppermute | solution.py:19
  11.0 4.2 %collective-permute-done.1 = f32[9,8,8,128]{3,2,1,0:T(8,128)S(1)} collective-permute-done((f32[9,8,8,128]{3,2,1,0:T(8,128)S(1)}, f32[9,8,8,128]{3,2,1,0:T(8,128)S(1)}, u32[]{:S(2)}, u32[]{:S(2)}) %collective-permute-start.1) | collective-permute-done | bytes 294944 | tf_op jit(solution)/shard_map/ppermute | solution.py:19
  15.3 1.6 %collective-permute-start.2 = (f32[11,1,32,128]{3,2,0,1:T(8,128)S(1)}, f32[11,1,32,128]{3,2,0,1:T(8,128)S(1)}, u32[]{:S(2)}, u32[]{:S(2)}) collective-permute-start(f32[11,1,32,128]{3,2,0,1:T(8,128)S(1)} %pad_maximum_fusion.6), channel_id=1, source_target_pairs={{0,4},{4,8},{8,12},{12,16},{16,20},{20,24},{24,28},{28,0},{1,5},{5... | collective-permute-start | bytes 540680 | tf_op jit(solution)/shard_map/ppermute | solution.py:138
  16.9 3.3 %collective-permute-start.3 = (f32[19,1,32,128]{3,2,0,1:T(8,128)S(1)}, f32[19,1,32,128]{3,2,0,1:T(8,128)S(1)}, u32[]{:S(2)}, u32[]{:S(2)}) collective-permute-start(f32[19,1,32,128]{3,2,0,1:T(8,128)S(1)} %pad_maximum_fusion.2), channel_id=1, source_target_pairs={{4,0},{8,4},{12,8},{16,12},{20,16},{24,20},{28,24},{0,28},{5,1},{9... | collective-permute-start | bytes 933896 | tf_op jit(solution)/shard_map/ppermute | solution.py:139
  20.3 1.0 %copy-done = f32[9,8,32,128]{3,2,1,0:T(8,128)} copy-done((f32[9,8,32,128]{3,2,1,0:T(8,128)}, f32[9,8,32,128]{3,2,1,0:T(8,128)S(1)}, u32[]{:S(2)}) %copy-start) | copy-done | bytes 1179672
  21.3 2.3 %collective-permute-done.2 = f32[11,1,32,128]{3,2,0,1:T(8,128)S(1)} collective-permute-done((f32[11,1,32,128]{3,2,0,1:T(8,128)S(1)}, f32[11,1,32,128]{3,2,0,1:T(8,128)S(1)}, u32[]{:S(2)}, u32[]{:S(2)}) %collective-permute-start.2) | collective-permute-done | bytes 180256 | tf_op jit(solution)/shard_map/ppermute | solution.py:138
  23.7 5.2 %collective-permute-done.3 = f32[19,1,32,128]{3,2,0,1:T(8,128)S(1)} collective-permute-done((f32[19,1,32,128]{3,2,0,1:T(8,128)S(1)}, f32[19,1,32,128]{3,2,0,1:T(8,128)S(1)}, u32[]{:S(2)}, u32[]{:S(2)}) %collective-permute-start.3) | collective-permute-done | bytes 311328 | tf_op jit(solution)/shard_map/ppermute | solution.py:139
  28.9 1.7 %slice_reduce_fusion.12 = (f32[14,32]{1,0:T(8,128)S(1)}, f32[14,32]{1,0:T(8,128)S(1)}, f32[14,32]{1,0:T(8,128)S(1)}, f32[14,32]{1,0:T(8,128)S(1)}, f32[14,32]{1,...) fusion(f32[14,14,32]{0,2,1:T(8,128)S(1)} %fusion), kind=kLoop, calls=%fused_computation.21 | loop fusion | bytes 50176 | tf_op jit(solution)/shard_map/slice | solution.py:149
  31.1 0.6 %select_reduce_fusion.6 = (f32[]{:T(128)}, f32[512]{0:T(512)S(1)}) fusion(s32[512]{0:T(512)S(1)} %copy-done.3, s32[]{:T(128)S(6)} %mul.402, s32[512]{0:T(512)S(1)} %copy-done.4, s32[]{:T(128)S(6)} %mul.401, f32[512]{0:T(512)S(1)} %select_reduce_fusion.1, f32[512]{0:T(512)S(1)} %copy-done.6), kind=kLoop, calls=%fused_computation.278 | loop fusion | flops 13311 | bytes 10252 | tf_op jit(solution)/shard_map/reduce_sum | solution.py:191
  32.4 0.7 %pad_maximum_fusion.7 = f32[129]{0:T(256)S(1)} fusion(f32[64]{0:T(128)S(1)} %get-tuple-element.25, f32[64]{0:T(128)S(1)} %get-tuple-element.24, f32[1]{0:T(128)} %bitcast.47), kind=kLoop, calls=%fused_computation.281 | loop fusion | flops 258 | bytes 1032 | tf_op jit(solution)/shard_map/concatenate | solution.py:279
  33.1 2.1 %collective-permute-start.4 = (f32[129]{0:T(256)S(1)}, f32[129]{0:T(256)S(1)}, u32[]{:S(2)}, u32[]{:S(2)}) collective-permute-start(f32[129]{0:T(256)S(1)} %pad_maximum_fusion.7), channel_id=1, source_target_pairs={{0,1},{1,0},{2,3},{3,2},{4,5},{5,4},{6,7},{7,6},{8,9},{9,8},{10,11... | collective-permute-start | bytes 1556 | tf_op jit(solution)/shard_map/ppermute | solution.py:67
  36.3 0.7 %fusion.128 = f32[129]{0:T(256)S(1)} fusion(f32[129]{0:T(256)S(1)} %collective-permute-done.4, f32[64]{0:T(128)S(1)} %get-tuple-element.25, f32[64]{0:T(128)S(1)} %get-tuple-element.24, f32[1]{0:T(128)} %bitcast.47), kind=kLoop, calls=%fused_computation.289 | loop fusion | flops 387 | bytes 1548 | tf_op jit(solution)/shard_map/add | solution.py:67
  37.0 3.5 %collective-permute-done.5 = f32[129]{0:T(256)S(1)} collective-permute-done((f32[129]{0:T(256)S(1)}, f32[129]{0:T(256)S(1)}, u32[]{:S(2)}, u32[]{:S(2)}) %collective-permute-start.5) | collective-permute-done | bytes 548 | tf_op jit(solution)/shard_map/ppermute | solution.py:67
  41.1 3.0 %collective-permute-done.6 = f32[129]{0:T(256)S(1)} collective-permute-done((f32[129]{0:T(256)S(1)}, f32[129]{0:T(256)S(1)}, u32[]{:S(2)}, u32[]{:S(2)}) %collective-permute-start.6) | collective-permute-done | bytes 548 | tf_op jit(solution)/shard_map/ppermute | solution.py:67
  44.2 0.8 %collective-permute-start.7 = (f32[129]{0:T(256)S(1)}, f32[129]{0:T(256)S(1)}, u32[]{:S(2)}, u32[]{:S(2)}) collective-permute-start(f32[129]{0:T(256)S(1)} %add.235), channel_id=1, source_target_pairs={{0,8},{4,12},{8,0},{12,4},{16,24},{20,28},{24,16},{28,20},{1,9},{5... | collective-permute-start | bytes 1556 | tf_op jit(solution)/shard_map/ppermute | solution.py:67
  45.0 2.7 %collective-permute-done.7 = f32[129]{0:T(256)S(1)} collective-permute-done((f32[129]{0:T(256)S(1)}, f32[129]{0:T(256)S(1)}, u32[]{:S(2)}, u32[]{:S(2)}) %collective-permute-start.7) | collective-permute-done | bytes 548 | tf_op jit(solution)/shard_map/ppermute | solution.py:67
  47.7 1.9 %collective-permute-start.8 = (f32[129]{0:T(256)S(1)}, f32[129]{0:T(256)S(1)}, u32[]{:S(2)}, u32[]{:S(2)}) collective-permute-start(f32[129]{0:T(256)S(1)} %add.236), channel_id=1, source_target_pairs={{0,16},{4,20},{8,24},{12,28},{16,0},{20,4},{24,8},{28,12},{1,17},{... | collective-permute-start | bytes 1556 | tf_op jit(solution)/shard_map/ppermute | solution.py:67
  49.6 2.6 %collective-permute-done.8 = f32[129]{0:T(256)S(1)} collective-permute-done((f32[129]{0:T(256)S(1)}, f32[129]{0:T(256)S(1)}, u32[]{:S(2)}, u32[]{:S(2)}) %collective-permute-start.8) | collective-permute-done | bytes 548 | tf_op jit(solution)/shard_map/ppermute | solution.py:67
  54.0 0.9 %maximum_add_fusion = f32[4,8,16,128]{3,2,1,0:T(8,128)} fusion(f32[1,8,16,128]{3,2,1,0:T(8,128)S(1)} %fusion.14, f32[1,8,16,128]{3,2,1,0:T(8,128)S(1)} %fusion.31, f32[1,8,16,128]{3,2,1,0:T(8,128)S(1)} %fusion.40, f32[1,8,16,128]{3,2,1,0:T(8,128)S(1)} %fusion.52, f32[4,8,16]{2,1,0:T(8,128)S(1)} %get-tuple-element.63, f32[4,8,16]{2,1,0:T(8,128)S(1)} %get-tuple-element.62, ...), kind=kLoop, calls=%fused_computation.8 | loop fusion | flops 393216 | bytes 528640 | tf_op jit(solution)/shard_map/add | solution.py:291
  (106 shorter events, 6.6 us)
Async XLA Ops:
  0.6 3.7 %copy-start.1 = (f32[4,8,16,128]{3,2,1,0:T(8,128)S(1)}, f32[4,8,16,128]{3,2,1,0:T(8,128)}, u32[]{:S(2)}) copy-start(f32[4,8,16,128]{3,2,1,0:T(8,128)} %param.11) | copy-start | bytes 786436
  4.3 2.2 %copy-start.2 = (s32[8,16]{1,0:T(8,128)S(1)}, s32[8,16]{1,0:T(8,128)}, u32[]{:S(2)}) copy-start(s32[8,16]{1,0:T(8,128)} %param.14) | copy-start | bytes 1540
  4.4 2.2 %copy-start.7 = (f32[64]{0:T(128)S(1)}, f32[64]{0:T(128)}, u32[]{:S(2)}) copy-start(f32[64]{0:T(128)} %param.13) | copy-start | bytes 772
  4.4 2.4 %copy-start.5 = (s32[8,16]{1,0:T(8,128)S(1)}, s32[8,16]{1,0:T(8,128)}, u32[]{:S(2)}) copy-start(s32[8,16]{1,0:T(8,128)} %param.15) | copy-start | bytes 1540
  4.4 2.4 %copy-start.8 = (f32[64]{0:T(128)S(1)}, f32[64]{0:T(128)}, u32[]{:S(2)}) copy-start(f32[64]{0:T(128)} %param.16) | copy-start | bytes 772
  6.2 4.7 %copy-start.3 = (s32[512]{0:T(512)S(1)}, s32[512]{0:T(512)}, u32[]{:S(2)}) copy-start(s32[512]{0:T(512)} %param.18) | copy-start | bytes 6148
  6.3 4.7 %copy-start.4 = (s32[512]{0:T(512)S(1)}, s32[512]{0:T(512)}, u32[]{:S(2)}) copy-start(s32[512]{0:T(512)} %param.17) | copy-start | bytes 6148
  7.3 3.7 %collective-permute-start = (f32[9,8,8,128]{3,2,1,0:T(8,128)S(1)}, f32[9,8,8,128]{3,2,1,0:T(8,128)S(1)}, u32[]{:S(2)}, u32[]{:S(2)}) collective-permute-start(f32[9,8,8,128]{3,2,1,0:T(8,128)S(1)} %get-tuple-element.44), channel_id=1, source_target_pairs={{0,1},{1,2},{2,3},{4,5},{5,6},{6,7},{8,9},{9,10},{10,11},{12,13},{... | collective-permute-start | bytes 884744 | tf_op jit(solution)/shard_map/ppermute | solution.py:16
  9.7 5.6 %collective-permute-start.1 = (f32[9,8,8,128]{3,2,1,0:T(8,128)S(1)}, f32[9,8,8,128]{3,2,1,0:T(8,128)S(1)}, u32[]{:S(2)}, u32[]{:S(2)}) collective-permute-start(f32[9,8,8,128]{3,2,1,0:T(8,128)S(1)} %get-tuple-element.45), channel_id=1, source_target_pairs={{1,0},{2,1},{3,2},{5,4},{6,5},{7,6},{9,8},{10,9},{11,10},{13,12},{... | collective-permute-start | bytes 884744 | tf_op jit(solution)/shard_map/ppermute | solution.py:19
  15.3 8.4 %collective-permute-start.2 = (f32[11,1,32,128]{3,2,0,1:T(8,128)S(1)}, f32[11,1,32,128]{3,2,0,1:T(8,128)S(1)}, u32[]{:S(2)}, u32[]{:S(2)}) collective-permute-start(f32[11,1,32,128]{3,2,0,1:T(8,128)S(1)} %pad_maximum_fusion.6), channel_id=1, source_target_pairs={{0,4},{4,8},{8,12},{12,16},{16,20},{20,24},{24,28},{28,0},{1,5},{5... | collective-permute-start | bytes 540680 | tf_op jit(solution)/shard_map/ppermute | solution.py:138
  16.9 11.9 %collective-permute-start.3 = (f32[19,1,32,128]{3,2,0,1:T(8,128)S(1)}, f32[19,1,32,128]{3,2,0,1:T(8,128)S(1)}, u32[]{:S(2)}, u32[]{:S(2)}) collective-permute-start(f32[19,1,32,128]{3,2,0,1:T(8,128)S(1)} %pad_maximum_fusion.2), channel_id=1, source_target_pairs={{4,0},{8,4},{12,8},{16,12},{20,16},{24,20},{28,24},{0,28},{5,1},{9... | collective-permute-start | bytes 933896 | tf_op jit(solution)/shard_map/ppermute | solution.py:139
  20.3 1.0 %copy-start = (f32[9,8,32,128]{3,2,1,0:T(8,128)}, f32[9,8,32,128]{3,2,1,0:T(8,128)S(1)}, u32[]{:S(2)}) copy-start(f32[9,8,32,128]{3,2,1,0:T(8,128)S(1)} %pad_maximum_fusion.1) | copy-start | bytes 3538948
  28.9 2.3 %copy-start.6 = (f32[512]{0:T(512)S(1)}, f32[512]{0:T(512)}, u32[]{:S(2)}) copy-start(f32[512]{0:T(512)} %param.19) | copy-start | bytes 6148
  30.6 4.7 %slice-start = ((f32[9,8,32,128]{3,2,1,0:T(8,128)}), f32[8,8,32,128]{3,2,1,0:T(8,128)S(1)}, s32[]{:S(2)}) async-start(f32[9,8,32,128]{3,2,1,0:T(8,128)} %copy-done), calls=%async_computation | async-start | bytes 2097152 | tf_op jit(solution)/shard_map/slice | solution.py:141
  33.1 3.2 %collective-permute-start.4 = (f32[129]{0:T(256)S(1)}, f32[129]{0:T(256)S(1)}, u32[]{:S(2)}, u32[]{:S(2)}) collective-permute-start(f32[129]{0:T(256)S(1)} %pad_maximum_fusion.7), channel_id=1, source_target_pairs={{0,1},{1,0},{2,3},{3,2},{4,5},{5,4},{6,7},{7,6},{8,9},{9,8},{10,11... | collective-permute-start | bytes 1556 | tf_op jit(solution)/shard_map/ppermute | solution.py:67
  37.0 3.6 %collective-permute-start.5 = (f32[129]{0:T(256)S(1)}, f32[129]{0:T(256)S(1)}, u32[]{:S(2)}, u32[]{:S(2)}) collective-permute-start(f32[129]{0:T(256)S(1)} %fusion.128), channel_id=1, source_target_pairs={{0,2},{1,3},{2,0},{3,1},{4,6},{5,7},{6,4},{7,5},{8,10},{9,11},{10,... | collective-permute-start | bytes 1556 | tf_op jit(solution)/shard_map/ppermute | solution.py:67
  40.6 3.6 %collective-permute-start.6 = (f32[129]{0:T(256)S(1)}, f32[129]{0:T(256)S(1)}, u32[]{:S(2)}, u32[]{:S(2)}) collective-permute-start(f32[129]{0:T(256)S(1)} %add.234), channel_id=1, source_target_pairs={{0,4},{4,0},{8,12},{12,8},{16,20},{20,16},{24,28},{28,24},{1,5},{5... | collective-permute-start | bytes 1556 | tf_op jit(solution)/shard_map/ppermute | solution.py:67
  44.2 3.6 %collective-permute-start.7 = (f32[129]{0:T(256)S(1)}, f32[129]{0:T(256)S(1)}, u32[]{:S(2)}, u32[]{:S(2)}) collective-permute-start(f32[129]{0:T(256)S(1)} %add.235), channel_id=1, source_target_pairs={{0,8},{4,12},{8,0},{12,4},{16,24},{20,28},{24,16},{28,20},{1,9},{5... | collective-permute-start | bytes 1556 | tf_op jit(solution)/shard_map/ppermute | solution.py:67
  47.7 4.5 %collective-permute-start.8 = (f32[129]{0:T(256)S(1)}, f32[129]{0:T(256)S(1)}, u32[]{:S(2)}, u32[]{:S(2)}) collective-permute-start(f32[129]{0:T(256)S(1)} %add.236), channel_id=1, source_target_pairs={{0,16},{4,20},{8,24},{12,28},{16,0},{20,4},{24,8},{28,12},{1,17},{... | collective-permute-start | bytes 1556 | tf_op jit(solution)/shard_map/ppermute | solution.py:67

commit v6 on v5

--- a/solution.py
+++ b/solution.py
@@ -124,25 +124,23 @@
     size_az, length_a = (lax.axis_size("az"), widened.shape[1])
     up = [(i, (i + 1) % size_az) for i in range(size_az)]
     down = [(j, i) for i, j in up]
-    row_shape = (1,) + widened.shape[2:]
-    sent_up = jnp.concatenate(
-        [widened[:n_f, length_a - 1 :], widened[n_f, length_a - reach :].reshape((reach,) + row_shape)], axis=0
-    )
-    sent_down = jnp.concatenate(
-        [
-            widened[:n_f, :2].reshape((2 * n_f,) + row_shape),
-            widened[n_f, :reach].reshape((reach,) + row_shape),
-        ],
-        axis=0,
+    sent_up = jnp.stack(
+        [widened[f, length_a - 1] for f in (0, 1, 2, 3, 5, 6, 7)]
+        + [widened[n_f, length_a - reach + k] for k in range(reach)]
+    )
+    sent_down = jnp.stack(
+        [widened[f, 0] for f in (0, 1, 2, 3, 5, 7)] + [widened[7, 1]] + [widened[n_f, k] for k in range(reach)]
     )
     from_below = lax.ppermute(sent_up, "az", up)
     from_above = lax.ppermute(sent_down, "az", down)
+    blank = jnp.zeros_like(from_below[0])
+    row_before = jnp.stack([from_below[i] for i in (0, 1, 2, 3)] + [blank] + [from_below[i] for i in (4, 5, 6)])
+    row_after = jnp.stack([from_above[i] for i in (0, 1, 2, 3)] + [blank, from_above[4], blank, from_above[5]])
+    row_after2 = jnp.stack([blank] * 7 + [from_above[6]])
     wide_f = jnp.concatenate(
-        [from_below[:n_f], widened[:n_f], from_above[: 2 * n_f].reshape((n_f, 2) + widened.shape[2:])], axis=1
-    )
-    wide_packed = jnp.concatenate(
-        [from_below[n_f:, 0], widened[n_f], from_above[2 * n_f :, 0]], axis=0
-    )
+        [row_before[:, None], widened[:n_f], row_after[:, None], row_after2[:, None]], axis=1
+    )
+    wide_packed = jnp.concatenate([from_below[7:], widened[n_f], from_above[7:]], axis=0)
     wide_c = jnp.transpose(wide_packed[:, :, :n_planes], (2, 0, 1))
 
     oc = (reach, tile)

time: 56.4 us -> 52.1 us (0.924)
  waiting for transfers between devices: 23.6 us -> 16.9 us
  starting transfers between devices: 13.8 us -> 17.4 us
  local copies, waits for them, and re-layouts: 8.56 us -> 7.23 us
    ppermute x1, waiting for transfers between devices: 5.16 us -> 0.46 us  [shards(): from_above = lax.ppermute(sent_down, 'az', down)]
    ppermute x5, starting transfers between devices: 5.32 us -> 8.96 us  [butterfly_sum(): lax.ppermute(values, axis, [(i, i ^ step) for i in range(size)])]
    ppermute x5, waiting for transfers between devices: 11.9 us -> 10.1 us  [butterfly_sum(): lax.ppermute(values, axis, [(i, i ^ step) for i in range(size)])]
    slice x3, local copies, waits for them, and re-layouts: 1.72 us -> 0.02 us  [the longest x1 0.01 us: shards(): from_below[7:]]
    unnamed x41 -> x46, local copies, waits for them, and re-layouts: 3.28 us -> 3.47 us
  transfers between devices with their start and end apart: 9 -> 9, of which waited for: 7 -> 7; matrix products, arithmetic and copies ran while one was open for 2% -> 3% of each run, Pallas kernels for 0% -> 0%
where the time goes in v6:
time: 52.1 us; the launch traced here: 51.8 us
  starting transfers between devices  17.4 us (33%)
  waiting for transfers between devices  16.9 us (32%)
  local copies, waits for them, and re-layouts  7.23 us (14%)
  other arithmetic  7.16 us (14%)
  between operations  3.1 us (6%)
    ppermute x5, waiting for transfers between devices, butterfly_sum(): lax.ppermute(values, axis, [(i, i ^ step) for i in range(size)])  10.1 us
    ppermute x5, starting transfers between devices, butterfly_sum(): lax.ppermute(values, axis, [(i, i ^ step) for i in range(size)])  8.96 us
    ppermute x1, waiting for transfers between devices, with_halo(): lax.ppermute(lax.slice_in_dim(array, 0, after, axis=dim), axis, down)  4.05 us
    unnamed x46, local copies, waits for them, and re-layouts  3.47 us
    ppermute x1, starting transfers between devices, shards(): from_above = lax.ppermute(sent_down, 'az', down)  3.2 us
    ppermute x1, starting transfers between devices, with_halo(): lax.ppermute(lax.slice_in_dim(array, length - before, length, axis=dim),...  2.37 us
    ppermute x1, waiting for transfers between devices, shards(): from_below = lax.ppermute(sent_up, 'az', up)  2.24 us
    ppermute x1, starting transfers between devices, shards(): from_below = lax.ppermute(sent_up, 'az', up)  1.57 us
  transfers between devices with their start and end apart: 9, of which 7 were waited for; matrix products, arithmetic and copies ran while one was open for 3% of the time, Pallas kernels for 0%

profile of v6, /device:TPU:0, one launch (start us, length us, event | category | flops | bytes accessed | tf_op | source)
XLA Modules:
  0.0 51.8 jit_solution(13163396390109579734)
XLA Ops:
  0.6 1.0 %constant_dynamic-update-slice_fusion.17 = f32[9,8,16,128]{3,2,1,0:T(8,128)S(1)} fusion(f32[4,8,16,128]{3,2,1,0:T(8,128)} %param.12), kind=kLoop, calls=%fused_computation.40 | loop fusion | bytes 524288
  1.7 0.9 %slice.877 = f32[1,8,16,1]{3,2,1,0:T(8,128)S(1)} slice(f32[4,8,16,128]{3,2,1,0:T(8,128)} %param.12), slice={[3:4], [0:8], [0:16], [127:128]} | slice | bytes 1024 | tf_op jit(solution)/shard_map/slice | solution.py:272
  2.6 1.1 %fusion.124 = (f32[1,8,16,1]{3,2,1,0:T(8,128)S(1)}, f32[1,8,16,1]{3,2,1,0:T(8,128)S(1)}, f32[1,8,16,1]{3,2,1,0:T(8,128)S(1)}, f32[1,8,16,1]{3,2,1,0:T(8,128)S(1)}, f32[1,8,16,1]{3,2,1,0:T(8,128)S(1)}) fusion(f32[4,8,16,128]{3,2,1,0:T(8,128)} %param.10), kind=kLoop, calls=%fused_computation.324 | loop fusion | bytes 5120 | tf_op jit(solution)/shard_map/slice | solution.py:105
  4.4 0.9 %slice_bitcast_fusion.8 = (f32[8,16,128]{2,1,0:T(8,128)S(1)}, f32[9,8,16,128]{3,2,1,0:T(8,128)S(1)}, f32[1,8,16,128]{3,2,1,0:T(8,128)S(1)}, f32[1,8,16,128]{3,2,1,0:T(8,128)S(1)}) fusion(f32[4,8,16,128]{3,2,1,0:T(8,128)} %param.12, f32[9,8,16,128]{3,2,1,0:T(8,128)S(1)} %constant_dynamic-update-slice_fusion.16, f32[4,8,16,128]{3,2,1,0:T(8,128)S(1)} %copy-done.1), kind=kLoop, calls=%fused_computation.166 | loop fusion | flops 65536 | bytes 589824 | tf_op jit(solution)/shard_map/squeeze | solution.py:96
  7.3 2.4 %collective-permute-start = (f32[9,8,8,128]{3,2,1,0:T(8,128)S(1)}, f32[9,8,8,128]{3,2,1,0:T(8,128)S(1)}, u32[]{:S(2)}, u32[]{:S(2)}) collective-permute-start(f32[9,8,8,128]{3,2,1,0:T(8,128)S(1)} %get-tuple-element.48), channel_id=1, source_target_pairs={{0,1},{1,2},{2,3},{4,5},{5,6},{6,7},{8,9},{9,10},{10,11},{12,13},{... | collective-permute-start | bytes 884744 | tf_op jit(solution)/shard_map/ppermute | solution.py:16
  9.7 1.3 %collective-permute-start.1 = (f32[9,8,8,128]{3,2,1,0:T(8,128)S(1)}, f32[9,8,8,128]{3,2,1,0:T(8,128)S(1)}, u32[]{:S(2)}, u32[]{:S(2)}) collective-permute-start(f32[9,8,8,128]{3,2,1,0:T(8,128)S(1)} %get-tuple-element.49), channel_id=1, source_target_pairs={{1,0},{2,1},{3,2},{5,4},{6,5},{7,6},{9,8},{10,9},{11,10},{13,12},{... | collective-permute-start | bytes 884744 | tf_op jit(solution)/shard_map/ppermute | solution.py:19
  11.2 4.0 %collective-permute-done.1 = f32[9,8,8,128]{3,2,1,0:T(8,128)S(1)} collective-permute-done((f32[9,8,8,128]{3,2,1,0:T(8,128)S(1)}, f32[9,8,8,128]{3,2,1,0:T(8,128)S(1)}, u32[]{:S(2)}, u32[]{:S(2)}) %collective-permute-start.1) | collective-permute-done | bytes 294944 | tf_op jit(solution)/shard_map/ppermute | solution.py:19
  15.4 1.6 %collective-permute-start.2 = (f32[10,32,128]{2,1,0:T(8,128)S(1)}, f32[10,32,128]{2,1,0:T(8,128)S(1)}, u32[]{:S(2)}, u32[]{:S(2)}) collective-permute-start(f32[10,32,128]{2,1,0:T(8,128)S(1)} %get-tuple-element.28), channel_id=1, source_target_pairs={{0,4},{4,8},{8,12},{12,16},{16,20},{20,24},{24,28},{28,0},{1,5},{5... | collective-permute-start | bytes 491528 | tf_op jit(solution)/shard_map/ppermute | solution.py:134
  16.9 3.2 %collective-permute-start.3 = (f32[10,32,128]{2,1,0:T(8,128)S(1)}, f32[10,32,128]{2,1,0:T(8,128)S(1)}, u32[]{:S(2)}, u32[]{:S(2)}) collective-permute-start(f32[10,32,128]{2,1,0:T(8,128)S(1)} %get-tuple-element.29), channel_id=1, source_target_pairs={{4,0},{8,4},{12,8},{16,12},{20,16},{24,20},{28,24},{0,28},{5,1},{9... | collective-permute-start | bytes 491528 | tf_op jit(solution)/shard_map/ppermute | solution.py:135
  20.3 1.0 %copy-done = f32[9,8,32,128]{3,2,1,0:T(8,128)} copy-done((f32[9,8,32,128]{3,2,1,0:T(8,128)}, f32[9,8,32,128]{3,2,1,0:T(8,128)S(1)}, u32[]{:S(2)}) %copy-start) | copy-done | bytes 1179672
  21.3 2.2 %collective-permute-done.2 = f32[10,32,128]{2,1,0:T(8,128)S(1)} collective-permute-done((f32[10,32,128]{2,1,0:T(8,128)S(1)}, f32[10,32,128]{2,1,0:T(8,128)S(1)}, u32[]{:S(2)}, u32[]{:S(2)}) %collective-permute-start.2) | collective-permute-done | bytes 163872 | tf_op jit(solution)/shard_map/ppermute | solution.py:134
  24.8 0.6 %select_reduce_fusion.6 = (f32[]{:T(128)}, f32[512]{0:T(512)S(1)}) fusion(s32[512]{0:T(512)S(1)} %copy-done.3, s32[]{:T(128)S(6)} %mul.402, s32[512]{0:T(512)S(1)} %copy-done.4, s32[]{:T(128)S(6)} %mul.401, f32[512]{0:T(512)S(1)} %select_reduce_fusion.1, f32[512]{0:T(512)S(1)} %copy-done.6), kind=kLoop, calls=%fused_computation.315 | loop fusion | flops 13311 | bytes 10252 | tf_op jit(solution)/shard_map/reduce_sum | solution.py:189
  26.1 0.7 %pad_maximum_fusion.4 = f32[129]{0:T(256)S(1)} fusion(f32[64]{0:T(128)S(1)} %get-tuple-element.11, f32[64]{0:T(128)S(1)} %get-tuple-element.10, f32[1]{0:T(128)} %bitcast.80), kind=kLoop, calls=%fused_computation.318 | loop fusion | flops 258 | bytes 1032 | tf_op jit(solution)/shard_map/concatenate | solution.py:277
  26.8 3.9 %collective-permute-start.4 = (f32[129]{0:T(256)S(1)}, f32[129]{0:T(256)S(1)}, u32[]{:S(2)}, u32[]{:S(2)}) collective-permute-start(f32[129]{0:T(256)S(1)} %pad_maximum_fusion.4), channel_id=1, source_target_pairs={{0,1},{1,0},{2,3},{3,2},{4,5},{5,4},{6,7},{7,6},{8,9},{9,8},{10,11... | collective-permute-start | bytes 1556 | tf_op jit(solution)/shard_map/ppermute | solution.py:67
  32.0 0.7 %fusion.127 = f32[129]{0:T(256)S(1)} fusion(f32[129]{0:T(256)S(1)} %collective-permute-done.4, f32[64]{0:T(128)S(1)} %get-tuple-element.11, f32[64]{0:T(128)S(1)} %get-tuple-element.10, f32[1]{0:T(128)} %bitcast.80), kind=kLoop, calls=%fused_computation.327 | loop fusion | flops 387 | bytes 1548 | tf_op jit(solution)/shard_map/add | solution.py:67
  32.7 0.9 %collective-permute-start.5 = (f32[129]{0:T(256)S(1)}, f32[129]{0:T(256)S(1)}, u32[]{:S(2)}, u32[]{:S(2)}) collective-permute-start(f32[129]{0:T(256)S(1)} %fusion.127), channel_id=1, source_target_pairs={{0,2},{1,3},{2,0},{3,1},{4,6},{5,7},{6,4},{7,5},{8,10},{9,11},{10,... | collective-permute-start | bytes 1556 | tf_op jit(solution)/shard_map/ppermute | solution.py:67
  33.6 2.7 %collective-permute-done.5 = f32[129]{0:T(256)S(1)} collective-permute-done((f32[129]{0:T(256)S(1)}, f32[129]{0:T(256)S(1)}, u32[]{:S(2)}, u32[]{:S(2)}) %collective-permute-start.5) | collective-permute-done | bytes 548 | tf_op jit(solution)/shard_map/ppermute | solution.py:67
  36.3 0.7 %collective-permute-start.6 = (f32[129]{0:T(256)S(1)}, f32[129]{0:T(256)S(1)}, u32[]{:S(2)}, u32[]{:S(2)}) collective-permute-start(f32[129]{0:T(256)S(1)} %add.234), channel_id=1, source_target_pairs={{0,4},{4,0},{8,12},{12,8},{16,20},{20,16},{24,28},{28,24},{1,5},{5... | collective-permute-start | bytes 1556 | tf_op jit(solution)/shard_map/ppermute | solution.py:67
  36.9 2.9 %collective-permute-done.6 = f32[129]{0:T(256)S(1)} collective-permute-done((f32[129]{0:T(256)S(1)}, f32[129]{0:T(256)S(1)}, u32[]{:S(2)}, u32[]{:S(2)}) %collective-permute-start.6) | collective-permute-done | bytes 548 | tf_op jit(solution)/shard_map/ppermute | solution.py:67
  39.9 1.2 %collective-permute-start.7 = (f32[129]{0:T(256)S(1)}, f32[129]{0:T(256)S(1)}, u32[]{:S(2)}, u32[]{:S(2)}) collective-permute-start(f32[129]{0:T(256)S(1)} %add.235), channel_id=1, source_target_pairs={{0,8},{4,12},{8,0},{12,4},{16,24},{20,28},{24,16},{28,20},{1,9},{5... | collective-permute-start | bytes 1556 | tf_op jit(solution)/shard_map/ppermute | solution.py:67
  41.1 2.3 %collective-permute-done.7 = f32[129]{0:T(256)S(1)} collective-permute-done((f32[129]{0:T(256)S(1)}, f32[129]{0:T(256)S(1)}, u32[]{:S(2)}, u32[]{:S(2)}) %collective-permute-start.7) | collective-permute-done | bytes 548 | tf_op jit(solution)/shard_map/ppermute | solution.py:67
  43.4 2.2 %collective-permute-start.8 = (f32[129]{0:T(256)S(1)}, f32[129]{0:T(256)S(1)}, u32[]{:S(2)}, u32[]{:S(2)}) collective-permute-start(f32[129]{0:T(256)S(1)} %add.236), channel_id=1, source_target_pairs={{0,16},{4,20},{8,24},{12,28},{16,0},{20,4},{24,8},{28,12},{1,17},{... | collective-permute-start | bytes 1556 | tf_op jit(solution)/shard_map/ppermute | solution.py:67
  45.7 2.2 %collective-permute-done.8 = f32[129]{0:T(256)S(1)} collective-permute-done((f32[129]{0:T(256)S(1)}, f32[129]{0:T(256)S(1)}, u32[]{:S(2)}, u32[]{:S(2)}) %collective-permute-start.8) | collective-permute-done | bytes 548 | tf_op jit(solution)/shard_map/ppermute | solution.py:67
  49.7 0.9 %maximum_add_fusion = f32[4,8,16,128]{3,2,1,0:T(8,128)} fusion(f32[1,8,16,128]{3,2,1,0:T(8,128)S(1)} %fusion.12, f32[1,8,16,128]{3,2,1,0:T(8,128)S(1)} %fusion.29, f32[1,8,16,128]{3,2,1,0:T(8,128)S(1)} %fusion.38, f32[1,8,16,128]{3,2,1,0:T(8,128)S(1)} %fusion.50, f32[4,8,16]{2,1,0:T(8,128)S(1)} %get-tuple-element.85, f32[4,8,16]{2,1,0:T(8,128)S(1)} %get-tuple-element.84, ...), kind=kLoop, calls=%fused_computation.6 | loop fusion | flops 393216 | bytes 528640 | tf_op jit(solution)/shard_map/add | solution.py:289
  (122 shorter events, 7.0 us)
Async XLA Ops:
  0.6 3.7 %copy-start.1 = (f32[4,8,16,128]{3,2,1,0:T(8,128)S(1)}, f32[4,8,16,128]{3,2,1,0:T(8,128)}, u32[]{:S(2)}) copy-start(f32[4,8,16,128]{3,2,1,0:T(8,128)} %param.11) | copy-start | bytes 786436
  4.3 2.2 %copy-start.2 = (s32[8,16]{1,0:T(8,128)S(1)}, s32[8,16]{1,0:T(8,128)}, u32[]{:S(2)}) copy-start(s32[8,16]{1,0:T(8,128)} %param.14) | copy-start | bytes 1540
  4.4 2.2 %copy-start.7 = (f32[64]{0:T(128)S(1)}, f32[64]{0:T(128)}, u32[]{:S(2)}) copy-start(f32[64]{0:T(128)} %param.13) | copy-start | bytes 772
  4.4 2.4 %copy-start.5 = (s32[8,16]{1,0:T(8,128)S(1)}, s32[8,16]{1,0:T(8,128)}, u32[]{:S(2)}) copy-start(s32[8,16]{1,0:T(8,128)} %param.15) | copy-start | bytes 1540
  4.4 2.4 %copy-start.8 = (f32[64]{0:T(128)S(1)}, f32[64]{0:T(128)}, u32[]{:S(2)}) copy-start(f32[64]{0:T(128)} %param.16) | copy-start | bytes 772
  6.2 4.9 %copy-start.3 = (s32[512]{0:T(512)S(1)}, s32[512]{0:T(512)}, u32[]{:S(2)}) copy-start(s32[512]{0:T(512)} %param.18) | copy-start | bytes 6148
  6.3 4.9 %copy-start.4 = (s32[512]{0:T(512)S(1)}, s32[512]{0:T(512)}, u32[]{:S(2)}) copy-start(s32[512]{0:T(512)} %param.17) | copy-start | bytes 6148
  7.3 3.9 %collective-permute-start = (f32[9,8,8,128]{3,2,1,0:T(8,128)S(1)}, f32[9,8,8,128]{3,2,1,0:T(8,128)S(1)}, u32[]{:S(2)}, u32[]{:S(2)}) collective-permute-start(f32[9,8,8,128]{3,2,1,0:T(8,128)S(1)} %get-tuple-element.48), channel_id=1, source_target_pairs={{0,1},{1,2},{2,3},{4,5},{5,6},{6,7},{8,9},{9,10},{10,11},{12,13},{... | collective-permute-start | bytes 884744 | tf_op jit(solution)/shard_map/ppermute | solution.py:16
  9.7 5.6 %collective-permute-start.1 = (f32[9,8,8,128]{3,2,1,0:T(8,128)S(1)}, f32[9,8,8,128]{3,2,1,0:T(8,128)S(1)}, u32[]{:S(2)}, u32[]{:S(2)}) collective-permute-start(f32[9,8,8,128]{3,2,1,0:T(8,128)S(1)} %get-tuple-element.49), channel_id=1, source_target_pairs={{1,0},{2,1},{3,2},{5,4},{6,5},{7,6},{9,8},{10,9},{11,10},{13,12},{... | collective-permute-start | bytes 884744 | tf_op jit(solution)/shard_map/ppermute | solution.py:19
  15.4 8.2 %collective-permute-start.2 = (f32[10,32,128]{2,1,0:T(8,128)S(1)}, f32[10,32,128]{2,1,0:T(8,128)S(1)}, u32[]{:S(2)}, u32[]{:S(2)}) collective-permute-start(f32[10,32,128]{2,1,0:T(8,128)S(1)} %get-tuple-element.28), channel_id=1, source_target_pairs={{0,4},{4,8},{8,12},{12,16},{16,20},{20,24},{24,28},{28,0},{1,5},{5... | collective-permute-start | bytes 491528 | tf_op jit(solution)/shard_map/ppermute | solution.py:134
  16.9 7.1 %collective-permute-start.3 = (f32[10,32,128]{2,1,0:T(8,128)S(1)}, f32[10,32,128]{2,1,0:T(8,128)S(1)}, u32[]{:S(2)}, u32[]{:S(2)}) collective-permute-start(f32[10,32,128]{2,1,0:T(8,128)S(1)} %get-tuple-element.29), channel_id=1, source_target_pairs={{4,0},{8,4},{12,8},{16,12},{20,16},{24,20},{28,24},{0,28},{5,1},{9... | collective-permute-start | bytes 491528 | tf_op jit(solution)/shard_map/ppermute | solution.py:135
  20.3 1.0 %copy-start = (f32[9,8,32,128]{3,2,1,0:T(8,128)}, f32[9,8,32,128]{3,2,1,0:T(8,128)S(1)}, u32[]{:S(2)}) copy-start(f32[9,8,32,128]{3,2,1,0:T(8,128)S(1)} %pad_maximum_fusion.1) | copy-start | bytes 3538948
  20.3 4.5 %copy-start.6 = (f32[512]{0:T(512)S(1)}, f32[512]{0:T(512)}, u32[]{:S(2)}) copy-start(f32[512]{0:T(512)} %param.19) | copy-start | bytes 6148
  23.5 7.4 %slice-start = ((f32[9,8,32,128]{3,2,1,0:T(8,128)}), f32[8,8,32,128]{3,2,1,0:T(8,128)S(1)}, s32[]{:S(2)}) async-start(f32[9,8,32,128]{3,2,1,0:T(8,128)} %copy-done), calls=%async_computation | async-start | bytes 2097152 | tf_op jit(solution)/shard_map/slice | solution.py:141
  26.8 5.2 %collective-permute-start.4 = (f32[129]{0:T(256)S(1)}, f32[129]{0:T(256)S(1)}, u32[]{:S(2)}, u32[]{:S(2)}) collective-permute-start(f32[129]{0:T(256)S(1)} %pad_maximum_fusion.4), channel_id=1, source_target_pairs={{0,1},{1,0},{2,3},{3,2},{4,5},{5,4},{6,7},{7,6},{8,9},{9,8},{10,11... | collective-permute-start | bytes 1556 | tf_op jit(solution)/shard_map/ppermute | solution.py:67
  32.7 3.6 %collective-permute-start.5 = (f32[129]{0:T(256)S(1)}, f32[129]{0:T(256)S(1)}, u32[]{:S(2)}, u32[]{:S(2)}) collective-permute-start(f32[129]{0:T(256)S(1)} %fusion.127), channel_id=1, source_target_pairs={{0,2},{1,3},{2,0},{3,1},{4,6},{5,7},{6,4},{7,5},{8,10},{9,11},{10,... | collective-permute-start | bytes 1556 | tf_op jit(solution)/shard_map/ppermute | solution.py:67
  36.3 3.6 %collective-permute-start.6 = (f32[129]{0:T(256)S(1)}, f32[129]{0:T(256)S(1)}, u32[]{:S(2)}, u32[]{:S(2)}) collective-permute-start(f32[129]{0:T(256)S(1)} %add.234), channel_id=1, source_target_pairs={{0,4},{4,0},{8,12},{12,8},{16,20},{20,16},{24,28},{28,24},{1,5},{5... | collective-permute-start | bytes 1556 | tf_op jit(solution)/shard_map/ppermute | solution.py:67
  39.9 3.6 %collective-permute-start.7 = (f32[129]{0:T(256)S(1)}, f32[129]{0:T(256)S(1)}, u32[]{:S(2)}, u32[]{:S(2)}) collective-permute-start(f32[129]{0:T(256)S(1)} %add.235), channel_id=1, source_target_pairs={{0,8},{4,12},{8,0},{12,4},{16,24},{20,28},{24,16},{28,20},{1,9},{5... | collective-permute-start | bytes 1556 | tf_op jit(solution)/shard_map/ppermute | solution.py:67
  43.4 4.5 %collective-permute-start.8 = (f32[129]{0:T(256)S(1)}, f32[129]{0:T(256)S(1)}, u32[]{:S(2)}, u32[]{:S(2)}) collective-permute-start(f32[129]{0:T(256)S(1)} %add.236), channel_id=1, source_target_pairs={{0,16},{4,20},{8,24},{12,28},{16,0},{20,4},{24,8},{28,12},{1,17},{... | collective-permute-start | bytes 1556 | tf_op jit(solution)/shard_map/ppermute | solution.py:67

commit v7 on v6

--- a/solution.py
+++ b/solution.py
@@ -274,7 +274,7 @@
     seg_base = jnp.sum(jnp.where(segment_hot, sens_base[:, :, None], 0.0), axis=(0, 1))
     seg_placed = jnp.sum(jnp.where(segment_hot, sens_placed[:, :, None], 0.0), axis=(0, 1))
 
-    totals = butterfly_sum(jnp.concatenate([square_sum[None], seg_base, seg_placed]), ("ax", "az"))
+    totals = butterfly_sum(jnp.concatenate([square_sum[None], seg_base, seg_placed]), ("az", "ax"))
     mean_sq = totals[0] / mic_az.shape[0] + epsilon
     grad_scale = (na * lax.axis_size("az") * nx * lax.axis_size("ax") / nseg) ** (-0.5)
     liner_grad = (totals[1 : 1 + nseg] + totals[1 + nseg :] / mean_sq) * grad_scale

time: 52.1 us -> 50.8 us (0.975)
  waiting for transfers between devices: 16.9 us -> 15.9 us
    ppermute x5, waiting for transfers between devices: 10.1 us -> 9.11 us  [butterfly_sum(): lax.ppermute(values, axis, [(i, i ^ step) for i in range(size)])]
  transfers between devices with their start and end apart: 9 -> 9, of which waited for: 7 -> 8; matrix products, arithmetic and copies ran while one was open for 3% -> 3% of each run, Pallas kernels for 0% -> 0%
where the time goes in v7:
time: 50.8 us; the launch traced here: 50.5 us
  starting transfers between devices  17.1 us (34%)
  waiting for transfers between devices  15.9 us (31%)
  local copies, waits for them, and re-layouts  7.23 us (14%)
  other arithmetic  7.15 us (14%)
  between operations  3.1 us (6%)
    ppermute x5, waiting for transfers between devices, butterfly_sum(): lax.ppermute(values, axis, [(i, i ^ step) for i in range(size)])  9.11 us
    ppermute x5, starting transfers between devices, butterfly_sum(): lax.ppermute(values, axis, [(i, i ^ step) for i in range(size)])  8.71 us
    ppermute x1, waiting for transfers between devices, with_halo(): lax.ppermute(lax.slice_in_dim(array, 0, after, axis=dim), axis, down)  4.05 us
    unnamed x46, local copies, waits for them, and re-layouts  3.47 us
    ppermute x1, starting transfers between devices, shards(): from_above = lax.ppermute(sent_down, 'az', down)  3.2 us
    ppermute x1, starting transfers between devices, with_halo(): lax.ppermute(lax.slice_in_dim(array, length - before, length, axis=dim),...  2.37 us
    ppermute x1, waiting for transfers between devices, shards(): from_below = lax.ppermute(sent_up, 'az', up)  2.24 us
    ppermute x1, starting transfers between devices, shards(): from_below = lax.ppermute(sent_up, 'az', up)  1.57 us
  transfers between devices with their start and end apart: 9, of which 8 were waited for; matrix products, arithmetic and copies ran while one was open for 3% of the time, Pallas kernels for 0%

profile of v7, /device:TPU:0, one launch (start us, length us, event | category | flops | bytes accessed | tf_op | source)
XLA Modules:
  0.0 50.5 jit_solution(9086956265094664629)
XLA Ops:
  0.6 1.0 %constant_dynamic-update-slice_fusion.17 = f32[9,8,16,128]{3,2,1,0:T(8,128)S(1)} fusion(f32[4,8,16,128]{3,2,1,0:T(8,128)} %param.12), kind=kLoop, calls=%fused_computation.40 | loop fusion | bytes 524288
  1.7 0.9 %slice.877 = f32[1,8,16,1]{3,2,1,0:T(8,128)S(1)} slice(f32[4,8,16,128]{3,2,1,0:T(8,128)} %param.12), slice={[3:4], [0:8], [0:16], [127:128]} | slice | bytes 1024 | tf_op jit(solution)/shard_map/slice | solution.py:272
  2.6 1.1 %fusion.124 = (f32[1,8,16,1]{3,2,1,0:T(8,128)S(1)}, f32[1,8,16,1]{3,2,1,0:T(8,128)S(1)}, f32[1,8,16,1]{3,2,1,0:T(8,128)S(1)}, f32[1,8,16,1]{3,2,1,0:T(8,128)S(1)}, f32[1,8,16,1]{3,2,1,0:T(8,128)S(1)}) fusion(f32[4,8,16,128]{3,2,1,0:T(8,128)} %param.10), kind=kLoop, calls=%fused_computation.324 | loop fusion | bytes 5120 | tf_op jit(solution)/shard_map/slice | solution.py:105
  4.4 0.9 %slice_bitcast_fusion.8 = (f32[8,16,128]{2,1,0:T(8,128)S(1)}, f32[9,8,16,128]{3,2,1,0:T(8,128)S(1)}, f32[1,8,16,128]{3,2,1,0:T(8,128)S(1)}, f32[1,8,16,128]{3,2,1,0:T(8,128)S(1)}) fusion(f32[4,8,16,128]{3,2,1,0:T(8,128)} %param.12, f32[9,8,16,128]{3,2,1,0:T(8,128)S(1)} %constant_dynamic-update-slice_fusion.16, f32[4,8,16,128]{3,2,1,0:T(8,128)S(1)} %copy-done.1), kind=kLoop, calls=%fused_computation.166 | loop fusion | flops 65536 | bytes 589824 | tf_op jit(solution)/shard_map/squeeze | solution.py:96
  7.3 2.4 %collective-permute-start = (f32[9,8,8,128]{3,2,1,0:T(8,128)S(1)}, f32[9,8,8,128]{3,2,1,0:T(8,128)S(1)}, u32[]{:S(2)}, u32[]{:S(2)}) collective-permute-start(f32[9,8,8,128]{3,2,1,0:T(8,128)S(1)} %get-tuple-element.48), channel_id=1, source_target_pairs={{0,1},{1,2},{2,3},{4,5},{5,6},{6,7},{8,9},{9,10},{10,11},{12,13},{... | collective-permute-start | bytes 884744 | tf_op jit(solution)/shard_map/ppermute | solution.py:16
  9.7 1.3 %collective-permute-start.1 = (f32[9,8,8,128]{3,2,1,0:T(8,128)S(1)}, f32[9,8,8,128]{3,2,1,0:T(8,128)S(1)}, u32[]{:S(2)}, u32[]{:S(2)}) collective-permute-start(f32[9,8,8,128]{3,2,1,0:T(8,128)S(1)} %get-tuple-element.49), channel_id=1, source_target_pairs={{1,0},{2,1},{3,2},{5,4},{6,5},{7,6},{9,8},{10,9},{11,10},{13,12},{... | collective-permute-start | bytes 884744 | tf_op jit(solution)/shard_map/ppermute | solution.py:19
  11.2 4.0 %collective-permute-done.1 = f32[9,8,8,128]{3,2,1,0:T(8,128)S(1)} collective-permute-done((f32[9,8,8,128]{3,2,1,0:T(8,128)S(1)}, f32[9,8,8,128]{3,2,1,0:T(8,128)S(1)}, u32[]{:S(2)}, u32[]{:S(2)}) %collective-permute-start.1) | collective-permute-done | bytes 294944 | tf_op jit(solution)/shard_map/ppermute | solution.py:19
  15.4 1.6 %collective-permute-start.2 = (f32[10,32,128]{2,1,0:T(8,128)S(1)}, f32[10,32,128]{2,1,0:T(8,128)S(1)}, u32[]{:S(2)}, u32[]{:S(2)}) collective-permute-start(f32[10,32,128]{2,1,0:T(8,128)S(1)} %get-tuple-element.28), channel_id=1, source_target_pairs={{0,4},{4,8},{8,12},{12,16},{16,20},{20,24},{24,28},{28,0},{1,5},{5... | collective-permute-start | bytes 491528 | tf_op jit(solution)/shard_map/ppermute | solution.py:134
  16.9 3.2 %collective-permute-start.3 = (f32[10,32,128]{2,1,0:T(8,128)S(1)}, f32[10,32,128]{2,1,0:T(8,128)S(1)}, u32[]{:S(2)}, u32[]{:S(2)}) collective-permute-start(f32[10,32,128]{2,1,0:T(8,128)S(1)} %get-tuple-element.29), channel_id=1, source_target_pairs={{4,0},{8,4},{12,8},{16,12},{20,16},{24,20},{28,24},{0,28},{5,1},{9... | collective-permute-start | bytes 491528 | tf_op jit(solution)/shard_map/ppermute | solution.py:135
  20.3 1.0 %copy-done = f32[9,8,32,128]{3,2,1,0:T(8,128)} copy-done((f32[9,8,32,128]{3,2,1,0:T(8,128)}, f32[9,8,32,128]{3,2,1,0:T(8,128)S(1)}, u32[]{:S(2)}) %copy-start) | copy-done | bytes 1179672
  21.3 2.2 %collective-permute-done.2 = f32[10,32,128]{2,1,0:T(8,128)S(1)} collective-permute-done((f32[10,32,128]{2,1,0:T(8,128)S(1)}, f32[10,32,128]{2,1,0:T(8,128)S(1)}, u32[]{:S(2)}, u32[]{:S(2)}) %collective-permute-start.2) | collective-permute-done | bytes 163872 | tf_op jit(solution)/shard_map/ppermute | solution.py:134
  24.8 0.6 %select_reduce_fusion.6 = (f32[]{:T(128)}, f32[512]{0:T(512)S(1)}) fusion(s32[512]{0:T(512)S(1)} %copy-done.3, s32[]{:T(128)S(6)} %mul.402, s32[512]{0:T(512)S(1)} %copy-done.4, s32[]{:T(128)S(6)} %mul.401, f32[512]{0:T(512)S(1)} %select_reduce_fusion.1, f32[512]{0:T(512)S(1)} %copy-done.6), kind=kLoop, calls=%fused_computation.315 | loop fusion | flops 13311 | bytes 10252 | tf_op jit(solution)/shard_map/reduce_sum | solution.py:189
  26.1 0.7 %pad_maximum_fusion.4 = f32[129]{0:T(256)S(1)} fusion(f32[64]{0:T(128)S(1)} %get-tuple-element.11, f32[64]{0:T(128)S(1)} %get-tuple-element.10, f32[1]{0:T(128)} %bitcast.80), kind=kLoop, calls=%fused_computation.318 | loop fusion | flops 258 | bytes 1032 | tf_op jit(solution)/shard_map/concatenate | solution.py:277
  26.8 0.7 %collective-permute-start.4 = (f32[129]{0:T(256)S(1)}, f32[129]{0:T(256)S(1)}, u32[]{:S(2)}, u32[]{:S(2)}) collective-permute-start(f32[129]{0:T(256)S(1)} %pad_maximum_fusion.4), channel_id=1, source_target_pairs={{0,4},{4,0},{8,12},{12,8},{16,20},{20,16},{24,28},{28,24},{1,5},{5... | collective-permute-start | bytes 1556 | tf_op jit(solution)/shard_map/ppermute | solution.py:67
  28.7 1.7 %collective-permute-done.4 = f32[129]{0:T(256)S(1)} collective-permute-done((f32[129]{0:T(256)S(1)}, f32[129]{0:T(256)S(1)}, u32[]{:S(2)}, u32[]{:S(2)}) %collective-permute-start.4) | collective-permute-done | bytes 548 | tf_op jit(solution)/shard_map/ppermute | solution.py:67
  30.4 0.7 %fusion.127 = f32[129]{0:T(256)S(1)} fusion(f32[129]{0:T(256)S(1)} %collective-permute-done.4, f32[64]{0:T(128)S(1)} %get-tuple-element.11, f32[64]{0:T(128)S(1)} %get-tuple-element.10, f32[1]{0:T(128)} %bitcast.80), kind=kLoop, calls=%fused_computation.327 | loop fusion | flops 387 | bytes 1548 | tf_op jit(solution)/shard_map/add | solution.py:67
  31.1 1.0 %collective-permute-start.5 = (f32[129]{0:T(256)S(1)}, f32[129]{0:T(256)S(1)}, u32[]{:S(2)}, u32[]{:S(2)}) collective-permute-start(f32[129]{0:T(256)S(1)} %fusion.127), channel_id=1, source_target_pairs={{0,8},{4,12},{8,0},{12,4},{16,24},{20,28},{24,16},{28,20},{1,9},{5... | collective-permute-start | bytes 1556 | tf_op jit(solution)/shard_map/ppermute | solution.py:67
  32.1 2.6 %collective-permute-done.5 = f32[129]{0:T(256)S(1)} collective-permute-done((f32[129]{0:T(256)S(1)}, f32[129]{0:T(256)S(1)}, u32[]{:S(2)}, u32[]{:S(2)}) %collective-permute-start.5) | collective-permute-done | bytes 548 | tf_op jit(solution)/shard_map/ppermute | solution.py:67
  34.7 2.0 %collective-permute-start.6 = (f32[129]{0:T(256)S(1)}, f32[129]{0:T(256)S(1)}, u32[]{:S(2)}, u32[]{:S(2)}) collective-permute-start(f32[129]{0:T(256)S(1)} %add.234), channel_id=1, source_target_pairs={{0,16},{4,20},{8,24},{12,28},{16,0},{20,4},{24,8},{28,12},{1,17},{... | collective-permute-start | bytes 1556 | tf_op jit(solution)/shard_map/ppermute | solution.py:67
  36.6 2.5 %collective-permute-done.6 = f32[129]{0:T(256)S(1)} collective-permute-done((f32[129]{0:T(256)S(1)}, f32[129]{0:T(256)S(1)}, u32[]{:S(2)}, u32[]{:S(2)}) %collective-permute-start.6) | collective-permute-done | bytes 548 | tf_op jit(solution)/shard_map/ppermute | solution.py:67
  39.6 0.8 %collective-permute-done.7 = f32[129]{0:T(256)S(1)} collective-permute-done((f32[129]{0:T(256)S(1)}, f32[129]{0:T(256)S(1)}, u32[]{:S(2)}, u32[]{:S(2)}) %collective-permute-start.7) | collective-permute-done | bytes 548 | tf_op jit(solution)/shard_map/ppermute | solution.py:67
  40.4 4.6 %collective-permute-start.8 = (f32[129]{0:T(256)S(1)}, f32[129]{0:T(256)S(1)}, u32[]{:S(2)}, u32[]{:S(2)}) collective-permute-start(f32[129]{0:T(256)S(1)} %add.236), channel_id=1, source_target_pairs={{0,2},{1,3},{2,0},{3,1},{4,6},{5,7},{6,4},{7,5},{8,10},{9,11},{10,... | collective-permute-start | bytes 1556 | tf_op jit(solution)/shard_map/ppermute | solution.py:67
  45.1 1.5 %collective-permute-done.8 = f32[129]{0:T(256)S(1)} collective-permute-done((f32[129]{0:T(256)S(1)}, f32[129]{0:T(256)S(1)}, u32[]{:S(2)}, u32[]{:S(2)}) %collective-permute-start.8) | collective-permute-done | bytes 548 | tf_op jit(solution)/shard_map/ppermute | solution.py:67
  48.5 0.9 %maximum_add_fusion = f32[4,8,16,128]{3,2,1,0:T(8,128)} fusion(f32[1,8,16,128]{3,2,1,0:T(8,128)S(1)} %fusion.12, f32[1,8,16,128]{3,2,1,0:T(8,128)S(1)} %fusion.29, f32[1,8,16,128]{3,2,1,0:T(8,128)S(1)} %fusion.38, f32[1,8,16,128]{3,2,1,0:T(8,128)S(1)} %fusion.50, f32[4,8,16]{2,1,0:T(8,128)S(1)} %get-tuple-element.85, f32[4,8,16]{2,1,0:T(8,128)S(1)} %get-tuple-element.84, ...), kind=kLoop, calls=%fused_computation.6 | loop fusion | flops 393216 | bytes 528640 | tf_op jit(solution)/shard_map/add | solution.py:289
  (122 shorter events, 7.4 us)
Async XLA Ops:
  0.6 3.7 %copy-start.1 = (f32[4,8,16,128]{3,2,1,0:T(8,128)S(1)}, f32[4,8,16,128]{3,2,1,0:T(8,128)}, u32[]{:S(2)}) copy-start(f32[4,8,16,128]{3,2,1,0:T(8,128)} %param.11) | copy-start | bytes 786436
  4.3 2.2 %copy-start.2 = (s32[8,16]{1,0:T(8,128)S(1)}, s32[8,16]{1,0:T(8,128)}, u32[]{:S(2)}) copy-start(s32[8,16]{1,0:T(8,128)} %param.14) | copy-start | bytes 1540
  4.4 2.2 %copy-start.7 = (f32[64]{0:T(128)S(1)}, f32[64]{0:T(128)}, u32[]{:S(2)}) copy-start(f32[64]{0:T(128)} %param.13) | copy-start | bytes 772
  4.4 2.4 %copy-start.5 = (s32[8,16]{1,0:T(8,128)S(1)}, s32[8,16]{1,0:T(8,128)}, u32[]{:S(2)}) copy-start(s32[8,16]{1,0:T(8,128)} %param.15) | copy-start | bytes 1540
  4.4 2.4 %copy-start.8 = (f32[64]{0:T(128)S(1)}, f32[64]{0:T(128)}, u32[]{:S(2)}) copy-start(f32[64]{0:T(128)} %param.16) | copy-start | bytes 772
  6.2 4.9 %copy-start.3 = (s32[512]{0:T(512)S(1)}, s32[512]{0:T(512)}, u32[]{:S(2)}) copy-start(s32[512]{0:T(512)} %param.18) | copy-start | bytes 6148
  6.3 4.9 %copy-start.4 = (s32[512]{0:T(512)S(1)}, s32[512]{0:T(512)}, u32[]{:S(2)}) copy-start(s32[512]{0:T(512)} %param.17) | copy-start | bytes 6148
  7.3 3.9 %collective-permute-start = (f32[9,8,8,128]{3,2,1,0:T(8,128)S(1)}, f32[9,8,8,128]{3,2,1,0:T(8,128)S(1)}, u32[]{:S(2)}, u32[]{:S(2)}) collective-permute-start(f32[9,8,8,128]{3,2,1,0:T(8,128)S(1)} %get-tuple-element.48), channel_id=1, source_target_pairs={{0,1},{1,2},{2,3},{4,5},{5,6},{6,7},{8,9},{9,10},{10,11},{12,13},{... | collective-permute-start | bytes 884744 | tf_op jit(solution)/shard_map/ppermute | solution.py:16
  9.7 5.6 %collective-permute-start.1 = (f32[9,8,8,128]{3,2,1,0:T(8,128)S(1)}, f32[9,8,8,128]{3,2,1,0:T(8,128)S(1)}, u32[]{:S(2)}, u32[]{:S(2)}) collective-permute-start(f32[9,8,8,128]{3,2,1,0:T(8,128)S(1)} %get-tuple-element.49), channel_id=1, source_target_pairs={{1,0},{2,1},{3,2},{5,4},{6,5},{7,6},{9,8},{10,9},{11,10},{13,12},{... | collective-permute-start | bytes 884744 | tf_op jit(solution)/shard_map/ppermute | solution.py:19
  15.4 8.2 %collective-permute-start.2 = (f32[10,32,128]{2,1,0:T(8,128)S(1)}, f32[10,32,128]{2,1,0:T(8,128)S(1)}, u32[]{:S(2)}, u32[]{:S(2)}) collective-permute-start(f32[10,32,128]{2,1,0:T(8,128)S(1)} %get-tuple-element.28), channel_id=1, source_target_pairs={{0,4},{4,8},{8,12},{12,16},{16,20},{20,24},{24,28},{28,0},{1,5},{5... | collective-permute-start | bytes 491528 | tf_op jit(solution)/shard_map/ppermute | solution.py:134
  16.9 7.1 %collective-permute-start.3 = (f32[10,32,128]{2,1,0:T(8,128)S(1)}, f32[10,32,128]{2,1,0:T(8,128)S(1)}, u32[]{:S(2)}, u32[]{:S(2)}) collective-permute-start(f32[10,32,128]{2,1,0:T(8,128)S(1)} %get-tuple-element.29), channel_id=1, source_target_pairs={{4,0},{8,4},{12,8},{16,12},{20,16},{24,20},{28,24},{0,28},{5,1},{9... | collective-permute-start | bytes 491528 | tf_op jit(solution)/shard_map/ppermute | solution.py:135
  20.3 1.0 %copy-start = (f32[9,8,32,128]{3,2,1,0:T(8,128)}, f32[9,8,32,128]{3,2,1,0:T(8,128)S(1)}, u32[]{:S(2)}) copy-start(f32[9,8,32,128]{3,2,1,0:T(8,128)S(1)} %pad_maximum_fusion.1) | copy-start | bytes 3538948
  20.3 4.5 %copy-start.6 = (f32[512]{0:T(512)S(1)}, f32[512]{0:T(512)}, u32[]{:S(2)}) copy-start(f32[512]{0:T(512)} %param.19) | copy-start | bytes 6148
  23.5 4.1 %slice-start = ((f32[9,8,32,128]{3,2,1,0:T(8,128)}), f32[8,8,32,128]{3,2,1,0:T(8,128)S(1)}, s32[]{:S(2)}) async-start(f32[9,8,32,128]{3,2,1,0:T(8,128)} %copy-done), calls=%async_computation | async-start | bytes 2097152 | tf_op jit(solution)/shard_map/slice | solution.py:141
  26.8 3.6 %collective-permute-start.4 = (f32[129]{0:T(256)S(1)}, f32[129]{0:T(256)S(1)}, u32[]{:S(2)}, u32[]{:S(2)}) collective-permute-start(f32[129]{0:T(256)S(1)} %pad_maximum_fusion.4), channel_id=1, source_target_pairs={{0,4},{4,0},{8,12},{12,8},{16,20},{20,16},{24,28},{28,24},{1,5},{5... | collective-permute-start | bytes 1556 | tf_op jit(solution)/shard_map/ppermute | solution.py:67
  31.1 3.6 %collective-permute-start.5 = (f32[129]{0:T(256)S(1)}, f32[129]{0:T(256)S(1)}, u32[]{:S(2)}, u32[]{:S(2)}) collective-permute-start(f32[129]{0:T(256)S(1)} %fusion.127), channel_id=1, source_target_pairs={{0,8},{4,12},{8,0},{12,4},{16,24},{20,28},{24,16},{28,20},{1,9},{5... | collective-permute-start | bytes 1556 | tf_op jit(solution)/shard_map/ppermute | solution.py:67
  34.7 4.5 %collective-permute-start.6 = (f32[129]{0:T(256)S(1)}, f32[129]{0:T(256)S(1)}, u32[]{:S(2)}, u32[]{:S(2)}) collective-permute-start(f32[129]{0:T(256)S(1)} %add.234), channel_id=1, source_target_pairs={{0,16},{4,20},{8,24},{12,28},{16,0},{20,4},{24,8},{28,12},{1,17},{... | collective-permute-start | bytes 1556 | tf_op jit(solution)/shard_map/ppermute | solution.py:67
  39.1 1.3 %collective-permute-start.7 = (f32[129]{0:T(256)S(1)}, f32[129]{0:T(256)S(1)}, u32[]{:S(2)}, u32[]{:S(2)}) collective-permute-start(f32[129]{0:T(256)S(1)} %add.235), channel_id=1, source_target_pairs={{0,1},{1,0},{2,3},{3,2},{4,5},{5,4},{6,7},{7,6},{8,9},{9,8},{10,11... | collective-permute-start | bytes 1556 | tf_op jit(solution)/shard_map/ppermute | solution.py:67
  40.4 6.2 %collective-permute-start.8 = (f32[129]{0:T(256)S(1)}, f32[129]{0:T(256)S(1)}, u32[]{:S(2)}, u32[]{:S(2)}) collective-permute-start(f32[129]{0:T(256)S(1)} %add.236), channel_id=1, source_target_pairs={{0,2},{1,3},{2,0},{3,1},{4,6},{5,7},{6,4},{7,5},{8,10},{9,11},{10,... | collective-permute-start | bytes 1556 | tf_op jit(solution)/shard_map/ppermute | solution.py:67

commit v8 on v7

--- a/solution.py
+++ b/solution.py
@@ -5,6 +5,7 @@
 
 step_dt = 0.25
 epsilon = 1e-06
+highest = lax.Precision.HIGHEST
 
 
 def with_halo(array, axis, dim, before, after, wrap):
@@ -97,8 +98,9 @@
     push = -step_dt * stiffness * a0
     stack_f = jnp.stack([a0, adjoint_in[1], adjoint_in[2], adjoint_in[3], axial_flow, swirl_flow, buoyancy, push])
     top, below = nr - 1, nr - 2
+    press_top = acoustic[0, :, :, top]
     planes = [
-        acoustic[0, :, :, top],
+        press_top,
         acoustic[0, :, :, below],
         acoustic[1, :, :, top],
         acoustic[2, :, :, top],
@@ -112,24 +114,47 @@
         stiffness[:, :, top],
         wall,
         source_top,
+        press_top * (adjoint_in[3, :, :, top] + push[:, :, top]),
+        segment_id.astype(jnp.float32),
     ]
-    stack_c = jnp.stack(planes)
     n_planes = len(planes)
+    group = jnp.stack(planes)
+    size_ax, me_ax = (lax.axis_size("ax"), lax.axis_index("ax"))
+    if size_ax & (size_ax - 1):
+        group = lax.all_gather(group, "ax", axis=2, tiled=True)
+    else:
+        step = 1
+        while step < size_ax:
+            other = lax.ppermute(group, "ax", [(i, i ^ step) for i in range(size_ax)])
+            group = jnp.where(
+                (me_ax // step) % 2 == 0,
+                jnp.concatenate([group, other], axis=2),
+                jnp.concatenate([other, group], axis=2),
+            )
+            step *= 2
+    width = group.shape[2]
     tile = 8
     reach = 3
-    packed = jnp.pad(jnp.transpose(stack_c, (1, 2, 0)), ((0, 0), (0, 0), (0, nr - n_planes)))
-    stack_all = jnp.concatenate([stack_f, packed[None]], axis=0)
     n_f = stack_f.shape[0]
-    widened = with_halo(stack_all, "ax", 2, tile, tile, False)
+    widened = with_halo(stack_f, "ax", 2, tile, tile, False)
     size_az, length_a = (lax.axis_size("az"), widened.shape[1])
     up = [(i, (i + 1) % size_az) for i in range(size_az)]
     down = [(j, i) for i, j in up]
-    sent_up = jnp.stack(
-        [widened[f, length_a - 1] for f in (0, 1, 2, 3, 5, 6, 7)]
-        + [widened[n_f, length_a - reach + k] for k in range(reach)]
-    )
-    sent_down = jnp.stack(
-        [widened[f, 0] for f in (0, 1, 2, 3, 5, 7)] + [widened[7, 1]] + [widened[n_f, k] for k in range(reach)]
+    slot = widened.shape[2] * widened.shape[3]
+
+    def as_slots(rows):
+        flat = rows.reshape(-1)
+        count = -(-flat.shape[0] // slot)
+        return jnp.pad(flat, (0, count * slot - flat.shape[0])).reshape((count,) + widened.shape[2:])
+
+    def from_slots(slots):
+        return slots.reshape(-1)[: n_planes * reach * width].reshape(n_planes, reach, width)
+
+    sent_up = jnp.concatenate(
+        [jnp.stack([widened[f, length_a - 1] for f in (0, 1, 2, 3, 5, 6, 7)]), as_slots(group[:, length_a - reach :])]
+    )
+    sent_down = jnp.concatenate(
+        [jnp.stack([widened[f, 0] for f in (0, 1, 2, 3, 5, 7)] + [widened[7, 1]]), as_slots(group[:, :reach])]
     )
     from_below = lax.ppermute(sent_up, "az", up)
     from_above = lax.ppermute(sent_down, "az", down)
@@ -140,12 +165,12 @@
     wide_f = jnp.concatenate(
         [row_before[:, None], widened[:n_f], row_after[:, None], row_after2[:, None]], axis=1
     )
-    wide_packed = jnp.concatenate([from_below[7:], widened[n_f], from_above[7:]], axis=0)
-    wide_c = jnp.transpose(wide_packed[:, :, :n_planes], (2, 0, 1))
-
-    oc = (reach, tile)
-    p_t, p_b, va_t, vx_t, vr_b, u_t, u_b, w_t, w_b, b_t, b_b, s_t, wall_c, src_c = [wide_c[i] for i in range(14)]
-    ea, ex = na + 3, nx + 3
+    group_wide = jnp.concatenate([from_slots(from_below[7:]), group, from_slots(from_above[7:])], axis=1)
+    group_wide = jnp.pad(group_wide, ((0, 0), (0, 0), (reach, reach)))
+
+    oc = (reach, reach)
+    p_t, p_b, va_t, vx_t, vr_b, u_t, u_b, w_t, w_b, b_t, b_b, s_t, wall_c, src_c = [group_wide[i] for i in range(14)]
+    ea, eg, ex = (na + 3, width + 3, nx + 3)
 
     def c(f, da, dx, la, lx):
         return win(f, oc, da, dx, la, lx)
@@ -155,39 +180,52 @@
             w, da, dx, la, lx
         ) * (c(f, da + 1, dx, la, lx) - c(f, da - 1, dx, la, lx)) * 0.5
 
-    new_az = c(va_t, -2, -1, ea + 1, ex) - step_dt * (
-        advect_c(va_t, u_t, w_t, -2, -1, ea + 1, ex)
-        + c(b_t, -2, -1, ea + 1, ex) * (c(p_t, -1, -1, ea + 1, ex) - c(p_t, -2, -1, ea + 1, ex))
-    )
-    new_ax = c(vx_t, -1, -2, ea, ex + 1) - step_dt * (
-        advect_c(vx_t, u_t, w_t, -1, -2, ea, ex + 1)
-        + c(b_t, -1, -2, ea, ex + 1) * (c(p_t, -1, -1, ea, ex + 1) - c(p_t, -1, -2, ea, ex + 1))
-    )
-    rad_top = c(wall_c, -1, -1, ea, ex) * c(p_t, -1, -1, ea, ex)
-    rad_below = c(vr_b, -1, -1, ea, ex) - step_dt * (
-        advect_c(vr_b, u_b, w_b, -1, -1, ea, ex)
-        + c(b_b, -1, -1, ea, ex) * (c(p_t, -1, -1, ea, ex) - c(p_b, -1, -1, ea, ex))
+    new_az = c(va_t, -2, -1, ea + 1, eg) - step_dt * (
+        advect_c(va_t, u_t, w_t, -2, -1, ea + 1, eg)
+        + c(b_t, -2, -1, ea + 1, eg) * (c(p_t, -1, -1, ea + 1, eg) - c(p_t, -2, -1, ea + 1, eg))
+    )
+    new_ax = c(vx_t, -1, -2, ea, eg + 1) - step_dt * (
+        advect_c(vx_t, u_t, w_t, -1, -2, ea, eg + 1)
+        + c(b_t, -1, -2, ea, eg + 1) * (c(p_t, -1, -1, ea, eg + 1) - c(p_t, -1, -2, ea, eg + 1))
+    )
+    rad_top = c(wall_c, -1, -1, ea, eg) * c(p_t, -1, -1, ea, eg)
+    rad_below = c(vr_b, -1, -1, ea, eg) - step_dt * (
+        advect_c(vr_b, u_b, w_b, -1, -1, ea, eg)
+        + c(b_b, -1, -1, ea, eg) * (c(p_t, -1, -1, ea, eg) - c(p_b, -1, -1, ea, eg))
     )
     spread = (new_az[1:] - new_az[:-1]) + (new_ax[:, 1:] - new_ax[:, :-1]) + (rad_top - rad_below)
-    press_ring = (
-        c(p_t, -1, -1, ea, ex)
-        - step_dt * (advect_c(p_t, u_t, w_t, -1, -1, ea, ex) + c(s_t, -1, -1, ea, ex) * spread)
-        + step_dt * c(src_c, -1, -1, ea, ex)
+    press_grid = (
+        c(p_t, -1, -1, ea, eg)
+        - step_dt * (advect_c(p_t, u_t, w_t, -1, -1, ea, eg) + c(s_t, -1, -1, ea, eg) * spread)
+        + step_dt * c(src_c, -1, -1, ea, eg)
     )
 
     total_az = na * lax.axis_size("az")
     first_az = lax.axis_index("az") * na
-    first_ax = lax.axis_index("ax") * nx
-    ring_az = jnp.remainder(mic_az - first_az + 1, total_az)
-    ring_ax = mic_ax - first_ax + 1
-    on_ring = (ring_az < ea) & (ring_ax >= 0) & (ring_ax < ex)
-    owned = (ring_az >= 1) & (ring_az <= na) & (ring_ax >= 1) & (ring_ax <= nx)
-    ring_cell = jnp.where(on_ring, ring_az * ex + ring_ax, -1)
-    cell_hot = ring_cell[:, None] == lax.broadcasted_iota(jnp.int32, (1, ea * ex), 1)
-    heard = jnp.sum(jnp.where(cell_hot, press_ring.reshape(1, ea * ex), 0.0), axis=1)
+    grid_az = jnp.remainder(mic_az - first_az + 1, total_az)
+    row_hot = (grid_az[:, None] == lax.broadcasted_iota(jnp.int32, (1, ea), 1)).astype(jnp.float32)
+    col_hot = (mic_ax + 1)[:, None] == lax.broadcasted_iota(jnp.int32, (1, eg), 1)
+    heard = jnp.sum(jnp.where(col_hot, jnp.dot(row_hot, press_grid, precision=highest), 0.0), axis=1)
     misses = heard - measured
-    square_sum = jnp.sum(jnp.where(owned, misses * misses, 0.0))
-    placed = jnp.sum(jnp.where(cell_hot, misses[:, None], 0.0), axis=0).reshape(ea, ex)
+    in_group = (grid_az >= 1) & (grid_az <= na)
+    square_sum = jnp.sum(jnp.where(in_group, misses * misses, 0.0))
+    placed_grid = jnp.dot(row_hot.T, jnp.where(col_hot, misses[:, None], 0.0), precision=highest)
+
+    rows_own = slice(reach, reach + na)
+    cols_own = slice(reach, reach + width)
+    segment_group = group_wide[15, rows_own, cols_own].astype(jnp.int32)
+    segment_hot_group = segment_group[:, :, None] == lax.broadcasted_iota(jnp.int32, (1, 1, nseg), 2)
+    sens_placed = (
+        group_wide[0, rows_own, cols_own]
+        * (-step_dt * group_wide[11, rows_own, cols_own])
+        * placed_grid[1 : 1 + na, 1 : 1 + width]
+    )
+    seg_base = jnp.sum(jnp.where(segment_hot_group, group_wide[14, rows_own, cols_own][:, :, None], 0.0), axis=(0, 1))
+    seg_placed = jnp.sum(jnp.where(segment_hot_group, sens_placed[:, :, None], 0.0), axis=(0, 1))
+
+    local = lax.dynamic_slice_in_dim(group_wide, me_ax * nx, nx + 2 * reach, axis=2)
+    placed = lax.dynamic_slice_in_dim(placed_grid, me_ax * nx, ex, axis=1)
+    p_t, p_b, va_t, vx_t, vr_b, u_t, u_b, w_t, w_b, b_t, b_b, s_t, wall_c, src_c = [local[i] for i in range(14)]
 
     push_e = -step_dt * c(s_t, -1, -1, ea, ex) * placed
     r1a, r1x = na + 2, nx + 2
@@ -268,13 +306,7 @@
     )
     base = jnp.stack([back_press] + backs)
 
-    press_top = acoustic[0, :, :, top]
-    sens_base = press_top * (adjoint_in[3, :, :, top] + push[:, :, top])
-    sens_placed = press_top * push_0
-    seg_base = jnp.sum(jnp.where(segment_hot, sens_base[:, :, None], 0.0), axis=(0, 1))
-    seg_placed = jnp.sum(jnp.where(segment_hot, sens_placed[:, :, None], 0.0), axis=(0, 1))
-
-    totals = butterfly_sum(jnp.concatenate([square_sum[None], seg_base, seg_placed]), ("az", "ax"))
+    totals = butterfly_sum(jnp.concatenate([square_sum[None], seg_base, seg_placed]), ("az",))
     mean_sq = totals[0] / mic_az.shape[0] + epsilon
     grad_scale = (na * lax.axis_size("az") * nx * lax.axis_size("ax") / nseg) ** (-0.5)
     liner_grad = (totals[1 : 1 + nseg] + totals[1 + nseg :] / mean_sq) * grad_scale

time: 50.8 us -> 50.7 us (level)
  waiting for transfers between devices: 15.9 us -> 20.5 us
  starting transfers between devices: 17.1 us -> 13.6 us
  local copies, waits for them, and re-layouts: 7.23 us -> 3.95 us
  other arithmetic: 7.15 us -> 8.39 us
  matrix products: 0 us -> 0.8 us
    ppermute x5 -> x3, starting transfers between devices: 8.71 us -> 0.03 us  [butterfly_sum(): lax.ppermute(values, axis, [(i, i ^ step) for i in range(size)])]
    ppermute x0 -> x2, starting transfers between devices: none -> 5.32 us  [shards(): other = lax.ppermute(group, 'ax', [(i, i ^ step) for i in range(size_ax)])]
    ppermute x1, waiting for transfers between devices: 4.05 us -> 0.01 us  [with_halo(): lax.ppermute(lax.slice_in_dim(array, 0, after, axis=dim), axis, down)]
    ppermute x0 -> x2, waiting for transfers between devices: none -> 3.12 us  [shards(): other = lax.ppermute(group, 'ax', [(i, i ^ step) for i in range(size_ax)])]
    ppermute x1, waiting for transfers between devices: 2.24 us -> 5.06 us  [shards(): from_below = lax.ppermute(sent_up, 'az', up)]
    unnamed x46 -> x45, local copies, waits for them, and re-layouts: 3.47 us -> 1.32 us
    ppermute x1, waiting for transfers between devices: 0.46 us -> 2.51 us  [shards(): from_above = lax.ppermute(sent_down, 'az', down)]
    ppermute x1, starting transfers between devices: 1.57 us -> 0.01 us  [shards(): from_below = lax.ppermute(sent_up, 'az', up)]
  transfers between devices with their start and end apart: 9 -> 9, of which waited for: 8 -> 7; matrix products, arithmetic and copies ran while one was open for 3% -> 9% of each run, Pallas kernels for 0% -> 0%
where the time goes in v8:
time: 50.7 us; the launch traced here: 50.4 us
  waiting for transfers between devices  20.5 us (40%)
  starting transfers between devices  13.6 us (27%)
  other arithmetic  8.39 us (17%)
  local copies, waits for them, and re-layouts  3.95 us (8%)
  between operations  3.16 us (6%)
  matrix products  0.8 us (2%)
    ppermute x3, waiting for transfers between devices, butterfly_sum(): lax.ppermute(values, axis, [(i, i ^ step) for i in range(size)])  9.8 us
    ppermute x2, starting transfers between devices, shards(): other = lax.ppermute(group, 'ax', [(i, i ^ step) for i in range(size_ax)])  5.32 us
    ppermute x1, waiting for transfers between devices, shards(): from_below = lax.ppermute(sent_up, 'az', up)  5.06 us
    ppermute x1, starting transfers between devices, shards(): from_above = lax.ppermute(sent_down, 'az', down)  4.61 us
    ppermute x2, waiting for transfers between devices, shards(): other = lax.ppermute(group, 'ax', [(i, i ^ step) for i in range(size_ax)])  3.12 us
    ppermute x1, waiting for transfers between devices, shards(): from_above = lax.ppermute(sent_down, 'az', down)  2.51 us
    ppermute x1, starting transfers between devices, with_halo(): lax.ppermute(lax.slice_in_dim(array, length - before, length, axis=dim),...  2.37 us
    unnamed x45, local copies, waits for them, and re-layouts  1.32 us
  transfers between devices with their start and end apart: 9, of which 7 were waited for; matrix products, arithmetic and copies ran while one was open for 9% of the time, Pallas kernels for 0%

profile of v8, /device:TPU:0, one launch (start us, length us, event | category | flops | bytes accessed | tf_op | source)
XLA Modules:
  0.0 50.4 jit_solution(9182477539374383718)
XLA Ops:
  0.6 0.9 %slice.715 = f32[2,8,16,128]{3,2,1,0:T(8,128)S(1)} slice(f32[4,8,16,128]{3,2,1,0:T(8,128)} %param.11), slice={[0:2], [0:8], [0:16], [0:128]} | slice | bytes 262144 | tf_op jit(solution)/shard_map/slice | solution.py:89
  1.6 1.1 %slice_bitcast_fusion.8 = (f32[8,16,128]{2,1,0:T(8,128)S(1)}, f32[1,8,16,128]{3,2,1,0:T(8,128)S(1)}, f32[1,8,16,128]{3,2,1,0:T(8,128)S(1)}, f32[1,8,16,128]{3,2,1,0:T(8,128)S(1)}, f32[1,8,16,128]{3,2,1,0:T(8,128)S(1)}) fusion(f32[4,8,16,128]{3,2,1,0:T(8,128)} %param.12, f32[4,8,16,128]{3,2,1,0:T(8,128)} %param.11), kind=kLoop, calls=%fused_computation.170 | loop fusion | flops 81920 | bytes 655360 | tf_op jit(solution)/shard_map/squeeze | solution.py:97
  2.6 1.0 %pad_maximum_fusion.1 = f32[8,8,16,128]{3,2,1,0:T(8,128)S(1)} fusion(f32[1,8,16,128]{3,2,1,0:T(8,128)S(1)} %get-tuple-element.42, f32[1,8,16,128]{3,2,1,0:T(8,128)S(1)} %get-tuple-element.45, f32[2,8,16,128]{3,2,1,0:T(8,128)S(1)} %slice.715, f32[4,8,16,128]{3,2,1,0:T(8,128)} %param.12), kind=kLoop, calls=%fused_computation.3 | loop fusion | flops 393216 | bytes 1048576 | tf_op jit(solution)/shard_map/stack | solution.py:99
  3.7 2.4 %collective-permute-start = (f32[8,8,8,128]{3,2,1,0:T(8,128)S(1)}, f32[8,8,8,128]{3,2,1,0:T(8,128)S(1)}, u32[]{:S(2)}, u32[]{:S(2)}) collective-permute-start(f32[8,8,8,128]{3,2,1,0:T(8,128)S(1)} %get-tuple-element.37), channel_id=1, source_target_pairs={{0,1},{1,2},{2,3},{4,5},{5,6},{6,7},{8,9},{9,10},{10,11},{12,13},{... | collective-permute-start | bytes 786440 | tf_op jit(solution)/shard_map/ppermute | solution.py:17
  6.1 1.3 %collective-permute-start.1 = (f32[8,8,8,128]{3,2,1,0:T(8,128)S(1)}, f32[8,8,8,128]{3,2,1,0:T(8,128)S(1)}, u32[]{:S(2)}, u32[]{:S(2)}) collective-permute-start(f32[8,8,8,128]{3,2,1,0:T(8,128)S(1)} %get-tuple-element.38), channel_id=1, source_target_pairs={{1,0},{2,1},{3,2},{5,4},{6,5},{7,6},{9,8},{10,9},{11,10},{13,12},{... | collective-permute-start | bytes 786440 | tf_op jit(solution)/shard_map/ppermute | solution.py:20
  9.8 3.3 %collective-permute-start.2 = (f32[16,8,16]{2,1,0:T(8,128)S(1)}, f32[16,8,16]{2,1,0:T(8,128)S(1)}, u32[]{:S(2)}, u32[]{:S(2)}) collective-permute-start(f32[16,8,16]{2,1,0:T(8,128)S(1)} %constant_dynamic-update-slice_fusion), channel_id=1, source_target_pairs={{0,1},{1,0},{2,3},{3,2},{4,5},{5,4},{6,7},{7,6},{8,9},{9,8},{10,11... | collective-permute-start | bytes 24584 | tf_op jit(solution)/shard_map/ppermute | solution.py:128
  13.1 0.9 %collective-permute-done.2 = f32[16,8,16]{2,1,0:T(8,128)S(1)} collective-permute-done((f32[16,8,16]{2,1,0:T(8,128)S(1)}, f32[16,8,16]{2,1,0:T(8,128)S(1)}, u32[]{:S(2)}, u32[]{:S(2)}) %collective-permute-start.2) | collective-permute-done | bytes 8224 | tf_op jit(solution)/shard_map/ppermute | solution.py:128
  14.1 2.0 %collective-permute-start.3 = (f32[16,8,32]{2,1,0:T(8,128)S(1)}, f32[16,8,32]{2,1,0:T(8,128)S(1)}, u32[]{:S(2)}, u32[]{:S(2)}) collective-permute-start(f32[16,8,32]{2,1,0:T(8,128)S(1)} %maximum_select_fusion), channel_id=1, source_target_pairs={{0,2},{1,3},{2,0},{3,1},{4,6},{5,7},{6,4},{7,5},{8,10},{9,11},{10,... | collective-permute-start | bytes 49160 | tf_op jit(solution)/shard_map/ppermute | solution.py:128
  16.3 2.2 %collective-permute-done.3 = f32[16,8,32]{2,1,0:T(8,128)S(1)} collective-permute-done((f32[16,8,32]{2,1,0:T(8,128)S(1)}, f32[16,8,32]{2,1,0:T(8,128)S(1)}, u32[]{:S(2)}, u32[]{:S(2)}) %collective-permute-start.3) | collective-permute-done | bytes 16416 | tf_op jit(solution)/shard_map/ppermute | solution.py:128
  19.0 4.6 %collective-permute-start.5 = (f32[8,32,128]{2,1,0:T(8,128)S(1)}, f32[8,32,128]{2,1,0:T(8,128)S(1)}, u32[]{:S(2)}, u32[]{:S(2)}) collective-permute-start(f32[8,32,128]{2,1,0:T(8,128)S(1)} %constant_dynamic-update-slice_fusion.24), channel_id=1, source_target_pairs={{4,0},{8,4},{12,8},{16,12},{20,16},{24,20},{28,24},{0,28},{5,1},{9... | collective-permute-start | bytes 393224 | tf_op jit(solution)/shard_map/ppermute | solution.py:160
  23.6 2.5 %collective-permute-done.5 = f32[8,32,128]{2,1,0:T(8,128)S(1)} collective-permute-done((f32[8,32,128]{2,1,0:T(8,128)S(1)}, f32[8,32,128]{2,1,0:T(8,128)S(1)}, u32[]{:S(2)}, u32[]{:S(2)}) %collective-permute-start.5) | collective-permute-done | bytes 131104 | tf_op jit(solution)/shard_map/ppermute | solution.py:160
  26.2 5.1 %collective-permute-done.4 = f32[8,32,128]{2,1,0:T(8,128)S(1)} collective-permute-done((f32[8,32,128]{2,1,0:T(8,128)S(1)}, f32[8,32,128]{2,1,0:T(8,128)S(1)}, u32[]{:S(2)}, u32[]{:S(2)}) %collective-permute-start.4) | collective-permute-done | bytes 131104 | tf_op jit(solution)/shard_map/ppermute | solution.py:159
  31.7 0.5 fusion
  32.1 0.6 %select_reduce_fusion.4 = (f32[]{:T(128)}, f32[512]{0:T(512)S(1)}) fusion(s32[512]{0:T(512)S(1)} %get-tuple-element.103, f32[512]{0:T(512)S(1)} %fusion, f32[512]{0:T(512)S(1)} %copy-done.7), kind=kLoop, calls=%fused_computation.352 | loop fusion | flops 3583 | bytes 8196 | tf_op jit(solution)/shard_map/reduce_sum | solution.py:211
  32.7 0.3 fusion.2
  33.2 0.3 select_reduce_fusion.1
  33.5 0.7 %pad_maximum_fusion.7 = f32[129]{0:T(256)S(1)} fusion(f32[64]{0:T(128)S(1)} %get-tuple-element.8, f32[64]{0:T(128)S(1)} %get-tuple-element.7, f32[1]{0:T(128)} %bitcast.82), kind=kLoop, calls=%fused_computation.353 | loop fusion | flops 258 | bytes 1032 | tf_op jit(solution)/shard_map/concatenate | solution.py:309
  36.0 1.8 %collective-permute-done.6 = f32[129]{0:T(256)S(1)} collective-permute-done((f32[129]{0:T(256)S(1)}, f32[129]{0:T(256)S(1)}, u32[]{:S(2)}, u32[]{:S(2)}) %collective-permute-start.6) | collective-permute-done | bytes 548 | tf_op jit(solution)/shard_map/ppermute | solution.py:68
  37.8 0.7 %fusion.168 = f32[129]{0:T(256)S(1)} fusion(f32[129]{0:T(256)S(1)} %collective-permute-done.6, f32[64]{0:T(128)S(1)} %get-tuple-element.8, f32[64]{0:T(128)S(1)} %get-tuple-element.7, f32[1]{0:T(128)} %bitcast.82), kind=kLoop, calls=%fused_computation.366 | loop fusion | flops 387 | bytes 1548 | tf_op jit(solution)/shard_map/add | solution.py:68
  38.5 3.5 %collective-permute-done.7 = f32[129]{0:T(256)S(1)} collective-permute-done((f32[129]{0:T(256)S(1)}, f32[129]{0:T(256)S(1)}, u32[]{:S(2)}, u32[]{:S(2)}) %collective-permute-start.7) | collective-permute-done | bytes 548 | tf_op jit(solution)/shard_map/ppermute | solution.py:68
  42.1 4.5 %collective-permute-done.8 = f32[129]{0:T(256)S(1)} collective-permute-done((f32[129]{0:T(256)S(1)}, f32[129]{0:T(256)S(1)}, u32[]{:S(2)}, u32[]{:S(2)}) %collective-permute-start.8) | collective-permute-done | bytes 548 | tf_op jit(solution)/shard_map/ppermute | solution.py:68
  46.5 0.5 %slice.919 = f32[1]{0:T(128)} slice(f32[129]{0:T(256)S(1)} %add.254), slice={[0:1]} | slice | bytes 8 | tf_op jit(solution)/shard_map/slice | solution.py:310
  47.7 0.6 %fusion.159 = f32[64]{0:T(128)} fusion(f32[129]{0:T(256)S(1)} %add.254, f32[]{:T(128)} %bitcast.86), kind=kLoop, calls=%fused_computation.358 | loop fusion | flops 192 | bytes 772 | tf_op jit(solution)/shard_map/mul | solution.py:312
  48.4 0.9 %maximum_add_fusion = f32[4,8,16,128]{3,2,1,0:T(8,128)} fusion(f32[1,8,16,128]{3,2,1,0:T(8,128)S(1)} %fusion.20, f32[1,8,16,128]{3,2,1,0:T(8,128)S(1)} %fusion.37, f32[1,8,16,128]{3,2,1,0:T(8,128)S(1)} %fusion.46, f32[1,8,16,128]{3,2,1,0:T(8,128)S(1)} %fusion.58, f32[4,8,16]{2,1,0:T(8,128)S(1)} %get-tuple-element.85, f32[4,8,16]{2,1,0:T(8,128)S(1)} %get-tuple-element.84, ...), kind=kLoop, calls=%fused_computation.4 | loop fusion | flops 393216 | bytes 528640 | tf_op jit(solution)/shard_map/add | solution.py:321
  (121 shorter events, 5.0 us)
Async XLA Ops:
  1.5 5.8 %copy-start.1 = (f32[4,8,16,128]{3,2,1,0:T(8,128)S(1)}, f32[4,8,16,128]{3,2,1,0:T(8,128)}, u32[]{:S(2)}) copy-start(f32[4,8,16,128]{3,2,1,0:T(8,128)} %param.11) | copy-start | bytes 786436
  1.6 5.9 %copy-start = (f32[4,8,16,128]{3,2,1,0:T(8,128)S(1)}, f32[4,8,16,128]{3,2,1,0:T(8,128)}, u32[]{:S(2)}) copy-start(f32[4,8,16,128]{3,2,1,0:T(8,128)} %param.12) | copy-start | bytes 786436
  1.6 6.0 %copy-start.2 = (f32[4,8,16,128]{3,2,1,0:T(8,128)S(1)}, f32[4,8,16,128]{3,2,1,0:T(8,128)}, u32[]{:S(2)}) copy-start(f32[4,8,16,128]{3,2,1,0:T(8,128)} %param.10) | copy-start | bytes 786436
  3.7 15.1 %collective-permute-start = (f32[8,8,8,128]{3,2,1,0:T(8,128)S(1)}, f32[8,8,8,128]{3,2,1,0:T(8,128)S(1)}, u32[]{:S(2)}, u32[]{:S(2)}) collective-permute-start(f32[8,8,8,128]{3,2,1,0:T(8,128)S(1)} %get-tuple-element.37), channel_id=1, source_target_pairs={{0,1},{1,2},{2,3},{4,5},{5,6},{6,7},{8,9},{9,10},{10,11},{12,13},{... | collective-permute-start | bytes 786440 | tf_op jit(solution)/shard_map/ppermute | solution.py:17
  6.1 12.7 %collective-permute-start.1 = (f32[8,8,8,128]{3,2,1,0:T(8,128)S(1)}, f32[8,8,8,128]{3,2,1,0:T(8,128)S(1)}, u32[]{:S(2)}, u32[]{:S(2)}) collective-permute-start(f32[8,8,8,128]{3,2,1,0:T(8,128)S(1)} %get-tuple-element.38), channel_id=1, source_target_pairs={{1,0},{2,1},{3,2},{5,4},{6,5},{7,6},{9,8},{10,9},{11,10},{13,12},{... | collective-permute-start | bytes 786440 | tf_op jit(solution)/shard_map/ppermute | solution.py:20
  7.4 1.9 %copy-start.3 = (s32[8,16]{1,0:T(8,128)S(1)}, s32[8,16]{1,0:T(8,128)}, u32[]{:S(2)}) copy-start(s32[8,16]{1,0:T(8,128)} %param.14) | copy-start | bytes 1540
  7.4 1.9 %copy-start.8 = (f32[64]{0:T(128)S(1)}, f32[64]{0:T(128)}, u32[]{:S(2)}) copy-start(f32[64]{0:T(128)} %param.13) | copy-start | bytes 772
  7.4 2.1 %copy-start.4 = (s32[8,16]{1,0:T(8,128)S(1)}, s32[8,16]{1,0:T(8,128)}, u32[]{:S(2)}) copy-start(s32[8,16]{1,0:T(8,128)} %param.15) | copy-start | bytes 1540
  7.5 2.1 %copy-start.9 = (f32[64]{0:T(128)S(1)}, f32[64]{0:T(128)}, u32[]{:S(2)}) copy-start(f32[64]{0:T(128)} %param.16) | copy-start | bytes 772
  7.5 5.6 %copy-start.5 = (s32[512]{0:T(512)S(1)}, s32[512]{0:T(512)}, u32[]{:S(2)}) copy-start(s32[512]{0:T(512)} %param.17) | copy-start | bytes 6148
  7.5 5.6 %copy-start.6 = (s32[512]{0:T(512)S(1)}, s32[512]{0:T(512)}, u32[]{:S(2)}) copy-start(s32[512]{0:T(512)} %param.18) | copy-start | bytes 6148
  9.8 4.2 %collective-permute-start.2 = (f32[16,8,16]{2,1,0:T(8,128)S(1)}, f32[16,8,16]{2,1,0:T(8,128)S(1)}, u32[]{:S(2)}, u32[]{:S(2)}) collective-permute-start(f32[16,8,16]{2,1,0:T(8,128)S(1)} %constant_dynamic-update-slice_fusion), channel_id=1, source_target_pairs={{0,1},{1,0},{2,3},{3,2},{4,5},{5,4},{6,7},{7,6},{8,9},{9,8},{10,11... | collective-permute-start | bytes 24584 | tf_op jit(solution)/shard_map/ppermute | solution.py:128
  14.1 4.5 %collective-permute-start.3 = (f32[16,8,32]{2,1,0:T(8,128)S(1)}, f32[16,8,32]{2,1,0:T(8,128)S(1)}, u32[]{:S(2)}, u32[]{:S(2)}) collective-permute-start(f32[16,8,32]{2,1,0:T(8,128)S(1)} %maximum_select_fusion), channel_id=1, source_target_pairs={{0,2},{1,3},{2,0},{3,1},{4,6},{5,7},{6,4},{7,5},{8,10},{9,11},{10,... | collective-permute-start | bytes 49160 | tf_op jit(solution)/shard_map/ppermute | solution.py:128
  18.9 13.2 %copy-start.7 = (f32[512]{0:T(512)S(1)}, f32[512]{0:T(512)}, u32[]{:S(2)}) copy-start(f32[512]{0:T(512)} %param.19) | copy-start | bytes 6148
  19.0 7.1 %collective-permute-start.5 = (f32[8,32,128]{2,1,0:T(8,128)S(1)}, f32[8,32,128]{2,1,0:T(8,128)S(1)}, u32[]{:S(2)}, u32[]{:S(2)}) collective-permute-start(f32[8,32,128]{2,1,0:T(8,128)S(1)} %constant_dynamic-update-slice_fusion.24), channel_id=1, source_target_pairs={{4,0},{8,4},{12,8},{16,12},{20,16},{24,20},{28,24},{0,28},{5,1},{9... | collective-permute-start | bytes 393224 | tf_op jit(solution)/shard_map/ppermute | solution.py:160
  23.6 7.7 %collective-permute-start.4 = (f32[8,32,128]{2,1,0:T(8,128)S(1)}, f32[8,32,128]{2,1,0:T(8,128)S(1)}, u32[]{:S(2)}, u32[]{:S(2)}) collective-permute-start(f32[8,32,128]{2,1,0:T(8,128)S(1)} %constant_dynamic-update-slice_fusion.16), channel_id=1, source_target_pairs={{0,4},{4,8},{8,12},{12,16},{16,20},{20,24},{24,28},{28,0},{1,5},{5... | collective-permute-start | bytes 393224 | tf_op jit(solution)/shard_map/ppermute | solution.py:159
  34.2 3.6 %collective-permute-start.6 = (f32[129]{0:T(256)S(1)}, f32[129]{0:T(256)S(1)}, u32[]{:S(2)}, u32[]{:S(2)}) collective-permute-start(f32[129]{0:T(256)S(1)} %pad_maximum_fusion.7), channel_id=1, source_target_pairs={{0,4},{4,0},{8,12},{12,8},{16,20},{20,16},{24,28},{28,24},{1,5},{5... | collective-permute-start | bytes 1556 | tf_op jit(solution)/shard_map/ppermute | solution.py:68
  38.5 3.6 %collective-permute-start.7 = (f32[129]{0:T(256)S(1)}, f32[129]{0:T(256)S(1)}, u32[]{:S(2)}, u32[]{:S(2)}) collective-permute-start(f32[129]{0:T(256)S(1)} %fusion.168), channel_id=1, source_target_pairs={{0,8},{4,12},{8,0},{12,4},{16,24},{20,28},{24,16},{28,20},{1,9},{5... | collective-permute-start | bytes 1556 | tf_op jit(solution)/shard_map/ppermute | solution.py:68
  42.1 4.5 %collective-permute-start.8 = (f32[129]{0:T(256)S(1)}, f32[129]{0:T(256)S(1)}, u32[]{:S(2)}, u32[]{:S(2)}) collective-permute-start(f32[129]{0:T(256)S(1)} %add.253), channel_id=1, source_target_pairs={{0,16},{4,20},{8,24},{12,28},{16,0},{20,4},{24,8},{28,12},{1,17},{... | collective-permute-start | bytes 1556 | tf_op jit(solution)/shard_map/ppermute | solution.py:68

commit v9 on v7

--- a/solution.py
+++ b/solution.py
@@ -117,19 +117,45 @@
     n_planes = len(planes)
     tile = 8
     reach = 3
-    packed = jnp.pad(jnp.transpose(stack_c, (1, 2, 0)), ((0, 0), (0, 0), (0, nr - n_planes)))
-    stack_all = jnp.concatenate([stack_f, packed[None]], axis=0)
     n_f = stack_f.shape[0]
-    widened = with_halo(stack_all, "ax", 2, tile, tile, False)
+    row_slot = tile * nr
+
+    def to_slot(block):
+        per_row = jnp.transpose(block, (1, 0, 2)).reshape(block.shape[1], -1)
+        return jnp.pad(per_row, ((0, 0), (0, row_slot - per_row.shape[1]))).reshape(block.shape[1], tile, nr)
+
+    def from_slot(slot_rows):
+        flat = slot_rows.reshape(slot_rows.shape[0], -1)[:, : n_planes * nx]
+        return jnp.transpose(flat.reshape(slot_rows.shape[0], n_planes, nx), (1, 0, 2))
+
+    casing_slot = to_slot(stack_c)[None]
+    size_ax = lax.axis_size("ax")
+    right = [(i, i + 1) for i in range(size_ax - 1)]
+    left = [(j, i) for i, j in right]
+    from_left = lax.ppermute(jnp.concatenate([stack_f[:, :, nx - tile :], casing_slot]), "ax", right)
+    from_right = lax.ppermute(jnp.concatenate([stack_f[:, :, :tile], casing_slot]), "ax", left)
+    widened = jnp.concatenate([from_left[:n_f], stack_f, from_right[:n_f]], axis=2)
+    wide_x_c = jnp.concatenate(
+        [from_slot(from_left[n_f])[:, :, nx - reach :], stack_c, from_slot(from_right[n_f])[:, :, :reach]], axis=2
+    )
     size_az, length_a = (lax.axis_size("az"), widened.shape[1])
     up = [(i, (i + 1) % size_az) for i in range(size_az)]
     down = [(j, i) for i, j in up]
-    sent_up = jnp.stack(
-        [widened[f, length_a - 1] for f in (0, 1, 2, 3, 5, 6, 7)]
-        + [widened[n_f, length_a - reach + k] for k in range(reach)]
-    )
-    sent_down = jnp.stack(
-        [widened[f, 0] for f in (0, 1, 2, 3, 5, 7)] + [widened[7, 1]] + [widened[n_f, k] for k in range(reach)]
+    slot = widened.shape[2] * widened.shape[3]
+
+    def as_slots(rows):
+        flat = rows.reshape(-1)
+        count = -(-flat.shape[0] // slot)
+        return jnp.pad(flat, (0, count * slot - flat.shape[0])).reshape((count,) + widened.shape[2:])
+
+    def from_slots(slots):
+        return slots.reshape(-1)[: n_planes * reach * (nx + 2 * reach)].reshape(n_planes, reach, nx + 2 * reach)
+
+    sent_up = jnp.concatenate(
+        [jnp.stack([widened[f, length_a - 1] for f in (0, 1, 2, 3, 5, 6, 7)]), as_slots(wide_x_c[:, length_a - reach :])]
+    )
+    sent_down = jnp.concatenate(
+        [jnp.stack([widened[f, 0] for f in (0, 1, 2, 3, 5, 7)] + [widened[7, 1]]), as_slots(wide_x_c[:, :reach])]
     )
     from_below = lax.ppermute(sent_up, "az", up)
     from_above = lax.ppermute(sent_down, "az", down)
@@ -140,10 +166,9 @@
     wide_f = jnp.concatenate(
         [row_before[:, None], widened[:n_f], row_after[:, None], row_after2[:, None]], axis=1
     )
-    wide_packed = jnp.concatenate([from_below[7:], widened[n_f], from_above[7:]], axis=0)
-    wide_c = jnp.transpose(wide_packed[:, :, :n_planes], (2, 0, 1))
-
-    oc = (reach, tile)
+    wide_c = jnp.concatenate([from_slots(from_below[7:]), wide_x_c, from_slots(from_above[7:])], axis=1)
+
+    oc = (reach, reach)
     p_t, p_b, va_t, vx_t, vr_b, u_t, u_b, w_t, w_b, b_t, b_b, s_t, wall_c, src_c = [wide_c[i] for i in range(14)]
     ea, ex = na + 3, nx + 3
 

time: 50.8 us -> 55.5 us (1.093)
  waiting for transfers between devices: 15.9 us -> 24.5 us
  starting transfers between devices: 17.1 us -> 13.3 us
  local copies, waits for them, and re-layouts: 7.23 us -> 5.68 us
  other arithmetic: 7.15 us -> 8.37 us
    ppermute x5, starting transfers between devices: 8.71 us -> 5.01 us  [butterfly_sum(): lax.ppermute(values, axis, [(i, i ^ step) for i in range(size)])]
    ppermute x5, waiting for transfers between devices: 9.11 us -> 12.8 us  [butterfly_sum(): lax.ppermute(values, axis, [(i, i ^ step) for i in range(size)])]
    ppermute x1, waiting for transfers between devices: 2.24 us -> 5.32 us  [shards(): from_below = lax.ppermute(sent_up, 'az', up)]
    unnamed x46 -> x47, local copies, waits for them, and re-layouts: 3.47 us -> 1.32 us
    ppermute x1, waiting for transfers between devices: 0.46 us -> 2.16 us  [shards(): from_above = lax.ppermute(sent_down, 'az', down)]
    ppermute x1, starting transfers between devices: 1.57 us -> 0.06 us  [shards(): from_below = lax.ppermute(sent_up, 'az', up)]
    ppermute x1, starting transfers between devices: 3.2 us -> 4.61 us  [shards(): from_above = lax.ppermute(sent_down, 'az', down)]
    slice x5 -> x10, local copies, waits for them, and re-layouts: 0.09 us -> 1.11 us  [the longest x1 0.92 us: shards(): axial_flow, swirl_flow = (mean_flow[0], mean_flow[1])]
where the time goes in v9:
time: 55.5 us; the launch traced here: 55.1 us
  waiting for transfers between devices  24.5 us (44%)
  starting transfers between devices  13.3 us (24%)
  other arithmetic  8.37 us (15%)
  local copies, waits for them, and re-layouts  5.68 us (10%)
  between operations  3.28 us (6%)
    ppermute x5, waiting for transfers between devices, butterfly_sum(): lax.ppermute(values, axis, [(i, i ^ step) for i in range(size)])  12.8 us
    ppermute x1, waiting for transfers between devices, shards(): from_below = lax.ppermute(sent_up, 'az', up)  5.32 us
    ppermute x5, starting transfers between devices, butterfly_sum(): lax.ppermute(values, axis, [(i, i ^ step) for i in range(size)])  5.01 us
    ppermute x1, starting transfers between devices, shards(): from_above = lax.ppermute(sent_down, 'az', down)  4.61 us
    ppermute x1, waiting for transfers between devices, shards(): lax.ppermute(jnp.concatenate([stack_f[:, :, :tile], casing_slot]), 'ax',...  4.18 us
    ppermute x1, starting transfers between devices, shards(): lax.ppermute(jnp.concatenate([stack_f[:, :, nx - tile:], casing_slot]), '...  2.37 us
    ppermute x1, waiting for transfers between devices, shards(): from_above = lax.ppermute(sent_down, 'az', down)  2.16 us
    unnamed x47, local copies, waits for them, and re-layouts  1.32 us
  transfers between devices with their start and end apart: 9, of which 8 were waited for; matrix products, arithmetic and copies ran while one was open for 3% of the time, Pallas kernels for 0%

profile of v9, /device:TPU:0, one launch (start us, length us, event | category | flops | bytes accessed | tf_op | source)
XLA Modules:
  0.0 55.1 jit_solution(15128887984194793617)
XLA Ops:
  0.6 0.9 %multiply_multiply_fusion = (f32[8,16,128]{2,1,0:T(8,128)S(1)}, f32[8,16,128]{2,1,0:T(8,128)S(1)}) fusion(f32[4,8,16,128]{3,2,1,0:T(8,128)} %param.11), kind=kLoop, calls=%fused_computation.19 | loop fusion | flops 49152 | bytes 262144 | tf_op jit(solution)/shard_map/mul | solution.py:87
  1.6 1.0 %slice_divide_fusion = (f32[1,8,16,128]{3,2,1,0:T(8,128)S(1)}, f32[1,8,16,128]{3,2,1,0:T(8,128)S(1)}, f32[8,16,128]{2,1,0:T(8,128)S(1)}, f32[1,8,16,128]{3,2,1,0:T(8,128)S(1)}, f32[1,8,16,128]{3,2,1,0:T(8,128)S(1)}) fusion(f32[4,8,16,128]{3,2,1,0:T(8,128)} %param.11, f32[4,8,16,128]{3,2,1,0:T(8,128)} %param.12), kind=kLoop, calls=%fused_computation.160 | loop fusion | flops 81920 | bytes 655360 | tf_op jit(solution)/shard_map/div | solution.py:86
  2.6 0.9 %slice.889 = f32[1,8,16,1]{3,2,1,0:T(8,128)S(1)} slice(f32[4,8,16,128]{3,2,1,0:T(8,128)} %param.12), slice={[3:4], [0:8], [0:16], [127:128]} | slice | bytes 1024 | tf_op jit(solution)/shard_map/slice | solution.py:297
  3.5 0.9 %slice.691 = f32[2,8,16,128]{3,2,1,0:T(8,128)S(1)} slice(f32[4,8,16,128]{3,2,1,0:T(8,128)} %param.11), slice={[0:2], [0:8], [0:16], [0:128]} | slice | bytes 262144 | tf_op jit(solution)/shard_map/slice | solution.py:88
  5.2 0.3 copy.107
  6.2 0.3 fusion.4
  7.2 2.4 %collective-permute-start = (f32[9,8,8,128]{3,2,1,0:T(8,128)S(1)}, f32[9,8,8,128]{3,2,1,0:T(8,128)S(1)}, u32[]{:S(2)}, u32[]{:S(2)}) collective-permute-start(f32[9,8,8,128]{3,2,1,0:T(8,128)S(1)} %get-tuple-element.77), channel_id=1, source_target_pairs={{0,1},{1,2},{2,3},{4,5},{5,6},{6,7},{8,9},{9,10},{10,11},{12,13},{... | collective-permute-start | bytes 884744 | tf_op jit(solution)/shard_map/ppermute | solution.py:135
  9.6 1.3 %collective-permute-start.1 = (f32[9,8,8,128]{3,2,1,0:T(8,128)S(1)}, f32[9,8,8,128]{3,2,1,0:T(8,128)S(1)}, u32[]{:S(2)}, u32[]{:S(2)}) collective-permute-start(f32[9,8,8,128]{3,2,1,0:T(8,128)S(1)} %get-tuple-element.78), channel_id=1, source_target_pairs={{1,0},{2,1},{3,2},{5,4},{6,5},{7,6},{9,8},{10,9},{11,10},{13,12},{... | collective-permute-start | bytes 884744 | tf_op jit(solution)/shard_map/ppermute | solution.py:136
  11.0 4.2 %collective-permute-done.1 = f32[9,8,8,128]{3,2,1,0:T(8,128)S(1)} collective-permute-done((f32[9,8,8,128]{3,2,1,0:T(8,128)S(1)}, f32[9,8,8,128]{3,2,1,0:T(8,128)S(1)}, u32[]{:S(2)}, u32[]{:S(2)}) %collective-permute-start.1) | collective-permute-done | bytes 294944 | tf_op jit(solution)/shard_map/ppermute | solution.py:136
  16.0 4.6 %collective-permute-start.3 = (f32[8,32,128]{2,1,0:T(8,128)S(1)}, f32[8,32,128]{2,1,0:T(8,128)S(1)}, u32[]{:S(2)}, u32[]{:S(2)}) collective-permute-start(f32[8,32,128]{2,1,0:T(8,128)S(1)} %constant_dynamic-update-slice_fusion.22), channel_id=1, source_target_pairs={{4,0},{8,4},{12,8},{16,12},{20,16},{24,20},{28,24},{0,28},{5,1},{9... | collective-permute-start | bytes 393224 | tf_op jit(solution)/shard_map/ppermute | solution.py:161
  20.9 2.2 %collective-permute-done.3 = f32[8,32,128]{2,1,0:T(8,128)S(1)} collective-permute-done((f32[8,32,128]{2,1,0:T(8,128)S(1)}, f32[8,32,128]{2,1,0:T(8,128)S(1)}, u32[]{:S(2)}, u32[]{:S(2)}) %collective-permute-start.3) | collective-permute-done | bytes 131104 | tf_op jit(solution)/shard_map/ppermute | solution.py:161
  23.3 5.3 %collective-permute-done.2 = f32[8,32,128]{2,1,0:T(8,128)S(1)} collective-permute-done((f32[8,32,128]{2,1,0:T(8,128)S(1)}, f32[8,32,128]{2,1,0:T(8,128)S(1)}, u32[]{:S(2)}, u32[]{:S(2)}) %collective-permute-start.2) | collective-permute-done | bytes 131104 | tf_op jit(solution)/shard_map/ppermute | solution.py:160
  29.4 0.6 %select_reduce_fusion.6 = (f32[]{:T(128)}, f32[512]{0:T(512)S(1)}) fusion(s32[512]{0:T(512)S(1)} %copy-done.3, s32[]{:T(128)S(6)} %mul.402, s32[512]{0:T(512)S(1)} %copy-done.4, s32[]{:T(128)S(6)} %mul.401, f32[512]{0:T(512)S(1)} %select_reduce_fusion.1, f32[512]{0:T(512)S(1)} %copy-done.6), kind=kLoop, calls=%fused_computation.315 | loop fusion | flops 13311 | bytes 10252 | tf_op jit(solution)/shard_map/reduce_sum | solution.py:214
  30.7 0.7 %pad_maximum_fusion.11 = f32[129]{0:T(256)S(1)} fusion(f32[64]{0:T(128)S(1)} %get-tuple-element.8, f32[64]{0:T(128)S(1)} %get-tuple-element.7, f32[1]{0:T(128)} %bitcast.77), kind=kLoop, calls=%fused_computation.318 | loop fusion | flops 258 | bytes 1032 | tf_op jit(solution)/shard_map/concatenate | solution.py:302
  32.7 2.3 %collective-permute-done.4 = f32[129]{0:T(256)S(1)} collective-permute-done((f32[129]{0:T(256)S(1)}, f32[129]{0:T(256)S(1)}, u32[]{:S(2)}, u32[]{:S(2)}) %collective-permute-start.4) | collective-permute-done | bytes 548 | tf_op jit(solution)/shard_map/ppermute | solution.py:67
  35.0 0.7 %fusion.128 = f32[129]{0:T(256)S(1)} fusion(f32[129]{0:T(256)S(1)} %collective-permute-done.4, f32[64]{0:T(128)S(1)} %get-tuple-element.8, f32[64]{0:T(128)S(1)} %get-tuple-element.7, f32[1]{0:T(128)} %bitcast.77), kind=kLoop, calls=%fused_computation.327 | loop fusion | flops 387 | bytes 1548 | tf_op jit(solution)/shard_map/add | solution.py:67
  35.8 3.5 %collective-permute-done.5 = f32[129]{0:T(256)S(1)} collective-permute-done((f32[129]{0:T(256)S(1)}, f32[129]{0:T(256)S(1)}, u32[]{:S(2)}, u32[]{:S(2)}) %collective-permute-start.5) | collective-permute-done | bytes 548 | tf_op jit(solution)/shard_map/ppermute | solution.py:67
  39.3 4.5 %collective-permute-done.6 = f32[129]{0:T(256)S(1)} collective-permute-done((f32[129]{0:T(256)S(1)}, f32[129]{0:T(256)S(1)}, u32[]{:S(2)}, u32[]{:S(2)}) %collective-permute-start.6) | collective-permute-done | bytes 548 | tf_op jit(solution)/shard_map/ppermute | solution.py:67
  44.0 0.9 %collective-permute-done.7 = f32[129]{0:T(256)S(1)} collective-permute-done((f32[129]{0:T(256)S(1)}, f32[129]{0:T(256)S(1)}, u32[]{:S(2)}, u32[]{:S(2)}) %collective-permute-start.7) | collective-permute-done | bytes 548 | tf_op jit(solution)/shard_map/ppermute | solution.py:67
  44.9 4.8 %collective-permute-start.8 = (f32[129]{0:T(256)S(1)}, f32[129]{0:T(256)S(1)}, u32[]{:S(2)}, u32[]{:S(2)}) collective-permute-start(f32[129]{0:T(256)S(1)} %add.240), channel_id=1, source_target_pairs={{0,2},{1,3},{2,0},{3,1},{4,6},{5,7},{6,4},{7,5},{8,10},{9,11},{10,... | collective-permute-start | bytes 1556 | tf_op jit(solution)/shard_map/ppermute | solution.py:67
  49.7 1.5 %collective-permute-done.8 = f32[129]{0:T(256)S(1)} collective-permute-done((f32[129]{0:T(256)S(1)}, f32[129]{0:T(256)S(1)}, u32[]{:S(2)}, u32[]{:S(2)}) %collective-permute-start.8) | collective-permute-done | bytes 548 | tf_op jit(solution)/shard_map/ppermute | solution.py:67
  51.3 0.5 slice.891
  52.4 0.6 %fusion.122 = f32[64]{0:T(128)} fusion(f32[129]{0:T(256)S(1)} %add.241, f32[]{:T(128)} %bitcast.82), kind=kLoop, calls=%fused_computation.322 | loop fusion | flops 192 | bytes 772 | tf_op jit(solution)/shard_map/mul | solution.py:305
  53.1 0.9 %maximum_add_fusion = f32[4,8,16,128]{3,2,1,0:T(8,128)} fusion(f32[1,8,16,128]{3,2,1,0:T(8,128)S(1)} %fusion.12, f32[1,8,16,128]{3,2,1,0:T(8,128)S(1)} %fusion.29, f32[1,8,16,128]{3,2,1,0:T(8,128)S(1)} %fusion.38, f32[1,8,16,128]{3,2,1,0:T(8,128)S(1)} %fusion.50, f32[4,8,16]{2,1,0:T(8,128)S(1)} %get-tuple-element.76, f32[4,8,16]{2,1,0:T(8,128)S(1)} %get-tuple-element.75, ...), kind=kLoop, calls=%fused_computation.7 | loop fusion | flops 393216 | bytes 528640 | tf_op jit(solution)/shard_map/add | solution.py:314
  (139 shorter events, 6.0 us)
Async XLA Ops:
  0.6 3.8 %copy-start.1 = (f32[4,8,16,128]{3,2,1,0:T(8,128)S(1)}, f32[4,8,16,128]{3,2,1,0:T(8,128)}, u32[]{:S(2)}) copy-start(f32[4,8,16,128]{3,2,1,0:T(8,128)} %param.10) | copy-start | bytes 786436
  4.4 2.1 %copy-start.2 = (s32[8,16]{1,0:T(8,128)S(1)}, s32[8,16]{1,0:T(8,128)}, u32[]{:S(2)}) copy-start(s32[8,16]{1,0:T(8,128)} %param.14) | copy-start | bytes 1540
  4.4 2.1 %copy-start.7 = (f32[64]{0:T(128)S(1)}, f32[64]{0:T(128)}, u32[]{:S(2)}) copy-start(f32[64]{0:T(128)} %param.13) | copy-start | bytes 772
  4.5 2.3 %copy-start.5 = (s32[8,16]{1,0:T(8,128)S(1)}, s32[8,16]{1,0:T(8,128)}, u32[]{:S(2)}) copy-start(s32[8,16]{1,0:T(8,128)} %param.15) | copy-start | bytes 1540
  4.5 2.3 %copy-start.8 = (f32[64]{0:T(128)S(1)}, f32[64]{0:T(128)}, u32[]{:S(2)}) copy-start(f32[64]{0:T(128)} %param.16) | copy-start | bytes 772
  4.6 2.4 %copy-start = (f32[4,8,16,128]{3,2,1,0:T(8,128)S(1)}, f32[4,8,16,128]{3,2,1,0:T(8,128)}, u32[]{:S(2)}) copy-start(f32[4,8,16,128]{3,2,1,0:T(8,128)} %param.12) | copy-start | bytes 786436
  7.1 3.9 %copy-start.3 = (s32[512]{0:T(512)S(1)}, s32[512]{0:T(512)}, u32[]{:S(2)}) copy-start(s32[512]{0:T(512)} %param.18) | copy-start | bytes 6148
  7.1 3.9 %copy-start.4 = (s32[512]{0:T(512)S(1)}, s32[512]{0:T(512)}, u32[]{:S(2)}) copy-start(s32[512]{0:T(512)} %param.17) | copy-start | bytes 6148
  7.2 3.7 %collective-permute-start = (f32[9,8,8,128]{3,2,1,0:T(8,128)S(1)}, f32[9,8,8,128]{3,2,1,0:T(8,128)S(1)}, u32[]{:S(2)}, u32[]{:S(2)}) collective-permute-start(f32[9,8,8,128]{3,2,1,0:T(8,128)S(1)} %get-tuple-element.77), channel_id=1, source_target_pairs={{0,1},{1,2},{2,3},{4,5},{5,6},{6,7},{8,9},{9,10},{10,11},{12,13},{... | collective-permute-start | bytes 884744 | tf_op jit(solution)/shard_map/ppermute | solution.py:135
  9.6 5.6 %collective-permute-start.1 = (f32[9,8,8,128]{3,2,1,0:T(8,128)S(1)}, f32[9,8,8,128]{3,2,1,0:T(8,128)S(1)}, u32[]{:S(2)}, u32[]{:S(2)}) collective-permute-start(f32[9,8,8,128]{3,2,1,0:T(8,128)S(1)} %get-tuple-element.78), channel_id=1, source_target_pairs={{1,0},{2,1},{3,2},{5,4},{6,5},{7,6},{9,8},{10,9},{11,10},{13,12},{... | collective-permute-start | bytes 884744 | tf_op jit(solution)/shard_map/ppermute | solution.py:136
  15.3 14.1 %copy-start.6 = (f32[512]{0:T(512)S(1)}, f32[512]{0:T(512)}, u32[]{:S(2)}) copy-start(f32[512]{0:T(512)} %param.19) | copy-start | bytes 6148
  16.0 7.1 %collective-permute-start.3 = (f32[8,32,128]{2,1,0:T(8,128)S(1)}, f32[8,32,128]{2,1,0:T(8,128)S(1)}, u32[]{:S(2)}, u32[]{:S(2)}) collective-permute-start(f32[8,32,128]{2,1,0:T(8,128)S(1)} %constant_dynamic-update-slice_fusion.22), channel_id=1, source_target_pairs={{4,0},{8,4},{12,8},{16,12},{20,16},{24,20},{28,24},{0,28},{5,1},{9... | collective-permute-start | bytes 393224 | tf_op jit(solution)/shard_map/ppermute | solution.py:161
  20.9 7.7 %collective-permute-start.2 = (f32[8,32,128]{2,1,0:T(8,128)S(1)}, f32[8,32,128]{2,1,0:T(8,128)S(1)}, u32[]{:S(2)}, u32[]{:S(2)}) collective-permute-start(f32[8,32,128]{2,1,0:T(8,128)S(1)} %constant_dynamic-update-slice_fusion.14), channel_id=1, source_target_pairs={{0,4},{4,8},{8,12},{12,16},{16,20},{20,24},{24,28},{28,0},{1,5},{5... | collective-permute-start | bytes 393224 | tf_op jit(solution)/shard_map/ppermute | solution.py:160
  31.4 3.6 %collective-permute-start.4 = (f32[129]{0:T(256)S(1)}, f32[129]{0:T(256)S(1)}, u32[]{:S(2)}, u32[]{:S(2)}) collective-permute-start(f32[129]{0:T(256)S(1)} %pad_maximum_fusion.11), channel_id=1, source_target_pairs={{0,4},{4,0},{8,12},{12,8},{16,20},{20,16},{24,28},{28,24},{1,5},{5... | collective-permute-start | bytes 1556 | tf_op jit(solution)/shard_map/ppermute | solution.py:67
  35.7 3.6 %collective-permute-start.5 = (f32[129]{0:T(256)S(1)}, f32[129]{0:T(256)S(1)}, u32[]{:S(2)}, u32[]{:S(2)}) collective-permute-start(f32[129]{0:T(256)S(1)} %fusion.128), channel_id=1, source_target_pairs={{0,8},{4,12},{8,0},{12,4},{16,24},{20,28},{24,16},{28,20},{1,9},{5... | collective-permute-start | bytes 1556 | tf_op jit(solution)/shard_map/ppermute | solution.py:67
  39.3 4.5 %collective-permute-start.6 = (f32[129]{0:T(256)S(1)}, f32[129]{0:T(256)S(1)}, u32[]{:S(2)}, u32[]{:S(2)}) collective-permute-start(f32[129]{0:T(256)S(1)} %add.238), channel_id=1, source_target_pairs={{0,16},{4,20},{8,24},{12,28},{16,0},{20,4},{24,8},{28,12},{1,17},{... | collective-permute-start | bytes 1556 | tf_op jit(solution)/shard_map/ppermute | solution.py:67
  43.8 1.1 %collective-permute-start.7 = (f32[129]{0:T(256)S(1)}, f32[129]{0:T(256)S(1)}, u32[]{:S(2)}, u32[]{:S(2)}) collective-permute-start(f32[129]{0:T(256)S(1)} %add.239), channel_id=1, source_target_pairs={{0,1},{1,0},{2,3},{3,2},{4,5},{5,4},{6,7},{7,6},{8,9},{9,8},{10,11... | collective-permute-start | bytes 1556 | tf_op jit(solution)/shard_map/ppermute | solution.py:67
  44.9 6.3 %collective-permute-start.8 = (f32[129]{0:T(256)S(1)}, f32[129]{0:T(256)S(1)}, u32[]{:S(2)}, u32[]{:S(2)}) collective-permute-start(f32[129]{0:T(256)S(1)} %add.240), channel_id=1, source_target_pairs={{0,2},{1,3},{2,0},{3,1},{4,6},{5,7},{6,4},{7,5},{8,10},{9,11},{10,... | collective-permute-start | bytes 1556 | tf_op jit(solution)/shard_map/ppermute | solution.py:67

commit v10 on v7

--- a/solution.py
+++ b/solution.py
@@ -5,6 +5,7 @@
 
 step_dt = 0.25
 epsilon = 1e-06
+highest = lax.Precision.HIGHEST
 
 
 def with_halo(array, axis, dim, before, after, wrap):
@@ -97,27 +98,41 @@
     push = -step_dt * stiffness * a0
     stack_f = jnp.stack([a0, adjoint_in[1], adjoint_in[2], adjoint_in[3], axial_flow, swirl_flow, buoyancy, push])
     top, below = nr - 1, nr - 2
-    planes = [
-        acoustic[0, :, :, top],
-        acoustic[0, :, :, below],
-        acoustic[1, :, :, top],
-        acoustic[2, :, :, top],
-        acoustic[3, :, :, below],
-        axial_flow[:, :, top],
-        axial_flow[:, :, below],
-        swirl_flow[:, :, top],
-        swirl_flow[:, :, below],
-        buoyancy[:, :, top],
-        buoyancy[:, :, below],
-        stiffness[:, :, top],
-        wall,
-        source_top,
-    ]
-    stack_c = jnp.stack(planes)
-    n_planes = len(planes)
+    taken = [(0, top), (0, below), (1, top), (2, top), (3, below)]
+    taken_coef = [(0, top), (0, below), (1, top), (1, below), (2, top), (2, below), (3, top)]
+    n_planes = len(taken) + len(taken_coef) + 2
+    lane_in = lax.broadcasted_iota(jnp.int32, (nr, nr), 0)
+    lane_out = lax.broadcasted_iota(jnp.int32, (nr, nr), 1)
+
+    def chooser(picks, first):
+        return jnp.stack(
+            [
+                sum(
+                    ((lane_in == r) & (lane_out == first + k)).astype(jnp.float32)
+                    for k, (f, r) in enumerate(picks)
+                    if f == field
+                )
+                + jnp.zeros((nr, nr), jnp.float32)
+                for field in range(4)
+            ]
+        )
+
+    coefficients = jnp.stack([axial_flow, swirl_flow, buoyancy, stiffness])
+    packed = jnp.einsum("faxr,frk->axk", acoustic, chooser(taken, 0), precision=highest) + jnp.einsum(
+        "faxr,frk->axk", coefficients, chooser(taken_coef, len(taken)), precision=highest
+    )
+    hot_both = jnp.concatenate([segment_hot, noise_hot], axis=2).astype(jnp.float32)
+    n_tab = noise_table.shape[0]
+    wall_lane, source_lane = (n_planes - 2, n_planes - 1)
+    row = lax.broadcasted_iota(jnp.int32, (nseg + n_tab, nr), 0)
+    col = lax.broadcasted_iota(jnp.int32, (nseg + n_tab, nr), 1)
+    table_both = jnp.concatenate([admittance, noise_table * top_profile])
+    spread_table = jnp.where(
+        ((row < nseg) & (col == wall_lane)) | ((row >= nseg) & (col == source_lane)), table_both[:, None], 0.0
+    )
+    packed = packed + jnp.einsum("axs,sk->axk", hot_both, spread_table, precision=highest)
     tile = 8
     reach = 3
-    packed = jnp.pad(jnp.transpose(stack_c, (1, 2, 0)), ((0, 0), (0, 0), (0, nr - n_planes)))
     stack_all = jnp.concatenate([stack_f, packed[None]], axis=0)
     n_f = stack_f.shape[0]
     widened = with_halo(stack_all, "ax", 2, tile, tile, False)

time: 50.8 us -> 61.5 us (1.21)
  other arithmetic: 7.15 us -> 15.5 us
  local copies, waits for them, and re-layouts: 7.23 us -> 8.54 us
  matrix products: 0 us -> 1.08 us
    eq x1 -> x9, other arithmetic: 0.01 us -> 4.58 us  [the longest x5 2.84 us: chooser(): lane_out == first + k]
    convert_element_type x0 -> x2, other arithmetic: none -> 1.5 us  [chooser(): ((lane_in == r) & (lane_out == first + k)).astype(jnp.float32)]
    mul x0 -> x2, local copies, waits for them, and re-layouts: none -> 1.44 us  [the longest x1 1.25 us: shards(): push = -step_dt * stiffness * a0]
    mul x2, other arithmetic: 0.29 us -> 1.59 us  [the longest x1 0.9 us: shards(): push = -step_dt * stiffness * a0]
    unnamed x46 -> x47, local copies, waits for them, and re-layouts: 3.47 us -> 2.21 us
    ppermute x1, waiting for transfers between devices: 4.05 us -> 2.79 us  [with_halo(): lax.ppermute(lax.slice_in_dim(array, 0, after, axis=dim), axis, down)]
    dot_general x0 -> x3, matrix products: none -> 1.08 us  [the longest x1 0.4 us: shards(): jnp.einsum('faxr,frk->axk', acoustic, chooser(taken, 0), precision=highest)]
    div x0 -> x2, local copies, waits for them, and re-layouts: none -> 1.04 us  [shards(): buoyancy = 1.0 / mean_flow[2]]
  transfers between devices with their start and end apart: 9 -> 9, of which waited for: 8 -> 8; matrix products, arithmetic and copies ran while one was open for 3% -> 4% of each run, Pallas kernels for 0% -> 0%
where the time goes in v10:
time: 61.5 us; the launch traced here: 61.1 us
  starting transfers between devices  16.8 us (27%)
  waiting for transfers between devices  16.1 us (26%)
  other arithmetic  15.5 us (25%)
  local copies, waits for them, and re-layouts  8.54 us (14%)
  between operations  3.09 us (5%)
  matrix products  1.08 us (2%)
    ppermute x5, waiting for transfers between devices, butterfly_sum(): lax.ppermute(values, axis, [(i, i ^ step) for i in range(size)])  9.52 us
    ppermute x5, starting transfers between devices, butterfly_sum(): lax.ppermute(values, axis, [(i, i ^ step) for i in range(size)])  8.28 us
    ppermute x1, starting transfers between devices, shards(): from_above = lax.ppermute(sent_down, 'az', down)  3.26 us
    ppermute x1, waiting for transfers between devices, shards(): from_below = lax.ppermute(sent_up, 'az', up)  3.17 us
    eq x5, other arithmetic, chooser(): lane_out == first + k  2.84 us
    ppermute x1, waiting for transfers between devices, with_halo(): lax.ppermute(lax.slice_in_dim(array, 0, after, axis=dim), axis, down)  2.79 us
    ppermute x1, starting transfers between devices, with_halo(): lax.ppermute(lax.slice_in_dim(array, length - before, length, axis=dim),...  2.36 us
    unnamed x47, local copies, waits for them, and re-layouts  2.21 us
  transfers between devices with their start and end apart: 9, of which 8 were waited for; matrix products, arithmetic and copies ran while one was open for 4% of the time, Pallas kernels for 0%

profile of v10, /device:TPU:0, one launch (start us, length us, event | category | flops | bytes accessed | tf_op | source)
XLA Modules:
  0.0 61.1 jit_solution(12892010948875237982)
XLA Ops:
  5.7 1.0 %constant_dynamic-update-slice_fusion.3 = f32[9,8,16,128]{3,2,1,0:T(8,128)S(1)} fusion(f32[4,8,16,128]{3,2,1,0:T(8,128)} %param.12), kind=kLoop, calls=%fused_computation.156 | loop fusion | bytes 524288
  6.7 0.9 %fusion.165 = (f32[1,8,16,128]{3,2,1,0:T(8,128)S(1)}, f32[1,8,16,128]{3,2,1,0:T(8,128)S(1)}) fusion(f32[4,8,16,128]{3,2,1,0:T(8,128)} %param.11), kind=kLoop, calls=%fused_computation.370 | loop fusion | bytes 262144 | tf_op jit(solution)/shard_map/slice | solution.py:88
  8.3 0.9 %multiply_multiply_fusion.1 = (f32[1,8,16,128]{2,1,3,0:T(8,128)}, f32[1,8,16,128]{2,1,3,0:T(8,128)S(1)}, f32[1,8,16,128]{2,1,3,0:T(8,128)S(1)}) fusion(f32[1,8,16,128]{2,1,3,0:T(8,128)S(1)} %copy.128, f32[1,8,16,128]{2,1,3,0:T(8,128)S(1)} %copy.127, f32[1,8,16,128]{2,1,3,0:T(8,128)S(1)} %copy.126), kind=kLoop, calls=%fused_computation.9 | loop fusion | flops 81920 | bytes 393216 | tf_op jit(solution)/shard_map/mul | solution.py:98
  9.4 0.9 %copy.112 = f32[1,8,16,128]{3,2,0,1:T(8,128)} copy(f32[1,8,16,128]{2,1,3,0:T(8,128)S(1)} %get-tuple-element.52) | data formatting | bytes 131072 | tf_op jit(solution)/shard_map/div | solution.py:87
  11.0 1.2 %copy.116 = f32[1,8,16,128]{3,2,1,0:T(8,128)S(1)} copy(f32[1,8,16,128]{2,1,3,0:T(8,128)} %get-tuple-element.20) | data formatting | bytes 131072 | tf_op jit(solution)/shard_map/mul | solution.py:98
  14.1 0.8 %and_convert_fusion.3 = (f32[1,128,128]{2,1,0:T(8,128)S(1)}, f32[1,128,128]{2,1,0:T(8,128)S(1)}, f32[1,128,128]{2,1,0:T(8,128)S(1)}) fusion(pred[128]{0:T(512)(128)(4,1)} %get-tuple-element.108, pred[128]{0:T(512)(128)(4,1)S(1)} %get-tuple-element.105, pred[128]{0:T(512)(128)(4,1)} %get-tuple-element.107, pred[128]{0:T(512)(128)(4,1)} %get-tuple-element.106), kind=kLoop, calls=%fused_computation.152 | loop fusion | flops 98304 | bytes 197120 | tf_op jit(solution)/shard_map/convert_element_type | solution.py:111
  14.9 0.8 %convert_add_fusion.3 = (f32[1,128,128]{2,1,0:T(8,128)S(1)}, f32[1,128,128]{2,1,0:T(8,128)S(1)}, f32[1,128,128]{2,1,0:T(8,128)S(1)}, f32[1,128,128]{2,1,0:T(8,128)S(1)}) fusion(pred[128]{0:T(512)(128)(4,1)} %get-tuple-element.115, pred[128]{0:T(512)(128)(4,1)} %get-tuple-element.116, pred[128]{0:T(512)(128)(4,1)S(1)} %get-tuple-element.117, ...), kind=kLoop, calls=%fused_computation.142 | loop fusion | flops 327680 | bytes 263424 | tf_op jit(solution)/shard_map/add | solution.py:110
  16.9 0.8 %fusion.163 = (f32[9,8,8,128]{3,2,1,0:T(8,128)}, f32[9,8,8,128]{3,2,1,0:T(8,128)S(1)}) fusion(f32[9,8,16,128]{3,2,1,0:T(8,128)S(1)} %fusion.1), kind=kLoop, calls=%fused_computation.368 | loop fusion | bytes 1179648 | tf_op jit(solution)/shard_map/slice | solution.py:17
  17.7 2.4 %collective-permute-start = (f32[9,8,8,128]{3,2,1,0:T(8,128)}, f32[9,8,8,128]{3,2,1,0:T(8,128)S(1)}, u32[]{:S(2)}, u32[]{:S(2)}) collective-permute-start(f32[9,8,8,128]{3,2,1,0:T(8,128)} %get-tuple-element.50), channel_id=1, source_target_pairs={{0,1},{1,2},{2,3},{4,5},{5,6},{6,7},{8,9},{9,10},{10,11},{12,13},{... | collective-permute-start | bytes 884744 | tf_op jit(solution)/shard_map/ppermute | solution.py:17
  20.0 1.3 %collective-permute-start.1 = (f32[9,8,8,128]{3,2,1,0:T(8,128)S(1)}, f32[9,8,8,128]{3,2,1,0:T(8,128)S(1)}, u32[]{:S(2)}, u32[]{:S(2)}) collective-permute-start(f32[9,8,8,128]{3,2,1,0:T(8,128)S(1)} %get-tuple-element.51), channel_id=1, source_target_pairs={{1,0},{2,1},{3,2},{5,4},{6,5},{7,6},{9,8},{10,9},{11,10},{13,12},{... | collective-permute-start | bytes 884744 | tf_op jit(solution)/shard_map/ppermute | solution.py:20
  21.4 0.9 %slice.826 = f32[1,8,16,1]{3,2,1,0:T(8,128)S(1)} slice(f32[4,8,16,128]{3,2,1,0:T(8,128)} %param.10), slice={[0:1], [0:8], [0:16], [127:128]} | slice | bytes 1024 | tf_op jit(solution)/shard_map/slice | solution.py:286
  22.8 2.8 %collective-permute-done.1 = f32[9,8,8,128]{3,2,1,0:T(8,128)S(1)} collective-permute-done((f32[9,8,8,128]{3,2,1,0:T(8,128)S(1)}, f32[9,8,8,128]{3,2,1,0:T(8,128)S(1)}, u32[]{:S(2)}, u32[]{:S(2)}) %collective-permute-start.1) | collective-permute-done | bytes 294944 | tf_op jit(solution)/shard_map/ppermute | solution.py:20
  25.7 1.6 %collective-permute-start.2 = (f32[10,32,128]{2,1,0:T(8,128)S(1)}, f32[10,32,128]{2,1,0:T(8,128)S(1)}, u32[]{:S(2)}, u32[]{:S(2)}) collective-permute-start(f32[10,32,128]{2,1,0:T(8,128)S(1)} %get-tuple-element.30), channel_id=1, source_target_pairs={{0,4},{4,8},{8,12},{12,16},{16,20},{20,24},{24,28},{28,0},{1,5},{5... | collective-permute-start | bytes 491528 | tf_op jit(solution)/shard_map/ppermute | solution.py:149
  27.5 3.3 %collective-permute-start.3 = (f32[10,32,128]{2,1,0:T(8,128)S(1)}, f32[10,32,128]{2,1,0:T(8,128)S(1)}, u32[]{:S(2)}, u32[]{:S(2)}) collective-permute-start(f32[10,32,128]{2,1,0:T(8,128)S(1)} %get-tuple-element.31), channel_id=1, source_target_pairs={{4,0},{8,4},{12,8},{16,12},{20,16},{24,20},{28,24},{0,28},{5,1},{9... | collective-permute-start | bytes 491528 | tf_op jit(solution)/shard_map/ppermute | solution.py:150
  30.7 3.2 %collective-permute-done.2 = f32[10,32,128]{2,1,0:T(8,128)S(1)} collective-permute-done((f32[10,32,128]{2,1,0:T(8,128)S(1)}, f32[10,32,128]{2,1,0:T(8,128)S(1)}, u32[]{:S(2)}, u32[]{:S(2)}) %collective-permute-start.2) | collective-permute-done | bytes 163872 | tf_op jit(solution)/shard_map/ppermute | solution.py:149
  39.3 1.6 %collective-permute-done.4 = f32[129]{0:T(256)S(1)} collective-permute-done((f32[129]{0:T(256)S(1)}, f32[129]{0:T(256)S(1)}, u32[]{:S(2)}, u32[]{:S(2)}) %collective-permute-start.4) | collective-permute-done | bytes 548 | tf_op jit(solution)/shard_map/ppermute | solution.py:68
  41.7 0.8 %collective-permute-start.5 = (f32[129]{0:T(256)S(1)}, f32[129]{0:T(256)S(1)}, u32[]{:S(2)}, u32[]{:S(2)}) collective-permute-start(f32[129]{0:T(256)S(1)} %fusion.169), channel_id=1, source_target_pairs={{0,8},{4,12},{8,0},{12,4},{16,24},{20,28},{24,16},{28,20},{1,9},{5... | collective-permute-start | bytes 1556 | tf_op jit(solution)/shard_map/ppermute | solution.py:68
  42.5 2.8 %collective-permute-done.5 = f32[129]{0:T(256)S(1)} collective-permute-done((f32[129]{0:T(256)S(1)}, f32[129]{0:T(256)S(1)}, u32[]{:S(2)}, u32[]{:S(2)}) %collective-permute-start.5) | collective-permute-done | bytes 548 | tf_op jit(solution)/shard_map/ppermute | solution.py:68
  45.3 1.8 %collective-permute-start.6 = (f32[129]{0:T(256)S(1)}, f32[129]{0:T(256)S(1)}, u32[]{:S(2)}, u32[]{:S(2)}) collective-permute-start(f32[129]{0:T(256)S(1)} %add.284), channel_id=1, source_target_pairs={{0,16},{4,20},{8,24},{12,28},{16,0},{20,4},{24,8},{28,12},{1,17},{... | collective-permute-start | bytes 1556 | tf_op jit(solution)/shard_map/ppermute | solution.py:68
  47.0 2.7 %collective-permute-done.6 = f32[129]{0:T(256)S(1)} collective-permute-done((f32[129]{0:T(256)S(1)}, f32[129]{0:T(256)S(1)}, u32[]{:S(2)}, u32[]{:S(2)}) %collective-permute-start.6) | collective-permute-done | bytes 548 | tf_op jit(solution)/shard_map/ppermute | solution.py:68
  50.2 0.8 %collective-permute-done.7 = f32[129]{0:T(256)S(1)} collective-permute-done((f32[129]{0:T(256)S(1)}, f32[129]{0:T(256)S(1)}, u32[]{:S(2)}, u32[]{:S(2)}) %collective-permute-start.7) | collective-permute-done | bytes 548 | tf_op jit(solution)/shard_map/ppermute | solution.py:68
  51.1 4.6 %collective-permute-start.8 = (f32[129]{0:T(256)S(1)}, f32[129]{0:T(256)S(1)}, u32[]{:S(2)}, u32[]{:S(2)}) collective-permute-start(f32[129]{0:T(256)S(1)} %add.286), channel_id=1, source_target_pairs={{0,2},{1,3},{2,0},{3,1},{4,6},{5,7},{6,4},{7,5},{8,10},{9,11},{10,... | collective-permute-start | bytes 1556 | tf_op jit(solution)/shard_map/ppermute | solution.py:68
  55.7 1.5 %collective-permute-done.8 = f32[129]{0:T(256)S(1)} collective-permute-done((f32[129]{0:T(256)S(1)}, f32[129]{0:T(256)S(1)}, u32[]{:S(2)}, u32[]{:S(2)}) %collective-permute-start.8) | collective-permute-done | bytes 548 | tf_op jit(solution)/shard_map/ppermute | solution.py:68
  59.1 0.9 %maximum_add_fusion = f32[4,8,16,128]{3,2,1,0:T(8,128)} fusion(f32[1,8,16,128]{3,2,1,0:T(8,128)S(1)} %fusion.29, f32[1,8,16,128]{3,2,1,0:T(8,128)S(1)} %fusion.46, f32[1,8,16,128]{3,2,1,0:T(8,128)S(1)} %fusion.55, f32[1,8,16,128]{3,2,1,0:T(8,128)S(1)} %fusion.67, f32[4,8,16]{2,1,0:T(8,128)S(1)} %get-tuple-element.81, f32[4,8,16]{2,1,0:T(8,128)S(1)} %get-tuple-element.80, ...), kind=kLoop, calls=%fused_computation.33 | loop fusion | flops 393216 | bytes 528640 | tf_op jit(solution)/shard_map/add | solution.py:304
  (138 shorter events, 17.9 us)
Async XLA Ops:
  0.6 7.2 %slice-start.1 = ((f32[4,8,16,128]{3,2,1,0:T(8,128)}), f32[1,8,16,128]{3,2,1,0:T(8,128)S(1)}, s32[]{:S(2)}) async-start(f32[4,8,16,128]{3,2,1,0:T(8,128)} %param.12), calls=%async_computation.1 | async-start | bytes 131072 | tf_op jit(solution)/shard_map/slice | solution.py:97
  2.3 12.6 %copy-start.8 = (pred[128]{0:T(512)(128)(4,1)}, pred[128]{0:T(512)(128)(4,1)S(1)}, u32[]{:S(2)}) copy-start(pred[128]{0:T(512)(128)(4,1)S(1)} %get-tuple-element.117) | copy-start | bytes 388
  10.3 5.4 %copy-start.3 = (f32[1,8,16,128]{3,2,0,1:T(8,128)S(1)}, f32[1,8,16,128]{3,2,0,1:T(8,128)}, u32[]{:S(2)}) copy-start(f32[1,8,16,128]{3,2,0,1:T(8,128)} %copy.112) | copy-start | bytes 196612
  11.0 5.1 %copy-start.4 = (f32[4,8,16,128]{3,2,1,0:T(8,128)S(1)}, f32[4,8,16,128]{3,2,1,0:T(8,128)}, u32[]{:S(2)}) copy-start(f32[4,8,16,128]{3,2,1,0:T(8,128)} %param.10) | copy-start | bytes 786436
  12.4 4.1 %copy-start.13 = (pred[128]{0:T(512)(128)(4,1)S(1)}, pred[128]{0:T(512)(128)(4,1)}, u32[]{:S(2)}) copy-start(pred[128]{0:T(512)(128)(4,1)} %get-tuple-element.123) | copy-start | bytes 388
  12.4 4.1 %copy-start.14 = (pred[128]{0:T(512)(128)(4,1)S(1)}, pred[128]{0:T(512)(128)(4,1)}, u32[]{:S(2)}) copy-start(pred[128]{0:T(512)(128)(4,1)} %get-tuple-element.124) | copy-start | bytes 388
  12.5 4.1 %copy-start.15 = (pred[128]{0:T(512)(128)(4,1)S(1)}, pred[128]{0:T(512)(128)(4,1)}, u32[]{:S(2)}) copy-start(pred[128]{0:T(512)(128)(4,1)} %get-tuple-element.121) | copy-start | bytes 388
  12.5 4.1 %copy-start.16 = (pred[128]{0:T(512)(128)(4,1)S(1)}, pred[128]{0:T(512)(128)(4,1)}, u32[]{:S(2)}) copy-start(pred[128]{0:T(512)(128)(4,1)} %get-tuple-element.122) | copy-start | bytes 388
  15.7 5.6 %copy-start.6 = (s32[512]{0:T(512)S(1)}, s32[512]{0:T(512)}, u32[]{:S(2)}) copy-start(s32[512]{0:T(512)} %param.18) | copy-start | bytes 6148
  15.7 5.6 %copy-start.7 = (s32[512]{0:T(512)S(1)}, s32[512]{0:T(512)}, u32[]{:S(2)}) copy-start(s32[512]{0:T(512)} %param.17) | copy-start | bytes 6148
  15.7 6.6 %copy-start.1 = (f32[4,8,16,128]{3,2,1,0:T(8,128)S(1)}, f32[4,8,16,128]{3,2,1,0:T(8,128)}, u32[]{:S(2)}) copy-start(f32[4,8,16,128]{3,2,1,0:T(8,128)} %param.12) | copy-start | bytes 786436
  17.7 5.1 %collective-permute-start = (f32[9,8,8,128]{3,2,1,0:T(8,128)}, f32[9,8,8,128]{3,2,1,0:T(8,128)S(1)}, u32[]{:S(2)}, u32[]{:S(2)}) collective-permute-start(f32[9,8,8,128]{3,2,1,0:T(8,128)} %get-tuple-element.50), channel_id=1, source_target_pairs={{0,1},{1,2},{2,3},{4,5},{5,6},{6,7},{8,9},{9,10},{10,11},{12,13},{... | collective-permute-start | bytes 884744 | tf_op jit(solution)/shard_map/ppermute | solution.py:17
  20.0 5.6 %collective-permute-start.1 = (f32[9,8,8,128]{3,2,1,0:T(8,128)S(1)}, f32[9,8,8,128]{3,2,1,0:T(8,128)S(1)}, u32[]{:S(2)}, u32[]{:S(2)}) collective-permute-start(f32[9,8,8,128]{3,2,1,0:T(8,128)S(1)} %get-tuple-element.51), channel_id=1, source_target_pairs={{1,0},{2,1},{3,2},{5,4},{6,5},{7,6},{9,8},{10,9},{11,10},{13,12},{... | collective-permute-start | bytes 884744 | tf_op jit(solution)/shard_map/ppermute | solution.py:20
  25.7 8.2 %collective-permute-start.2 = (f32[10,32,128]{2,1,0:T(8,128)S(1)}, f32[10,32,128]{2,1,0:T(8,128)S(1)}, u32[]{:S(2)}, u32[]{:S(2)}) collective-permute-start(f32[10,32,128]{2,1,0:T(8,128)S(1)} %get-tuple-element.30), channel_id=1, source_target_pairs={{0,4},{4,8},{8,12},{12,16},{16,20},{20,24},{24,28},{28,0},{1,5},{5... | collective-permute-start | bytes 491528 | tf_op jit(solution)/shard_map/ppermute | solution.py:149
  27.4 7.9 %copy-start.11 = (f32[512]{0:T(512)S(1)}, f32[512]{0:T(512)}, u32[]{:S(2)}) copy-start(f32[512]{0:T(512)} %param.19) | copy-start | bytes 6148
  27.4 9.1 %copy-start.12 = (f32[64]{0:T(128)S(1)}, f32[64]{0:T(128)}, u32[]{:S(2)}) copy-start(f32[64]{0:T(128)} %param.13) | copy-start | bytes 772
  27.5 7.1 %collective-permute-start.3 = (f32[10,32,128]{2,1,0:T(8,128)S(1)}, f32[10,32,128]{2,1,0:T(8,128)S(1)}, u32[]{:S(2)}, u32[]{:S(2)}) collective-permute-start(f32[10,32,128]{2,1,0:T(8,128)S(1)} %get-tuple-element.31), channel_id=1, source_target_pairs={{4,0},{8,4},{12,8},{16,12},{20,16},{24,20},{28,24},{0,28},{5,1},{9... | collective-permute-start | bytes 491528 | tf_op jit(solution)/shard_map/ppermute | solution.py:150
  33.9 4.3 %slice-start = ((f32[9,8,32,128]{3,2,1,0:T(8,128)}), f32[8,8,32,128]{3,2,1,0:T(8,128)S(1)}, s32[]{:S(2)}) async-start(f32[9,8,32,128]{3,2,1,0:T(8,128)} %copy-done), calls=%async_computation | async-start | bytes 2097152 | tf_op jit(solution)/shard_map/slice | solution.py:156
  37.4 3.6 %collective-permute-start.4 = (f32[129]{0:T(256)S(1)}, f32[129]{0:T(256)S(1)}, u32[]{:S(2)}, u32[]{:S(2)}) collective-permute-start(f32[129]{0:T(256)S(1)} %pad_maximum_fusion.4), channel_id=1, source_target_pairs={{0,4},{4,0},{8,12},{12,8},{16,20},{20,16},{24,28},{28,24},{1,5},{5... | collective-permute-start | bytes 1556 | tf_op jit(solution)/shard_map/ppermute | solution.py:68
  39.0 20.0 %copy-start.9 = (pred[128]{0:T(512)(128)(4,1)S(1)}, pred[128]{0:T(512)(128)(4,1)}, u32[]{:S(2)}) copy-start(pred[128]{0:T(512)(128)(4,1)} %copy-done.8) | copy-start | bytes 388
  41.7 3.6 %collective-permute-start.5 = (f32[129]{0:T(256)S(1)}, f32[129]{0:T(256)S(1)}, u32[]{:S(2)}, u32[]{:S(2)}) collective-permute-start(f32[129]{0:T(256)S(1)} %fusion.169), channel_id=1, source_target_pairs={{0,8},{4,12},{8,0},{12,4},{16,24},{20,28},{24,16},{28,20},{1,9},{5... | collective-permute-start | bytes 1556 | tf_op jit(solution)/shard_map/ppermute | solution.py:68
  45.3 4.5 %collective-permute-start.6 = (f32[129]{0:T(256)S(1)}, f32[129]{0:T(256)S(1)}, u32[]{:S(2)}, u32[]{:S(2)}) collective-permute-start(f32[129]{0:T(256)S(1)} %add.284), channel_id=1, source_target_pairs={{0,16},{4,20},{8,24},{12,28},{16,0},{20,4},{24,8},{28,12},{1,17},{... | collective-permute-start | bytes 1556 | tf_op jit(solution)/shard_map/ppermute | solution.py:68
  49.8 1.3 %collective-permute-start.7 = (f32[129]{0:T(256)S(1)}, f32[129]{0:T(256)S(1)}, u32[]{:S(2)}, u32[]{:S(2)}) collective-permute-start(f32[129]{0:T(256)S(1)} %add.285), channel_id=1, source_target_pairs={{0,1},{1,0},{2,3},{3,2},{4,5},{5,4},{6,7},{7,6},{8,9},{9,8},{10,11... | collective-permute-start | bytes 1556 | tf_op jit(solution)/shard_map/ppermute | solution.py:68
  51.1 6.2 %collective-permute-start.8 = (f32[129]{0:T(256)S(1)}, f32[129]{0:T(256)S(1)}, u32[]{:S(2)}, u32[]{:S(2)}) collective-permute-start(f32[129]{0:T(256)S(1)} %add.286), channel_id=1, source_target_pairs={{0,2},{1,3},{2,0},{3,1},{4,6},{5,7},{6,4},{7,5},{8,10},{9,11},{10,... | collective-permute-start | bytes 1556 | tf_op jit(solution)/shard_map/ppermute | solution.py:68
  (4 other events, 13.9 us)

commit v11 on v7

--- a/solution.py
+++ b/solution.py
@@ -120,16 +120,30 @@
     packed = jnp.pad(jnp.transpose(stack_c, (1, 2, 0)), ((0, 0), (0, 0), (0, nr - n_planes)))
     stack_all = jnp.concatenate([stack_f, packed[None]], axis=0)
     n_f = stack_f.shape[0]
-    widened = with_halo(stack_all, "ax", 2, tile, tile, False)
+    sent_x = jnp.concatenate([stack_all[:5], stack_all[6:]], axis=0)
+    size_ax = lax.axis_size("ax")
+    right = [(i, i + 1) for i in range(size_ax - 1)]
+    left = [(j, i) for i, j in right]
+    length_x = stack_all.shape[2]
+    x_before = lax.ppermute(sent_x[:, :, length_x - tile :], "ax", right)
+    x_after = lax.ppermute(sent_x[:, :, :tile], "ax", left)
+    no_w = jnp.zeros_like(x_before[:1])
+    x_before = jnp.concatenate([x_before[:5], no_w, x_before[5:]], axis=0)
+    x_after = jnp.concatenate([x_after[:5], no_w, x_after[5:]], axis=0)
+    widened = jnp.concatenate([x_before, stack_all, x_after], axis=2)
     size_az, length_a = (lax.axis_size("az"), widened.shape[1])
     up = [(i, (i + 1) % size_az) for i in range(size_az)]
     down = [(j, i) for i, j in up]
+    def casing_rows(rows):
+        joined = jnp.concatenate([widened[n_f, r, :, :n_planes] for r in rows], axis=-1)
+        return jnp.pad(joined, ((0, 0), (0, nr - joined.shape[-1])))
+
     sent_up = jnp.stack(
         [widened[f, length_a - 1] for f in (0, 1, 2, 3, 5, 6, 7)]
-        + [widened[n_f, length_a - reach + k] for k in range(reach)]
+        + [casing_rows(range(length_a - reach, length_a))]
     )
     sent_down = jnp.stack(
-        [widened[f, 0] for f in (0, 1, 2, 3, 5, 7)] + [widened[7, 1]] + [widened[n_f, k] for k in range(reach)]
+        [widened[f, 0] for f in (0, 1, 2, 3, 5, 7)] + [widened[7, 1]] + [casing_rows(range(reach))]
     )
     from_below = lax.ppermute(sent_up, "az", up)
     from_above = lax.ppermute(sent_down, "az", down)
@@ -140,7 +154,12 @@
     wide_f = jnp.concatenate(
         [row_before[:, None], widened[:n_f], row_after[:, None], row_after2[:, None]], axis=1
     )
-    wide_packed = jnp.concatenate([from_below[7:], widened[n_f], from_above[7:]], axis=0)
+    def casing_unpack(row):
+        return jnp.stack([row[:, k * n_planes : (k + 1) * n_planes] for k in range(reach)])
+
+    wide_packed = jnp.concatenate(
+        [casing_unpack(from_below[7]), widened[n_f, :, :, :n_planes], casing_unpack(from_above[7])], axis=0
+    )
     wide_c = jnp.transpose(wide_packed[:, :, :n_planes], (2, 0, 1))
 
     oc = (reach, tile)

time: 50.8 us -> 69.6 us (1.37)
  waiting for transfers between devices: 15.9 us -> 37.1 us
  starting transfers between devices: 17.1 us -> 10.1 us
  local copies, waits for them, and re-layouts: 7.23 us -> 9.48 us
  other arithmetic: 7.15 us -> 9.08 us
    ppermute x1, waiting for transfers between devices: 2.24 us -> 15.2 us  [shards(): from_below = lax.ppermute(sent_up, 'az', up)]
    ppermute x5, starting transfers between devices: 8.71 us -> 1.59 us  [butterfly_sum(): lax.ppermute(values, axis, [(i, i ^ step) for i in range(size)])]
    ppermute x1, waiting for transfers between devices: 0.46 us -> 7.05 us  [shards(): from_above = lax.ppermute(sent_down, 'az', down)]
    ppermute x5, waiting for transfers between devices: 9.11 us -> 13 us  [butterfly_sum(): lax.ppermute(values, axis, [(i, i ^ step) for i in range(size)])]
    ppermute x2, waiting for transfers between devices: 4.05 us -> 1.8 us  [the longest x1 1.8 us: shards(): x_after = lax.ppermute(sent_x[:, :, :tile], 'ax', left)]
    another operation x4, local copies, waits for them, and re-layouts: 0.16 us -> 1.17 us  [shards(): row_after2 = jnp.stack([blank] * 7 + [from_above[6]])]
    slice x1, local copies, waits for them, and re-layouts: 1.12 us -> 0.14 us  [shards(): acoustic[3, :, :, below]]
    unnamed x46 -> x82, local copies, waits for them, and re-layouts: 3.47 us -> 4.37 us
  transfers between devices with their start and end apart: 9 -> 9, of which waited for: 8 -> 8; matrix products, arithmetic and copies ran while one was open for 3% -> 7% of each run, Pallas kernels for 0% -> 0%
where the time goes in v11:
time: 69.6 us; the launch traced here: 69.2 us
  waiting for transfers between devices  37.1 us (53%)
  starting transfers between devices  10.1 us (15%)
  local copies, waits for them, and re-layouts  9.48 us (14%)
  other arithmetic  9.08 us (13%)
  between operations  3.41 us (5%)
    ppermute x1, waiting for transfers between devices, shards(): from_below = lax.ppermute(sent_up, 'az', up)  15.2 us
    ppermute x5, waiting for transfers between devices, butterfly_sum(): lax.ppermute(values, axis, [(i, i ^ step) for i in range(size)])  13 us
    ppermute x1, waiting for transfers between devices, shards(): from_above = lax.ppermute(sent_down, 'az', down)  7.05 us
    unnamed x82, local copies, waits for them, and re-layouts  4.37 us
    ppermute x1, starting transfers between devices, shards(): from_above = lax.ppermute(sent_down, 'az', down)  3.26 us
    ppermute x1, starting transfers between devices, shards(): x_before = lax.ppermute(sent_x[:, :, length_x - tile:], 'ax', right)  2.37 us
    ppermute x1, waiting for transfers between devices, shards(): x_after = lax.ppermute(sent_x[:, :, :tile], 'ax', left)  1.8 us
    ppermute x5, starting transfers between devices, butterfly_sum(): lax.ppermute(values, axis, [(i, i ^ step) for i in range(size)])  1.59 us
  transfers between devices with their start and end apart: 9, of which 8 were waited for; matrix products, arithmetic and copies ran while one was open for 7% of the time, Pallas kernels for 0%

profile of v11, /device:TPU:0, one launch (start us, length us, event | category | flops | bytes accessed | tf_op | source)
XLA Modules:
  0.0 69.2 jit_solution(3550199681527916389)
XLA Ops:
  0.7 1.0 %slice.922 = f32[1,8,16,1]{3,2,1,0:T(8,128)S(1)} slice(f32[4,8,16,128]{3,2,1,0:T(8,128)} %param.12), slice={[3:4], [0:8], [0:16], [127:128]} | slice | bytes 1024 | tf_op jit(solution)/shard_map/slice | solution.py:291
  1.6 1.0 %constant_dynamic-update-slice_fusion.18 = f32[9,8,16,128]{3,2,1,0:T(8,128)S(1)} fusion(f32[4,8,16,128]{3,2,1,0:T(8,128)} %param.12), kind=kLoop, calls=%fused_computation.43 | loop fusion | bytes 524288
  2.8 0.9 %multiply_multiply_fusion = (f32[8,16,128]{2,1,0:T(8,128)S(1)}, f32[8,16,128]{2,1,0:T(8,128)S(1)}) fusion(f32[4,8,16,128]{3,2,1,0:T(8,128)} %param.11), kind=kLoop, calls=%fused_computation.23 | loop fusion | flops 49152 | bytes 262144 | tf_op jit(solution)/shard_map/mul | solution.py:87
  5.8 0.8 %fusion.7 = (f32[8,16]{1,0:T(8,128)}, f32[8,16]{1,0:T(8,128)S(1)}, f32[8,16]{1,0:T(8,128)S(1)}, f32[8,16]{1,0:T(8,128)S(1)}) fusion(f32[8,16,1]{2,1,0:T(8,128)S(1)} %copy.162, f32[8,16,1]{2,1,0:T(8,128)S(1)} %copy.161, f32[8,16,128]{2,1,0:T(8,128)S(1)} %get-tuple-element.60, f32[8,16,128]{2,1,0:T(8,128)S(1)} %get-tuple-element.63, ...), kind=kLoop, calls=%fused_computation.70 | loop fusion | flops 512 | bytes 5120 | tf_op jit(solution)/shard_map/mul | solution.py:291
  7.0 2.4 %collective-permute-start = (f32[8,8,8,128]{3,2,1,0:T(8,128)S(1)}, f32[8,8,8,128]{3,2,1,0:T(8,128)S(1)}, u32[]{:S(2)}, u32[]{:S(2)}) collective-permute-start(f32[8,8,8,128]{3,2,1,0:T(8,128)S(1)} %get-tuple-element.54), channel_id=1, source_target_pairs={{0,1},{1,2},{2,3},{4,5},{5,6},{6,7},{8,9},{9,10},{10,11},{12,13},{... | collective-permute-start | bytes 786440 | tf_op jit(solution)/shard_map/ppermute | solution.py:128
  9.3 1.3 %collective-permute-start.1 = (f32[8,8,8,128]{3,2,1,0:T(8,128)S(1)}, f32[8,8,8,128]{3,2,1,0:T(8,128)S(1)}, u32[]{:S(2)}, u32[]{:S(2)}) collective-permute-start(f32[8,8,8,128]{3,2,1,0:T(8,128)S(1)} %get-tuple-element.55), channel_id=1, source_target_pairs={{1,0},{2,1},{3,2},{5,4},{6,5},{7,6},{9,8},{10,9},{11,10},{13,12},{... | collective-permute-start | bytes 786440 | tf_op jit(solution)/shard_map/ppermute | solution.py:129
  13.1 1.8 %collective-permute-done.1 = f32[8,8,8,128]{3,2,1,0:T(8,128)S(1)} collective-permute-done((f32[8,8,8,128]{3,2,1,0:T(8,128)S(1)}, f32[8,8,8,128]{3,2,1,0:T(8,128)S(1)}, u32[]{:S(2)}, u32[]{:S(2)}) %collective-permute-start.1) | collective-permute-done | bytes 262176 | tf_op jit(solution)/shard_map/ppermute | solution.py:129
  15.2 0.8 %copy-done.5 = f32[8,32,128]{2,1,0:T(8,128)} copy-done((f32[8,32,128]{2,1,0:T(8,128)}, f32[8,32,128]{2,1,0:T(8,128)S(1)}, u32[]{:S(2)}) %copy-start.5) | copy-done | bytes 131096
  16.2 1.6 %collective-permute-start.2 = (f32[8,32,128]{1,2,0:T(8,128)S(1)}, f32[8,32,128]{1,2,0:T(8,128)S(1)}, u32[]{:S(2)}, u32[]{:S(2)}) collective-permute-start(f32[8,32,128]{1,2,0:T(8,128)S(1)} %copy.144), channel_id=1, source_target_pairs={{0,4},{4,8},{8,12},{12,16},{16,20},{20,24},{24,28},{28,0},{1,5},{5... | collective-permute-start | bytes 393224 | tf_op jit(solution)/shard_map/ppermute | solution.py:148
  17.8 0.7 %copy.170 = f32[1,8,32,14]{2,1,3,0:T(8,128)} copy(f32[1,8,32,14]{3,2,1,0:T(8,128)S(1)} %maximum_maximum_fusion.1) | data formatting | bytes 28672
  19.0 3.3 %collective-permute-start.3 = (f32[8,32,128]{1,2,0:T(8,128)S(1)}, f32[8,32,128]{1,2,0:T(8,128)S(1)}, u32[]{:S(2)}, u32[]{:S(2)}) collective-permute-start(f32[8,32,128]{1,2,0:T(8,128)S(1)} %copy.147), channel_id=1, source_target_pairs={{4,0},{8,4},{12,8},{16,12},{20,16},{24,20},{28,24},{0,28},{5,1},{9... | collective-permute-start | bytes 393224 | tf_op jit(solution)/shard_map/ppermute | solution.py:149
  22.3 15.2 %collective-permute-done.2 = f32[8,32,128]{1,2,0:T(8,128)S(1)} collective-permute-done((f32[8,32,128]{1,2,0:T(8,128)S(1)}, f32[8,32,128]{1,2,0:T(8,128)S(1)}, u32[]{:S(2)}, u32[]{:S(2)}) %collective-permute-start.2) | collective-permute-done | bytes 131104 | tf_op jit(solution)/shard_map/ppermute | solution.py:148
  37.9 7.0 %collective-permute-done.3 = f32[8,32,128]{1,2,0:T(8,128)S(1)} collective-permute-done((f32[8,32,128]{1,2,0:T(8,128)S(1)}, f32[8,32,128]{1,2,0:T(8,128)S(1)}, u32[]{:S(2)}, u32[]{:S(2)}) %collective-permute-start.3) | collective-permute-done | bytes 131104 | tf_op jit(solution)/shard_map/ppermute | solution.py:149
  46.0 0.6 select_reduce_fusion.6
  47.5 0.7 %pad_maximum_fusion.1 = f32[129]{0:T(256)S(1)} fusion(f32[64]{0:T(128)S(1)} %get-tuple-element.11, f32[64]{0:T(128)S(1)} %get-tuple-element.10, f32[1]{0:T(128)} %bitcast.88), kind=kLoop, calls=%fused_computation.331 | loop fusion | flops 258 | bytes 1032 | tf_op jit(solution)/shard_map/concatenate | solution.py:296
  49.9 1.9 %collective-permute-done.4 = f32[129]{0:T(256)S(1)} collective-permute-done((f32[129]{0:T(256)S(1)}, f32[129]{0:T(256)S(1)}, u32[]{:S(2)}, u32[]{:S(2)}) %collective-permute-start.4) | collective-permute-done | bytes 548 | tf_op jit(solution)/shard_map/ppermute | solution.py:67
  51.8 0.7 %fusion.134 = f32[129]{0:T(256)S(1)} fusion(f32[129]{0:T(256)S(1)} %collective-permute-done.4, f32[64]{0:T(128)S(1)} %get-tuple-element.11, f32[64]{0:T(128)S(1)} %get-tuple-element.10, f32[1]{0:T(128)} %bitcast.88), kind=kLoop, calls=%fused_computation.341 | loop fusion | flops 387 | bytes 1548 | tf_op jit(solution)/shard_map/add | solution.py:67
  52.6 3.5 %collective-permute-done.5 = f32[129]{0:T(256)S(1)} collective-permute-done((f32[129]{0:T(256)S(1)}, f32[129]{0:T(256)S(1)}, u32[]{:S(2)}, u32[]{:S(2)}) %collective-permute-start.5) | collective-permute-done | bytes 548 | tf_op jit(solution)/shard_map/ppermute | solution.py:67
  56.1 0.8 %collective-permute-start.6 = (f32[129]{0:T(256)S(1)}, f32[129]{0:T(256)S(1)}, u32[]{:S(2)}, u32[]{:S(2)}) collective-permute-start(f32[129]{0:T(256)S(1)} %add.238), channel_id=1, source_target_pairs={{0,16},{4,20},{8,24},{12,28},{16,0},{20,4},{24,8},{28,12},{1,17},{... | collective-permute-start | bytes 1556 | tf_op jit(solution)/shard_map/ppermute | solution.py:67
  56.9 3.7 %collective-permute-done.6 = f32[129]{0:T(256)S(1)} collective-permute-done((f32[129]{0:T(256)S(1)}, f32[129]{0:T(256)S(1)}, u32[]{:S(2)}, u32[]{:S(2)}) %collective-permute-start.6) | collective-permute-done | bytes 548 | tf_op jit(solution)/shard_map/ppermute | solution.py:67
  60.6 1.1 %collective-permute-done.7 = f32[129]{0:T(256)S(1)} collective-permute-done((f32[129]{0:T(256)S(1)}, f32[129]{0:T(256)S(1)}, u32[]{:S(2)}, u32[]{:S(2)}) %collective-permute-start.7) | collective-permute-done | bytes 548 | tf_op jit(solution)/shard_map/ppermute | solution.py:67
  61.7 0.8 %collective-permute-start.8 = (f32[129]{0:T(256)S(1)}, f32[129]{0:T(256)S(1)}, u32[]{:S(2)}, u32[]{:S(2)}) collective-permute-start(f32[129]{0:T(256)S(1)} %add.240), channel_id=1, source_target_pairs={{0,2},{1,3},{2,0},{3,1},{4,6},{5,7},{6,4},{7,5},{8,10},{9,11},{10,... | collective-permute-start | bytes 1556 | tf_op jit(solution)/shard_map/ppermute | solution.py:67
  62.5 2.8 %collective-permute-done.8 = f32[129]{0:T(256)S(1)} collective-permute-done((f32[129]{0:T(256)S(1)}, f32[129]{0:T(256)S(1)}, u32[]{:S(2)}, u32[]{:S(2)}) %collective-permute-start.8) | collective-permute-done | bytes 548 | tf_op jit(solution)/shard_map/ppermute | solution.py:67
  67.1 0.9 %maximum_add_fusion = f32[4,8,16,128]{3,2,1,0:T(8,128)} fusion(f32[1,8,16,128]{3,2,1,0:T(8,128)S(1)} %fusion.15, f32[1,8,16,128]{3,2,1,0:T(8,128)S(1)} %fusion.32, f32[1,8,16,128]{3,2,1,0:T(8,128)S(1)} %fusion.41, f32[1,8,16,128]{3,2,1,0:T(8,128)S(1)} %fusion.53, f32[4,8,16]{2,1,0:T(8,128)S(1)} %get-tuple-element.96, f32[4,8,16]{2,1,0:T(8,128)S(1)} %get-tuple-element.95, ...), kind=kLoop, calls=%fused_computation.11 | loop fusion | flops 393216 | bytes 528640 | tf_op jit(solution)/shard_map/add | solution.py:308
  (184 shorter events, 10.5 us)
Async XLA Ops:
  0.6 4.0 %copy-start.2 = (f32[4,8,16,128]{3,2,1,0:T(8,128)S(1)}, f32[4,8,16,128]{3,2,1,0:T(8,128)}, u32[]{:S(2)}) copy-start(f32[4,8,16,128]{3,2,1,0:T(8,128)} %param.11) | copy-start | bytes 786436
  0.6 3.1 %copy-start.3 = (f32[4,8,16,128]{3,2,1,0:T(8,128)S(1)}, f32[4,8,16,128]{3,2,1,0:T(8,128)}, u32[]{:S(2)}) copy-start(f32[4,8,16,128]{3,2,1,0:T(8,128)} %param.10) | copy-start | bytes 786436
  6.8 5.6 %copy-start.15 = (s32[512]{0:T(512)S(1)}, s32[512]{0:T(512)}, u32[]{:S(2)}) copy-start(s32[512]{0:T(512)} %param.18) | copy-start | bytes 6148
  6.8 5.6 %copy-start.17 = (s32[512]{0:T(512)S(1)}, s32[512]{0:T(512)}, u32[]{:S(2)}) copy-start(s32[512]{0:T(512)} %param.17) | copy-start | bytes 6148
  7.0 6.1 %collective-permute-start = (f32[8,8,8,128]{3,2,1,0:T(8,128)S(1)}, f32[8,8,8,128]{3,2,1,0:T(8,128)S(1)}, u32[]{:S(2)}, u32[]{:S(2)}) collective-permute-start(f32[8,8,8,128]{3,2,1,0:T(8,128)S(1)} %get-tuple-element.54), channel_id=1, source_target_pairs={{0,1},{1,2},{2,3},{4,5},{5,6},{6,7},{8,9},{9,10},{10,11},{12,13},{... | collective-permute-start | bytes 786440 | tf_op jit(solution)/shard_map/ppermute | solution.py:128
  9.3 5.5 %collective-permute-start.1 = (f32[8,8,8,128]{3,2,1,0:T(8,128)S(1)}, f32[8,8,8,128]{3,2,1,0:T(8,128)S(1)}, u32[]{:S(2)}, u32[]{:S(2)}) collective-permute-start(f32[8,8,8,128]{3,2,1,0:T(8,128)S(1)} %get-tuple-element.55), channel_id=1, source_target_pairs={{1,0},{2,1},{3,2},{5,4},{6,5},{7,6},{9,8},{10,9},{11,10},{13,12},{... | collective-permute-start | bytes 786440 | tf_op jit(solution)/shard_map/ppermute | solution.py:129
  15.1 3.5 %copy-start = (f32[9,8,32,128]{3,2,1,0:T(8,128)}, f32[9,8,32,128]{3,2,1,0:T(8,128)S(1)}, u32[]{:S(2)}) copy-start(f32[9,8,32,128]{3,2,1,0:T(8,128)S(1)} %maximum_maximum_fusion) | copy-start | bytes 3538948
  16.2 21.3 %collective-permute-start.2 = (f32[8,32,128]{1,2,0:T(8,128)S(1)}, f32[8,32,128]{1,2,0:T(8,128)S(1)}, u32[]{:S(2)}, u32[]{:S(2)}) collective-permute-start(f32[8,32,128]{1,2,0:T(8,128)S(1)} %copy.144), channel_id=1, source_target_pairs={{0,4},{4,8},{8,12},{12,16},{16,20},{20,24},{24,28},{28,0},{1,5},{5... | collective-permute-start | bytes 393224 | tf_op jit(solution)/shard_map/ppermute | solution.py:148
  19.0 25.9 %collective-permute-start.3 = (f32[8,32,128]{1,2,0:T(8,128)S(1)}, f32[8,32,128]{1,2,0:T(8,128)S(1)}, u32[]{:S(2)}, u32[]{:S(2)}) collective-permute-start(f32[8,32,128]{1,2,0:T(8,128)S(1)} %copy.147), channel_id=1, source_target_pairs={{4,0},{8,4},{12,8},{16,12},{20,16},{24,20},{28,24},{0,28},{5,1},{9... | collective-permute-start | bytes 393224 | tf_op jit(solution)/shard_map/ppermute | solution.py:149
  37.6 7.6 %copy-start.4 = (f32[1,8,32,14]{2,1,3,0:T(8,128)S(1)}, f32[1,8,32,14]{2,1,3,0:T(8,128)}, u32[]{:S(2)}) copy-start(f32[1,8,32,14]{2,1,3,0:T(8,128)} %copy.170) | copy-start | bytes 43012
  37.8 8.0 %copy-start.11 = (s32[512]{0:T(512)S(1)}, s32[512]{0:T(512)}, u32[]{:S(2)}) copy-start(s32[512]{0:T(512)} %add_select_fusion.1) | copy-start | bytes 6148
  37.8 8.1 %copy-start.16 = (s32[512]{0:T(512)S(1)}, s32[512]{0:T(512)}, u32[]{:S(2)}) copy-start(s32[512]{0:T(512)} %param.18) | copy-start | bytes 6148
  37.8 8.1 %copy-start.18 = (s32[512]{0:T(512)S(1)}, s32[512]{0:T(512)}, u32[]{:S(2)}) copy-start(s32[512]{0:T(512)} %param.17) | copy-start | bytes 6148
  37.9 8.1 %copy-start.21 = (f32[512]{0:T(512)S(1)}, f32[512]{0:T(512)}, u32[]{:S(2)}) copy-start(f32[512]{0:T(512)} %param.19) | copy-start | bytes 6148
  45.0 2.4 %copy-start.12 = (f32[8,16]{1,0:T(8,128)S(1)}, f32[8,16]{1,0:T(8,128)}, u32[]{:S(2)}) copy-start(f32[8,16]{1,0:T(8,128)} %get-tuple-element.6) | copy-start | bytes 1540
  45.1 3.3 %copy-start.22 = (f32[8]{0:T(128)S(1)}, f32[8]{0:T(128)}, u32[]{:S(2)}) copy-start(f32[8]{0:T(128)} %pad.42.clone) | copy-start | bytes 100
  45.1 3.3 %copy-start.23 = (f32[8]{0:T(128)S(1)}, f32[8]{0:T(128)}, u32[]{:S(2)}) copy-start(f32[8]{0:T(128)} %pad.41.clone) | copy-start | bytes 100
  45.1 3.3 %slice-start = ((f32[9,8,32,128]{3,2,1,0:T(8,128)}), f32[8,8,32,128]{3,2,1,0:T(8,128)S(1)}, s32[]{:S(2)}) async-start(f32[9,8,32,128]{3,2,1,0:T(8,128)} %copy-done), calls=%async_computation | async-start | bytes 2097152 | tf_op jit(solution)/shard_map/slice | solution.py:155
  48.3 3.6 %collective-permute-start.4 = (f32[129]{0:T(256)S(1)}, f32[129]{0:T(256)S(1)}, u32[]{:S(2)}, u32[]{:S(2)}) collective-permute-start(f32[129]{0:T(256)S(1)} %pad_maximum_fusion.1), channel_id=1, source_target_pairs={{0,4},{4,0},{8,12},{12,8},{16,20},{20,16},{24,28},{28,24},{1,5},{5... | collective-permute-start | bytes 1556 | tf_op jit(solution)/shard_map/ppermute | solution.py:67
  49.6 17.5 %copy-start.26 = (pred[128]{0:T(512)(128)(4,1)S(1)}, pred[128]{0:T(512)(128)(4,1)}, u32[]{:S(2)}) copy-start(pred[128]{0:T(512)(128)(4,1)} %get-tuple-element.115) | copy-start | bytes 388
  52.5 3.6 %collective-permute-start.5 = (f32[129]{0:T(256)S(1)}, f32[129]{0:T(256)S(1)}, u32[]{:S(2)}, u32[]{:S(2)}) collective-permute-start(f32[129]{0:T(256)S(1)} %fusion.134), channel_id=1, source_target_pairs={{0,8},{4,12},{8,0},{12,4},{16,24},{20,28},{24,16},{28,20},{1,9},{5... | collective-permute-start | bytes 1556 | tf_op jit(solution)/shard_map/ppermute | solution.py:67
  56.1 4.5 %collective-permute-start.6 = (f32[129]{0:T(256)S(1)}, f32[129]{0:T(256)S(1)}, u32[]{:S(2)}, u32[]{:S(2)}) collective-permute-start(f32[129]{0:T(256)S(1)} %add.238), channel_id=1, source_target_pairs={{0,16},{4,20},{8,24},{12,28},{16,0},{20,4},{24,8},{28,12},{1,17},{... | collective-permute-start | bytes 1556 | tf_op jit(solution)/shard_map/ppermute | solution.py:67
  60.6 1.1 %collective-permute-start.7 = (f32[129]{0:T(256)S(1)}, f32[129]{0:T(256)S(1)}, u32[]{:S(2)}, u32[]{:S(2)}) collective-permute-start(f32[129]{0:T(256)S(1)} %add.239), channel_id=1, source_target_pairs={{0,1},{1,0},{2,3},{3,2},{4,5},{5,4},{6,7},{7,6},{8,9},{9,8},{10,11... | collective-permute-start | bytes 1556 | tf_op jit(solution)/shard_map/ppermute | solution.py:67
  61.7 3.6 %collective-permute-start.8 = (f32[129]{0:T(256)S(1)}, f32[129]{0:T(256)S(1)}, u32[]{:S(2)}, u32[]{:S(2)}) collective-permute-start(f32[129]{0:T(256)S(1)} %add.240), channel_id=1, source_target_pairs={{0,2},{1,3},{2,0},{3,1},{4,6},{5,7},{6,4},{7,5},{8,10},{9,11},{10,... | collective-permute-start | bytes 1556 | tf_op jit(solution)/shard_map/ppermute | solution.py:67
  (13 other events, 13.8 us)

commit v12 on v8

--- a/solution.py
+++ b/solution.py
@@ -156,8 +156,10 @@
     sent_down = jnp.concatenate(
         [jnp.stack([widened[f, 0] for f in (0, 1, 2, 3, 5, 7)] + [widened[7, 1]]), as_slots(group[:, :reach])]
     )
-    from_below = lax.ppermute(sent_up, "az", up)
-    from_above = lax.ppermute(sent_down, "az", down)
+    sent_up = jnp.concatenate([sent_up, jnp.zeros_like(sent_up[:2])])
+    sent_down = jnp.concatenate([sent_down, jnp.zeros_like(sent_down[:2])])
+    from_below = lax.ppermute(sent_up, "az", up)[:8]
+    from_above = lax.ppermute(sent_down, "az", down)[:8]
     blank = jnp.zeros_like(from_below[0])
     row_before = jnp.stack([from_below[i] for i in (0, 1, 2, 3)] + [blank] + [from_below[i] for i in (4, 5, 6)])
     row_after = jnp.stack([from_above[i] for i in (0, 1, 2, 3)] + [blank, from_above[4], blank, from_above[5]])

time: 50.7 us -> 53.6 us (1.057)
  waiting for transfers between devices: 20.5 us -> 22.8 us
  local copies, waits for them, and re-layouts: 3.95 us -> 5.05 us
    ppermute x2, waiting for transfers between devices: 3.12 us -> 5.11 us  [shards(): other = lax.ppermute(group, 'ax', [(i, i ^ step) for i in range(size_ax)])]
    slice x1, local copies, waits for them, and re-layouts: 0.14 us -> 1.15 us  [shards(): acoustic[3, :, :, below]]
    another operation x1, other arithmetic: 0.99 us -> 0.04 us  [shards(): jnp.stack([a0, adjoint_in[1], adjoint_in[2], adjoint_in[3], axial_flow, s...]
    slice x1, local copies, waits for them, and re-layouts: 0.92 us -> 0.01 us  [shards(): axial_flow, swirl_flow = (mean_flow[0], mean_flow[1])]
    slice x1, local copies, waits for them, and re-layouts: 0.08 us -> 0.96 us  [shards(): adjoint_in[3, :, :, top] + push[:, :, top]]
    mul x1, other arithmetic: 0.02 us -> 0.89 us  [shards(): stiffness = mean_flow[2] * mean_flow[3] * mean_flow[3]]
    unnamed x45 -> x44, local copies, waits for them, and re-layouts: 1.32 us -> 1.31 us
  transfers between devices with their start and end apart: 9 -> 9, of which waited for: 7 -> 6; matrix products, arithmetic and copies ran while one was open for 9% -> 4% of each run, Pallas kernels for 0% -> 0%
where the time goes in v12:
time: 53.6 us; the launch traced here: 53.3 us
  waiting for transfers between devices  22.8 us (43%)
  starting transfers between devices  13.3 us (25%)
  other arithmetic  8.18 us (15%)
  local copies, waits for them, and re-layouts  5.05 us (9%)
  between operations  3.18 us (6%)
  matrix products  0.8 us (1%)
    ppermute x3, waiting for transfers between devices, butterfly_sum(): lax.ppermute(values, axis, [(i, i ^ step) for i in range(size)])  9.79 us
    ppermute x2, starting transfers between devices, shards(): other = lax.ppermute(group, 'ax', [(i, i ^ step) for i in range(size_ax)])  5.39 us
    ppermute x2, waiting for transfers between devices, shards(): other = lax.ppermute(group, 'ax', [(i, i ^ step) for i in range(size_ax)])  5.11 us
    ppermute x1, waiting for transfers between devices, shards(): from_below = lax.ppermute(sent_up, 'az', up)[:8]  5.09 us
    ppermute x1, starting transfers between devices, shards(): from_above = lax.ppermute(sent_down, 'az', down)[:8]  4.61 us
    ppermute x1, waiting for transfers between devices, shards(): from_above = lax.ppermute(sent_down, 'az', down)[:8]  2.82 us
    ppermute x1, starting transfers between devices, with_halo(): lax.ppermute(lax.slice_in_dim(array, length - before, length, axis=dim),...  1.98 us
    unnamed x44, local copies, waits for them, and re-layouts  1.31 us
  transfers between devices with their start and end apart: 9, of which 6 were waited for; matrix products, arithmetic and copies ran while one was open for 4% of the time, Pallas kernels for 0%

profile of v12, /device:TPU:0, one launch (start us, length us, event | category | flops | bytes accessed | tf_op | source)
XLA Modules:
  0.0 53.3 jit_solution(4425254642762506796)
XLA Ops:
  0.6 0.9 %multiply_multiply_fusion = (f32[8,16,128]{2,1,0:T(8,128)S(1)}, f32[8,16,128]{2,1,0:T(8,128)S(1)}) fusion(f32[4,8,16,128]{3,2,1,0:T(8,128)} %param.11), kind=kLoop, calls=%fused_computation.30 | loop fusion | flops 49152 | bytes 262144 | tf_op jit(solution)/shard_map/mul | solution.py:88
  1.5 1.0 %slice_bitcast_fusion.8 = (f32[8,16,128]{2,1,0:T(8,128)S(1)}, f32[1,8,16,128]{3,2,1,0:T(8,128)S(1)}, f32[1,8,16,128]{3,2,1,0:T(8,128)S(1)}, f32[1,8,16,128]{3,2,1,0:T(8,128)S(1)}, f32[1,8,16,128]{3,2,1,0:T(8,128)S(1)}) fusion(f32[4,8,16,128]{3,2,1,0:T(8,128)} %param.12, f32[4,8,16,128]{3,2,1,0:T(8,128)} %param.11), kind=kLoop, calls=%fused_computation.172 | loop fusion | flops 81920 | bytes 655360 | tf_op jit(solution)/shard_map/squeeze | solution.py:97
  2.6 1.0 %slice.760 = f32[1,8,16,1]{3,2,1,0:T(8,128)S(1)} slice(f32[4,8,16,128]{3,2,1,0:T(8,128)} %param.12), slice={[3:4], [0:8], [0:16], [127:128]} | slice | bytes 1024 | tf_op jit(solution)/shard_map/slice | solution.py:117
  3.6 1.2 %fusion.165 = (f32[1,8,16,1]{3,2,1,0:T(8,128)S(1)}, f32[1,8,16,1]{3,2,1,0:T(8,128)S(1)}, f32[1,8,16,1]{3,2,1,0:T(8,128)S(1)}, f32[1,8,16,1]{3,2,1,0:T(8,128)S(1)}, f32[1,8,16,1]{3,2,1,0:T(8,128)S(1)}) fusion(f32[4,8,16,128]{3,2,1,0:T(8,128)} %param.10), kind=kLoop, calls=%fused_computation.365 | loop fusion | bytes 5120 | tf_op jit(solution)/shard_map/slice | solution.py:107
  6.9 0.5 collective-permute-start.2
  7.5 2.0 %collective-permute-start = (f32[8,8,8,128]{3,2,1,0:T(8,128)S(1)}, f32[8,8,8,128]{3,2,1,0:T(8,128)S(1)}, u32[]{:S(2)}, u32[]{:S(2)}) collective-permute-start(f32[8,8,8,128]{3,2,1,0:T(8,128)S(1)} %get-tuple-element.37), channel_id=1, source_target_pairs={{0,1},{1,2},{2,3},{4,5},{5,6},{6,7},{8,9},{9,10},{10,11},{12,13},{... | collective-permute-start | bytes 786440 | tf_op jit(solution)/shard_map/ppermute | solution.py:17
  9.5 1.3 %collective-permute-start.1 = (f32[8,8,8,128]{3,2,1,0:T(8,128)S(1)}, f32[8,8,8,128]{3,2,1,0:T(8,128)S(1)}, u32[]{:S(2)}, u32[]{:S(2)}) collective-permute-start(f32[8,8,8,128]{3,2,1,0:T(8,128)S(1)} %get-tuple-element.38), channel_id=1, source_target_pairs={{1,0},{2,1},{3,2},{5,4},{6,5},{7,6},{9,8},{10,9},{11,10},{13,12},{... | collective-permute-start | bytes 786440 | tf_op jit(solution)/shard_map/ppermute | solution.py:20
  11.0 4.9 %collective-permute-start.3 = (f32[16,8,32]{2,1,0:T(8,128)S(1)}, f32[16,8,32]{2,1,0:T(8,128)S(1)}, u32[]{:S(2)}, u32[]{:S(2)}) collective-permute-start(f32[16,8,32]{2,1,0:T(8,128)S(1)} %maximum_select_fusion), channel_id=1, source_target_pairs={{0,2},{1,3},{2,0},{3,1},{4,6},{5,7},{6,4},{7,5},{8,10},{9,11},{10,... | collective-permute-start | bytes 49160 | tf_op jit(solution)/shard_map/ppermute | solution.py:128
  16.0 5.1 %collective-permute-done.3 = f32[16,8,32]{2,1,0:T(8,128)S(1)} collective-permute-done((f32[16,8,32]{2,1,0:T(8,128)S(1)}, f32[16,8,32]{2,1,0:T(8,128)S(1)}, u32[]{:S(2)}, u32[]{:S(2)}) %collective-permute-start.3) | collective-permute-done | bytes 16416 | tf_op jit(solution)/shard_map/ppermute | solution.py:128
  21.5 4.6 %collective-permute-start.5 = (f32[10,32,128]{2,1,0:T(8,128)S(1)}, f32[10,32,128]{2,1,0:T(8,128)S(1)}, u32[]{:S(2)}, u32[]{:S(2)}) collective-permute-start(f32[10,32,128]{2,1,0:T(8,128)S(1)} %constant_dynamic-update-slice_fusion.25), channel_id=1, source_target_pairs={{4,0},{8,4},{12,8},{16,12},{20,16},{24,20},{28,24},{0,28},{5,1},{9... | collective-permute-start | bytes 491528 | tf_op jit(solution)/shard_map/ppermute | solution.py:162
  26.1 2.8 %collective-permute-done.5 = f32[10,32,128]{2,1,0:T(8,128)S(1)} collective-permute-done((f32[10,32,128]{2,1,0:T(8,128)S(1)}, f32[10,32,128]{2,1,0:T(8,128)S(1)}, u32[]{:S(2)}, u32[]{:S(2)}) %collective-permute-start.5) | collective-permute-done | bytes 163872 | tf_op jit(solution)/shard_map/ppermute | solution.py:162
  29.0 5.1 %collective-permute-done.4 = f32[10,32,128]{2,1,0:T(8,128)S(1)} collective-permute-done((f32[10,32,128]{2,1,0:T(8,128)S(1)}, f32[10,32,128]{2,1,0:T(8,128)S(1)}, u32[]{:S(2)}, u32[]{:S(2)}) %collective-permute-start.4) | collective-permute-done | bytes 163872 | tf_op jit(solution)/shard_map/ppermute | solution.py:161
  34.6 0.5 fusion
  35.0 0.6 %select_reduce_fusion.4 = (f32[]{:T(128)}, f32[512]{0:T(512)S(1)}) fusion(s32[512]{0:T(512)S(1)} %get-tuple-element.103, f32[512]{0:T(512)S(1)} %fusion, f32[512]{0:T(512)S(1)} %copy-done.6), kind=kLoop, calls=%fused_computation.354 | loop fusion | flops 3583 | bytes 8196 | tf_op jit(solution)/shard_map/reduce_sum | solution.py:213
  35.6 0.3 fusion.2
  36.1 0.3 select_reduce_fusion.1
  36.4 0.7 %pad_maximum_fusion.7 = f32[129]{0:T(256)S(1)} fusion(f32[64]{0:T(128)S(1)} %get-tuple-element.8, f32[64]{0:T(128)S(1)} %get-tuple-element.7, f32[1]{0:T(128)} %bitcast.82), kind=kLoop, calls=%fused_computation.355 | loop fusion | flops 258 | bytes 1032 | tf_op jit(solution)/shard_map/concatenate | solution.py:311
  38.9 1.8 %collective-permute-done.6 = f32[129]{0:T(256)S(1)} collective-permute-done((f32[129]{0:T(256)S(1)}, f32[129]{0:T(256)S(1)}, u32[]{:S(2)}, u32[]{:S(2)}) %collective-permute-start.6) | collective-permute-done | bytes 548 | tf_op jit(solution)/shard_map/ppermute | solution.py:68
  40.7 0.7 %fusion.168 = f32[129]{0:T(256)S(1)} fusion(f32[129]{0:T(256)S(1)} %collective-permute-done.6, f32[64]{0:T(128)S(1)} %get-tuple-element.8, f32[64]{0:T(128)S(1)} %get-tuple-element.7, f32[1]{0:T(128)} %bitcast.82), kind=kLoop, calls=%fused_computation.368 | loop fusion | flops 387 | bytes 1548 | tf_op jit(solution)/shard_map/add | solution.py:68
  41.4 3.5 %collective-permute-done.7 = f32[129]{0:T(256)S(1)} collective-permute-done((f32[129]{0:T(256)S(1)}, f32[129]{0:T(256)S(1)}, u32[]{:S(2)}, u32[]{:S(2)}) %collective-permute-start.7) | collective-permute-done | bytes 548 | tf_op jit(solution)/shard_map/ppermute | solution.py:68
  45.0 4.5 %collective-permute-done.8 = f32[129]{0:T(256)S(1)} collective-permute-done((f32[129]{0:T(256)S(1)}, f32[129]{0:T(256)S(1)}, u32[]{:S(2)}, u32[]{:S(2)}) %collective-permute-start.8) | collective-permute-done | bytes 548 | tf_op jit(solution)/shard_map/ppermute | solution.py:68
  49.4 0.5 slice.937
  50.6 0.6 %fusion.159 = f32[64]{0:T(128)} fusion(f32[129]{0:T(256)S(1)} %add.254, f32[]{:T(128)} %bitcast.86), kind=kLoop, calls=%fused_computation.360 | loop fusion | flops 192 | bytes 772 | tf_op jit(solution)/shard_map/mul | solution.py:314
  51.3 0.9 %maximum_add_fusion = f32[4,8,16,128]{3,2,1,0:T(8,128)} fusion(f32[1,8,16,128]{3,2,1,0:T(8,128)S(1)} %fusion.20, f32[1,8,16,128]{3,2,1,0:T(8,128)S(1)} %fusion.37, f32[1,8,16,128]{3,2,1,0:T(8,128)S(1)} %fusion.46, f32[1,8,16,128]{3,2,1,0:T(8,128)S(1)} %fusion.58, f32[4,8,16]{2,1,0:T(8,128)S(1)} %get-tuple-element.85, f32[4,8,16]{2,1,0:T(8,128)S(1)} %get-tuple-element.84, ...), kind=kLoop, calls=%fused_computation.4 | loop fusion | flops 393216 | bytes 528640 | tf_op jit(solution)/shard_map/add | solution.py:323
  (120 shorter events, 4.9 us)
Async XLA Ops:
  2.5 3.9 %copy-start.2 = (s32[8,16]{1,0:T(8,128)S(1)}, s32[8,16]{1,0:T(8,128)}, u32[]{:S(2)}) copy-start(s32[8,16]{1,0:T(8,128)} %param.14) | copy-start | bytes 1540
  2.5 3.9 %copy-start.7 = (f32[64]{0:T(128)S(1)}, f32[64]{0:T(128)}, u32[]{:S(2)}) copy-start(f32[64]{0:T(128)} %param.13) | copy-start | bytes 772
  2.5 4.1 %copy-start.3 = (s32[8,16]{1,0:T(8,128)S(1)}, s32[8,16]{1,0:T(8,128)}, u32[]{:S(2)}) copy-start(s32[8,16]{1,0:T(8,128)} %param.15) | copy-start | bytes 1540
  2.6 4.1 %copy-start.8 = (f32[64]{0:T(128)S(1)}, f32[64]{0:T(128)}, u32[]{:S(2)}) copy-start(f32[64]{0:T(128)} %param.16) | copy-start | bytes 772
  2.6 4.8 %copy-start.1 = (f32[4,8,16,128]{3,2,1,0:T(8,128)S(1)}, f32[4,8,16,128]{3,2,1,0:T(8,128)}, u32[]{:S(2)}) copy-start(f32[4,8,16,128]{3,2,1,0:T(8,128)} %param.11) | copy-start | bytes 786436
  3.5 3.9 %copy-start = (f32[4,8,16,128]{3,2,1,0:T(8,128)S(1)}, f32[4,8,16,128]{3,2,1,0:T(8,128)}, u32[]{:S(2)}) copy-start(f32[4,8,16,128]{3,2,1,0:T(8,128)} %param.12) | copy-start | bytes 786436
  5.9 4.9 %copy-start.4 = (s32[512]{0:T(512)S(1)}, s32[512]{0:T(512)}, u32[]{:S(2)}) copy-start(s32[512]{0:T(512)} %param.17) | copy-start | bytes 6148
  5.9 4.9 %copy-start.5 = (s32[512]{0:T(512)S(1)}, s32[512]{0:T(512)}, u32[]{:S(2)}) copy-start(s32[512]{0:T(512)} %param.18) | copy-start | bytes 6148
  6.9 4.0 %collective-permute-start.2 = (f32[16,8,16]{2,1,0:T(8,128)S(1)}, f32[16,8,16]{2,1,0:T(8,128)S(1)}, u32[]{:S(2)}, u32[]{:S(2)}) collective-permute-start(f32[16,8,16]{2,1,0:T(8,128)S(1)} %constant_dynamic-update-slice_fusion), channel_id=1, source_target_pairs={{0,1},{1,0},{2,3},{3,2},{4,5},{5,4},{6,7},{7,6},{8,9},{9,8},{10,11... | collective-permute-start | bytes 24584 | tf_op jit(solution)/shard_map/ppermute | solution.py:128
  7.5 13.8 %collective-permute-start = (f32[8,8,8,128]{3,2,1,0:T(8,128)S(1)}, f32[8,8,8,128]{3,2,1,0:T(8,128)S(1)}, u32[]{:S(2)}, u32[]{:S(2)}) collective-permute-start(f32[8,8,8,128]{3,2,1,0:T(8,128)S(1)} %get-tuple-element.37), channel_id=1, source_target_pairs={{0,1},{1,2},{2,3},{4,5},{5,6},{6,7},{8,9},{9,10},{10,11},{12,13},{... | collective-permute-start | bytes 786440 | tf_op jit(solution)/shard_map/ppermute | solution.py:17
  9.5 11.8 %collective-permute-start.1 = (f32[8,8,8,128]{3,2,1,0:T(8,128)S(1)}, f32[8,8,8,128]{3,2,1,0:T(8,128)S(1)}, u32[]{:S(2)}, u32[]{:S(2)}) collective-permute-start(f32[8,8,8,128]{3,2,1,0:T(8,128)S(1)} %get-tuple-element.38), channel_id=1, source_target_pairs={{1,0},{2,1},{3,2},{5,4},{6,5},{7,6},{9,8},{10,9},{11,10},{13,12},{... | collective-permute-start | bytes 786440 | tf_op jit(solution)/shard_map/ppermute | solution.py:20
  11.0 10.1 %collective-permute-start.3 = (f32[16,8,32]{2,1,0:T(8,128)S(1)}, f32[16,8,32]{2,1,0:T(8,128)S(1)}, u32[]{:S(2)}, u32[]{:S(2)}) collective-permute-start(f32[16,8,32]{2,1,0:T(8,128)S(1)} %maximum_select_fusion), channel_id=1, source_target_pairs={{0,2},{1,3},{2,0},{3,1},{4,6},{5,7},{6,4},{7,5},{8,10},{9,11},{10,... | collective-permute-start | bytes 49160 | tf_op jit(solution)/shard_map/ppermute | solution.py:128
  21.5 13.6 %copy-start.6 = (f32[512]{0:T(512)S(1)}, f32[512]{0:T(512)}, u32[]{:S(2)}) copy-start(f32[512]{0:T(512)} %param.19) | copy-start | bytes 6148
  21.5 7.4 %collective-permute-start.5 = (f32[10,32,128]{2,1,0:T(8,128)S(1)}, f32[10,32,128]{2,1,0:T(8,128)S(1)}, u32[]{:S(2)}, u32[]{:S(2)}) collective-permute-start(f32[10,32,128]{2,1,0:T(8,128)S(1)} %constant_dynamic-update-slice_fusion.25), channel_id=1, source_target_pairs={{4,0},{8,4},{12,8},{16,12},{20,16},{24,20},{28,24},{0,28},{5,1},{9... | collective-permute-start | bytes 491528 | tf_op jit(solution)/shard_map/ppermute | solution.py:162
  26.1 8.0 %collective-permute-start.4 = (f32[10,32,128]{2,1,0:T(8,128)S(1)}, f32[10,32,128]{2,1,0:T(8,128)S(1)}, u32[]{:S(2)}, u32[]{:S(2)}) collective-permute-start(f32[10,32,128]{2,1,0:T(8,128)S(1)} %constant_dynamic-update-slice_fusion.16), channel_id=1, source_target_pairs={{0,4},{4,8},{8,12},{12,16},{16,20},{20,24},{24,28},{28,0},{1,5},{5... | collective-permute-start | bytes 491528 | tf_op jit(solution)/shard_map/ppermute | solution.py:161
  37.1 3.6 %collective-permute-start.6 = (f32[129]{0:T(256)S(1)}, f32[129]{0:T(256)S(1)}, u32[]{:S(2)}, u32[]{:S(2)}) collective-permute-start(f32[129]{0:T(256)S(1)} %pad_maximum_fusion.7), channel_id=1, source_target_pairs={{0,4},{4,0},{8,12},{12,8},{16,20},{20,16},{24,28},{28,24},{1,5},{5... | collective-permute-start | bytes 1556 | tf_op jit(solution)/shard_map/ppermute | solution.py:68
  41.4 3.6 %collective-permute-start.7 = (f32[129]{0:T(256)S(1)}, f32[129]{0:T(256)S(1)}, u32[]{:S(2)}, u32[]{:S(2)}) collective-permute-start(f32[129]{0:T(256)S(1)} %fusion.168), channel_id=1, source_target_pairs={{0,8},{4,12},{8,0},{12,4},{16,24},{20,28},{24,16},{28,20},{1,9},{5... | collective-permute-start | bytes 1556 | tf_op jit(solution)/shard_map/ppermute | solution.py:68
  45.0 4.5 %collective-permute-start.8 = (f32[129]{0:T(256)S(1)}, f32[129]{0:T(256)S(1)}, u32[]{:S(2)}, u32[]{:S(2)}) collective-permute-start(f32[129]{0:T(256)S(1)} %add.253), channel_id=1, source_target_pairs={{0,16},{4,20},{8,24},{12,28},{16,0},{20,4},{24,8},{28,12},{1,17},{... | collective-permute-start | bytes 1556 | tf_op jit(solution)/shard_map/ppermute | solution.py:68

commit v13 on v7

--- a/solution.py
+++ b/solution.py
@@ -61,6 +61,12 @@
         size = lax.axis_size(axis)
         if size & (size - 1):
             values = lax.psum(values, axis)
+            continue
+        if axis == "ax" and size <= 4:
+            terms = [values] + [lax.ppermute(values, axis, [(i, i ^ k) for i in range(size)]) for k in range(1, size)]
+            while len(terms) > 1:
+                terms = [terms[j] + terms[j + 1] for j in range(0, len(terms), 2)]
+            values = terms[0]
             continue
         step = 1
         while step < size:

time: 50.8 us -> 51.2 us (level)
    ppermute x5 -> x3, starting transfers between devices: 8.71 us -> 3.6 us  [butterfly_sum(): lax.ppermute(values, axis, [(i, i ^ step) for i in range(size)])]
    ppermute x0 -> x3, starting transfers between devices: none -> 4.94 us  [butterfly_sum(): lax.ppermute(values, axis, [(i, i ^ k) for i in range(size)])]
    ppermute x0 -> x3, waiting for transfers between devices: none -> 2.84 us  [butterfly_sum(): lax.ppermute(values, axis, [(i, i ^ k) for i in range(size)])]
    ppermute x5 -> x3, waiting for transfers between devices: 9.11 us -> 6.75 us  [butterfly_sum(): lax.ppermute(values, axis, [(i, i ^ step) for i in range(size)])]
  transfers between devices with their start and end apart: 9 -> 10, of which waited for: 8 -> 8; matrix products, arithmetic and copies ran while one was open for 3% -> 3% of each run, Pallas kernels for 0% -> 0%
where the time goes in v13:
time: 51.2 us; the launch traced here: 50.8 us
  starting transfers between devices  17 us (33%)
  waiting for transfers between devices  16.3 us (32%)
  local copies, waits for them, and re-layouts  7.24 us (14%)
  other arithmetic  7.15 us (14%)
  between operations  3.1 us (6%)
    ppermute x3, waiting for transfers between devices, butterfly_sum(): lax.ppermute(values, axis, [(i, i ^ step) for i in range(size)])  6.75 us
    ppermute x3, starting transfers between devices, butterfly_sum(): lax.ppermute(values, axis, [(i, i ^ k) for i in range(size)])  4.94 us
    ppermute x1, waiting for transfers between devices, with_halo(): lax.ppermute(lax.slice_in_dim(array, 0, after, axis=dim), axis, down)  4.05 us
    ppermute x3, starting transfers between devices, butterfly_sum(): lax.ppermute(values, axis, [(i, i ^ step) for i in range(size)])  3.6 us
    unnamed x46, local copies, waits for them, and re-layouts  3.48 us
    ppermute x1, starting transfers between devices, shards(): from_above = lax.ppermute(sent_down, 'az', down)  3.2 us
    ppermute x3, waiting for transfers between devices, butterfly_sum(): lax.ppermute(values, axis, [(i, i ^ k) for i in range(size)])  2.84 us
    ppermute x1, starting transfers between devices, with_halo(): lax.ppermute(lax.slice_in_dim(array, length - before, length, axis=dim),...  2.37 us
  transfers between devices with their start and end apart: 10, of which 8 were waited for; matrix products, arithmetic and copies ran while one was open for 3% of the time, Pallas kernels for 0%

profile of v13, /device:TPU:0, one launch (start us, length us, event | category | flops | bytes accessed | tf_op | source)
XLA Modules:
  0.0 50.8 jit_solution(1948831082431254919)
XLA Ops:
  0.6 1.0 %constant_dynamic-update-slice_fusion.17 = f32[9,8,16,128]{3,2,1,0:T(8,128)S(1)} fusion(f32[4,8,16,128]{3,2,1,0:T(8,128)} %param.12), kind=kLoop, calls=%fused_computation.40 | loop fusion | bytes 524288
  1.7 0.9 %slice.877 = f32[1,8,16,1]{3,2,1,0:T(8,128)S(1)} slice(f32[4,8,16,128]{3,2,1,0:T(8,128)} %param.12), slice={[3:4], [0:8], [0:16], [127:128]} | slice | bytes 1024 | tf_op jit(solution)/shard_map/slice | solution.py:278
  2.6 1.1 %fusion.124 = (f32[1,8,16,1]{3,2,1,0:T(8,128)S(1)}, f32[1,8,16,1]{3,2,1,0:T(8,128)S(1)}, f32[1,8,16,1]{3,2,1,0:T(8,128)S(1)}, f32[1,8,16,1]{3,2,1,0:T(8,128)S(1)}, f32[1,8,16,1]{3,2,1,0:T(8,128)S(1)}) fusion(f32[4,8,16,128]{3,2,1,0:T(8,128)} %param.10), kind=kLoop, calls=%fused_computation.325 | loop fusion | bytes 5120 | tf_op jit(solution)/shard_map/slice | solution.py:111
  4.4 0.9 %slice_bitcast_fusion.8 = (f32[8,16,128]{2,1,0:T(8,128)S(1)}, f32[9,8,16,128]{3,2,1,0:T(8,128)S(1)}, f32[1,8,16,128]{3,2,1,0:T(8,128)S(1)}, f32[1,8,16,128]{3,2,1,0:T(8,128)S(1)}) fusion(f32[4,8,16,128]{3,2,1,0:T(8,128)} %param.12, f32[9,8,16,128]{3,2,1,0:T(8,128)S(1)} %constant_dynamic-update-slice_fusion.16, f32[4,8,16,128]{3,2,1,0:T(8,128)S(1)} %copy-done.1), kind=kLoop, calls=%fused_computation.166 | loop fusion | flops 65536 | bytes 589824 | tf_op jit(solution)/shard_map/squeeze | solution.py:102
  7.3 2.4 %collective-permute-start = (f32[9,8,8,128]{3,2,1,0:T(8,128)S(1)}, f32[9,8,8,128]{3,2,1,0:T(8,128)S(1)}, u32[]{:S(2)}, u32[]{:S(2)}) collective-permute-start(f32[9,8,8,128]{3,2,1,0:T(8,128)S(1)} %get-tuple-element.48), channel_id=1, source_target_pairs={{0,1},{1,2},{2,3},{4,5},{5,6},{6,7},{8,9},{9,10},{10,11},{12,13},{... | collective-permute-start | bytes 884744 | tf_op jit(solution)/shard_map/ppermute | solution.py:16
  9.7 1.3 %collective-permute-start.1 = (f32[9,8,8,128]{3,2,1,0:T(8,128)S(1)}, f32[9,8,8,128]{3,2,1,0:T(8,128)S(1)}, u32[]{:S(2)}, u32[]{:S(2)}) collective-permute-start(f32[9,8,8,128]{3,2,1,0:T(8,128)S(1)} %get-tuple-element.49), channel_id=1, source_target_pairs={{1,0},{2,1},{3,2},{5,4},{6,5},{7,6},{9,8},{10,9},{11,10},{13,12},{... | collective-permute-start | bytes 884744 | tf_op jit(solution)/shard_map/ppermute | solution.py:19
  11.2 4.0 %collective-permute-done.1 = f32[9,8,8,128]{3,2,1,0:T(8,128)S(1)} collective-permute-done((f32[9,8,8,128]{3,2,1,0:T(8,128)S(1)}, f32[9,8,8,128]{3,2,1,0:T(8,128)S(1)}, u32[]{:S(2)}, u32[]{:S(2)}) %collective-permute-start.1) | collective-permute-done | bytes 294944 | tf_op jit(solution)/shard_map/ppermute | solution.py:19
  15.4 1.6 %collective-permute-start.2 = (f32[10,32,128]{2,1,0:T(8,128)S(1)}, f32[10,32,128]{2,1,0:T(8,128)S(1)}, u32[]{:S(2)}, u32[]{:S(2)}) collective-permute-start(f32[10,32,128]{2,1,0:T(8,128)S(1)} %get-tuple-element.28), channel_id=1, source_target_pairs={{0,4},{4,8},{8,12},{12,16},{16,20},{20,24},{24,28},{28,0},{1,5},{5... | collective-permute-start | bytes 491528 | tf_op jit(solution)/shard_map/ppermute | solution.py:140
  16.9 3.2 %collective-permute-start.3 = (f32[10,32,128]{2,1,0:T(8,128)S(1)}, f32[10,32,128]{2,1,0:T(8,128)S(1)}, u32[]{:S(2)}, u32[]{:S(2)}) collective-permute-start(f32[10,32,128]{2,1,0:T(8,128)S(1)} %get-tuple-element.29), channel_id=1, source_target_pairs={{4,0},{8,4},{12,8},{16,12},{20,16},{24,20},{28,24},{0,28},{5,1},{9... | collective-permute-start | bytes 491528 | tf_op jit(solution)/shard_map/ppermute | solution.py:141
  20.3 1.0 %copy-done = f32[9,8,32,128]{3,2,1,0:T(8,128)} copy-done((f32[9,8,32,128]{3,2,1,0:T(8,128)}, f32[9,8,32,128]{3,2,1,0:T(8,128)S(1)}, u32[]{:S(2)}) %copy-start) | copy-done | bytes 1179672
  21.3 2.2 %collective-permute-done.2 = f32[10,32,128]{2,1,0:T(8,128)S(1)} collective-permute-done((f32[10,32,128]{2,1,0:T(8,128)S(1)}, f32[10,32,128]{2,1,0:T(8,128)S(1)}, u32[]{:S(2)}, u32[]{:S(2)}) %collective-permute-start.2) | collective-permute-done | bytes 163872 | tf_op jit(solution)/shard_map/ppermute | solution.py:140
  24.8 0.6 %select_reduce_fusion.6 = (f32[]{:T(128)}, f32[512]{0:T(512)S(1)}) fusion(s32[512]{0:T(512)S(1)} %copy-done.3, s32[]{:T(128)S(6)} %mul.402, s32[512]{0:T(512)S(1)} %copy-done.4, s32[]{:T(128)S(6)} %mul.401, f32[512]{0:T(512)S(1)} %select_reduce_fusion.1, f32[512]{0:T(512)S(1)} %copy-done.6), kind=kLoop, calls=%fused_computation.315 | loop fusion | flops 13311 | bytes 10252 | tf_op jit(solution)/shard_map/reduce_sum | solution.py:195
  26.1 0.7 %pad_maximum_fusion.4 = f32[129]{0:T(256)S(1)} fusion(f32[64]{0:T(128)S(1)} %get-tuple-element.11, f32[64]{0:T(128)S(1)} %get-tuple-element.10, f32[1]{0:T(128)} %bitcast.80), kind=kLoop, calls=%fused_computation.318 | loop fusion | flops 258 | bytes 1032 | tf_op jit(solution)/shard_map/concatenate | solution.py:283
  26.8 0.7 %collective-permute-start.4 = (f32[129]{0:T(256)S(1)}, f32[129]{0:T(256)S(1)}, u32[]{:S(2)}, u32[]{:S(2)}) collective-permute-start(f32[129]{0:T(256)S(1)} %pad_maximum_fusion.4), channel_id=1, source_target_pairs={{0,4},{4,0},{8,12},{12,8},{16,20},{20,16},{24,28},{28,24},{1,5},{5... | collective-permute-start | bytes 1556 | tf_op jit(solution)/shard_map/ppermute | solution.py:73
  28.7 1.6 %collective-permute-done.4 = f32[129]{0:T(256)S(1)} collective-permute-done((f32[129]{0:T(256)S(1)}, f32[129]{0:T(256)S(1)}, u32[]{:S(2)}, u32[]{:S(2)}) %collective-permute-start.4) | collective-permute-done | bytes 548 | tf_op jit(solution)/shard_map/ppermute | solution.py:73
  30.4 0.7 %fusion.127 = f32[129]{0:T(256)S(1)} fusion(f32[129]{0:T(256)S(1)} %collective-permute-done.4, f32[64]{0:T(128)S(1)} %get-tuple-element.11, f32[64]{0:T(128)S(1)} %get-tuple-element.10, f32[1]{0:T(128)} %bitcast.80), kind=kLoop, calls=%fused_computation.328 | loop fusion | flops 387 | bytes 1548 | tf_op jit(solution)/shard_map/add | solution.py:73
  31.1 1.0 %collective-permute-start.5 = (f32[129]{0:T(256)S(1)}, f32[129]{0:T(256)S(1)}, u32[]{:S(2)}, u32[]{:S(2)}) collective-permute-start(f32[129]{0:T(256)S(1)} %fusion.127), channel_id=1, source_target_pairs={{0,8},{4,12},{8,0},{12,4},{16,24},{20,28},{24,16},{28,20},{1,9},{5... | collective-permute-start | bytes 1556 | tf_op jit(solution)/shard_map/ppermute | solution.py:73
  32.1 2.6 %collective-permute-done.5 = f32[129]{0:T(256)S(1)} collective-permute-done((f32[129]{0:T(256)S(1)}, f32[129]{0:T(256)S(1)}, u32[]{:S(2)}, u32[]{:S(2)}) %collective-permute-start.5) | collective-permute-done | bytes 548 | tf_op jit(solution)/shard_map/ppermute | solution.py:73
  34.7 2.0 %collective-permute-start.6 = (f32[129]{0:T(256)S(1)}, f32[129]{0:T(256)S(1)}, u32[]{:S(2)}, u32[]{:S(2)}) collective-permute-start(f32[129]{0:T(256)S(1)} %add.237), channel_id=1, source_target_pairs={{0,16},{4,20},{8,24},{12,28},{16,0},{20,4},{24,8},{28,12},{1,17},{... | collective-permute-start | bytes 1556 | tf_op jit(solution)/shard_map/ppermute | solution.py:73
  36.6 2.5 %collective-permute-done.6 = f32[129]{0:T(256)S(1)} collective-permute-done((f32[129]{0:T(256)S(1)}, f32[129]{0:T(256)S(1)}, u32[]{:S(2)}, u32[]{:S(2)}) %collective-permute-start.6) | collective-permute-done | bytes 548 | tf_op jit(solution)/shard_map/ppermute | solution.py:73
  39.6 4.3 %collective-permute-start.8 = (f32[129]{0:T(256)S(1)}, f32[129]{0:T(256)S(1)}, u32[]{:S(2)}, u32[]{:S(2)}) collective-permute-start(f32[129]{0:T(256)S(1)} %add.238), channel_id=1, source_target_pairs={{0,2},{1,3},{2,0},{3,1},{4,6},{5,7},{6,4},{7,5},{8,10},{9,11},{10,... | collective-permute-start | bytes 1556 | tf_op jit(solution)/shard_map/ppermute | solution.py:66
  44.1 1.4 %collective-permute-done.8 = f32[129]{0:T(256)S(1)} collective-permute-done((f32[129]{0:T(256)S(1)}, f32[129]{0:T(256)S(1)}, u32[]{:S(2)}, u32[]{:S(2)}) %collective-permute-start.8) | collective-permute-done | bytes 548 | tf_op jit(solution)/shard_map/ppermute | solution.py:66
  45.5 1.4 %collective-permute-done.9 = f32[129]{0:T(256)S(1)} collective-permute-done((f32[129]{0:T(256)S(1)}, f32[129]{0:T(256)S(1)}, u32[]{:S(2)}, u32[]{:S(2)}) %collective-permute-start.9) | collective-permute-done | bytes 548 | tf_op jit(solution)/shard_map/ppermute | solution.py:66
  48.8 0.9 %maximum_add_fusion = f32[4,8,16,128]{3,2,1,0:T(8,128)} fusion(f32[1,8,16,128]{3,2,1,0:T(8,128)S(1)} %fusion.12, f32[1,8,16,128]{3,2,1,0:T(8,128)S(1)} %fusion.29, f32[1,8,16,128]{3,2,1,0:T(8,128)S(1)} %fusion.38, f32[1,8,16,128]{3,2,1,0:T(8,128)S(1)} %fusion.50, f32[4,8,16]{2,1,0:T(8,128)S(1)} %get-tuple-element.85, f32[4,8,16]{2,1,0:T(8,128)S(1)} %get-tuple-element.84, ...), kind=kLoop, calls=%fused_computation.6 | loop fusion | flops 393216 | bytes 528640 | tf_op jit(solution)/shard_map/add | solution.py:295
  (123 shorter events, 7.6 us)
Async XLA Ops:
  0.6 3.7 %copy-start.1 = (f32[4,8,16,128]{3,2,1,0:T(8,128)S(1)}, f32[4,8,16,128]{3,2,1,0:T(8,128)}, u32[]{:S(2)}) copy-start(f32[4,8,16,128]{3,2,1,0:T(8,128)} %param.11) | copy-start | bytes 786436
  4.3 2.2 %copy-start.2 = (s32[8,16]{1,0:T(8,128)S(1)}, s32[8,16]{1,0:T(8,128)}, u32[]{:S(2)}) copy-start(s32[8,16]{1,0:T(8,128)} %param.14) | copy-start | bytes 1540
  4.4 2.2 %copy-start.7 = (f32[64]{0:T(128)S(1)}, f32[64]{0:T(128)}, u32[]{:S(2)}) copy-start(f32[64]{0:T(128)} %param.13) | copy-start | bytes 772
  4.4 2.4 %copy-start.5 = (s32[8,16]{1,0:T(8,128)S(1)}, s32[8,16]{1,0:T(8,128)}, u32[]{:S(2)}) copy-start(s32[8,16]{1,0:T(8,128)} %param.15) | copy-start | bytes 1540
  4.4 2.4 %copy-start.8 = (f32[64]{0:T(128)S(1)}, f32[64]{0:T(128)}, u32[]{:S(2)}) copy-start(f32[64]{0:T(128)} %param.16) | copy-start | bytes 772
  6.2 4.9 %copy-start.3 = (s32[512]{0:T(512)S(1)}, s32[512]{0:T(512)}, u32[]{:S(2)}) copy-start(s32[512]{0:T(512)} %param.18) | copy-start | bytes 6148
  6.3 4.9 %copy-start.4 = (s32[512]{0:T(512)S(1)}, s32[512]{0:T(512)}, u32[]{:S(2)}) copy-start(s32[512]{0:T(512)} %param.17) | copy-start | bytes 6148
  7.3 3.9 %collective-permute-start = (f32[9,8,8,128]{3,2,1,0:T(8,128)S(1)}, f32[9,8,8,128]{3,2,1,0:T(8,128)S(1)}, u32[]{:S(2)}, u32[]{:S(2)}) collective-permute-start(f32[9,8,8,128]{3,2,1,0:T(8,128)S(1)} %get-tuple-element.48), channel_id=1, source_target_pairs={{0,1},{1,2},{2,3},{4,5},{5,6},{6,7},{8,9},{9,10},{10,11},{12,13},{... | collective-permute-start | bytes 884744 | tf_op jit(solution)/shard_map/ppermute | solution.py:16
  9.7 5.6 %collective-permute-start.1 = (f32[9,8,8,128]{3,2,1,0:T(8,128)S(1)}, f32[9,8,8,128]{3,2,1,0:T(8,128)S(1)}, u32[]{:S(2)}, u32[]{:S(2)}) collective-permute-start(f32[9,8,8,128]{3,2,1,0:T(8,128)S(1)} %get-tuple-element.49), channel_id=1, source_target_pairs={{1,0},{2,1},{3,2},{5,4},{6,5},{7,6},{9,8},{10,9},{11,10},{13,12},{... | collective-permute-start | bytes 884744 | tf_op jit(solution)/shard_map/ppermute | solution.py:19
  15.4 8.2 %collective-permute-start.2 = (f32[10,32,128]{2,1,0:T(8,128)S(1)}, f32[10,32,128]{2,1,0:T(8,128)S(1)}, u32[]{:S(2)}, u32[]{:S(2)}) collective-permute-start(f32[10,32,128]{2,1,0:T(8,128)S(1)} %get-tuple-element.28), channel_id=1, source_target_pairs={{0,4},{4,8},{8,12},{12,16},{16,20},{20,24},{24,28},{28,0},{1,5},{5... | collective-permute-start | bytes 491528 | tf_op jit(solution)/shard_map/ppermute | solution.py:140
  16.9 7.1 %collective-permute-start.3 = (f32[10,32,128]{2,1,0:T(8,128)S(1)}, f32[10,32,128]{2,1,0:T(8,128)S(1)}, u32[]{:S(2)}, u32[]{:S(2)}) collective-permute-start(f32[10,32,128]{2,1,0:T(8,128)S(1)} %get-tuple-element.29), channel_id=1, source_target_pairs={{4,0},{8,4},{12,8},{16,12},{20,16},{24,20},{28,24},{0,28},{5,1},{9... | collective-permute-start | bytes 491528 | tf_op jit(solution)/shard_map/ppermute | solution.py:141
  20.3 1.0 %copy-start = (f32[9,8,32,128]{3,2,1,0:T(8,128)}, f32[9,8,32,128]{3,2,1,0:T(8,128)S(1)}, u32[]{:S(2)}) copy-start(f32[9,8,32,128]{3,2,1,0:T(8,128)S(1)} %pad_maximum_fusion.1) | copy-start | bytes 3538948
  20.3 4.5 %copy-start.6 = (f32[512]{0:T(512)S(1)}, f32[512]{0:T(512)}, u32[]{:S(2)}) copy-start(f32[512]{0:T(512)} %param.19) | copy-start | bytes 6148
  23.5 4.1 %slice-start = ((f32[9,8,32,128]{3,2,1,0:T(8,128)}), f32[8,8,32,128]{3,2,1,0:T(8,128)S(1)}, s32[]{:S(2)}) async-start(f32[9,8,32,128]{3,2,1,0:T(8,128)} %copy-done), calls=%async_computation | async-start | bytes 2097152 | tf_op jit(solution)/shard_map/slice | solution.py:147
  26.8 3.6 %collective-permute-start.4 = (f32[129]{0:T(256)S(1)}, f32[129]{0:T(256)S(1)}, u32[]{:S(2)}, u32[]{:S(2)}) collective-permute-start(f32[129]{0:T(256)S(1)} %pad_maximum_fusion.4), channel_id=1, source_target_pairs={{0,4},{4,0},{8,12},{12,8},{16,20},{20,16},{24,28},{28,24},{1,5},{5... | collective-permute-start | bytes 1556 | tf_op jit(solution)/shard_map/ppermute | solution.py:73
  31.1 3.6 %collective-permute-start.5 = (f32[129]{0:T(256)S(1)}, f32[129]{0:T(256)S(1)}, u32[]{:S(2)}, u32[]{:S(2)}) collective-permute-start(f32[129]{0:T(256)S(1)} %fusion.127), channel_id=1, source_target_pairs={{0,8},{4,12},{8,0},{12,4},{16,24},{20,28},{24,16},{28,20},{1,9},{5... | collective-permute-start | bytes 1556 | tf_op jit(solution)/shard_map/ppermute | solution.py:73
  34.7 4.5 %collective-permute-start.6 = (f32[129]{0:T(256)S(1)}, f32[129]{0:T(256)S(1)}, u32[]{:S(2)}, u32[]{:S(2)}) collective-permute-start(f32[129]{0:T(256)S(1)} %add.237), channel_id=1, source_target_pairs={{0,16},{4,20},{8,24},{12,28},{16,0},{20,4},{24,8},{28,12},{1,17},{... | collective-permute-start | bytes 1556 | tf_op jit(solution)/shard_map/ppermute | solution.py:73
  39.1 4.9 %collective-permute-start.7 = (f32[129]{0:T(256)S(1)}, f32[129]{0:T(256)S(1)}, u32[]{:S(2)}, u32[]{:S(2)}) collective-permute-start(f32[129]{0:T(256)S(1)} %add.238), channel_id=1, source_target_pairs={{0,1},{1,0},{2,3},{3,2},{4,5},{5,4},{6,7},{7,6},{8,9},{9,8},{10,11... | collective-permute-start | bytes 1556 | tf_op jit(solution)/shard_map/ppermute | solution.py:66
  39.6 5.9 %collective-permute-start.8 = (f32[129]{0:T(256)S(1)}, f32[129]{0:T(256)S(1)}, u32[]{:S(2)}, u32[]{:S(2)}) collective-permute-start(f32[129]{0:T(256)S(1)} %add.238), channel_id=1, source_target_pairs={{0,2},{1,3},{2,0},{3,1},{4,6},{5,7},{6,4},{7,5},{8,10},{9,11},{10,... | collective-permute-start | bytes 1556 | tf_op jit(solution)/shard_map/ppermute | solution.py:66
  43.9 3.0 %collective-permute-start.9 = (f32[129]{0:T(256)S(1)}, f32[129]{0:T(256)S(1)}, u32[]{:S(2)}, u32[]{:S(2)}) collective-permute-start(f32[129]{0:T(256)S(1)} %add.238), channel_id=1, source_target_pairs={{0,3},{1,2},{2,1},{3,0},{4,7},{5,6},{6,5},{7,4},{8,11},{9,10},{10,... | collective-permute-start | bytes 1556 | tf_op jit(solution)/shard_map/ppermute | solution.py:66

commit v14 on v7

--- a/solution.py
+++ b/solution.py
@@ -268,8 +268,9 @@
     )
     base = jnp.stack([back_press] + backs)
 
-    press_top = acoustic[0, :, :, top]
-    sens_base = press_top * (adjoint_in[3, :, :, top] + push[:, :, top])
+    late_rad, late_push, late_press, _ = lax.optimization_barrier((adjoint_in[3], push, acoustic[0], widened))
+    press_top = late_press[:, :, top]
+    sens_base = press_top * (late_rad[:, :, top] + late_push[:, :, top])
     sens_placed = press_top * push_0
     seg_base = jnp.sum(jnp.where(segment_hot, sens_base[:, :, None], 0.0), axis=(0, 1))
     seg_placed = jnp.sum(jnp.where(segment_hot, sens_placed[:, :, None], 0.0), axis=(0, 1))

time: 50.8 us -> 47.9 us (0.943)
  local copies, waits for them, and re-layouts: 7.23 us -> 5.17 us
  other arithmetic: 7.15 us -> 6.18 us
  starting transfers between devices: 17.1 us -> 17.7 us
    unnamed x46 -> x56, local copies, waits for them, and re-layouts: 3.47 us -> 1.45 us
    squeeze x2 -> x1, other arithmetic: 0.88 us -> 0.03 us  [shards(): adjoint_in[3]]
    ppermute x1, waiting for transfers between devices: 4.05 us -> 3.21 us  [with_halo(): lax.ppermute(lax.slice_in_dim(array, 0, after, axis=dim), axis, down)]
    slice x1, local copies, waits for them, and re-layouts: 0.92 us -> 0.22 us  [shards(): buoyancy[:, :, below]]
    ppermute x1, starting transfers between devices: 3.2 us -> 3.85 us  [shards(): from_above = lax.ppermute(sent_down, 'az', down)]
    squeeze x2, local copies, waits for them, and re-layouts: 0.25 us -> 0.86 us  [the longest x1 0.85 us: shards(): acoustic[0]]
  transfers between devices with their start and end apart: 9 -> 9, of which waited for: 8 -> 8; matrix products, arithmetic and copies ran while one was open for 3% -> 5% of each run, Pallas kernels for 0% -> 0%
where the time goes in v14:
time: 47.9 us; the launch traced here: 47.7 us
  starting transfers between devices  17.7 us (37%)
  waiting for transfers between devices  15.5 us (32%)
  other arithmetic  6.18 us (13%)
  local copies, waits for them, and re-layouts  5.17 us (11%)
  between operations  3.15 us (7%)
    ppermute x5, waiting for transfers between devices, butterfly_sum(): lax.ppermute(values, axis, [(i, i ^ step) for i in range(size)])  9.25 us
    ppermute x5, starting transfers between devices, butterfly_sum(): lax.ppermute(values, axis, [(i, i ^ step) for i in range(size)])  8.58 us
    ppermute x1, starting transfers between devices, shards(): from_above = lax.ppermute(sent_down, 'az', down)  3.85 us
    ppermute x1, waiting for transfers between devices, with_halo(): lax.ppermute(lax.slice_in_dim(array, 0, after, axis=dim), axis, down)  3.21 us
    ppermute x1, waiting for transfers between devices, shards(): from_below = lax.ppermute(sent_up, 'az', up)  2.5 us
    ppermute x1, starting transfers between devices, with_halo(): lax.ppermute(lax.slice_in_dim(array, length - before, length, axis=dim),...  2.37 us
    ppermute x1, starting transfers between devices, shards(): from_below = lax.ppermute(sent_up, 'az', up)  1.57 us
    unnamed x56, local copies, waits for them, and re-layouts  1.45 us
  transfers between devices with their start and end apart: 9, of which 8 were waited for; matrix products, arithmetic and copies ran while one was open for 5% of the time, Pallas kernels for 0%

profile of v14, /device:TPU:0, one launch (start us, length us, event | category | flops | bytes accessed | tf_op | source)
XLA Modules:
  0.0 47.7 jit_solution(13809332659674111848)
XLA Ops:
  0.7 1.2 %fusion.121 = (f32[1,8,16,1]{3,2,1,0:T(8,128)S(1)}, f32[1,8,16,1]{3,2,1,0:T(8,128)S(1)}, f32[1,8,16,1]{3,2,1,0:T(8,128)S(1)}, f32[1,8,16,1]{3,2,1,0:T(8,128)S(1)}, f32[1,8,16,1]{3,2,1,0:T(8,128)S(1)}) fusion(f32[4,8,16,128]{3,2,1,0:T(8,128)} %param.10), kind=kLoop, calls=%fused_computation.324 | loop fusion | bytes 5120 | tf_op jit(solution)/shard_map/slice | solution.py:105
  4.2 2.4 %collective-permute-start = (f32[9,8,8,128]{3,2,1,0:T(8,128)S(1)}, f32[9,8,8,128]{3,2,1,0:T(8,128)S(1)}, u32[]{:S(2)}, u32[]{:S(2)}) collective-permute-start(f32[9,8,8,128]{3,2,1,0:T(8,128)S(1)} %get-tuple-element.56), channel_id=1, source_target_pairs={{0,1},{1,2},{2,3},{4,5},{5,6},{6,7},{8,9},{9,10},{10,11},{12,13},{... | collective-permute-start | bytes 884744 | tf_op jit(solution)/shard_map/ppermute | solution.py:16
  6.6 1.3 %collective-permute-start.1 = (f32[9,8,8,128]{3,2,1,0:T(8,128)S(1)}, f32[9,8,8,128]{3,2,1,0:T(8,128)S(1)}, u32[]{:S(2)}, u32[]{:S(2)}) collective-permute-start(f32[9,8,8,128]{3,2,1,0:T(8,128)S(1)} %get-tuple-element.57), channel_id=1, source_target_pairs={{1,0},{2,1},{3,2},{5,4},{6,5},{7,6},{9,8},{10,9},{11,10},{13,12},{... | collective-permute-start | bytes 884744 | tf_op jit(solution)/shard_map/ppermute | solution.py:19
  8.1 0.8 %slice_bitcast_fusion.9 = f32[8,16,128]{2,1,0:T(8,128)S(1)} fusion(f32[4,8,16,128]{3,2,1,0:T(8,128)} %param.10), kind=kLoop, calls=%fused_computation.159 | loop fusion | bytes 131072 | tf_op jit(solution)/shard_map/squeeze | solution.py:271
  9.0 3.2 %collective-permute-done.1 = f32[9,8,8,128]{3,2,1,0:T(8,128)S(1)} collective-permute-done((f32[9,8,8,128]{3,2,1,0:T(8,128)S(1)}, f32[9,8,8,128]{3,2,1,0:T(8,128)S(1)}, u32[]{:S(2)}, u32[]{:S(2)}) %collective-permute-start.1) | collective-permute-done | bytes 294944 | tf_op jit(solution)/shard_map/ppermute | solution.py:19
  12.4 1.6 %collective-permute-start.2 = (f32[10,32,128]{2,1,0:T(8,128)S(1)}, f32[10,32,128]{2,1,0:T(8,128)S(1)}, u32[]{:S(2)}, u32[]{:S(2)}) collective-permute-start(f32[10,32,128]{2,1,0:T(8,128)S(1)} %get-tuple-element.36), channel_id=1, source_target_pairs={{0,4},{4,8},{8,12},{12,16},{16,20},{20,24},{24,28},{28,0},{1,5},{5... | collective-permute-start | bytes 491528 | tf_op jit(solution)/shard_map/ppermute | solution.py:134
  14.0 3.8 %collective-permute-start.3 = (f32[10,32,128]{2,1,0:T(8,128)S(1)}, f32[10,32,128]{2,1,0:T(8,128)S(1)}, u32[]{:S(2)}, u32[]{:S(2)}) collective-permute-start(f32[10,32,128]{2,1,0:T(8,128)S(1)} %get-tuple-element.37), channel_id=1, source_target_pairs={{4,0},{8,4},{12,8},{16,12},{20,16},{24,20},{28,24},{0,28},{5,1},{9... | collective-permute-start | bytes 491528 | tf_op jit(solution)/shard_map/ppermute | solution.py:135
  18.1 2.5 %collective-permute-done.2 = f32[10,32,128]{2,1,0:T(8,128)S(1)} collective-permute-done((f32[10,32,128]{2,1,0:T(8,128)S(1)}, f32[10,32,128]{2,1,0:T(8,128)S(1)}, u32[]{:S(2)}, u32[]{:S(2)}) %collective-permute-start.2) | collective-permute-done | bytes 163872 | tf_op jit(solution)/shard_map/ppermute | solution.py:134
  20.6 0.5 %collective-permute-done.3 = f32[10,32,128]{2,1,0:T(8,128)S(1)} collective-permute-done((f32[10,32,128]{2,1,0:T(8,128)S(1)}, f32[10,32,128]{2,1,0:T(8,128)S(1)}, u32[]{:S(2)}, u32[]{:S(2)}) %collective-permute-start.3) | collective-permute-done | bytes 163872 | tf_op jit(solution)/shard_map/ppermute | solution.py:135
  21.9 0.6 %select_reduce_fusion.6 = (f32[]{:T(128)}, f32[512]{0:T(512)S(1)}) fusion(s32[512]{0:T(512)S(1)} %copy-done.4, s32[]{:T(128)S(6)} %mul.402, s32[512]{0:T(512)S(1)} %copy-done.5, s32[]{:T(128)S(6)} %mul.401, f32[512]{0:T(512)S(1)} %select_reduce_fusion.1, f32[512]{0:T(512)S(1)} %copy-done.7), kind=kLoop, calls=%fused_computation.315 | loop fusion | flops 13311 | bytes 10252 | tf_op jit(solution)/shard_map/reduce_sum | solution.py:189
  23.2 0.7 %pad_maximum_fusion.4 = f32[129]{0:T(256)S(1)} fusion(f32[64]{0:T(128)S(1)} %get-tuple-element.17, f32[64]{0:T(128)S(1)} %get-tuple-element.16, f32[1]{0:T(128)} %bitcast.80), kind=kLoop, calls=%fused_computation.318 | loop fusion | flops 258 | bytes 1032 | tf_op jit(solution)/shard_map/concatenate | solution.py:278
  24.0 0.7 %collective-permute-start.4 = (f32[129]{0:T(256)S(1)}, f32[129]{0:T(256)S(1)}, u32[]{:S(2)}, u32[]{:S(2)}) collective-permute-start(f32[129]{0:T(256)S(1)} %pad_maximum_fusion.4), channel_id=1, source_target_pairs={{0,4},{4,0},{8,12},{12,8},{16,20},{20,16},{24,28},{28,24},{1,5},{5... | collective-permute-start | bytes 1556 | tf_op jit(solution)/shard_map/ppermute | solution.py:67
  25.9 1.7 %collective-permute-done.4 = f32[129]{0:T(256)S(1)} collective-permute-done((f32[129]{0:T(256)S(1)}, f32[129]{0:T(256)S(1)}, u32[]{:S(2)}, u32[]{:S(2)}) %collective-permute-start.4) | collective-permute-done | bytes 548 | tf_op jit(solution)/shard_map/ppermute | solution.py:67
  27.5 0.7 %fusion.124 = f32[129]{0:T(256)S(1)} fusion(f32[129]{0:T(256)S(1)} %collective-permute-done.4, f32[64]{0:T(128)S(1)} %get-tuple-element.17, f32[64]{0:T(128)S(1)} %get-tuple-element.16, f32[1]{0:T(128)} %bitcast.80), kind=kLoop, calls=%fused_computation.327 | loop fusion | flops 387 | bytes 1548 | tf_op jit(solution)/shard_map/add | solution.py:67
  28.3 0.9 %collective-permute-start.5 = (f32[129]{0:T(256)S(1)}, f32[129]{0:T(256)S(1)}, u32[]{:S(2)}, u32[]{:S(2)}) collective-permute-start(f32[129]{0:T(256)S(1)} %fusion.124), channel_id=1, source_target_pairs={{0,8},{4,12},{8,0},{12,4},{16,24},{20,28},{24,16},{28,20},{1,9},{5... | collective-permute-start | bytes 1556 | tf_op jit(solution)/shard_map/ppermute | solution.py:67
  29.1 2.7 %collective-permute-done.5 = f32[129]{0:T(256)S(1)} collective-permute-done((f32[129]{0:T(256)S(1)}, f32[129]{0:T(256)S(1)}, u32[]{:S(2)}, u32[]{:S(2)}) %collective-permute-start.5) | collective-permute-done | bytes 548 | tf_op jit(solution)/shard_map/ppermute | solution.py:67
  31.8 1.9 %collective-permute-start.6 = (f32[129]{0:T(256)S(1)}, f32[129]{0:T(256)S(1)}, u32[]{:S(2)}, u32[]{:S(2)}) collective-permute-start(f32[129]{0:T(256)S(1)} %add.234), channel_id=1, source_target_pairs={{0,16},{4,20},{8,24},{12,28},{16,0},{20,4},{24,8},{28,12},{1,17},{... | collective-permute-start | bytes 1556 | tf_op jit(solution)/shard_map/ppermute | solution.py:67
  33.8 2.5 %collective-permute-done.6 = f32[129]{0:T(256)S(1)} collective-permute-done((f32[129]{0:T(256)S(1)}, f32[129]{0:T(256)S(1)}, u32[]{:S(2)}, u32[]{:S(2)}) %collective-permute-start.6) | collective-permute-done | bytes 548 | tf_op jit(solution)/shard_map/ppermute | solution.py:67
  36.3 0.8 %collective-permute-start.7 = (f32[129]{0:T(256)S(1)}, f32[129]{0:T(256)S(1)}, u32[]{:S(2)}, u32[]{:S(2)}) collective-permute-start(f32[129]{0:T(256)S(1)} %add.235), channel_id=1, source_target_pairs={{0,1},{1,0},{2,3},{3,2},{4,5},{5,4},{6,7},{7,6},{8,9},{9,8},{10,11... | collective-permute-start | bytes 1556 | tf_op jit(solution)/shard_map/ppermute | solution.py:67
  37.1 0.8 %collective-permute-done.7 = f32[129]{0:T(256)S(1)} collective-permute-done((f32[129]{0:T(256)S(1)}, f32[129]{0:T(256)S(1)}, u32[]{:S(2)}, u32[]{:S(2)}) %collective-permute-start.7) | collective-permute-done | bytes 548 | tf_op jit(solution)/shard_map/ppermute | solution.py:67
  37.9 4.3 %collective-permute-start.8 = (f32[129]{0:T(256)S(1)}, f32[129]{0:T(256)S(1)}, u32[]{:S(2)}, u32[]{:S(2)}) collective-permute-start(f32[129]{0:T(256)S(1)} %add.236), channel_id=1, source_target_pairs={{0,2},{1,3},{2,0},{3,1},{4,6},{5,7},{6,4},{7,5},{8,10},{9,11},{10,... | collective-permute-start | bytes 1556 | tf_op jit(solution)/shard_map/ppermute | solution.py:67
  42.3 1.5 %collective-permute-done.8 = f32[129]{0:T(256)S(1)} collective-permute-done((f32[129]{0:T(256)S(1)}, f32[129]{0:T(256)S(1)}, u32[]{:S(2)}, u32[]{:S(2)}) %collective-permute-start.8) | collective-permute-done | bytes 548 | tf_op jit(solution)/shard_map/ppermute | solution.py:67
  45.0 0.6 %fusion.118 = f32[64]{0:T(128)} fusion(f32[129]{0:T(256)S(1)} %add.237, f32[]{:T(128)} %bitcast.84), kind=kLoop, calls=%fused_computation.322 | loop fusion | flops 192 | bytes 772 | tf_op jit(solution)/shard_map/mul | solution.py:281
  45.6 0.9 %maximum_add_fusion = f32[4,8,16,128]{3,2,1,0:T(8,128)} fusion(f32[1,8,16,128]{3,2,1,0:T(8,128)S(1)} %fusion.9, f32[1,8,16,128]{3,2,1,0:T(8,128)S(1)} %fusion.26, f32[1,8,16,128]{3,2,1,0:T(8,128)S(1)} %fusion.35, f32[1,8,16,128]{3,2,1,0:T(8,128)S(1)} %fusion.47, f32[4,8,16]{2,1,0:T(8,128)S(1)} %get-tuple-element.92, f32[4,8,16]{2,1,0:T(8,128)S(1)} %get-tuple-element.91, ...), kind=kLoop, calls=%fused_computation.6 | loop fusion | flops 393216 | bytes 528640 | tf_op jit(solution)/shard_map/add | solution.py:290
  (122 shorter events, 5.8 us)
Async XLA Ops:
  0.6 1.8 %copy-start.2 = (f32[4,8,16,128]{3,2,1,0:T(8,128)S(1)}, f32[4,8,16,128]{3,2,1,0:T(8,128)}, u32[]{:S(2)}) copy-start(f32[4,8,16,128]{3,2,1,0:T(8,128)} %param.12) | copy-start | bytes 786436
  0.6 1.8 %copy-start.1 = (f32[4,8,16,128]{3,2,1,0:T(8,128)S(1)}, f32[4,8,16,128]{3,2,1,0:T(8,128)}, u32[]{:S(2)}) copy-start(f32[4,8,16,128]{3,2,1,0:T(8,128)} %param.11) | copy-start | bytes 786436
  2.5 1.0 %copy-start.3 = (s32[8,16]{1,0:T(8,128)S(1)}, s32[8,16]{1,0:T(8,128)}, u32[]{:S(2)}) copy-start(s32[8,16]{1,0:T(8,128)} %param.14) | copy-start | bytes 1540
  2.5 1.0 %copy-start.8 = (f32[64]{0:T(128)S(1)}, f32[64]{0:T(128)}, u32[]{:S(2)}) copy-start(f32[64]{0:T(128)} %param.13) | copy-start | bytes 772
  2.5 1.1 %copy-start.6 = (s32[8,16]{1,0:T(8,128)S(1)}, s32[8,16]{1,0:T(8,128)}, u32[]{:S(2)}) copy-start(s32[8,16]{1,0:T(8,128)} %param.15) | copy-start | bytes 1540
  2.6 1.1 %copy-start.9 = (f32[64]{0:T(128)S(1)}, f32[64]{0:T(128)}, u32[]{:S(2)}) copy-start(f32[64]{0:T(128)} %param.16) | copy-start | bytes 772
  3.9 4.2 %copy-start.4 = (s32[512]{0:T(512)S(1)}, s32[512]{0:T(512)}, u32[]{:S(2)}) copy-start(s32[512]{0:T(512)} %param.18) | copy-start | bytes 6148
  3.9 4.2 %copy-start.5 = (s32[512]{0:T(512)S(1)}, s32[512]{0:T(512)}, u32[]{:S(2)}) copy-start(s32[512]{0:T(512)} %param.17) | copy-start | bytes 6148
  4.2 4.7 %collective-permute-start = (f32[9,8,8,128]{3,2,1,0:T(8,128)S(1)}, f32[9,8,8,128]{3,2,1,0:T(8,128)S(1)}, u32[]{:S(2)}, u32[]{:S(2)}) collective-permute-start(f32[9,8,8,128]{3,2,1,0:T(8,128)S(1)} %get-tuple-element.56), channel_id=1, source_target_pairs={{0,1},{1,2},{2,3},{4,5},{5,6},{6,7},{8,9},{9,10},{10,11},{12,13},{... | collective-permute-start | bytes 884744 | tf_op jit(solution)/shard_map/ppermute | solution.py:16
  6.6 5.6 %collective-permute-start.1 = (f32[9,8,8,128]{3,2,1,0:T(8,128)S(1)}, f32[9,8,8,128]{3,2,1,0:T(8,128)S(1)}, u32[]{:S(2)}, u32[]{:S(2)}) collective-permute-start(f32[9,8,8,128]{3,2,1,0:T(8,128)S(1)} %get-tuple-element.57), channel_id=1, source_target_pairs={{1,0},{2,1},{3,2},{5,4},{6,5},{7,6},{9,8},{10,9},{11,10},{13,12},{... | collective-permute-start | bytes 884744 | tf_op jit(solution)/shard_map/ppermute | solution.py:19
  12.3 1.7 %copy-start = (f32[9,8,32,128]{3,2,1,0:T(8,128)}, f32[9,8,32,128]{3,2,1,0:T(8,128)S(1)}, u32[]{:S(2)}) copy-start(f32[9,8,32,128]{3,2,1,0:T(8,128)S(1)} %pad_maximum_fusion.1) | copy-start | bytes 3538948
  12.4 8.2 %collective-permute-start.2 = (f32[10,32,128]{2,1,0:T(8,128)S(1)}, f32[10,32,128]{2,1,0:T(8,128)S(1)}, u32[]{:S(2)}, u32[]{:S(2)}) collective-permute-start(f32[10,32,128]{2,1,0:T(8,128)S(1)} %get-tuple-element.36), channel_id=1, source_target_pairs={{0,4},{4,8},{8,12},{12,16},{16,20},{20,24},{24,28},{28,0},{1,5},{5... | collective-permute-start | bytes 491528 | tf_op jit(solution)/shard_map/ppermute | solution.py:134
  14.0 7.9 %copy-start.7 = (f32[512]{0:T(512)S(1)}, f32[512]{0:T(512)}, u32[]{:S(2)}) copy-start(f32[512]{0:T(512)} %param.19) | copy-start | bytes 6148
  14.0 7.1 %collective-permute-start.3 = (f32[10,32,128]{2,1,0:T(8,128)S(1)}, f32[10,32,128]{2,1,0:T(8,128)S(1)}, u32[]{:S(2)}, u32[]{:S(2)}) collective-permute-start(f32[10,32,128]{2,1,0:T(8,128)S(1)} %get-tuple-element.37), channel_id=1, source_target_pairs={{4,0},{8,4},{12,8},{16,12},{20,16},{24,20},{28,24},{0,28},{5,1},{9... | collective-permute-start | bytes 491528 | tf_op jit(solution)/shard_map/ppermute | solution.py:135
  21.2 3.6 %slice-start = ((f32[9,8,32,128]{3,2,1,0:T(8,128)}), f32[8,8,32,128]{3,2,1,0:T(8,128)S(1)}, s32[]{:S(2)}) async-start(f32[9,8,32,128]{3,2,1,0:T(8,128)} %copy-done), calls=%async_computation | async-start | bytes 2097152 | tf_op jit(solution)/shard_map/slice | solution.py:141
  24.0 3.6 %collective-permute-start.4 = (f32[129]{0:T(256)S(1)}, f32[129]{0:T(256)S(1)}, u32[]{:S(2)}, u32[]{:S(2)}) collective-permute-start(f32[129]{0:T(256)S(1)} %pad_maximum_fusion.4), channel_id=1, source_target_pairs={{0,4},{4,0},{8,12},{12,8},{16,20},{20,16},{24,28},{28,24},{1,5},{5... | collective-permute-start | bytes 1556 | tf_op jit(solution)/shard_map/ppermute | solution.py:67
  28.3 3.6 %collective-permute-start.5 = (f32[129]{0:T(256)S(1)}, f32[129]{0:T(256)S(1)}, u32[]{:S(2)}, u32[]{:S(2)}) collective-permute-start(f32[129]{0:T(256)S(1)} %fusion.124), channel_id=1, source_target_pairs={{0,8},{4,12},{8,0},{12,4},{16,24},{20,28},{24,16},{28,20},{1,9},{5... | collective-permute-start | bytes 1556 | tf_op jit(solution)/shard_map/ppermute | solution.py:67
  31.8 4.5 %collective-permute-start.6 = (f32[129]{0:T(256)S(1)}, f32[129]{0:T(256)S(1)}, u32[]{:S(2)}, u32[]{:S(2)}) collective-permute-start(f32[129]{0:T(256)S(1)} %add.234), channel_id=1, source_target_pairs={{0,16},{4,20},{8,24},{12,28},{16,0},{20,4},{24,8},{28,12},{1,17},{... | collective-permute-start | bytes 1556 | tf_op jit(solution)/shard_map/ppermute | solution.py:67
  36.3 1.6 %collective-permute-start.7 = (f32[129]{0:T(256)S(1)}, f32[129]{0:T(256)S(1)}, u32[]{:S(2)}, u32[]{:S(2)}) collective-permute-start(f32[129]{0:T(256)S(1)} %add.235), channel_id=1, source_target_pairs={{0,1},{1,0},{2,3},{3,2},{4,5},{5,4},{6,7},{7,6},{8,9},{9,8},{10,11... | collective-permute-start | bytes 1556 | tf_op jit(solution)/shard_map/ppermute | solution.py:67
  37.9 5.9 %collective-permute-start.8 = (f32[129]{0:T(256)S(1)}, f32[129]{0:T(256)S(1)}, u32[]{:S(2)}, u32[]{:S(2)}) collective-permute-start(f32[129]{0:T(256)S(1)} %add.236), channel_id=1, source_target_pairs={{0,2},{1,3},{2,0},{3,1},{4,6},{5,7},{6,4},{7,5},{8,10},{9,11},{10,... | collective-permute-start | bytes 1556 | tf_op jit(solution)/shard_map/ppermute | solution.py:67

commit v15 on v14

--- a/solution.py
+++ b/solution.py
@@ -280,14 +280,7 @@
     grad_scale = (na * lax.axis_size("az") * nx * lax.axis_size("ax") / nseg) ** (-0.5)
     liner_grad = (totals[1 : 1 + nseg] + totals[1 + nseg :] / mean_sq) * grad_scale
     misfit = 0.5 * jnp.log(mean_sq)
-    lane = lax.broadcasted_iota(jnp.int32, (1, 1, 1, nr), 3)
-    extra_scaled = extra / mean_sq
-    correction = jnp.where(
-        lane == nr - 1,
-        extra_scaled[..., 1:2],
-        jnp.where(lane == nr - 2, extra_scaled[..., 0:1], 0.0),
-    )
-    adjoint_out = base + correction
+    adjoint_out = lax.dynamic_update_slice(base, base[..., nr - 2 :] + extra / mean_sq, (0, 0, 0, nr - 2))
     return (adjoint_out, liner_grad, misfit)
 
 

time: 47.9 us -> 52.8 us (1.10)
  local copies, waits for them, and re-layouts: 5.17 us -> 11.3 us
  other arithmetic: 6.18 us -> 5.3 us
    dynamic_update_slice x0 -> x1, local copies, waits for them, and re-layouts: none -> 4.81 us  [shards(): lax.dynamic_update_slice(base, base[..., nr - 2:] + extra / mean_sq, (0,...]
    unnamed x56 -> x59, local copies, waits for them, and re-layouts: 1.45 us -> 2.38 us
    add x1, other arithmetic: 0.91 us -> 0.01 us  [shards(): base[..., nr - 2:] + extra / mean_sq]
where the time goes in v15:
time: 52.8 us; the launch traced here: 52.5 us
  starting transfers between devices  17.7 us (34%)
  waiting for transfers between devices  15.1 us (29%)
  local copies, waits for them, and re-layouts  11.3 us (21%)
  other arithmetic  5.3 us (10%)
  between operations  3.17 us (6%)
    ppermute x5, waiting for transfers between devices, butterfly_sum(): lax.ppermute(values, axis, [(i, i ^ step) for i in range(size)])  8.84 us
    ppermute x5, starting transfers between devices, butterfly_sum(): lax.ppermute(values, axis, [(i, i ^ step) for i in range(size)])  8.59 us
    dynamic_update_slice x1, local copies, waits for them, and re-layouts, shards(): lax.dynamic_update_slice(base, base[..., nr - 2:] + extra / mean_sq, (0,...  4.81 us
    ppermute x1, starting transfers between devices, shards(): from_above = lax.ppermute(sent_down, 'az', down)  3.85 us
    ppermute x1, waiting for transfers between devices, with_halo(): lax.ppermute(lax.slice_in_dim(array, 0, after, axis=dim), axis, down)  3.21 us
    ppermute x1, waiting for transfers between devices, shards(): from_below = lax.ppermute(sent_up, 'az', up)  2.49 us
    unnamed x59, local copies, waits for them, and re-layouts  2.38 us
    ppermute x1, starting transfers between devices, with_halo(): lax.ppermute(lax.slice_in_dim(array, length - before, length, axis=dim),...  2.37 us
  transfers between devices with their start and end apart: 9, of which 8 were waited for; matrix products, arithmetic and copies ran while one was open for 5% of the time, Pallas kernels for 0%

profile of v15, /device:TPU:0, one launch (start us, length us, event | category | flops | bytes accessed | tf_op | source)
XLA Modules:
  0.0 52.5 jit_solution(6533484554218008409)
XLA Ops:
  0.7 1.2 %fusion.122 = (f32[1,8,16,1]{3,2,1,0:T(8,128)S(1)}, f32[1,8,16,1]{3,2,1,0:T(8,128)S(1)}, f32[1,8,16,1]{3,2,1,0:T(8,128)S(1)}, f32[1,8,16,1]{3,2,1,0:T(8,128)S(1)}, f32[1,8,16,1]{3,2,1,0:T(8,128)S(1)}) fusion(f32[4,8,16,128]{3,2,1,0:T(8,128)} %param.10), kind=kLoop, calls=%fused_computation.322 | loop fusion | bytes 5120 | tf_op jit(solution)/shard_map/slice | solution.py:105
  4.2 2.4 %collective-permute-start = (f32[9,8,8,128]{3,2,1,0:T(8,128)S(1)}, f32[9,8,8,128]{3,2,1,0:T(8,128)S(1)}, u32[]{:S(2)}, u32[]{:S(2)}) collective-permute-start(f32[9,8,8,128]{3,2,1,0:T(8,128)S(1)} %get-tuple-element.56), channel_id=1, source_target_pairs={{0,1},{1,2},{2,3},{4,5},{5,6},{6,7},{8,9},{9,10},{10,11},{12,13},{... | collective-permute-start | bytes 884744 | tf_op jit(solution)/shard_map/ppermute | solution.py:16
  6.6 1.3 %collective-permute-start.1 = (f32[9,8,8,128]{3,2,1,0:T(8,128)S(1)}, f32[9,8,8,128]{3,2,1,0:T(8,128)S(1)}, u32[]{:S(2)}, u32[]{:S(2)}) collective-permute-start(f32[9,8,8,128]{3,2,1,0:T(8,128)S(1)} %get-tuple-element.57), channel_id=1, source_target_pairs={{1,0},{2,1},{3,2},{5,4},{6,5},{7,6},{9,8},{10,9},{11,10},{13,12},{... | collective-permute-start | bytes 884744 | tf_op jit(solution)/shard_map/ppermute | solution.py:19
  8.1 0.8 %slice_bitcast_fusion.9 = f32[8,16,128]{2,1,0:T(8,128)S(1)} fusion(f32[4,8,16,128]{3,2,1,0:T(8,128)} %param.10), kind=kLoop, calls=%fused_computation.159 | loop fusion | bytes 131072 | tf_op jit(solution)/shard_map/squeeze | solution.py:271
  9.0 3.2 %collective-permute-done.1 = f32[9,8,8,128]{3,2,1,0:T(8,128)S(1)} collective-permute-done((f32[9,8,8,128]{3,2,1,0:T(8,128)S(1)}, f32[9,8,8,128]{3,2,1,0:T(8,128)S(1)}, u32[]{:S(2)}, u32[]{:S(2)}) %collective-permute-start.1) | collective-permute-done | bytes 294944 | tf_op jit(solution)/shard_map/ppermute | solution.py:19
  12.4 1.6 %collective-permute-start.2 = (f32[10,32,128]{2,1,0:T(8,128)S(1)}, f32[10,32,128]{2,1,0:T(8,128)S(1)}, u32[]{:S(2)}, u32[]{:S(2)}) collective-permute-start(f32[10,32,128]{2,1,0:T(8,128)S(1)} %get-tuple-element.36), channel_id=1, source_target_pairs={{0,4},{4,8},{8,12},{12,16},{16,20},{20,24},{24,28},{28,0},{1,5},{5... | collective-permute-start | bytes 491528 | tf_op jit(solution)/shard_map/ppermute | solution.py:134
  14.0 3.9 %collective-permute-start.3 = (f32[10,32,128]{2,1,0:T(8,128)S(1)}, f32[10,32,128]{2,1,0:T(8,128)S(1)}, u32[]{:S(2)}, u32[]{:S(2)}) collective-permute-start(f32[10,32,128]{2,1,0:T(8,128)S(1)} %get-tuple-element.37), channel_id=1, source_target_pairs={{4,0},{8,4},{12,8},{16,12},{20,16},{24,20},{28,24},{0,28},{5,1},{9... | collective-permute-start | bytes 491528 | tf_op jit(solution)/shard_map/ppermute | solution.py:135
  18.1 2.5 %collective-permute-done.2 = f32[10,32,128]{2,1,0:T(8,128)S(1)} collective-permute-done((f32[10,32,128]{2,1,0:T(8,128)S(1)}, f32[10,32,128]{2,1,0:T(8,128)S(1)}, u32[]{:S(2)}, u32[]{:S(2)}) %collective-permute-start.2) | collective-permute-done | bytes 163872 | tf_op jit(solution)/shard_map/ppermute | solution.py:134
  21.9 0.6 %select_reduce_fusion.6 = (f32[]{:T(128)}, f32[512]{0:T(512)S(1)}) fusion(s32[512]{0:T(512)S(1)} %copy-done.5, s32[]{:T(128)S(6)} %mul.402, s32[512]{0:T(512)S(1)} %copy-done.6, s32[]{:T(128)S(6)} %mul.401, f32[512]{0:T(512)S(1)} %select_reduce_fusion.1, f32[512]{0:T(512)S(1)} %copy-done.8), kind=kLoop, calls=%fused_computation.314 | loop fusion | flops 13311 | bytes 10252 | tf_op jit(solution)/shard_map/reduce_sum | solution.py:189
  23.2 0.7 %pad_maximum_fusion.5 = f32[129]{0:T(256)S(1)} fusion(f32[64]{0:T(128)S(1)} %get-tuple-element.17, f32[64]{0:T(128)S(1)} %get-tuple-element.16, f32[1]{0:T(128)} %bitcast.80), kind=kLoop, calls=%fused_computation.317 | loop fusion | flops 258 | bytes 1032 | tf_op jit(solution)/shard_map/concatenate | solution.py:278
  24.0 0.7 %collective-permute-start.4 = (f32[129]{0:T(256)S(1)}, f32[129]{0:T(256)S(1)}, u32[]{:S(2)}, u32[]{:S(2)}) collective-permute-start(f32[129]{0:T(256)S(1)} %pad_maximum_fusion.5), channel_id=1, source_target_pairs={{0,4},{4,0},{8,12},{12,8},{16,20},{20,16},{24,28},{28,24},{1,5},{5... | collective-permute-start | bytes 1556 | tf_op jit(solution)/shard_map/ppermute | solution.py:67
  25.9 1.6 %collective-permute-done.4 = f32[129]{0:T(256)S(1)} collective-permute-done((f32[129]{0:T(256)S(1)}, f32[129]{0:T(256)S(1)}, u32[]{:S(2)}, u32[]{:S(2)}) %collective-permute-start.4) | collective-permute-done | bytes 548 | tf_op jit(solution)/shard_map/ppermute | solution.py:67
  27.5 0.7 %fusion.125 = f32[129]{0:T(256)S(1)} fusion(f32[129]{0:T(256)S(1)} %collective-permute-done.4, f32[64]{0:T(128)S(1)} %get-tuple-element.17, f32[64]{0:T(128)S(1)} %get-tuple-element.16, f32[1]{0:T(128)} %bitcast.80), kind=kLoop, calls=%fused_computation.325 | loop fusion | flops 387 | bytes 1548 | tf_op jit(solution)/shard_map/add | solution.py:67
  28.3 0.9 %collective-permute-start.5 = (f32[129]{0:T(256)S(1)}, f32[129]{0:T(256)S(1)}, u32[]{:S(2)}, u32[]{:S(2)}) collective-permute-start(f32[129]{0:T(256)S(1)} %fusion.125), channel_id=1, source_target_pairs={{0,8},{4,12},{8,0},{12,4},{16,24},{20,28},{24,16},{28,20},{1,9},{5... | collective-permute-start | bytes 1556 | tf_op jit(solution)/shard_map/ppermute | solution.py:67
  29.1 2.7 %collective-permute-done.5 = f32[129]{0:T(256)S(1)} collective-permute-done((f32[129]{0:T(256)S(1)}, f32[129]{0:T(256)S(1)}, u32[]{:S(2)}, u32[]{:S(2)}) %collective-permute-start.5) | collective-permute-done | bytes 548 | tf_op jit(solution)/shard_map/ppermute | solution.py:67
  31.8 1.9 %collective-permute-start.6 = (f32[129]{0:T(256)S(1)}, f32[129]{0:T(256)S(1)}, u32[]{:S(2)}, u32[]{:S(2)}) collective-permute-start(f32[129]{0:T(256)S(1)} %add.234), channel_id=1, source_target_pairs={{0,16},{4,20},{8,24},{12,28},{16,0},{20,4},{24,8},{28,12},{1,17},{... | collective-permute-start | bytes 1556 | tf_op jit(solution)/shard_map/ppermute | solution.py:67
  33.8 2.5 %collective-permute-done.6 = f32[129]{0:T(256)S(1)} collective-permute-done((f32[129]{0:T(256)S(1)}, f32[129]{0:T(256)S(1)}, u32[]{:S(2)}, u32[]{:S(2)}) %collective-permute-start.6) | collective-permute-done | bytes 548 | tf_op jit(solution)/shard_map/ppermute | solution.py:67
  36.3 0.8 %collective-permute-start.7 = (f32[129]{0:T(256)S(1)}, f32[129]{0:T(256)S(1)}, u32[]{:S(2)}, u32[]{:S(2)}) collective-permute-start(f32[129]{0:T(256)S(1)} %add.235), channel_id=1, source_target_pairs={{0,1},{1,0},{2,3},{3,2},{4,5},{5,4},{6,7},{7,6},{8,9},{9,8},{10,11... | collective-permute-start | bytes 1556 | tf_op jit(solution)/shard_map/ppermute | solution.py:67
  37.2 0.8 %collective-permute-done.7 = f32[129]{0:T(256)S(1)} collective-permute-done((f32[129]{0:T(256)S(1)}, f32[129]{0:T(256)S(1)}, u32[]{:S(2)}, u32[]{:S(2)}) %collective-permute-start.7) | collective-permute-done | bytes 548 | tf_op jit(solution)/shard_map/ppermute | solution.py:67
  38.0 4.3 %collective-permute-start.8 = (f32[129]{0:T(256)S(1)}, f32[129]{0:T(256)S(1)}, u32[]{:S(2)}, u32[]{:S(2)}) collective-permute-start(f32[129]{0:T(256)S(1)} %add.236), channel_id=1, source_target_pairs={{0,2},{1,3},{2,0},{3,1},{4,6},{5,7},{6,4},{7,5},{8,10},{9,11},{10,... | collective-permute-start | bytes 1556 | tf_op jit(solution)/shard_map/ppermute | solution.py:67
  42.6 1.2 %collective-permute-done.8 = f32[129]{0:T(256)S(1)} collective-permute-done((f32[129]{0:T(256)S(1)}, f32[129]{0:T(256)S(1)}, u32[]{:S(2)}, u32[]{:S(2)}) %collective-permute-start.8) | collective-permute-done | bytes 548 | tf_op jit(solution)/shard_map/ppermute | solution.py:67
  45.0 0.6 %fusion.119 = f32[64]{0:T(128)} fusion(f32[129]{0:T(256)S(1)} %add.237, f32[]{:T(128)} %bitcast.84), kind=kLoop, calls=%fused_computation.320 | loop fusion | flops 192 | bytes 772 | tf_op jit(solution)/shard_map/mul | solution.py:281
  45.9 4.8 %dynamic_update_slice.3 = f32[4,8,16,128]{3,2,1,0:T(8,128)S(1)} dynamic-update-slice(f32[4,8,16,128]{3,2,1,0:T(8,128)S(1)} %pad_maximum_fusion.2, f32[4,8,16,2]{3,2,1,0:T(8,128)S(1)} %copy.116, s32[]{:T(128)} %constant.34.clone.1, s32[]{:T(128)} %constant.34.clone.1, s32[]{:T(128)} %constant.34.clone.1, s32[]{:T(128)} %constant.89.clone.1) | dynamic-update-slice | bytes 8196 | tf_op jit(solution)/shard_map/dynamic_update_slice | solution.py:283
  50.7 0.7 %copy-done.2 = f32[4,8,16,128]{3,2,1,0:T(8,128)} copy-done((f32[4,8,16,128]{3,2,1,0:T(8,128)}, f32[4,8,16,128]{3,2,1,0:T(8,128)S(1)}, u32[]{:S(2)}) %copy-start.2) | copy-done | bytes 262168
  (127 shorter events, 7.0 us)
Async XLA Ops:
  0.6 1.8 %copy-start.3 = (f32[4,8,16,128]{3,2,1,0:T(8,128)S(1)}, f32[4,8,16,128]{3,2,1,0:T(8,128)}, u32[]{:S(2)}) copy-start(f32[4,8,16,128]{3,2,1,0:T(8,128)} %param.12) | copy-start | bytes 786436
  0.6 1.8 %copy-start.1 = (f32[4,8,16,128]{3,2,1,0:T(8,128)S(1)}, f32[4,8,16,128]{3,2,1,0:T(8,128)}, u32[]{:S(2)}) copy-start(f32[4,8,16,128]{3,2,1,0:T(8,128)} %param.11) | copy-start | bytes 786436
  2.5 1.0 %copy-start.4 = (s32[8,16]{1,0:T(8,128)S(1)}, s32[8,16]{1,0:T(8,128)}, u32[]{:S(2)}) copy-start(s32[8,16]{1,0:T(8,128)} %param.14) | copy-start | bytes 1540
  2.5 1.0 %copy-start.9 = (f32[64]{0:T(128)S(1)}, f32[64]{0:T(128)}, u32[]{:S(2)}) copy-start(f32[64]{0:T(128)} %param.13) | copy-start | bytes 772
  2.5 1.1 %copy-start.7 = (s32[8,16]{1,0:T(8,128)S(1)}, s32[8,16]{1,0:T(8,128)}, u32[]{:S(2)}) copy-start(s32[8,16]{1,0:T(8,128)} %param.15) | copy-start | bytes 1540
  2.6 1.1 %copy-start.10 = (f32[64]{0:T(128)S(1)}, f32[64]{0:T(128)}, u32[]{:S(2)}) copy-start(f32[64]{0:T(128)} %param.16) | copy-start | bytes 772
  3.9 4.2 %copy-start.5 = (s32[512]{0:T(512)S(1)}, s32[512]{0:T(512)}, u32[]{:S(2)}) copy-start(s32[512]{0:T(512)} %param.18) | copy-start | bytes 6148
  3.9 4.2 %copy-start.6 = (s32[512]{0:T(512)S(1)}, s32[512]{0:T(512)}, u32[]{:S(2)}) copy-start(s32[512]{0:T(512)} %param.17) | copy-start | bytes 6148
  4.2 4.7 %collective-permute-start = (f32[9,8,8,128]{3,2,1,0:T(8,128)S(1)}, f32[9,8,8,128]{3,2,1,0:T(8,128)S(1)}, u32[]{:S(2)}, u32[]{:S(2)}) collective-permute-start(f32[9,8,8,128]{3,2,1,0:T(8,128)S(1)} %get-tuple-element.56), channel_id=1, source_target_pairs={{0,1},{1,2},{2,3},{4,5},{5,6},{6,7},{8,9},{9,10},{10,11},{12,13},{... | collective-permute-start | bytes 884744 | tf_op jit(solution)/shard_map/ppermute | solution.py:16
  6.6 5.6 %collective-permute-start.1 = (f32[9,8,8,128]{3,2,1,0:T(8,128)S(1)}, f32[9,8,8,128]{3,2,1,0:T(8,128)S(1)}, u32[]{:S(2)}, u32[]{:S(2)}) collective-permute-start(f32[9,8,8,128]{3,2,1,0:T(8,128)S(1)} %get-tuple-element.57), channel_id=1, source_target_pairs={{1,0},{2,1},{3,2},{5,4},{6,5},{7,6},{9,8},{10,9},{11,10},{13,12},{... | collective-permute-start | bytes 884744 | tf_op jit(solution)/shard_map/ppermute | solution.py:19
  12.3 1.7 %copy-start = (f32[9,8,32,128]{3,2,1,0:T(8,128)}, f32[9,8,32,128]{3,2,1,0:T(8,128)S(1)}, u32[]{:S(2)}) copy-start(f32[9,8,32,128]{3,2,1,0:T(8,128)S(1)} %pad_maximum_fusion.1) | copy-start | bytes 3538948
  12.4 8.2 %collective-permute-start.2 = (f32[10,32,128]{2,1,0:T(8,128)S(1)}, f32[10,32,128]{2,1,0:T(8,128)S(1)}, u32[]{:S(2)}, u32[]{:S(2)}) collective-permute-start(f32[10,32,128]{2,1,0:T(8,128)S(1)} %get-tuple-element.36), channel_id=1, source_target_pairs={{0,4},{4,8},{8,12},{12,16},{16,20},{20,24},{24,28},{28,0},{1,5},{5... | collective-permute-start | bytes 491528 | tf_op jit(solution)/shard_map/ppermute | solution.py:134
  14.0 7.9 %copy-start.8 = (f32[512]{0:T(512)S(1)}, f32[512]{0:T(512)}, u32[]{:S(2)}) copy-start(f32[512]{0:T(512)} %param.19) | copy-start | bytes 6148
  14.0 7.1 %collective-permute-start.3 = (f32[10,32,128]{2,1,0:T(8,128)S(1)}, f32[10,32,128]{2,1,0:T(8,128)S(1)}, u32[]{:S(2)}, u32[]{:S(2)}) collective-permute-start(f32[10,32,128]{2,1,0:T(8,128)S(1)} %get-tuple-element.37), channel_id=1, source_target_pairs={{4,0},{8,4},{12,8},{16,12},{20,16},{24,20},{28,24},{0,28},{5,1},{9... | collective-permute-start | bytes 491528 | tf_op jit(solution)/shard_map/ppermute | solution.py:135
  21.2 3.6 %slice-start = ((f32[9,8,32,128]{3,2,1,0:T(8,128)}), f32[8,8,32,128]{3,2,1,0:T(8,128)S(1)}, s32[]{:S(2)}) async-start(f32[9,8,32,128]{3,2,1,0:T(8,128)} %copy-done), calls=%async_computation | async-start | bytes 2097152 | tf_op jit(solution)/shard_map/slice | solution.py:141
  24.0 3.6 %collective-permute-start.4 = (f32[129]{0:T(256)S(1)}, f32[129]{0:T(256)S(1)}, u32[]{:S(2)}, u32[]{:S(2)}) collective-permute-start(f32[129]{0:T(256)S(1)} %pad_maximum_fusion.5), channel_id=1, source_target_pairs={{0,4},{4,0},{8,12},{12,8},{16,20},{20,16},{24,28},{28,24},{1,5},{5... | collective-permute-start | bytes 1556 | tf_op jit(solution)/shard_map/ppermute | solution.py:67
  28.3 3.6 %collective-permute-start.5 = (f32[129]{0:T(256)S(1)}, f32[129]{0:T(256)S(1)}, u32[]{:S(2)}, u32[]{:S(2)}) collective-permute-start(f32[129]{0:T(256)S(1)} %fusion.125), channel_id=1, source_target_pairs={{0,8},{4,12},{8,0},{12,4},{16,24},{20,28},{24,16},{28,20},{1,9},{5... | collective-permute-start | bytes 1556 | tf_op jit(solution)/shard_map/ppermute | solution.py:67
  31.8 4.5 %collective-permute-start.6 = (f32[129]{0:T(256)S(1)}, f32[129]{0:T(256)S(1)}, u32[]{:S(2)}, u32[]{:S(2)}) collective-permute-start(f32[129]{0:T(256)S(1)} %add.234), channel_id=1, source_target_pairs={{0,16},{4,20},{8,24},{12,28},{16,0},{20,4},{24,8},{28,12},{1,17},{... | collective-permute-start | bytes 1556 | tf_op jit(solution)/shard_map/ppermute | solution.py:67
  36.3 1.7 %collective-permute-start.7 = (f32[129]{0:T(256)S(1)}, f32[129]{0:T(256)S(1)}, u32[]{:S(2)}, u32[]{:S(2)}) collective-permute-start(f32[129]{0:T(256)S(1)} %add.235), channel_id=1, source_target_pairs={{0,1},{1,0},{2,3},{3,2},{4,5},{5,4},{6,7},{7,6},{8,9},{9,8},{10,11... | collective-permute-start | bytes 1556 | tf_op jit(solution)/shard_map/ppermute | solution.py:67
  38.0 5.8 %collective-permute-start.8 = (f32[129]{0:T(256)S(1)}, f32[129]{0:T(256)S(1)}, u32[]{:S(2)}, u32[]{:S(2)}) collective-permute-start(f32[129]{0:T(256)S(1)} %add.236), channel_id=1, source_target_pairs={{0,2},{1,3},{2,0},{3,1},{4,6},{5,7},{6,4},{7,5},{8,10},{9,11},{10,... | collective-permute-start | bytes 1556 | tf_op jit(solution)/shard_map/ppermute | solution.py:67
  50.7 0.7 %copy-start.2 = (f32[4,8,16,128]{3,2,1,0:T(8,128)}, f32[4,8,16,128]{3,2,1,0:T(8,128)S(1)}, u32[]{:S(2)}) copy-start(f32[4,8,16,128]{3,2,1,0:T(8,128)S(1)} %dynamic_update_slice.3) | copy-start | bytes 786436

commit v16 on v14

--- a/solution.py
+++ b/solution.py
@@ -272,10 +272,25 @@
     press_top = late_press[:, :, top]
     sens_base = press_top * (late_rad[:, :, top] + late_push[:, :, top])
     sens_placed = press_top * push_0
-    seg_base = jnp.sum(jnp.where(segment_hot, sens_base[:, :, None], 0.0), axis=(0, 1))
-    seg_placed = jnp.sum(jnp.where(segment_hot, sens_placed[:, :, None], 0.0), axis=(0, 1))
-
-    totals = butterfly_sum(jnp.concatenate([square_sum[None], seg_base, seg_placed]), ("az", "ax"))
+    slot = lax.broadcasted_iota(jnp.int32, (1, 1, 1 + 2 * nseg), 2)
+    first_cell = (lax.broadcasted_iota(jnp.int32, (na, nx, 1), 0) == 0) & (
+        lax.broadcasted_iota(jnp.int32, (na, nx, 1), 1) == 0
+    )
+    seg_here = segment_id[:, :, None]
+    payload = jnp.sum(
+        jnp.where(
+            slot == 0,
+            jnp.where(first_cell, square_sum, 0.0),
+            jnp.where(
+                slot <= nseg,
+                jnp.where(seg_here == slot - 1, sens_base[:, :, None], 0.0),
+                jnp.where(seg_here == slot - 1 - nseg, sens_placed[:, :, None], 0.0),
+            ),
+        ),
+        axis=(0, 1),
+    )
+
+    totals = butterfly_sum(payload, ("az", "ax"))
     mean_sq = totals[0] / mic_az.shape[0] + epsilon
     grad_scale = (na * lax.axis_size("az") * nx * lax.axis_size("ax") / nseg) ** (-0.5)
     liner_grad = (totals[1 : 1 + nseg] + totals[1 + nseg :] / mean_sq) * grad_scale

time: 47.9 us -> 47.3 us (0.987)
  other arithmetic: 6.18 us -> 5.5 us
    select_n x0 -> x1, other arithmetic: none -> 0.72 us  [shards(): jnp.where(first_cell, square_sum, 0.0)]
    concatenate x1 -> x0, other arithmetic: 0.72 us -> none  [shards(): jnp.concatenate([square_sum[None], seg_base, seg_placed])]
    add x5, other arithmetic: 0.73 us -> 0.02 us  [butterfly_sum(): values + lax.ppermute(values, axis, [(i, i ^ step) for i in range(size)])]
where the time goes in v16:
time: 47.3 us; the launch traced here: 47 us
  starting transfers between devices  17.8 us (38%)
  waiting for transfers between devices  15.4 us (33%)
  other arithmetic  5.5 us (12%)
  local copies, waits for them, and re-layouts  5.17 us (11%)
  between operations  3.17 us (7%)
    ppermute x5, waiting for transfers between devices, butterfly_sum(): lax.ppermute(values, axis, [(i, i ^ step) for i in range(size)])  9.23 us
    ppermute x5, starting transfers between devices, butterfly_sum(): lax.ppermute(values, axis, [(i, i ^ step) for i in range(size)])  8.65 us
    ppermute x1, starting transfers between devices, shards(): from_above = lax.ppermute(sent_down, 'az', down)  3.86 us
    ppermute x1, waiting for transfers between devices, with_halo(): lax.ppermute(lax.slice_in_dim(array, 0, after, axis=dim), axis, down)  3.16 us
    ppermute x1, waiting for transfers between devices, shards(): from_below = lax.ppermute(sent_up, 'az', up)  2.48 us
    ppermute x1, starting transfers between devices, with_halo(): lax.ppermute(lax.slice_in_dim(array, length - before, length, axis=dim),...  2.37 us
    ppermute x1, starting transfers between devices, shards(): from_below = lax.ppermute(sent_up, 'az', up)  1.57 us
    unnamed x56, local copies, waits for them, and re-layouts  1.45 us
  transfers between devices with their start and end apart: 9, of which 8 were waited for; matrix products, arithmetic and copies ran while one was open for 5% of the time, Pallas kernels for 0%

profile of v16, /device:TPU:0, one launch (start us, length us, event | category | flops | bytes accessed | tf_op | source)
XLA Modules:
  0.0 47.0 jit_solution(5212393292053598000)
XLA Ops:
  0.7 1.2 %fusion.121 = (f32[1,8,16,1]{3,2,1,0:T(8,128)S(1)}, f32[1,8,16,1]{3,2,1,0:T(8,128)S(1)}, f32[1,8,16,1]{3,2,1,0:T(8,128)S(1)}, f32[1,8,16,1]{3,2,1,0:T(8,128)S(1)}, f32[1,8,16,1]{3,2,1,0:T(8,128)S(1)}) fusion(f32[4,8,16,128]{3,2,1,0:T(8,128)} %param.10), kind=kLoop, calls=%fused_computation.329 | loop fusion | bytes 5120 | tf_op jit(solution)/shard_map/slice | solution.py:105
  4.2 2.4 %collective-permute-start = (f32[9,8,8,128]{3,2,1,0:T(8,128)S(1)}, f32[9,8,8,128]{3,2,1,0:T(8,128)S(1)}, u32[]{:S(2)}, u32[]{:S(2)}) collective-permute-start(f32[9,8,8,128]{3,2,1,0:T(8,128)S(1)} %get-tuple-element.54), channel_id=1, source_target_pairs={{0,1},{1,2},{2,3},{4,5},{5,6},{6,7},{8,9},{9,10},{10,11},{12,13},{... | collective-permute-start | bytes 884744 | tf_op jit(solution)/shard_map/ppermute | solution.py:16
  6.6 1.3 %collective-permute-start.1 = (f32[9,8,8,128]{3,2,1,0:T(8,128)S(1)}, f32[9,8,8,128]{3,2,1,0:T(8,128)S(1)}, u32[]{:S(2)}, u32[]{:S(2)}) collective-permute-start(f32[9,8,8,128]{3,2,1,0:T(8,128)S(1)} %get-tuple-element.55), channel_id=1, source_target_pairs={{1,0},{2,1},{3,2},{5,4},{6,5},{7,6},{9,8},{10,9},{11,10},{13,12},{... | collective-permute-start | bytes 884744 | tf_op jit(solution)/shard_map/ppermute | solution.py:19
  8.2 0.8 %slice_bitcast_fusion.9 = f32[8,16,128]{2,1,0:T(8,128)S(1)} fusion(f32[4,8,16,128]{3,2,1,0:T(8,128)} %param.10), kind=kLoop, calls=%fused_computation.158 | loop fusion | bytes 131072 | tf_op jit(solution)/shard_map/squeeze | solution.py:271
  9.0 3.2 %collective-permute-done.1 = f32[9,8,8,128]{3,2,1,0:T(8,128)S(1)} collective-permute-done((f32[9,8,8,128]{3,2,1,0:T(8,128)S(1)}, f32[9,8,8,128]{3,2,1,0:T(8,128)S(1)}, u32[]{:S(2)}, u32[]{:S(2)}) %collective-permute-start.1) | collective-permute-done | bytes 294944 | tf_op jit(solution)/shard_map/ppermute | solution.py:19
  12.4 1.6 %collective-permute-start.2 = (f32[10,32,128]{2,1,0:T(8,128)S(1)}, f32[10,32,128]{2,1,0:T(8,128)S(1)}, u32[]{:S(2)}, u32[]{:S(2)}) collective-permute-start(f32[10,32,128]{2,1,0:T(8,128)S(1)} %get-tuple-element.34), channel_id=1, source_target_pairs={{0,4},{4,8},{8,12},{12,16},{16,20},{20,24},{24,28},{28,0},{1,5},{5... | collective-permute-start | bytes 491528 | tf_op jit(solution)/shard_map/ppermute | solution.py:134
  14.0 3.9 %collective-permute-start.3 = (f32[10,32,128]{2,1,0:T(8,128)S(1)}, f32[10,32,128]{2,1,0:T(8,128)S(1)}, u32[]{:S(2)}, u32[]{:S(2)}) collective-permute-start(f32[10,32,128]{2,1,0:T(8,128)S(1)} %get-tuple-element.35), channel_id=1, source_target_pairs={{4,0},{8,4},{12,8},{16,12},{20,16},{24,20},{28,24},{0,28},{5,1},{9... | collective-permute-start | bytes 491528 | tf_op jit(solution)/shard_map/ppermute | solution.py:135
  18.1 2.5 %collective-permute-done.2 = f32[10,32,128]{2,1,0:T(8,128)S(1)} collective-permute-done((f32[10,32,128]{2,1,0:T(8,128)S(1)}, f32[10,32,128]{2,1,0:T(8,128)S(1)}, u32[]{:S(2)}, u32[]{:S(2)}) %collective-permute-start.2) | collective-permute-done | bytes 163872 | tf_op jit(solution)/shard_map/ppermute | solution.py:134
  20.6 0.5 %collective-permute-done.3 = f32[10,32,128]{2,1,0:T(8,128)S(1)} collective-permute-done((f32[10,32,128]{2,1,0:T(8,128)S(1)}, f32[10,32,128]{2,1,0:T(8,128)S(1)}, u32[]{:S(2)}, u32[]{:S(2)}) %collective-permute-start.3) | collective-permute-done | bytes 163872 | tf_op jit(solution)/shard_map/ppermute | solution.py:135
  21.9 0.6 %select_reduce_fusion.5 = (f32[]{:T(128)}, f32[512]{0:T(512)S(1)}) fusion(s32[512]{0:T(512)S(1)} %copy-done.4, s32[]{:T(128)S(6)} %mul.402, s32[512]{0:T(512)S(1)} %copy-done.5, s32[]{:T(128)S(6)} %mul.401, f32[512]{0:T(512)S(1)} %select_reduce_fusion.1, f32[512]{0:T(512)S(1)} %copy-done.7), kind=kLoop, calls=%fused_computation.315 | loop fusion | flops 13311 | bytes 10252 | tf_op jit(solution)/shard_map/reduce_sum | solution.py:189
  23.0 0.7 %and_select_fusion = f32[8,16]{1,0:T(8,128)S(1)} fusion(f32[]{:T(128)} %get-tuple-element.16, pred[16]{0:T(512)(128)(4,1)S(1)} %iota_compare_fusion.6, pred[8]{0:T(512)(128)(4,1)S(1)} %iota_compare_fusion.7), kind=kLoop, calls=%fused_computation.309 | loop fusion | flops 256 | bytes 540 | tf_op jit(solution)/shard_map/jit(_where)/select_n | solution.py:283
  24.0 0.7 %collective-permute-start.4 = (f32[129]{0:T(256)S(1)}, f32[129]{0:T(256)S(1)}, u32[]{:S(2)}, u32[]{:S(2)}) collective-permute-start(f32[129]{0:T(256)S(1)} %select_reduce_fusion.2), channel_id=1, source_target_pairs={{0,4},{4,0},{8,12},{12,8},{16,20},{20,16},{24,28},{28,24},{1,5},{5... | collective-permute-start | bytes 1556 | tf_op jit(solution)/shard_map/ppermute | solution.py:67
  25.9 1.7 %collective-permute-done.4 = f32[129]{0:T(256)S(1)} collective-permute-done((f32[129]{0:T(256)S(1)}, f32[129]{0:T(256)S(1)}, u32[]{:S(2)}, u32[]{:S(2)}) %collective-permute-start.4) | collective-permute-done | bytes 548 | tf_op jit(solution)/shard_map/ppermute | solution.py:67
  27.6 0.9 %collective-permute-start.5 = (f32[129]{0:T(256)S(1)}, f32[129]{0:T(256)S(1)}, u32[]{:S(2)}, u32[]{:S(2)}) collective-permute-start(f32[129]{0:T(256)S(1)} %add.248), channel_id=1, source_target_pairs={{0,8},{4,12},{8,0},{12,4},{16,24},{20,28},{24,16},{28,20},{1,9},{5... | collective-permute-start | bytes 1556 | tf_op jit(solution)/shard_map/ppermute | solution.py:67
  28.5 2.7 %collective-permute-done.5 = f32[129]{0:T(256)S(1)} collective-permute-done((f32[129]{0:T(256)S(1)}, f32[129]{0:T(256)S(1)}, u32[]{:S(2)}, u32[]{:S(2)}) %collective-permute-start.5) | collective-permute-done | bytes 548 | tf_op jit(solution)/shard_map/ppermute | solution.py:67
  31.2 1.9 %collective-permute-start.6 = (f32[129]{0:T(256)S(1)}, f32[129]{0:T(256)S(1)}, u32[]{:S(2)}, u32[]{:S(2)}) collective-permute-start(f32[129]{0:T(256)S(1)} %add.249), channel_id=1, source_target_pairs={{0,16},{4,20},{8,24},{12,28},{16,0},{20,4},{24,8},{28,12},{1,17},{... | collective-permute-start | bytes 1556 | tf_op jit(solution)/shard_map/ppermute | solution.py:67
  33.1 2.5 %collective-permute-done.6 = f32[129]{0:T(256)S(1)} collective-permute-done((f32[129]{0:T(256)S(1)}, f32[129]{0:T(256)S(1)}, u32[]{:S(2)}, u32[]{:S(2)}) %collective-permute-start.6) | collective-permute-done | bytes 548 | tf_op jit(solution)/shard_map/ppermute | solution.py:67
  35.7 0.9 %collective-permute-start.7 = (f32[129]{0:T(256)S(1)}, f32[129]{0:T(256)S(1)}, u32[]{:S(2)}, u32[]{:S(2)}) collective-permute-start(f32[129]{0:T(256)S(1)} %add.250), channel_id=1, source_target_pairs={{0,1},{1,0},{2,3},{3,2},{4,5},{5,4},{6,7},{7,6},{8,9},{9,8},{10,11... | collective-permute-start | bytes 1556 | tf_op jit(solution)/shard_map/ppermute | solution.py:67
  36.5 0.8 %collective-permute-done.7 = f32[129]{0:T(256)S(1)} collective-permute-done((f32[129]{0:T(256)S(1)}, f32[129]{0:T(256)S(1)}, u32[]{:S(2)}, u32[]{:S(2)}) %collective-permute-start.7) | collective-permute-done | bytes 548 | tf_op jit(solution)/shard_map/ppermute | solution.py:67
  37.4 4.2 %collective-permute-start.8 = (f32[129]{0:T(256)S(1)}, f32[129]{0:T(256)S(1)}, u32[]{:S(2)}, u32[]{:S(2)}) collective-permute-start(f32[129]{0:T(256)S(1)} %add.251), channel_id=1, source_target_pairs={{0,2},{1,3},{2,0},{3,1},{4,6},{5,7},{6,4},{7,5},{8,10},{9,11},{10,... | collective-permute-start | bytes 1556 | tf_op jit(solution)/shard_map/ppermute | solution.py:67
  41.6 1.5 %collective-permute-done.8 = f32[129]{0:T(256)S(1)} collective-permute-done((f32[129]{0:T(256)S(1)}, f32[129]{0:T(256)S(1)}, u32[]{:S(2)}, u32[]{:S(2)}) %collective-permute-start.8) | collective-permute-done | bytes 548 | tf_op jit(solution)/shard_map/ppermute | solution.py:67
  43.1 0.5 %slice.890 = f32[1]{0:T(128)} slice(f32[129]{0:T(256)S(1)} %add.252), slice={[0:1]} | slice | bytes 8 | tf_op jit(solution)/shard_map/slice | solution.py:294
  44.3 0.6 %fusion.118 = f32[64]{0:T(128)} fusion(f32[129]{0:T(256)S(1)} %add.252, f32[]{:T(128)} %bitcast.83), kind=kLoop, calls=%fused_computation.327 | loop fusion | flops 192 | bytes 772 | tf_op jit(solution)/shard_map/mul | solution.py:296
  45.0 0.9 %maximum_add_fusion = f32[4,8,16,128]{3,2,1,0:T(8,128)} fusion(f32[1,8,16,128]{3,2,1,0:T(8,128)S(1)} %fusion.9, f32[1,8,16,128]{3,2,1,0:T(8,128)S(1)} %fusion.26, f32[1,8,16,128]{3,2,1,0:T(8,128)S(1)} %fusion.35, f32[1,8,16,128]{3,2,1,0:T(8,128)S(1)} %fusion.47, f32[4,8,16]{2,1,0:T(8,128)S(1)} %get-tuple-element.90, f32[4,8,16]{2,1,0:T(8,128)S(1)} %get-tuple-element.89, ...), kind=kLoop, calls=%fused_computation.6 | loop fusion | flops 393216 | bytes 528640 | tf_op jit(solution)/shard_map/add | solution.py:305
  (126 shorter events, 5.3 us)
Async XLA Ops:
  0.6 1.8 %copy-start.2 = (f32[4,8,16,128]{3,2,1,0:T(8,128)S(1)}, f32[4,8,16,128]{3,2,1,0:T(8,128)}, u32[]{:S(2)}) copy-start(f32[4,8,16,128]{3,2,1,0:T(8,128)} %param.12) | copy-start | bytes 786436
  0.6 1.8 %copy-start.1 = (f32[4,8,16,128]{3,2,1,0:T(8,128)S(1)}, f32[4,8,16,128]{3,2,1,0:T(8,128)}, u32[]{:S(2)}) copy-start(f32[4,8,16,128]{3,2,1,0:T(8,128)} %param.11) | copy-start | bytes 786436
  2.5 1.0 %copy-start.3 = (s32[8,16]{1,0:T(8,128)S(1)}, s32[8,16]{1,0:T(8,128)}, u32[]{:S(2)}) copy-start(s32[8,16]{1,0:T(8,128)} %param.14) | copy-start | bytes 1540
  2.5 1.0 %copy-start.8 = (f32[64]{0:T(128)S(1)}, f32[64]{0:T(128)}, u32[]{:S(2)}) copy-start(f32[64]{0:T(128)} %param.13) | copy-start | bytes 772
  2.5 1.1 %copy-start.6 = (s32[8,16]{1,0:T(8,128)S(1)}, s32[8,16]{1,0:T(8,128)}, u32[]{:S(2)}) copy-start(s32[8,16]{1,0:T(8,128)} %param.15) | copy-start | bytes 1540
  2.6 1.1 %copy-start.9 = (f32[64]{0:T(128)S(1)}, f32[64]{0:T(128)}, u32[]{:S(2)}) copy-start(f32[64]{0:T(128)} %param.16) | copy-start | bytes 772
  3.9 4.2 %copy-start.4 = (s32[512]{0:T(512)S(1)}, s32[512]{0:T(512)}, u32[]{:S(2)}) copy-start(s32[512]{0:T(512)} %param.18) | copy-start | bytes 6148
  3.9 4.2 %copy-start.5 = (s32[512]{0:T(512)S(1)}, s32[512]{0:T(512)}, u32[]{:S(2)}) copy-start(s32[512]{0:T(512)} %param.17) | copy-start | bytes 6148
  4.2 4.8 %collective-permute-start = (f32[9,8,8,128]{3,2,1,0:T(8,128)S(1)}, f32[9,8,8,128]{3,2,1,0:T(8,128)S(1)}, u32[]{:S(2)}, u32[]{:S(2)}) collective-permute-start(f32[9,8,8,128]{3,2,1,0:T(8,128)S(1)} %get-tuple-element.54), channel_id=1, source_target_pairs={{0,1},{1,2},{2,3},{4,5},{5,6},{6,7},{8,9},{9,10},{10,11},{12,13},{... | collective-permute-start | bytes 884744 | tf_op jit(solution)/shard_map/ppermute | solution.py:16
  6.6 5.6 %collective-permute-start.1 = (f32[9,8,8,128]{3,2,1,0:T(8,128)S(1)}, f32[9,8,8,128]{3,2,1,0:T(8,128)S(1)}, u32[]{:S(2)}, u32[]{:S(2)}) collective-permute-start(f32[9,8,8,128]{3,2,1,0:T(8,128)S(1)} %get-tuple-element.55), channel_id=1, source_target_pairs={{1,0},{2,1},{3,2},{5,4},{6,5},{7,6},{9,8},{10,9},{11,10},{13,12},{... | collective-permute-start | bytes 884744 | tf_op jit(solution)/shard_map/ppermute | solution.py:19
  12.3 1.7 %copy-start = (f32[9,8,32,128]{3,2,1,0:T(8,128)}, f32[9,8,32,128]{3,2,1,0:T(8,128)S(1)}, u32[]{:S(2)}) copy-start(f32[9,8,32,128]{3,2,1,0:T(8,128)S(1)} %pad_maximum_fusion.1) | copy-start | bytes 3538948
  12.4 8.2 %collective-permute-start.2 = (f32[10,32,128]{2,1,0:T(8,128)S(1)}, f32[10,32,128]{2,1,0:T(8,128)S(1)}, u32[]{:S(2)}, u32[]{:S(2)}) collective-permute-start(f32[10,32,128]{2,1,0:T(8,128)S(1)} %get-tuple-element.34), channel_id=1, source_target_pairs={{0,4},{4,8},{8,12},{12,16},{16,20},{20,24},{24,28},{28,0},{1,5},{5... | collective-permute-start | bytes 491528 | tf_op jit(solution)/shard_map/ppermute | solution.py:134
  14.0 7.9 %copy-start.7 = (f32[512]{0:T(512)S(1)}, f32[512]{0:T(512)}, u32[]{:S(2)}) copy-start(f32[512]{0:T(512)} %param.19) | copy-start | bytes 6148
  14.0 7.1 %collective-permute-start.3 = (f32[10,32,128]{2,1,0:T(8,128)S(1)}, f32[10,32,128]{2,1,0:T(8,128)S(1)}, u32[]{:S(2)}, u32[]{:S(2)}) collective-permute-start(f32[10,32,128]{2,1,0:T(8,128)S(1)} %get-tuple-element.35), channel_id=1, source_target_pairs={{4,0},{8,4},{12,8},{16,12},{20,16},{24,20},{28,24},{0,28},{5,1},{9... | collective-permute-start | bytes 491528 | tf_op jit(solution)/shard_map/ppermute | solution.py:135
  21.2 3.7 %slice-start = ((f32[9,8,32,128]{3,2,1,0:T(8,128)}), f32[8,8,32,128]{3,2,1,0:T(8,128)S(1)}, s32[]{:S(2)}) async-start(f32[9,8,32,128]{3,2,1,0:T(8,128)} %copy-done), calls=%async_computation | async-start | bytes 2097152 | tf_op jit(solution)/shard_map/slice | solution.py:141
  24.0 3.6 %collective-permute-start.4 = (f32[129]{0:T(256)S(1)}, f32[129]{0:T(256)S(1)}, u32[]{:S(2)}, u32[]{:S(2)}) collective-permute-start(f32[129]{0:T(256)S(1)} %select_reduce_fusion.2), channel_id=1, source_target_pairs={{0,4},{4,0},{8,12},{12,8},{16,20},{20,16},{24,28},{28,24},{1,5},{5... | collective-permute-start | bytes 1556 | tf_op jit(solution)/shard_map/ppermute | solution.py:67
  27.6 3.6 %collective-permute-start.5 = (f32[129]{0:T(256)S(1)}, f32[129]{0:T(256)S(1)}, u32[]{:S(2)}, u32[]{:S(2)}) collective-permute-start(f32[129]{0:T(256)S(1)} %add.248), channel_id=1, source_target_pairs={{0,8},{4,12},{8,0},{12,4},{16,24},{20,28},{24,16},{28,20},{1,9},{5... | collective-permute-start | bytes 1556 | tf_op jit(solution)/shard_map/ppermute | solution.py:67
  31.2 4.5 %collective-permute-start.6 = (f32[129]{0:T(256)S(1)}, f32[129]{0:T(256)S(1)}, u32[]{:S(2)}, u32[]{:S(2)}) collective-permute-start(f32[129]{0:T(256)S(1)} %add.249), channel_id=1, source_target_pairs={{0,16},{4,20},{8,24},{12,28},{16,0},{20,4},{24,8},{28,12},{1,17},{... | collective-permute-start | bytes 1556 | tf_op jit(solution)/shard_map/ppermute | solution.py:67
  35.7 1.7 %collective-permute-start.7 = (f32[129]{0:T(256)S(1)}, f32[129]{0:T(256)S(1)}, u32[]{:S(2)}, u32[]{:S(2)}) collective-permute-start(f32[129]{0:T(256)S(1)} %add.250), channel_id=1, source_target_pairs={{0,1},{1,0},{2,3},{3,2},{4,5},{5,4},{6,7},{7,6},{8,9},{9,8},{10,11... | collective-permute-start | bytes 1556 | tf_op jit(solution)/shard_map/ppermute | solution.py:67
  37.4 5.8 %collective-permute-start.8 = (f32[129]{0:T(256)S(1)}, f32[129]{0:T(256)S(1)}, u32[]{:S(2)}, u32[]{:S(2)}) collective-permute-start(f32[129]{0:T(256)S(1)} %add.251), channel_id=1, source_target_pairs={{0,2},{1,3},{2,0},{3,1},{4,6},{5,7},{6,4},{7,5},{8,10},{9,11},{10,... | collective-permute-start | bytes 1556 | tf_op jit(solution)/shard_map/ppermute | solution.py:67

commit v17 on v16

--- a/solution.py
+++ b/solution.py
@@ -56,13 +56,13 @@
     )
 
 
-def butterfly_sum(values, axes):
-    for axis in axes:
+def butterfly_sum(values, axes, skip_first=False):
+    for index, axis in enumerate(axes):
         size = lax.axis_size(axis)
         if size & (size - 1):
             values = lax.psum(values, axis)
             continue
-        step = 1
+        step = 2 if (skip_first and index == 0) else 1
         while step < size:
             values = values + lax.ppermute(values, axis, [(i, i ^ step) for i in range(size)])
             step *= 2
@@ -189,6 +189,73 @@
     square_sum = jnp.sum(jnp.where(owned, misses * misses, 0.0))
     placed = jnp.sum(jnp.where(cell_hot, misses[:, None], 0.0), axis=0).reshape(ea, ex)
 
+    of = (1, tile)
+    g_a0, g_a1, g_a2, g_a3, g_u, g_w, g_b, g_push = [wide_f[i] for i in range(8)]
+
+    def at(field, da, dx):
+        return win(field, of, da, dx, na, nx)
+
+    def head_az(da, dx):
+        return at(g_a1, da, dx) + at(g_push, da, dx) - at(g_push, da + 1, dx)
+
+    def head_ax(da, dx):
+        return at(g_a2, da, dx) + at(g_push, da, dx) - at(g_push, da, dx + 1)
+
+    casing = casing_mask((na, nx, nr))
+
+    def head_rad(da, dx):
+        push_here = at(g_push, da, dx)
+        return at(g_a3, da, dx) + push_here - rad_next(push_here)
+
+    def head_masked(da, dx):
+        return jnp.where(casing, 0.0, head_rad(da, dx))
+
+    def back_advect(head):
+        return 0.5 * (at(g_u, 0, -1) * head(0, -1) - at(g_u, 0, 1) * head(0, 1)) + 0.5 * (
+            at(g_w, -1, 0) * head(-1, 0) - at(g_w, 1, 0) * head(1, 0)
+        )
+
+    def seed(da, dx):
+        return at(g_a0, da, dx)
+
+    backs = [head(0, 0) - step_dt * back_advect(head) for head in (head_az, head_ax, head_masked)]
+    shove_r = step_dt * at(g_b, 0, 0) * head_masked(0, 0)
+    head_rad_own = head_rad(0, 0)
+    back_press = (
+        seed(0, 0)
+        - step_dt * back_advect(seed)
+        + (step_dt * at(g_b, 0, 0) * head_az(0, 0) - step_dt * at(g_b, -1, 0) * head_az(-1, 0))
+        + (step_dt * at(g_b, 0, 0) * head_ax(0, 0) - step_dt * at(g_b, 0, -1) * head_ax(0, -1))
+        + (shove_r - rad_prev(shove_r))
+        + jnp.where(casing, wall[:, :, None] * head_rad_own, 0.0)
+    )
+    base = jnp.stack([back_press] + backs)
+
+    late_rad, late_push, late_press, _ = lax.optimization_barrier((adjoint_in[3], push, acoustic[0], widened))
+    press_top = late_press[:, :, top]
+    sens_base = press_top * (late_rad[:, :, top] + late_push[:, :, top])
+    sens_placed = press_top * (-step_dt * c(s_t, 0, 0, na, nx) * placed[1 : 1 + na, 1 : 1 + nx])
+    slot = lax.broadcasted_iota(jnp.int32, (1, 1, 1 + 2 * nseg), 2)
+    first_cell = (lax.broadcasted_iota(jnp.int32, (na, nx, 1), 0) == 0) & (
+        lax.broadcasted_iota(jnp.int32, (na, nx, 1), 1) == 0
+    )
+    seg_here = segment_id[:, :, None]
+    payload = jnp.sum(
+        jnp.where(
+            slot == 0,
+            jnp.where(first_cell, square_sum, 0.0),
+            jnp.where(
+                slot <= nseg,
+                jnp.where(seg_here == slot - 1, sens_base[:, :, None], 0.0),
+                jnp.where(seg_here == slot - 1 - nseg, sens_placed[:, :, None], 0.0),
+            ),
+        ),
+        axis=(0, 1),
+    )
+
+    size_az = lax.axis_size("az")
+    first_round = payload + lax.ppermute(payload, "az", [(i, i ^ 1) for i in range(size_az)])
+    placed, _ = lax.optimization_barrier((placed, first_round))
     push_e = -step_dt * c(s_t, -1, -1, ea, ex) * placed
     r1a, r1x = na + 2, nx + 2
     head_az_e = push_e[:r1a, :r1x] - push_e[1 : 1 + r1a, :r1x]
@@ -226,71 +293,7 @@
         ]
     )
 
-    of = (1, tile)
-    g_a0, g_a1, g_a2, g_a3, g_u, g_w, g_b, g_push = [wide_f[i] for i in range(8)]
-
-    def at(field, da, dx):
-        return win(field, of, da, dx, na, nx)
-
-    def head_az(da, dx):
-        return at(g_a1, da, dx) + at(g_push, da, dx) - at(g_push, da + 1, dx)
-
-    def head_ax(da, dx):
-        return at(g_a2, da, dx) + at(g_push, da, dx) - at(g_push, da, dx + 1)
-
-    casing = casing_mask((na, nx, nr))
-
-    def head_rad(da, dx):
-        push_here = at(g_push, da, dx)
-        return at(g_a3, da, dx) + push_here - rad_next(push_here)
-
-    def head_masked(da, dx):
-        return jnp.where(casing, 0.0, head_rad(da, dx))
-
-    def back_advect(head):
-        return 0.5 * (at(g_u, 0, -1) * head(0, -1) - at(g_u, 0, 1) * head(0, 1)) + 0.5 * (
-            at(g_w, -1, 0) * head(-1, 0) - at(g_w, 1, 0) * head(1, 0)
-        )
-
-    def seed(da, dx):
-        return at(g_a0, da, dx)
-
-    backs = [head(0, 0) - step_dt * back_advect(head) for head in (head_az, head_ax, head_masked)]
-    shove_r = step_dt * at(g_b, 0, 0) * head_masked(0, 0)
-    head_rad_own = head_rad(0, 0)
-    back_press = (
-        seed(0, 0)
-        - step_dt * back_advect(seed)
-        + (step_dt * at(g_b, 0, 0) * head_az(0, 0) - step_dt * at(g_b, -1, 0) * head_az(-1, 0))
-        + (step_dt * at(g_b, 0, 0) * head_ax(0, 0) - step_dt * at(g_b, 0, -1) * head_ax(0, -1))
-        + (shove_r - rad_prev(shove_r))
-        + jnp.where(casing, wall[:, :, None] * head_rad_own, 0.0)
-    )
-    base = jnp.stack([back_press] + backs)
-
-    late_rad, late_push, late_press, _ = lax.optimization_barrier((adjoint_in[3], push, acoustic[0], widened))
-    press_top = late_press[:, :, top]
-    sens_base = press_top * (late_rad[:, :, top] + late_push[:, :, top])
-    sens_placed = press_top * push_0
-    slot = lax.broadcasted_iota(jnp.int32, (1, 1, 1 + 2 * nseg), 2)
-    first_cell = (lax.broadcasted_iota(jnp.int32, (na, nx, 1), 0) == 0) & (
-        lax.broadcasted_iota(jnp.int32, (na, nx, 1), 1) == 0
-    )
-    seg_here = segment_id[:, :, None]
-    payload = jnp.sum(
-        jnp.where(
-            slot == 0,
-            jnp.where(first_cell, square_sum, 0.0),
-            jnp.where(
-                slot <= nseg,
-                jnp.where(seg_here == slot - 1, sens_base[:, :, None], 0.0),
-                jnp.where(seg_here == slot - 1 - nseg, sens_placed[:, :, None], 0.0),
-            ),
-        ),
-        axis=(0, 1),
-    )
-
-    totals = butterfly_sum(payload, ("az", "ax"))
+    totals = butterfly_sum(first_round, ("az", "ax"), skip_first=True)
     mean_sq = totals[0] / mic_az.shape[0] + epsilon
     grad_scale = (na * lax.axis_size("az") * nx * lax.axis_size("ax") / nseg) ** (-0.5)
     liner_grad = (totals[1 : 1 + nseg] + totals[1 + nseg :] / mean_sq) * grad_scale

time: 47.3 us -> 47 us (level)
    ppermute x5 -> x4, waiting for transfers between devices: 9.23 us -> 7.02 us  [butterfly_sum(): lax.ppermute(values, axis, [(i, i ^ step) for i in range(size)])]
    ppermute x0 -> x1, waiting for transfers between devices: none -> 1.89 us  [shards(): lax.ppermute(payload, 'az', [(i, i ^ 1) for i in range(size_az)])]
    ppermute x5 -> x4, starting transfers between devices: 8.65 us -> 7.92 us  [butterfly_sum(): lax.ppermute(values, axis, [(i, i ^ step) for i in range(size)])]
    ppermute x0 -> x1, starting transfers between devices: none -> 0.73 us  [shards(): lax.ppermute(payload, 'az', [(i, i ^ 1) for i in range(size_az)])]
  transfers between devices with their start and end apart: 9 -> 9, of which waited for: 8 -> 8; matrix products, arithmetic and copies ran while one was open for 5% -> 6% of each run, Pallas kernels for 0% -> 0%
where the time goes in v17:
time: 47 us; the launch traced here: 46.8 us
  starting transfers between devices  17.8 us (38%)
  waiting for transfers between devices  15.1 us (32%)
  other arithmetic  5.58 us (12%)
  local copies, waits for them, and re-layouts  5.17 us (11%)
  between operations  3.18 us (7%)
    ppermute x4, starting transfers between devices, butterfly_sum(): lax.ppermute(values, axis, [(i, i ^ step) for i in range(size)])  7.92 us
    ppermute x4, waiting for transfers between devices, butterfly_sum(): lax.ppermute(values, axis, [(i, i ^ step) for i in range(size)])  7.02 us
    ppermute x1, starting transfers between devices, shards(): from_above = lax.ppermute(sent_down, 'az', down)  3.86 us
    ppermute x1, waiting for transfers between devices, with_halo(): lax.ppermute(lax.slice_in_dim(array, 0, after, axis=dim), axis, down)  3.16 us
    ppermute x1, waiting for transfers between devices, shards(): from_below = lax.ppermute(sent_up, 'az', up)  2.48 us
    ppermute x1, starting transfers between devices, with_halo(): lax.ppermute(lax.slice_in_dim(array, length - before, length, axis=dim),...  2.37 us
    ppermute x1, waiting for transfers between devices, shards(): lax.ppermute(payload, 'az', [(i, i ^ 1) for i in range(size_az)])  1.89 us
    ppermute x1, starting transfers between devices, shards(): from_below = lax.ppermute(sent_up, 'az', up)  1.57 us
  transfers between devices with their start and end apart: 9, of which 8 were waited for; matrix products, arithmetic and copies ran while one was open for 6% of the time, Pallas kernels for 0%

profile of v17, /device:TPU:0, one launch (start us, length us, event | category | flops | bytes accessed | tf_op | source)
XLA Modules:
  0.0 46.8 jit_solution(17610329039321155637)
XLA Ops:
  0.7 1.2 %fusion.122 = (f32[1,8,16,1]{3,2,1,0:T(8,128)S(1)}, f32[1,8,16,1]{3,2,1,0:T(8,128)S(1)}, f32[1,8,16,1]{3,2,1,0:T(8,128)S(1)}, f32[1,8,16,1]{3,2,1,0:T(8,128)S(1)}, f32[1,8,16,1]{3,2,1,0:T(8,128)S(1)}) fusion(f32[4,8,16,128]{3,2,1,0:T(8,128)} %param.10), kind=kLoop, calls=%fused_computation.331 | loop fusion | bytes 5120 | tf_op jit(solution)/shard_map/slice | solution.py:105
  4.2 2.4 %collective-permute-start = (f32[9,8,8,128]{3,2,1,0:T(8,128)S(1)}, f32[9,8,8,128]{3,2,1,0:T(8,128)S(1)}, u32[]{:S(2)}, u32[]{:S(2)}) collective-permute-start(f32[9,8,8,128]{3,2,1,0:T(8,128)S(1)} %get-tuple-element.56), channel_id=1, source_target_pairs={{0,1},{1,2},{2,3},{4,5},{5,6},{6,7},{8,9},{9,10},{10,11},{12,13},{... | collective-permute-start | bytes 884744 | tf_op jit(solution)/shard_map/ppermute | solution.py:16
  6.6 1.3 %collective-permute-start.1 = (f32[9,8,8,128]{3,2,1,0:T(8,128)S(1)}, f32[9,8,8,128]{3,2,1,0:T(8,128)S(1)}, u32[]{:S(2)}, u32[]{:S(2)}) collective-permute-start(f32[9,8,8,128]{3,2,1,0:T(8,128)S(1)} %get-tuple-element.57), channel_id=1, source_target_pairs={{1,0},{2,1},{3,2},{5,4},{6,5},{7,6},{9,8},{10,9},{11,10},{13,12},{... | collective-permute-start | bytes 884744 | tf_op jit(solution)/shard_map/ppermute | solution.py:19
  8.2 0.8 %slice_bitcast_fusion.9 = f32[8,16,128]{2,1,0:T(8,128)S(1)} fusion(f32[4,8,16,128]{3,2,1,0:T(8,128)} %param.10), kind=kLoop, calls=%fused_computation.158 | loop fusion | bytes 131072 | tf_op jit(solution)/shard_map/squeeze | solution.py:234
  9.0 3.2 %collective-permute-done.1 = f32[9,8,8,128]{3,2,1,0:T(8,128)S(1)} collective-permute-done((f32[9,8,8,128]{3,2,1,0:T(8,128)S(1)}, f32[9,8,8,128]{3,2,1,0:T(8,128)S(1)}, u32[]{:S(2)}, u32[]{:S(2)}) %collective-permute-start.1) | collective-permute-done | bytes 294944 | tf_op jit(solution)/shard_map/ppermute | solution.py:19
  12.4 1.6 %collective-permute-start.2 = (f32[10,32,128]{2,1,0:T(8,128)S(1)}, f32[10,32,128]{2,1,0:T(8,128)S(1)}, u32[]{:S(2)}, u32[]{:S(2)}) collective-permute-start(f32[10,32,128]{2,1,0:T(8,128)S(1)} %get-tuple-element.36), channel_id=1, source_target_pairs={{0,4},{4,8},{8,12},{12,16},{16,20},{20,24},{24,28},{28,0},{1,5},{5... | collective-permute-start | bytes 491528 | tf_op jit(solution)/shard_map/ppermute | solution.py:134
  14.0 3.9 %collective-permute-start.3 = (f32[10,32,128]{2,1,0:T(8,128)S(1)}, f32[10,32,128]{2,1,0:T(8,128)S(1)}, u32[]{:S(2)}, u32[]{:S(2)}) collective-permute-start(f32[10,32,128]{2,1,0:T(8,128)S(1)} %get-tuple-element.37), channel_id=1, source_target_pairs={{4,0},{8,4},{12,8},{16,12},{20,16},{24,20},{28,24},{0,28},{5,1},{9... | collective-permute-start | bytes 491528 | tf_op jit(solution)/shard_map/ppermute | solution.py:135
  18.1 2.5 %collective-permute-done.2 = f32[10,32,128]{2,1,0:T(8,128)S(1)} collective-permute-done((f32[10,32,128]{2,1,0:T(8,128)S(1)}, f32[10,32,128]{2,1,0:T(8,128)S(1)}, u32[]{:S(2)}, u32[]{:S(2)}) %collective-permute-start.2) | collective-permute-done | bytes 163872 | tf_op jit(solution)/shard_map/ppermute | solution.py:134
  20.6 0.5 %collective-permute-done.3 = f32[10,32,128]{2,1,0:T(8,128)S(1)} collective-permute-done((f32[10,32,128]{2,1,0:T(8,128)S(1)}, f32[10,32,128]{2,1,0:T(8,128)S(1)}, u32[]{:S(2)}, u32[]{:S(2)}) %collective-permute-start.3) | collective-permute-done | bytes 163872 | tf_op jit(solution)/shard_map/ppermute | solution.py:135
  21.9 0.6 %select_reduce_fusion.5 = (f32[]{:T(128)}, f32[512]{0:T(512)S(1)}) fusion(s32[512]{0:T(512)S(1)} %copy-done.4, s32[]{:T(128)S(6)} %mul.404, s32[512]{0:T(512)S(1)} %copy-done.5, s32[]{:T(128)S(6)} %mul.403, f32[512]{0:T(512)S(1)} %select_reduce_fusion.1, f32[512]{0:T(512)S(1)} %copy-done.7), kind=kLoop, calls=%fused_computation.317 | loop fusion | flops 13311 | bytes 10252 | tf_op jit(solution)/shard_map/reduce_sum | solution.py:189
  22.8 0.7 %and_select_fusion = f32[8,16]{1,0:T(8,128)S(1)} fusion(f32[]{:T(128)} %get-tuple-element.22, pred[16]{0:T(512)(128)(4,1)S(1)} %iota_compare_fusion.6, pred[8]{0:T(512)(128)(4,1)S(1)} %iota_compare_fusion.7), kind=kLoop, calls=%fused_computation.312 | loop fusion | flops 256 | bytes 540 | tf_op jit(solution)/shard_map/jit(_where)/select_n | solution.py:246
  23.7 0.7 %collective-permute-start.4 = (f32[129]{0:T(256)S(1)}, f32[129]{0:T(256)S(1)}, u32[]{:S(2)}, u32[]{:S(2)}) collective-permute-start(f32[129]{0:T(256)S(1)} %select_reduce_fusion.2), channel_id=1, source_target_pairs={{0,4},{4,0},{8,12},{12,8},{16,20},{20,16},{24,28},{28,24},{1,5},{5... | collective-permute-start | bytes 1556 | tf_op jit(solution)/shard_map/ppermute | solution.py:257
  25.5 1.9 %collective-permute-done.4 = f32[129]{0:T(256)S(1)} collective-permute-done((f32[129]{0:T(256)S(1)}, f32[129]{0:T(256)S(1)}, u32[]{:S(2)}, u32[]{:S(2)}) %collective-permute-start.4) | collective-permute-done | bytes 548 | tf_op jit(solution)/shard_map/ppermute | solution.py:257
  27.4 0.9 %collective-permute-start.5 = (f32[129]{0:T(256)S(1)}, f32[129]{0:T(256)S(1)}, u32[]{:S(2)}, u32[]{:S(2)}) collective-permute-start(f32[129]{0:T(256)S(1)} %add.244), channel_id=1, source_target_pairs={{0,8},{4,12},{8,0},{12,4},{16,24},{20,28},{24,16},{28,20},{1,9},{5... | collective-permute-start | bytes 1556 | tf_op jit(solution)/shard_map/ppermute | solution.py:67
  28.8 2.1 %collective-permute-done.5 = f32[129]{0:T(256)S(1)} collective-permute-done((f32[129]{0:T(256)S(1)}, f32[129]{0:T(256)S(1)}, u32[]{:S(2)}, u32[]{:S(2)}) %collective-permute-start.5) | collective-permute-done | bytes 548 | tf_op jit(solution)/shard_map/ppermute | solution.py:67
  30.9 1.9 %collective-permute-start.6 = (f32[129]{0:T(256)S(1)}, f32[129]{0:T(256)S(1)}, u32[]{:S(2)}, u32[]{:S(2)}) collective-permute-start(f32[129]{0:T(256)S(1)} %add.249), channel_id=1, source_target_pairs={{0,16},{4,20},{8,24},{12,28},{16,0},{20,4},{24,8},{28,12},{1,17},{... | collective-permute-start | bytes 1556 | tf_op jit(solution)/shard_map/ppermute | solution.py:67
  32.9 2.5 %collective-permute-done.6 = f32[129]{0:T(256)S(1)} collective-permute-done((f32[129]{0:T(256)S(1)}, f32[129]{0:T(256)S(1)}, u32[]{:S(2)}, u32[]{:S(2)}) %collective-permute-start.6) | collective-permute-done | bytes 548 | tf_op jit(solution)/shard_map/ppermute | solution.py:67
  35.4 0.7 %collective-permute-start.7 = (f32[129]{0:T(256)S(1)}, f32[129]{0:T(256)S(1)}, u32[]{:S(2)}, u32[]{:S(2)}) collective-permute-start(f32[129]{0:T(256)S(1)} %add.250), channel_id=1, source_target_pairs={{0,1},{1,0},{2,3},{3,2},{4,5},{5,4},{6,7},{7,6},{8,9},{9,8},{10,11... | collective-permute-start | bytes 1556 | tf_op jit(solution)/shard_map/ppermute | solution.py:67
  36.1 0.8 %collective-permute-done.7 = f32[129]{0:T(256)S(1)} collective-permute-done((f32[129]{0:T(256)S(1)}, f32[129]{0:T(256)S(1)}, u32[]{:S(2)}, u32[]{:S(2)}) %collective-permute-start.7) | collective-permute-done | bytes 548 | tf_op jit(solution)/shard_map/ppermute | solution.py:67
  36.9 4.5 %collective-permute-start.8 = (f32[129]{0:T(256)S(1)}, f32[129]{0:T(256)S(1)}, u32[]{:S(2)}, u32[]{:S(2)}) collective-permute-start(f32[129]{0:T(256)S(1)} %add.251), channel_id=1, source_target_pairs={{0,2},{1,3},{2,0},{3,1},{4,6},{5,7},{6,4},{7,5},{8,10},{9,11},{10,... | collective-permute-start | bytes 1556 | tf_op jit(solution)/shard_map/ppermute | solution.py:67
  41.4 1.5 %collective-permute-done.8 = f32[129]{0:T(256)S(1)} collective-permute-done((f32[129]{0:T(256)S(1)}, f32[129]{0:T(256)S(1)}, u32[]{:S(2)}, u32[]{:S(2)}) %collective-permute-start.8) | collective-permute-done | bytes 548 | tf_op jit(solution)/shard_map/ppermute | solution.py:67
  42.9 0.5 %slice.898 = f32[1]{0:T(128)} slice(f32[129]{0:T(256)S(1)} %add.252), slice={[0:1]} | slice | bytes 8 | tf_op jit(solution)/shard_map/slice | solution.py:297
  44.1 0.6 %fusion.119 = f32[64]{0:T(128)} fusion(f32[129]{0:T(256)S(1)} %add.252, f32[]{:T(128)} %bitcast.83), kind=kLoop, calls=%fused_computation.329 | loop fusion | flops 192 | bytes 772 | tf_op jit(solution)/shard_map/mul | solution.py:299
  44.7 0.9 %maximum_add_fusion = f32[4,8,16,128]{3,2,1,0:T(8,128)} fusion(f32[1,8,16,128]{3,2,1,0:T(8,128)S(1)} %fusion.9, f32[1,8,16,128]{3,2,1,0:T(8,128)S(1)} %fusion.26, f32[1,8,16,128]{3,2,1,0:T(8,128)S(1)} %fusion.35, f32[1,8,16,128]{3,2,1,0:T(8,128)S(1)} %fusion.47, f32[4,8,16]{2,1,0:T(8,128)S(1)} %get-tuple-element.92, f32[4,8,16]{2,1,0:T(8,128)S(1)} %get-tuple-element.91, ...), kind=kLoop, calls=%fused_computation.6 | loop fusion | flops 393216 | bytes 528640 | tf_op jit(solution)/shard_map/add | solution.py:308
  (127 shorter events, 5.4 us)
Async XLA Ops:
  0.6 1.8 %copy-start.2 = (f32[4,8,16,128]{3,2,1,0:T(8,128)S(1)}, f32[4,8,16,128]{3,2,1,0:T(8,128)}, u32[]{:S(2)}) copy-start(f32[4,8,16,128]{3,2,1,0:T(8,128)} %param.12) | copy-start | bytes 786436
  0.6 1.8 %copy-start.1 = (f32[4,8,16,128]{3,2,1,0:T(8,128)S(1)}, f32[4,8,16,128]{3,2,1,0:T(8,128)}, u32[]{:S(2)}) copy-start(f32[4,8,16,128]{3,2,1,0:T(8,128)} %param.11) | copy-start | bytes 786436
  2.5 1.0 %copy-start.3 = (s32[8,16]{1,0:T(8,128)S(1)}, s32[8,16]{1,0:T(8,128)}, u32[]{:S(2)}) copy-start(s32[8,16]{1,0:T(8,128)} %param.14) | copy-start | bytes 1540
  2.5 1.0 %copy-start.8 = (f32[64]{0:T(128)S(1)}, f32[64]{0:T(128)}, u32[]{:S(2)}) copy-start(f32[64]{0:T(128)} %param.13) | copy-start | bytes 772
  2.5 1.1 %copy-start.6 = (s32[8,16]{1,0:T(8,128)S(1)}, s32[8,16]{1,0:T(8,128)}, u32[]{:S(2)}) copy-start(s32[8,16]{1,0:T(8,128)} %param.15) | copy-start | bytes 1540
  2.6 1.1 %copy-start.9 = (f32[64]{0:T(128)S(1)}, f32[64]{0:T(128)}, u32[]{:S(2)}) copy-start(f32[64]{0:T(128)} %param.16) | copy-start | bytes 772
  3.9 4.2 %copy-start.4 = (s32[512]{0:T(512)S(1)}, s32[512]{0:T(512)}, u32[]{:S(2)}) copy-start(s32[512]{0:T(512)} %param.18) | copy-start | bytes 6148
  3.9 4.2 %copy-start.5 = (s32[512]{0:T(512)S(1)}, s32[512]{0:T(512)}, u32[]{:S(2)}) copy-start(s32[512]{0:T(512)} %param.17) | copy-start | bytes 6148
  4.2 4.8 %collective-permute-start = (f32[9,8,8,128]{3,2,1,0:T(8,128)S(1)}, f32[9,8,8,128]{3,2,1,0:T(8,128)S(1)}, u32[]{:S(2)}, u32[]{:S(2)}) collective-permute-start(f32[9,8,8,128]{3,2,1,0:T(8,128)S(1)} %get-tuple-element.56), channel_id=1, source_target_pairs={{0,1},{1,2},{2,3},{4,5},{5,6},{6,7},{8,9},{9,10},{10,11},{12,13},{... | collective-permute-start | bytes 884744 | tf_op jit(solution)/shard_map/ppermute | solution.py:16
  6.6 5.6 %collective-permute-start.1 = (f32[9,8,8,128]{3,2,1,0:T(8,128)S(1)}, f32[9,8,8,128]{3,2,1,0:T(8,128)S(1)}, u32[]{:S(2)}, u32[]{:S(2)}) collective-permute-start(f32[9,8,8,128]{3,2,1,0:T(8,128)S(1)} %get-tuple-element.57), channel_id=1, source_target_pairs={{1,0},{2,1},{3,2},{5,4},{6,5},{7,6},{9,8},{10,9},{11,10},{13,12},{... | collective-permute-start | bytes 884744 | tf_op jit(solution)/shard_map/ppermute | solution.py:19
  12.3 1.7 %copy-start = (f32[9,8,32,128]{3,2,1,0:T(8,128)}, f32[9,8,32,128]{3,2,1,0:T(8,128)S(1)}, u32[]{:S(2)}) copy-start(f32[9,8,32,128]{3,2,1,0:T(8,128)S(1)} %pad_maximum_fusion.1) | copy-start | bytes 3538948
  12.4 8.2 %collective-permute-start.2 = (f32[10,32,128]{2,1,0:T(8,128)S(1)}, f32[10,32,128]{2,1,0:T(8,128)S(1)}, u32[]{:S(2)}, u32[]{:S(2)}) collective-permute-start(f32[10,32,128]{2,1,0:T(8,128)S(1)} %get-tuple-element.36), channel_id=1, source_target_pairs={{0,4},{4,8},{8,12},{12,16},{16,20},{20,24},{24,28},{28,0},{1,5},{5... | collective-permute-start | bytes 491528 | tf_op jit(solution)/shard_map/ppermute | solution.py:134
  14.0 7.9 %copy-start.7 = (f32[512]{0:T(512)S(1)}, f32[512]{0:T(512)}, u32[]{:S(2)}) copy-start(f32[512]{0:T(512)} %param.19) | copy-start | bytes 6148
  14.0 7.1 %collective-permute-start.3 = (f32[10,32,128]{2,1,0:T(8,128)S(1)}, f32[10,32,128]{2,1,0:T(8,128)S(1)}, u32[]{:S(2)}, u32[]{:S(2)}) collective-permute-start(f32[10,32,128]{2,1,0:T(8,128)S(1)} %get-tuple-element.37), channel_id=1, source_target_pairs={{4,0},{8,4},{12,8},{16,12},{20,16},{24,20},{28,24},{0,28},{5,1},{9... | collective-permute-start | bytes 491528 | tf_op jit(solution)/shard_map/ppermute | solution.py:135
  21.2 3.4 %slice-start = ((f32[9,8,32,128]{3,2,1,0:T(8,128)}), f32[8,8,32,128]{3,2,1,0:T(8,128)S(1)}, s32[]{:S(2)}) async-start(f32[9,8,32,128]{3,2,1,0:T(8,128)} %copy-done), calls=%async_computation | async-start | bytes 2097152 | tf_op jit(solution)/shard_map/slice | solution.py:141
  23.7 3.6 %collective-permute-start.4 = (f32[129]{0:T(256)S(1)}, f32[129]{0:T(256)S(1)}, u32[]{:S(2)}, u32[]{:S(2)}) collective-permute-start(f32[129]{0:T(256)S(1)} %select_reduce_fusion.2), channel_id=1, source_target_pairs={{0,4},{4,0},{8,12},{12,8},{16,20},{20,16},{24,28},{28,24},{1,5},{5... | collective-permute-start | bytes 1556 | tf_op jit(solution)/shard_map/ppermute | solution.py:257
  27.4 3.6 %collective-permute-start.5 = (f32[129]{0:T(256)S(1)}, f32[129]{0:T(256)S(1)}, u32[]{:S(2)}, u32[]{:S(2)}) collective-permute-start(f32[129]{0:T(256)S(1)} %add.244), channel_id=1, source_target_pairs={{0,8},{4,12},{8,0},{12,4},{16,24},{20,28},{24,16},{28,20},{1,9},{5... | collective-permute-start | bytes 1556 | tf_op jit(solution)/shard_map/ppermute | solution.py:67
  30.9 4.5 %collective-permute-start.6 = (f32[129]{0:T(256)S(1)}, f32[129]{0:T(256)S(1)}, u32[]{:S(2)}, u32[]{:S(2)}) collective-permute-start(f32[129]{0:T(256)S(1)} %add.249), channel_id=1, source_target_pairs={{0,16},{4,20},{8,24},{12,28},{16,0},{20,4},{24,8},{28,12},{1,17},{... | collective-permute-start | bytes 1556 | tf_op jit(solution)/shard_map/ppermute | solution.py:67
  35.4 1.5 %collective-permute-start.7 = (f32[129]{0:T(256)S(1)}, f32[129]{0:T(256)S(1)}, u32[]{:S(2)}, u32[]{:S(2)}) collective-permute-start(f32[129]{0:T(256)S(1)} %add.250), channel_id=1, source_target_pairs={{0,1},{1,0},{2,3},{3,2},{4,5},{5,4},{6,7},{7,6},{8,9},{9,8},{10,11... | collective-permute-start | bytes 1556 | tf_op jit(solution)/shard_map/ppermute | solution.py:67
  36.9 6.0 %collective-permute-start.8 = (f32[129]{0:T(256)S(1)}, f32[129]{0:T(256)S(1)}, u32[]{:S(2)}, u32[]{:S(2)}) collective-permute-start(f32[129]{0:T(256)S(1)} %add.251), channel_id=1, source_target_pairs={{0,2},{1,3},{2,0},{3,1},{4,6},{5,7},{6,4},{7,5},{8,10},{9,11},{10,... | collective-permute-start | bytes 1556 | tf_op jit(solution)/shard_map/ppermute | solution.py:67

commit v18 on v17

--- a/solution.py
+++ b/solution.py
@@ -120,7 +120,17 @@
     packed = jnp.pad(jnp.transpose(stack_c, (1, 2, 0)), ((0, 0), (0, 0), (0, nr - n_planes)))
     stack_all = jnp.concatenate([stack_f, packed[None]], axis=0)
     n_f = stack_f.shape[0]
-    widened = with_halo(stack_all, "ax", 2, tile, tile, False)
+    sent_x = jnp.concatenate([stack_all[:5], stack_all[6:]], axis=0)
+    size_ax = lax.axis_size("ax")
+    right = [(i, i + 1) for i in range(size_ax - 1)]
+    left = [(j, i) for i, j in right]
+    length_x = stack_all.shape[2]
+    x_before = lax.ppermute(sent_x[:, :, length_x - tile :], "ax", right)
+    x_after = lax.ppermute(sent_x[:, :, :tile], "ax", left)
+    no_w = jnp.zeros_like(x_before[:1])
+    x_before = jnp.concatenate([x_before[:5], no_w, x_before[5:]], axis=0)
+    x_after = jnp.concatenate([x_after[:5], no_w, x_after[5:]], axis=0)
+    widened = jnp.concatenate([x_before, stack_all, x_after], axis=2)
     size_az, length_a = (lax.axis_size("az"), widened.shape[1])
     up = [(i, (i + 1) % size_az) for i in range(size_az)]
     down = [(j, i) for i, j in up]

time: 47 us -> 46.7 us (level)
  no operation moved by 1% of the time
where the time goes in v18:
time: 46.7 us; the launch traced here: 46.5 us
  starting transfers between devices  17.4 us (37%)
  waiting for transfers between devices  15 us (32%)
  other arithmetic  5.63 us (12%)
  local copies, waits for them, and re-layouts  5.18 us (11%)
  between operations  3.23 us (7%)
    ppermute x4, starting transfers between devices, butterfly_sum(): lax.ppermute(values, axis, [(i, i ^ step) for i in range(size)])  7.61 us
    ppermute x4, waiting for transfers between devices, butterfly_sum(): lax.ppermute(values, axis, [(i, i ^ step) for i in range(size)])  7.02 us
    ppermute x1, starting transfers between devices, shards(): from_above = lax.ppermute(sent_down, 'az', down)  3.86 us
    ppermute x1, waiting for transfers between devices, shards(): x_after = lax.ppermute(sent_x[:, :, :tile], 'ax', left)  3.05 us
    ppermute x1, waiting for transfers between devices, shards(): from_below = lax.ppermute(sent_up, 'az', up)  2.49 us
    ppermute x1, starting transfers between devices, shards(): x_before = lax.ppermute(sent_x[:, :, length_x - tile:], 'ax', right)  2.37 us
    ppermute x1, waiting for transfers between devices, shards(): lax.ppermute(payload, 'az', [(i, i ^ 1) for i in range(size_az)])  1.87 us
    ppermute x1, starting transfers between devices, shards(): from_below = lax.ppermute(sent_up, 'az', up)  1.57 us
  transfers between devices with their start and end apart: 9, of which 8 were waited for; matrix products, arithmetic and copies ran while one was open for 6% of the time, Pallas kernels for 0%

profile of v18, /device:TPU:0, one launch (start us, length us, event | category | flops | bytes accessed | tf_op | source)
XLA Modules:
  0.0 46.5 jit_solution(9228867976235200121)
XLA Ops:
  0.7 1.2 %fusion.126 = (f32[1,8,16,1]{3,2,1,0:T(8,128)S(1)}, f32[1,8,16,1]{3,2,1,0:T(8,128)S(1)}, f32[1,8,16,1]{3,2,1,0:T(8,128)S(1)}, f32[1,8,16,1]{3,2,1,0:T(8,128)S(1)}, f32[1,8,16,1]{3,2,1,0:T(8,128)S(1)}) fusion(f32[4,8,16,128]{3,2,1,0:T(8,128)} %param.10), kind=kLoop, calls=%fused_computation.337 | loop fusion | bytes 5120 | tf_op jit(solution)/shard_map/slice | solution.py:105
  4.2 2.4 %collective-permute-start = (f32[8,8,8,128]{3,2,1,0:T(8,128)S(1)}, f32[8,8,8,128]{3,2,1,0:T(8,128)S(1)}, u32[]{:S(2)}, u32[]{:S(2)}) collective-permute-start(f32[8,8,8,128]{3,2,1,0:T(8,128)S(1)} %get-tuple-element.58), channel_id=1, source_target_pairs={{0,1},{1,2},{2,3},{4,5},{5,6},{6,7},{8,9},{9,10},{10,11},{12,13},{... | collective-permute-start | bytes 786440 | tf_op jit(solution)/shard_map/ppermute | solution.py:128
  6.6 1.3 %collective-permute-start.1 = (f32[8,8,8,128]{3,2,1,0:T(8,128)S(1)}, f32[8,8,8,128]{3,2,1,0:T(8,128)S(1)}, u32[]{:S(2)}, u32[]{:S(2)}) collective-permute-start(f32[8,8,8,128]{3,2,1,0:T(8,128)S(1)} %get-tuple-element.59), channel_id=1, source_target_pairs={{1,0},{2,1},{3,2},{5,4},{6,5},{7,6},{9,8},{10,9},{11,10},{13,12},{... | collective-permute-start | bytes 786440 | tf_op jit(solution)/shard_map/ppermute | solution.py:129
  8.2 0.8 %slice_bitcast_fusion.9 = f32[8,16,128]{2,1,0:T(8,128)S(1)} fusion(f32[4,8,16,128]{3,2,1,0:T(8,128)} %param.10), kind=kLoop, calls=%fused_computation.163 | loop fusion | bytes 131072 | tf_op jit(solution)/shard_map/squeeze | solution.py:244
  9.1 3.1 %collective-permute-done.1 = f32[8,8,8,128]{3,2,1,0:T(8,128)S(1)} collective-permute-done((f32[8,8,8,128]{3,2,1,0:T(8,128)S(1)}, f32[8,8,8,128]{3,2,1,0:T(8,128)S(1)}, u32[]{:S(2)}, u32[]{:S(2)}) %collective-permute-start.1) | collective-permute-done | bytes 262176 | tf_op jit(solution)/shard_map/ppermute | solution.py:129
  12.5 1.6 %collective-permute-start.2 = (f32[10,32,128]{2,1,0:T(8,128)S(1)}, f32[10,32,128]{2,1,0:T(8,128)S(1)}, u32[]{:S(2)}, u32[]{:S(2)}) collective-permute-start(f32[10,32,128]{2,1,0:T(8,128)S(1)} %get-tuple-element.38), channel_id=1, source_target_pairs={{0,4},{4,8},{8,12},{12,16},{16,20},{20,24},{24,28},{28,0},{1,5},{5... | collective-permute-start | bytes 491528 | tf_op jit(solution)/shard_map/ppermute | solution.py:144
  14.1 3.9 %collective-permute-start.3 = (f32[10,32,128]{2,1,0:T(8,128)S(1)}, f32[10,32,128]{2,1,0:T(8,128)S(1)}, u32[]{:S(2)}, u32[]{:S(2)}) collective-permute-start(f32[10,32,128]{2,1,0:T(8,128)S(1)} %get-tuple-element.39), channel_id=1, source_target_pairs={{4,0},{8,4},{12,8},{16,12},{20,16},{24,20},{28,24},{0,28},{5,1},{9... | collective-permute-start | bytes 491528 | tf_op jit(solution)/shard_map/ppermute | solution.py:145
  18.1 2.5 %collective-permute-done.2 = f32[10,32,128]{2,1,0:T(8,128)S(1)} collective-permute-done((f32[10,32,128]{2,1,0:T(8,128)S(1)}, f32[10,32,128]{2,1,0:T(8,128)S(1)}, u32[]{:S(2)}, u32[]{:S(2)}) %collective-permute-start.2) | collective-permute-done | bytes 163872 | tf_op jit(solution)/shard_map/ppermute | solution.py:144
  20.6 0.5 %collective-permute-done.3 = f32[10,32,128]{2,1,0:T(8,128)S(1)} collective-permute-done((f32[10,32,128]{2,1,0:T(8,128)S(1)}, f32[10,32,128]{2,1,0:T(8,128)S(1)}, u32[]{:S(2)}, u32[]{:S(2)}) %collective-permute-start.3) | collective-permute-done | bytes 163872 | tf_op jit(solution)/shard_map/ppermute | solution.py:145
  22.0 0.6 %select_reduce_fusion.5 = (f32[]{:T(128)}, f32[512]{0:T(512)S(1)}) fusion(s32[512]{0:T(512)S(1)} %copy-done.4, s32[]{:T(128)S(6)} %mul.404, s32[512]{0:T(512)S(1)} %copy-done.5, s32[]{:T(128)S(6)} %mul.403, f32[512]{0:T(512)S(1)} %select_reduce_fusion.1, f32[512]{0:T(512)S(1)} %copy-done.7), kind=kLoop, calls=%fused_computation.323 | loop fusion | flops 13311 | bytes 10252 | tf_op jit(solution)/shard_map/reduce_sum | solution.py:199
  22.9 0.7 %and_select_fusion = f32[8,16]{1,0:T(8,128)S(1)} fusion(f32[]{:T(128)} %get-tuple-element.22, pred[16]{0:T(512)(128)(4,1)S(1)} %iota_compare_fusion.7, pred[8]{0:T(512)(128)(4,1)S(1)} %iota_compare_fusion.8), kind=kLoop, calls=%fused_computation.318 | loop fusion | flops 256 | bytes 540 | tf_op jit(solution)/shard_map/jit(_where)/select_n | solution.py:256
  23.7 0.7 %collective-permute-start.4 = (f32[129]{0:T(256)S(1)}, f32[129]{0:T(256)S(1)}, u32[]{:S(2)}, u32[]{:S(2)}) collective-permute-start(f32[129]{0:T(256)S(1)} %select_reduce_fusion.2), channel_id=1, source_target_pairs={{0,4},{4,0},{8,12},{12,8},{16,20},{20,16},{24,28},{28,24},{1,5},{5... | collective-permute-start | bytes 1556 | tf_op jit(solution)/shard_map/ppermute | solution.py:267
  25.5 1.9 %collective-permute-done.4 = f32[129]{0:T(256)S(1)} collective-permute-done((f32[129]{0:T(256)S(1)}, f32[129]{0:T(256)S(1)}, u32[]{:S(2)}, u32[]{:S(2)}) %collective-permute-start.4) | collective-permute-done | bytes 548 | tf_op jit(solution)/shard_map/ppermute | solution.py:267
  27.4 0.9 %collective-permute-start.5 = (f32[129]{0:T(256)S(1)}, f32[129]{0:T(256)S(1)}, u32[]{:S(2)}, u32[]{:S(2)}) collective-permute-start(f32[129]{0:T(256)S(1)} %add.244), channel_id=1, source_target_pairs={{0,8},{4,12},{8,0},{12,4},{16,24},{20,28},{24,16},{28,20},{1,9},{5... | collective-permute-start | bytes 1556 | tf_op jit(solution)/shard_map/ppermute | solution.py:67
  28.8 2.1 %collective-permute-done.5 = f32[129]{0:T(256)S(1)} collective-permute-done((f32[129]{0:T(256)S(1)}, f32[129]{0:T(256)S(1)}, u32[]{:S(2)}, u32[]{:S(2)}) %collective-permute-start.5) | collective-permute-done | bytes 548 | tf_op jit(solution)/shard_map/ppermute | solution.py:67
  31.0 1.9 %collective-permute-start.6 = (f32[129]{0:T(256)S(1)}, f32[129]{0:T(256)S(1)}, u32[]{:S(2)}, u32[]{:S(2)}) collective-permute-start(f32[129]{0:T(256)S(1)} %add.249), channel_id=1, source_target_pairs={{0,16},{4,20},{8,24},{12,28},{16,0},{20,4},{24,8},{28,12},{1,17},{... | collective-permute-start | bytes 1556 | tf_op jit(solution)/shard_map/ppermute | solution.py:67
  32.9 2.5 %collective-permute-done.6 = f32[129]{0:T(256)S(1)} collective-permute-done((f32[129]{0:T(256)S(1)}, f32[129]{0:T(256)S(1)}, u32[]{:S(2)}, u32[]{:S(2)}) %collective-permute-start.6) | collective-permute-done | bytes 548 | tf_op jit(solution)/shard_map/ppermute | solution.py:67
  35.4 0.4 collective-permute-start.7
  35.8 0.8 %collective-permute-done.7 = f32[129]{0:T(256)S(1)} collective-permute-done((f32[129]{0:T(256)S(1)}, f32[129]{0:T(256)S(1)}, u32[]{:S(2)}, u32[]{:S(2)}) %collective-permute-start.7) | collective-permute-done | bytes 548 | tf_op jit(solution)/shard_map/ppermute | solution.py:67
  36.6 4.4 %collective-permute-start.8 = (f32[129]{0:T(256)S(1)}, f32[129]{0:T(256)S(1)}, u32[]{:S(2)}, u32[]{:S(2)}) collective-permute-start(f32[129]{0:T(256)S(1)} %add.251), channel_id=1, source_target_pairs={{0,2},{1,3},{2,0},{3,1},{4,6},{5,7},{6,4},{7,5},{8,10},{9,11},{10,... | collective-permute-start | bytes 1556 | tf_op jit(solution)/shard_map/ppermute | solution.py:67
  41.1 1.5 %collective-permute-done.8 = f32[129]{0:T(256)S(1)} collective-permute-done((f32[129]{0:T(256)S(1)}, f32[129]{0:T(256)S(1)}, u32[]{:S(2)}, u32[]{:S(2)}) %collective-permute-start.8) | collective-permute-done | bytes 548 | tf_op jit(solution)/shard_map/ppermute | solution.py:67
  42.6 0.5 %slice.923 = f32[1]{0:T(128)} slice(f32[129]{0:T(256)S(1)} %add.252), slice={[0:1]} | slice | bytes 8 | tf_op jit(solution)/shard_map/slice | solution.py:307
  43.8 0.6 %fusion.122 = f32[64]{0:T(128)} fusion(f32[129]{0:T(256)S(1)} %add.252, f32[]{:T(128)} %bitcast.83), kind=kLoop, calls=%fused_computation.335 | loop fusion | flops 192 | bytes 772 | tf_op jit(solution)/shard_map/mul | solution.py:309
  44.4 0.9 %maximum_add_fusion = f32[4,8,16,128]{3,2,1,0:T(8,128)} fusion(f32[1,8,16,128]{3,2,1,0:T(8,128)S(1)} %fusion.12, f32[1,8,16,128]{3,2,1,0:T(8,128)S(1)} %fusion.29, f32[1,8,16,128]{3,2,1,0:T(8,128)S(1)} %fusion.38, f32[1,8,16,128]{3,2,1,0:T(8,128)S(1)} %fusion.50, f32[4,8,16]{2,1,0:T(8,128)S(1)} %get-tuple-element.96, f32[4,8,16]{2,1,0:T(8,128)S(1)} %get-tuple-element.95, ...), kind=kLoop, calls=%fused_computation.11 | loop fusion | flops 393216 | bytes 528640 | tf_op jit(solution)/shard_map/add | solution.py:318
  (133 shorter events, 5.5 us)
Async XLA Ops:
  0.6 1.8 %copy-start.1 = (f32[4,8,16,128]{3,2,1,0:T(8,128)S(1)}, f32[4,8,16,128]{3,2,1,0:T(8,128)}, u32[]{:S(2)}) copy-start(f32[4,8,16,128]{3,2,1,0:T(8,128)} %param.12) | copy-start | bytes 786436
  0.6 1.8 %copy-start.2 = (f32[4,8,16,128]{3,2,1,0:T(8,128)S(1)}, f32[4,8,16,128]{3,2,1,0:T(8,128)}, u32[]{:S(2)}) copy-start(f32[4,8,16,128]{3,2,1,0:T(8,128)} %param.11) | copy-start | bytes 786436
  2.5 1.0 %copy-start.3 = (s32[8,16]{1,0:T(8,128)S(1)}, s32[8,16]{1,0:T(8,128)}, u32[]{:S(2)}) copy-start(s32[8,16]{1,0:T(8,128)} %param.14) | copy-start | bytes 1540
  2.5 1.0 %copy-start.8 = (f32[64]{0:T(128)S(1)}, f32[64]{0:T(128)}, u32[]{:S(2)}) copy-start(f32[64]{0:T(128)} %param.13) | copy-start | bytes 772
  2.6 1.1 %copy-start.6 = (s32[8,16]{1,0:T(8,128)S(1)}, s32[8,16]{1,0:T(8,128)}, u32[]{:S(2)}) copy-start(s32[8,16]{1,0:T(8,128)} %param.15) | copy-start | bytes 1540
  2.6 1.1 %copy-start.9 = (f32[64]{0:T(128)S(1)}, f32[64]{0:T(128)}, u32[]{:S(2)}) copy-start(f32[64]{0:T(128)} %param.16) | copy-start | bytes 772
  4.1 3.9 %copy-start.4 = (s32[512]{0:T(512)S(1)}, s32[512]{0:T(512)}, u32[]{:S(2)}) copy-start(s32[512]{0:T(512)} %param.18) | copy-start | bytes 6148
  4.1 3.9 %copy-start.5 = (s32[512]{0:T(512)S(1)}, s32[512]{0:T(512)}, u32[]{:S(2)}) copy-start(s32[512]{0:T(512)} %param.17) | copy-start | bytes 6148
  4.2 4.8 %collective-permute-start = (f32[8,8,8,128]{3,2,1,0:T(8,128)S(1)}, f32[8,8,8,128]{3,2,1,0:T(8,128)S(1)}, u32[]{:S(2)}, u32[]{:S(2)}) collective-permute-start(f32[8,8,8,128]{3,2,1,0:T(8,128)S(1)} %get-tuple-element.58), channel_id=1, source_target_pairs={{0,1},{1,2},{2,3},{4,5},{5,6},{6,7},{8,9},{9,10},{10,11},{12,13},{... | collective-permute-start | bytes 786440 | tf_op jit(solution)/shard_map/ppermute | solution.py:128
  6.6 5.5 %collective-permute-start.1 = (f32[8,8,8,128]{3,2,1,0:T(8,128)S(1)}, f32[8,8,8,128]{3,2,1,0:T(8,128)S(1)}, u32[]{:S(2)}, u32[]{:S(2)}) collective-permute-start(f32[8,8,8,128]{3,2,1,0:T(8,128)S(1)} %get-tuple-element.59), channel_id=1, source_target_pairs={{1,0},{2,1},{3,2},{5,4},{6,5},{7,6},{9,8},{10,9},{11,10},{13,12},{... | collective-permute-start | bytes 786440 | tf_op jit(solution)/shard_map/ppermute | solution.py:129
  12.3 1.7 %copy-start = (f32[9,8,32,128]{3,2,1,0:T(8,128)}, f32[9,8,32,128]{3,2,1,0:T(8,128)S(1)}, u32[]{:S(2)}) copy-start(f32[9,8,32,128]{3,2,1,0:T(8,128)S(1)} %maximum_maximum_fusion) | copy-start | bytes 3538948
  12.5 8.2 %collective-permute-start.2 = (f32[10,32,128]{2,1,0:T(8,128)S(1)}, f32[10,32,128]{2,1,0:T(8,128)S(1)}, u32[]{:S(2)}, u32[]{:S(2)}) collective-permute-start(f32[10,32,128]{2,1,0:T(8,128)S(1)} %get-tuple-element.38), channel_id=1, source_target_pairs={{0,4},{4,8},{8,12},{12,16},{16,20},{20,24},{24,28},{28,0},{1,5},{5... | collective-permute-start | bytes 491528 | tf_op jit(solution)/shard_map/ppermute | solution.py:144
  14.0 7.9 %copy-start.7 = (f32[512]{0:T(512)S(1)}, f32[512]{0:T(512)}, u32[]{:S(2)}) copy-start(f32[512]{0:T(512)} %param.19) | copy-start | bytes 6148
  14.1 7.1 %collective-permute-start.3 = (f32[10,32,128]{2,1,0:T(8,128)S(1)}, f32[10,32,128]{2,1,0:T(8,128)S(1)}, u32[]{:S(2)}, u32[]{:S(2)}) collective-permute-start(f32[10,32,128]{2,1,0:T(8,128)S(1)} %get-tuple-element.39), channel_id=1, source_target_pairs={{4,0},{8,4},{12,8},{16,12},{20,16},{24,20},{28,24},{0,28},{5,1},{9... | collective-permute-start | bytes 491528 | tf_op jit(solution)/shard_map/ppermute | solution.py:145
  21.2 3.5 %slice-start = ((f32[9,8,32,128]{3,2,1,0:T(8,128)}), f32[8,8,32,128]{3,2,1,0:T(8,128)S(1)}, s32[]{:S(2)}) async-start(f32[9,8,32,128]{3,2,1,0:T(8,128)} %copy-done), calls=%async_computation | async-start | bytes 2097152 | tf_op jit(solution)/shard_map/slice | solution.py:151
  23.7 3.6 %collective-permute-start.4 = (f32[129]{0:T(256)S(1)}, f32[129]{0:T(256)S(1)}, u32[]{:S(2)}, u32[]{:S(2)}) collective-permute-start(f32[129]{0:T(256)S(1)} %select_reduce_fusion.2), channel_id=1, source_target_pairs={{0,4},{4,0},{8,12},{12,8},{16,20},{20,16},{24,28},{28,24},{1,5},{5... | collective-permute-start | bytes 1556 | tf_op jit(solution)/shard_map/ppermute | solution.py:267
  27.4 3.6 %collective-permute-start.5 = (f32[129]{0:T(256)S(1)}, f32[129]{0:T(256)S(1)}, u32[]{:S(2)}, u32[]{:S(2)}) collective-permute-start(f32[129]{0:T(256)S(1)} %add.244), channel_id=1, source_target_pairs={{0,8},{4,12},{8,0},{12,4},{16,24},{20,28},{24,16},{28,20},{1,9},{5... | collective-permute-start | bytes 1556 | tf_op jit(solution)/shard_map/ppermute | solution.py:67
  31.0 4.5 %collective-permute-start.6 = (f32[129]{0:T(256)S(1)}, f32[129]{0:T(256)S(1)}, u32[]{:S(2)}, u32[]{:S(2)}) collective-permute-start(f32[129]{0:T(256)S(1)} %add.249), channel_id=1, source_target_pairs={{0,16},{4,20},{8,24},{12,28},{16,0},{20,4},{24,8},{28,12},{1,17},{... | collective-permute-start | bytes 1556 | tf_op jit(solution)/shard_map/ppermute | solution.py:67
  35.4 1.2 %collective-permute-start.7 = (f32[129]{0:T(256)S(1)}, f32[129]{0:T(256)S(1)}, u32[]{:S(2)}, u32[]{:S(2)}) collective-permute-start(f32[129]{0:T(256)S(1)} %add.250), channel_id=1, source_target_pairs={{0,1},{1,0},{2,3},{3,2},{4,5},{5,4},{6,7},{7,6},{8,9},{9,8},{10,11... | collective-permute-start | bytes 1556 | tf_op jit(solution)/shard_map/ppermute | solution.py:67
  36.6 6.0 %collective-permute-start.8 = (f32[129]{0:T(256)S(1)}, f32[129]{0:T(256)S(1)}, u32[]{:S(2)}, u32[]{:S(2)}) collective-permute-start(f32[129]{0:T(256)S(1)} %add.251), channel_id=1, source_target_pairs={{0,2},{1,3},{2,0},{3,1},{4,6},{5,7},{6,4},{7,5},{8,10},{9,11},{10,... | collective-permute-start | bytes 1556 | tf_op jit(solution)/shard_map/ppermute | solution.py:67

commit v19 on v18

--- a/solution.py
+++ b/solution.py
@@ -126,10 +126,10 @@
     left = [(j, i) for i, j in right]
     length_x = stack_all.shape[2]
     x_before = lax.ppermute(sent_x[:, :, length_x - tile :], "ax", right)
-    x_after = lax.ppermute(sent_x[:, :, :tile], "ax", left)
+    x_after = lax.ppermute(jnp.concatenate([sent_x[:5, :, :tile], sent_x[6:, :, :tile]]), "ax", left)
     no_w = jnp.zeros_like(x_before[:1])
     x_before = jnp.concatenate([x_before[:5], no_w, x_before[5:]], axis=0)
-    x_after = jnp.concatenate([x_after[:5], no_w, x_after[5:]], axis=0)
+    x_after = jnp.concatenate([x_after[:5], no_w, no_w, x_after[5:]], axis=0)
     widened = jnp.concatenate([x_before, stack_all, x_after], axis=2)
     size_az, length_a = (lax.axis_size("az"), widened.shape[1])
     up = [(i, (i + 1) % size_az) for i in range(size_az)]

time: 46.7 us -> 46.5 us (level)
    ppermute x4, starting transfers between devices: 7.61 us -> 7.12 us  [butterfly_sum(): lax.ppermute(values, axis, [(i, i ^ step) for i in range(size)])]
    unnamed x56 -> x55, local copies, waits for them, and re-layouts: 1.45 us -> 1.43 us
where the time goes in v19:
time: 46.5 us; the launch traced here: 46.3 us
  starting transfers between devices  17 us (37%)
  waiting for transfers between devices  15 us (32%)
  other arithmetic  5.78 us (12%)
  local copies, waits for them, and re-layouts  5.22 us (11%)
  between operations  3.25 us (7%)
    ppermute x4, waiting for transfers between devices, butterfly_sum(): lax.ppermute(values, axis, [(i, i ^ step) for i in range(size)])  7.21 us
    ppermute x4, starting transfers between devices, butterfly_sum(): lax.ppermute(values, axis, [(i, i ^ step) for i in range(size)])  7.12 us
    ppermute x1, starting transfers between devices, shards(): from_above = lax.ppermute(sent_down, 'az', down)  3.86 us
    ppermute x1, waiting for transfers between devices, shards(): lax.ppermute(jnp.concatenate([sent_x[:5, :, :tile], sent_x[6:, :, :tile]]...  2.94 us
    ppermute x1, waiting for transfers between devices, shards(): from_below = lax.ppermute(sent_up, 'az', up)  2.48 us
    ppermute x1, starting transfers between devices, shards(): x_before = lax.ppermute(sent_x[:, :, length_x - tile:], 'ax', right)  2.37 us
    ppermute x1, waiting for transfers between devices, shards(): lax.ppermute(payload, 'az', [(i, i ^ 1) for i in range(size_az)])  1.84 us
    ppermute x1, starting transfers between devices, shards(): from_below = lax.ppermute(sent_up, 'az', up)  1.57 us
  transfers between devices with their start and end apart: 9, of which 8 were waited for; matrix products, arithmetic and copies ran while one was open for 6% of the time, Pallas kernels for 0%

profile of v19, /device:TPU:0, one launch (start us, length us, event | category | flops | bytes accessed | tf_op | source)
XLA Modules:
  0.0 46.3 jit_solution(17830792588727779728)
XLA Ops:
  0.7 1.2 %fusion.125 = (f32[1,8,16,1]{3,2,1,0:T(8,128)S(1)}, f32[1,8,16,1]{3,2,1,0:T(8,128)S(1)}, f32[1,8,16,1]{3,2,1,0:T(8,128)S(1)}, f32[1,8,16,1]{3,2,1,0:T(8,128)S(1)}, f32[1,8,16,1]{3,2,1,0:T(8,128)S(1)}) fusion(f32[4,8,16,128]{3,2,1,0:T(8,128)} %param.10), kind=kLoop, calls=%fused_computation.342 | loop fusion | bytes 5120 | tf_op jit(solution)/shard_map/slice | solution.py:105
  3.0 0.2 copy.133
  4.2 2.4 %collective-permute-start = (f32[8,8,8,128]{3,2,1,0:T(8,128)S(1)}, f32[8,8,8,128]{3,2,1,0:T(8,128)S(1)}, u32[]{:S(2)}, u32[]{:S(2)}) collective-permute-start(f32[8,8,8,128]{3,2,1,0:T(8,128)S(1)} %pad_maximum_fusion.1), channel_id=1, source_target_pairs={{0,1},{1,2},{2,3},{4,5},{5,6},{6,7},{8,9},{9,10},{10,11},{12,13},{... | collective-permute-start | bytes 786440 | tf_op jit(solution)/shard_map/ppermute | solution.py:128
  6.6 1.3 %collective-permute-start.1 = (f32[7,8,8,128]{3,2,1,0:T(8,128)S(1)}, f32[7,8,8,128]{3,2,1,0:T(8,128)S(1)}, u32[]{:S(2)}, u32[]{:S(2)}) collective-permute-start(f32[7,8,8,128]{3,2,1,0:T(8,128)S(1)} %fusion.1), channel_id=1, source_target_pairs={{1,0},{2,1},{3,2},{5,4},{6,5},{7,6},{9,8},{10,9},{11,10},{13,12},{... | collective-permute-start | bytes 688136 | tf_op jit(solution)/shard_map/ppermute | solution.py:129
  8.3 0.8 %slice_bitcast_fusion.9 = f32[8,16,128]{2,1,0:T(8,128)S(1)} fusion(f32[4,8,16,128]{3,2,1,0:T(8,128)} %param.10), kind=kLoop, calls=%fused_computation.168 | loop fusion | bytes 131072 | tf_op jit(solution)/shard_map/squeeze | solution.py:244
  9.1 2.9 %collective-permute-done.1 = f32[7,8,8,128]{3,2,1,0:T(8,128)S(1)} collective-permute-done((f32[7,8,8,128]{3,2,1,0:T(8,128)S(1)}, f32[7,8,8,128]{3,2,1,0:T(8,128)S(1)}, u32[]{:S(2)}, u32[]{:S(2)}) %collective-permute-start.1) | collective-permute-done | bytes 229408 | tf_op jit(solution)/shard_map/ppermute | solution.py:129
  12.5 1.6 %collective-permute-start.2 = (f32[10,32,128]{2,1,0:T(8,128)S(1)}, f32[10,32,128]{2,1,0:T(8,128)S(1)}, u32[]{:S(2)}, u32[]{:S(2)}) collective-permute-start(f32[10,32,128]{2,1,0:T(8,128)S(1)} %get-tuple-element.38), channel_id=1, source_target_pairs={{0,4},{4,8},{8,12},{12,16},{16,20},{20,24},{24,28},{28,0},{1,5},{5... | collective-permute-start | bytes 491528 | tf_op jit(solution)/shard_map/ppermute | solution.py:144
  14.2 3.9 %collective-permute-start.3 = (f32[10,32,128]{2,1,0:T(8,128)S(1)}, f32[10,32,128]{2,1,0:T(8,128)S(1)}, u32[]{:S(2)}, u32[]{:S(2)}) collective-permute-start(f32[10,32,128]{2,1,0:T(8,128)S(1)} %get-tuple-element.39), channel_id=1, source_target_pairs={{4,0},{8,4},{12,8},{16,12},{20,16},{24,20},{28,24},{0,28},{5,1},{9... | collective-permute-start | bytes 491528 | tf_op jit(solution)/shard_map/ppermute | solution.py:145
  18.2 2.5 %collective-permute-done.2 = f32[10,32,128]{2,1,0:T(8,128)S(1)} collective-permute-done((f32[10,32,128]{2,1,0:T(8,128)S(1)}, f32[10,32,128]{2,1,0:T(8,128)S(1)}, u32[]{:S(2)}, u32[]{:S(2)}) %collective-permute-start.2) | collective-permute-done | bytes 163872 | tf_op jit(solution)/shard_map/ppermute | solution.py:144
  20.7 0.5 %collective-permute-done.3 = f32[10,32,128]{2,1,0:T(8,128)S(1)} collective-permute-done((f32[10,32,128]{2,1,0:T(8,128)S(1)}, f32[10,32,128]{2,1,0:T(8,128)S(1)}, u32[]{:S(2)}, u32[]{:S(2)}) %collective-permute-start.3) | collective-permute-done | bytes 163872 | tf_op jit(solution)/shard_map/ppermute | solution.py:145
  22.0 0.6 %select_reduce_fusion.5 = (f32[]{:T(128)}, f32[512]{0:T(512)S(1)}) fusion(s32[512]{0:T(512)S(1)} %copy-done.4, s32[]{:T(128)S(6)} %mul.404, s32[512]{0:T(512)S(1)} %copy-done.5, s32[]{:T(128)S(6)} %mul.403, f32[512]{0:T(512)S(1)} %select_reduce_fusion.1, f32[512]{0:T(512)S(1)} %copy-done.7), kind=kLoop, calls=%fused_computation.328 | loop fusion | flops 13311 | bytes 10252 | tf_op jit(solution)/shard_map/reduce_sum | solution.py:199
  23.0 0.7 %and_select_fusion = f32[8,16]{1,0:T(8,128)S(1)} fusion(f32[]{:T(128)} %get-tuple-element.22, pred[16]{0:T(512)(128)(4,1)S(1)} %iota_compare_fusion.7, pred[8]{0:T(512)(128)(4,1)S(1)} %iota_compare_fusion.8), kind=kLoop, calls=%fused_computation.323 | loop fusion | flops 256 | bytes 540 | tf_op jit(solution)/shard_map/jit(_where)/select_n | solution.py:256
  23.8 0.8 %collective-permute-start.4 = (f32[129]{0:T(256)S(1)}, f32[129]{0:T(256)S(1)}, u32[]{:S(2)}, u32[]{:S(2)}) collective-permute-start(f32[129]{0:T(256)S(1)} %select_reduce_fusion.2), channel_id=1, source_target_pairs={{0,4},{4,0},{8,12},{12,8},{16,20},{20,16},{24,28},{28,24},{1,5},{5... | collective-permute-start | bytes 1556 | tf_op jit(solution)/shard_map/ppermute | solution.py:267
  25.6 1.8 %collective-permute-done.4 = f32[129]{0:T(256)S(1)} collective-permute-done((f32[129]{0:T(256)S(1)}, f32[129]{0:T(256)S(1)}, u32[]{:S(2)}, u32[]{:S(2)}) %collective-permute-start.4) | collective-permute-done | bytes 548 | tf_op jit(solution)/shard_map/ppermute | solution.py:267
  27.5 0.9 %collective-permute-start.5 = (f32[129]{0:T(256)S(1)}, f32[129]{0:T(256)S(1)}, u32[]{:S(2)}, u32[]{:S(2)}) collective-permute-start(f32[129]{0:T(256)S(1)} %add.244), channel_id=1, source_target_pairs={{0,8},{4,12},{8,0},{12,4},{16,24},{20,28},{24,16},{28,20},{1,9},{5... | collective-permute-start | bytes 1556 | tf_op jit(solution)/shard_map/ppermute | solution.py:67
  28.9 2.1 %collective-permute-done.5 = f32[129]{0:T(256)S(1)} collective-permute-done((f32[129]{0:T(256)S(1)}, f32[129]{0:T(256)S(1)}, u32[]{:S(2)}, u32[]{:S(2)}) %collective-permute-start.5) | collective-permute-done | bytes 548 | tf_op jit(solution)/shard_map/ppermute | solution.py:67
  31.0 1.9 %collective-permute-start.6 = (f32[129]{0:T(256)S(1)}, f32[129]{0:T(256)S(1)}, u32[]{:S(2)}, u32[]{:S(2)}) collective-permute-start(f32[129]{0:T(256)S(1)} %add.249), channel_id=1, source_target_pairs={{0,16},{4,20},{8,24},{12,28},{16,0},{20,4},{24,8},{28,12},{1,17},{... | collective-permute-start | bytes 1556 | tf_op jit(solution)/shard_map/ppermute | solution.py:67
  33.0 2.5 %collective-permute-done.6 = f32[129]{0:T(256)S(1)} collective-permute-done((f32[129]{0:T(256)S(1)}, f32[129]{0:T(256)S(1)}, u32[]{:S(2)}, u32[]{:S(2)}) %collective-permute-start.6) | collective-permute-done | bytes 548 | tf_op jit(solution)/shard_map/ppermute | solution.py:67
  35.6 1.0 %collective-permute-done.7 = f32[129]{0:T(256)S(1)} collective-permute-done((f32[129]{0:T(256)S(1)}, f32[129]{0:T(256)S(1)}, u32[]{:S(2)}, u32[]{:S(2)}) %collective-permute-start.7) | collective-permute-done | bytes 548 | tf_op jit(solution)/shard_map/ppermute | solution.py:67
  36.7 4.2 %collective-permute-start.8 = (f32[129]{0:T(256)S(1)}, f32[129]{0:T(256)S(1)}, u32[]{:S(2)}, u32[]{:S(2)}) collective-permute-start(f32[129]{0:T(256)S(1)} %add.251), channel_id=1, source_target_pairs={{0,2},{1,3},{2,0},{3,1},{4,6},{5,7},{6,4},{7,5},{8,10},{9,11},{10,... | collective-permute-start | bytes 1556 | tf_op jit(solution)/shard_map/ppermute | solution.py:67
  40.8 1.5 %collective-permute-done.8 = f32[129]{0:T(256)S(1)} collective-permute-done((f32[129]{0:T(256)S(1)}, f32[129]{0:T(256)S(1)}, u32[]{:S(2)}, u32[]{:S(2)}) %collective-permute-start.8) | collective-permute-done | bytes 548 | tf_op jit(solution)/shard_map/ppermute | solution.py:67
  42.4 0.5 %slice.929 = f32[1]{0:T(128)} slice(f32[129]{0:T(256)S(1)} %add.252), slice={[0:1]} | slice | bytes 8 | tf_op jit(solution)/shard_map/slice | solution.py:307
  43.6 0.6 %fusion.121 = f32[64]{0:T(128)} fusion(f32[129]{0:T(256)S(1)} %add.252, f32[]{:T(128)} %bitcast.83), kind=kLoop, calls=%fused_computation.340 | loop fusion | flops 192 | bytes 772 | tf_op jit(solution)/shard_map/mul | solution.py:309
  44.2 0.9 %maximum_add_fusion = f32[4,8,16,128]{3,2,1,0:T(8,128)} fusion(f32[1,8,16,128]{3,2,1,0:T(8,128)S(1)} %fusion.11, f32[1,8,16,128]{3,2,1,0:T(8,128)S(1)} %fusion.28, f32[1,8,16,128]{3,2,1,0:T(8,128)S(1)} %fusion.37, f32[1,8,16,128]{3,2,1,0:T(8,128)S(1)} %fusion.49, f32[4,8,16]{2,1,0:T(8,128)S(1)} %get-tuple-element.94, f32[4,8,16]{2,1,0:T(8,128)S(1)} %get-tuple-element.93, ...), kind=kLoop, calls=%fused_computation.12 | loop fusion | flops 393216 | bytes 528640 | tf_op jit(solution)/shard_map/add | solution.py:318
  (137 shorter events, 5.5 us)
Async XLA Ops:
  0.6 1.8 %copy-start.1 = (f32[4,8,16,128]{3,2,1,0:T(8,128)S(1)}, f32[4,8,16,128]{3,2,1,0:T(8,128)}, u32[]{:S(2)}) copy-start(f32[4,8,16,128]{3,2,1,0:T(8,128)} %param.12) | copy-start | bytes 786436
  0.6 1.8 %copy-start.2 = (f32[4,8,16,128]{3,2,1,0:T(8,128)S(1)}, f32[4,8,16,128]{3,2,1,0:T(8,128)}, u32[]{:S(2)}) copy-start(f32[4,8,16,128]{3,2,1,0:T(8,128)} %param.11) | copy-start | bytes 786436
  2.5 1.0 %copy-start.3 = (s32[8,16]{1,0:T(8,128)S(1)}, s32[8,16]{1,0:T(8,128)}, u32[]{:S(2)}) copy-start(s32[8,16]{1,0:T(8,128)} %param.14) | copy-start | bytes 1540
  2.5 1.0 %copy-start.8 = (f32[64]{0:T(128)S(1)}, f32[64]{0:T(128)}, u32[]{:S(2)}) copy-start(f32[64]{0:T(128)} %param.13) | copy-start | bytes 772
  2.6 1.1 %copy-start.6 = (s32[8,16]{1,0:T(8,128)S(1)}, s32[8,16]{1,0:T(8,128)}, u32[]{:S(2)}) copy-start(s32[8,16]{1,0:T(8,128)} %param.15) | copy-start | bytes 1540
  2.6 1.1 %copy-start.9 = (f32[64]{0:T(128)S(1)}, f32[64]{0:T(128)}, u32[]{:S(2)}) copy-start(f32[64]{0:T(128)} %param.16) | copy-start | bytes 772
  4.1 3.9 %copy-start.4 = (s32[512]{0:T(512)S(1)}, s32[512]{0:T(512)}, u32[]{:S(2)}) copy-start(s32[512]{0:T(512)} %param.18) | copy-start | bytes 6148
  4.1 3.9 %copy-start.5 = (s32[512]{0:T(512)S(1)}, s32[512]{0:T(512)}, u32[]{:S(2)}) copy-start(s32[512]{0:T(512)} %param.17) | copy-start | bytes 6148
  4.2 7.9 %collective-permute-start = (f32[8,8,8,128]{3,2,1,0:T(8,128)S(1)}, f32[8,8,8,128]{3,2,1,0:T(8,128)S(1)}, u32[]{:S(2)}, u32[]{:S(2)}) collective-permute-start(f32[8,8,8,128]{3,2,1,0:T(8,128)S(1)} %pad_maximum_fusion.1), channel_id=1, source_target_pairs={{0,1},{1,2},{2,3},{4,5},{5,6},{6,7},{8,9},{9,10},{10,11},{12,13},{... | collective-permute-start | bytes 786440 | tf_op jit(solution)/shard_map/ppermute | solution.py:128
  6.6 5.5 %collective-permute-start.1 = (f32[7,8,8,128]{3,2,1,0:T(8,128)S(1)}, f32[7,8,8,128]{3,2,1,0:T(8,128)S(1)}, u32[]{:S(2)}, u32[]{:S(2)}) collective-permute-start(f32[7,8,8,128]{3,2,1,0:T(8,128)S(1)} %fusion.1), channel_id=1, source_target_pairs={{1,0},{2,1},{3,2},{5,4},{6,5},{7,6},{9,8},{10,9},{11,10},{13,12},{... | collective-permute-start | bytes 688136 | tf_op jit(solution)/shard_map/ppermute | solution.py:129
  12.4 1.7 %copy-start = (f32[9,8,32,128]{3,2,1,0:T(8,128)}, f32[9,8,32,128]{3,2,1,0:T(8,128)S(1)}, u32[]{:S(2)}) copy-start(f32[9,8,32,128]{3,2,1,0:T(8,128)S(1)} %maximum_maximum_fusion) | copy-start | bytes 3538948
  12.5 8.2 %collective-permute-start.2 = (f32[10,32,128]{2,1,0:T(8,128)S(1)}, f32[10,32,128]{2,1,0:T(8,128)S(1)}, u32[]{:S(2)}, u32[]{:S(2)}) collective-permute-start(f32[10,32,128]{2,1,0:T(8,128)S(1)} %get-tuple-element.38), channel_id=1, source_target_pairs={{0,4},{4,8},{8,12},{12,16},{16,20},{20,24},{24,28},{28,0},{1,5},{5... | collective-permute-start | bytes 491528 | tf_op jit(solution)/shard_map/ppermute | solution.py:144
  14.1 7.9 %copy-start.7 = (f32[512]{0:T(512)S(1)}, f32[512]{0:T(512)}, u32[]{:S(2)}) copy-start(f32[512]{0:T(512)} %param.19) | copy-start | bytes 6148
  14.2 7.1 %collective-permute-start.3 = (f32[10,32,128]{2,1,0:T(8,128)S(1)}, f32[10,32,128]{2,1,0:T(8,128)S(1)}, u32[]{:S(2)}, u32[]{:S(2)}) collective-permute-start(f32[10,32,128]{2,1,0:T(8,128)S(1)} %get-tuple-element.39), channel_id=1, source_target_pairs={{4,0},{8,4},{12,8},{16,12},{20,16},{24,20},{28,24},{0,28},{5,1},{9... | collective-permute-start | bytes 491528 | tf_op jit(solution)/shard_map/ppermute | solution.py:145
  21.3 3.5 %slice-start = ((f32[9,8,32,128]{3,2,1,0:T(8,128)}), f32[8,8,32,128]{3,2,1,0:T(8,128)S(1)}, s32[]{:S(2)}) async-start(f32[9,8,32,128]{3,2,1,0:T(8,128)} %copy-done), calls=%async_computation | async-start | bytes 2097152 | tf_op jit(solution)/shard_map/slice | solution.py:151
  23.8 3.6 %collective-permute-start.4 = (f32[129]{0:T(256)S(1)}, f32[129]{0:T(256)S(1)}, u32[]{:S(2)}, u32[]{:S(2)}) collective-permute-start(f32[129]{0:T(256)S(1)} %select_reduce_fusion.2), channel_id=1, source_target_pairs={{0,4},{4,0},{8,12},{12,8},{16,20},{20,16},{24,28},{28,24},{1,5},{5... | collective-permute-start | bytes 1556 | tf_op jit(solution)/shard_map/ppermute | solution.py:267
  27.5 3.6 %collective-permute-start.5 = (f32[129]{0:T(256)S(1)}, f32[129]{0:T(256)S(1)}, u32[]{:S(2)}, u32[]{:S(2)}) collective-permute-start(f32[129]{0:T(256)S(1)} %add.244), channel_id=1, source_target_pairs={{0,8},{4,12},{8,0},{12,4},{16,24},{20,28},{24,16},{28,20},{1,9},{5... | collective-permute-start | bytes 1556 | tf_op jit(solution)/shard_map/ppermute | solution.py:67
  31.0 4.5 %collective-permute-start.6 = (f32[129]{0:T(256)S(1)}, f32[129]{0:T(256)S(1)}, u32[]{:S(2)}, u32[]{:S(2)}) collective-permute-start(f32[129]{0:T(256)S(1)} %add.249), channel_id=1, source_target_pairs={{0,16},{4,20},{8,24},{12,28},{16,0},{20,4},{24,8},{28,12},{1,17},{... | collective-permute-start | bytes 1556 | tf_op jit(solution)/shard_map/ppermute | solution.py:67
  35.5 1.1 %collective-permute-start.7 = (f32[129]{0:T(256)S(1)}, f32[129]{0:T(256)S(1)}, u32[]{:S(2)}, u32[]{:S(2)}) collective-permute-start(f32[129]{0:T(256)S(1)} %add.250), channel_id=1, source_target_pairs={{0,1},{1,0},{2,3},{3,2},{4,5},{5,4},{6,7},{7,6},{8,9},{9,8},{10,11... | collective-permute-start | bytes 1556 | tf_op jit(solution)/shard_map/ppermute | solution.py:67
  36.7 5.7 %collective-permute-start.8 = (f32[129]{0:T(256)S(1)}, f32[129]{0:T(256)S(1)}, u32[]{:S(2)}, u32[]{:S(2)}) collective-permute-start(f32[129]{0:T(256)S(1)} %add.251), channel_id=1, source_target_pairs={{0,2},{1,3},{2,0},{3,1},{4,6},{5,7},{6,4},{7,5},{8,10},{9,11},{10,... | collective-permute-start | bytes 1556 | tf_op jit(solution)/shard_map/ppermute | solution.py:67

commit v20 on v19

--- a/solution.py
+++ b/solution.py
@@ -62,7 +62,7 @@
         if size & (size - 1):
             values = lax.psum(values, axis)
             continue
-        step = 2 if (skip_first and index == 0) else 1
+        step = 2 if (skip_first and axis == "az") else 1
         while step < size:
             values = values + lax.ppermute(values, axis, [(i, i ^ step) for i in range(size)])
             step *= 2
@@ -303,7 +303,7 @@
         ]
     )
 
-    totals = butterfly_sum(first_round, ("az", "ax"), skip_first=True)
+    totals = butterfly_sum(first_round, ("ax", "az"), skip_first=True)
     mean_sq = totals[0] / mic_az.shape[0] + epsilon
     grad_scale = (na * lax.axis_size("az") * nx * lax.axis_size("ax") / nseg) ** (-0.5)
     liner_grad = (totals[1 : 1 + nseg] + totals[1 + nseg :] / mean_sq) * grad_scale

time: 46.5 us -> 46.5 us (level)
  starting transfers between devices: 17 us -> 17.5 us
  waiting for transfers between devices: 15 us -> 14.5 us
    ppermute x4, starting transfers between devices: 7.12 us -> 7.6 us  [butterfly_sum(): lax.ppermute(values, axis, [(i, i ^ step) for i in range(size)])]
    ppermute x4, waiting for transfers between devices: 7.21 us -> 6.72 us  [butterfly_sum(): lax.ppermute(values, axis, [(i, i ^ step) for i in range(size)])]
where the time goes in v20:
time: 46.5 us; the launch traced here: 46.3 us
  starting transfers between devices  17.5 us (38%)
  waiting for transfers between devices  14.5 us (31%)
  other arithmetic  5.78 us (12%)
  local copies, waits for them, and re-layouts  5.22 us (11%)
  between operations  3.25 us (7%)
    ppermute x4, starting transfers between devices, butterfly_sum(): lax.ppermute(values, axis, [(i, i ^ step) for i in range(size)])  7.6 us
    ppermute x4, waiting for transfers between devices, butterfly_sum(): lax.ppermute(values, axis, [(i, i ^ step) for i in range(size)])  6.72 us
    ppermute x1, starting transfers between devices, shards(): from_above = lax.ppermute(sent_down, 'az', down)  3.86 us
    ppermute x1, waiting for transfers between devices, shards(): lax.ppermute(jnp.concatenate([sent_x[:5, :, :tile], sent_x[6:, :, :tile]]...  2.94 us
    ppermute x1, waiting for transfers between devices, shards(): from_below = lax.ppermute(sent_up, 'az', up)  2.48 us
    ppermute x1, starting transfers between devices, shards(): x_before = lax.ppermute(sent_x[:, :, length_x - tile:], 'ax', right)  2.37 us
    ppermute x1, waiting for transfers between devices, shards(): lax.ppermute(payload, 'az', [(i, i ^ 1) for i in range(size_az)])  1.84 us
    ppermute x1, starting transfers between devices, shards(): from_below = lax.ppermute(sent_up, 'az', up)  1.57 us
  transfers between devices with their start and end apart: 9, of which 8 were waited for; matrix products, arithmetic and copies ran while one was open for 6% of the time, Pallas kernels for 0%

profile of v20, /device:TPU:0, one launch (start us, length us, event | category | flops | bytes accessed | tf_op | source)
XLA Modules:
  0.0 46.3 jit_solution(15314785484960782456)
XLA Ops:
  0.7 1.2 %fusion.125 = (f32[1,8,16,1]{3,2,1,0:T(8,128)S(1)}, f32[1,8,16,1]{3,2,1,0:T(8,128)S(1)}, f32[1,8,16,1]{3,2,1,0:T(8,128)S(1)}, f32[1,8,16,1]{3,2,1,0:T(8,128)S(1)}, f32[1,8,16,1]{3,2,1,0:T(8,128)S(1)}) fusion(f32[4,8,16,128]{3,2,1,0:T(8,128)} %param.10), kind=kLoop, calls=%fused_computation.342 | loop fusion | bytes 5120 | tf_op jit(solution)/shard_map/slice | solution.py:105
  4.2 2.4 %collective-permute-start = (f32[8,8,8,128]{3,2,1,0:T(8,128)S(1)}, f32[8,8,8,128]{3,2,1,0:T(8,128)S(1)}, u32[]{:S(2)}, u32[]{:S(2)}) collective-permute-start(f32[8,8,8,128]{3,2,1,0:T(8,128)S(1)} %pad_maximum_fusion.1), channel_id=1, source_target_pairs={{0,1},{1,2},{2,3},{4,5},{5,6},{6,7},{8,9},{9,10},{10,11},{12,13},{... | collective-permute-start | bytes 786440 | tf_op jit(solution)/shard_map/ppermute | solution.py:128
  6.6 1.3 %collective-permute-start.1 = (f32[7,8,8,128]{3,2,1,0:T(8,128)S(1)}, f32[7,8,8,128]{3,2,1,0:T(8,128)S(1)}, u32[]{:S(2)}, u32[]{:S(2)}) collective-permute-start(f32[7,8,8,128]{3,2,1,0:T(8,128)S(1)} %fusion.1), channel_id=1, source_target_pairs={{1,0},{2,1},{3,2},{5,4},{6,5},{7,6},{9,8},{10,9},{11,10},{13,12},{... | collective-permute-start | bytes 688136 | tf_op jit(solution)/shard_map/ppermute | solution.py:129
  8.3 0.8 %slice_bitcast_fusion.9 = f32[8,16,128]{2,1,0:T(8,128)S(1)} fusion(f32[4,8,16,128]{3,2,1,0:T(8,128)} %param.10), kind=kLoop, calls=%fused_computation.168 | loop fusion | bytes 131072 | tf_op jit(solution)/shard_map/squeeze | solution.py:244
  9.1 2.9 %collective-permute-done.1 = f32[7,8,8,128]{3,2,1,0:T(8,128)S(1)} collective-permute-done((f32[7,8,8,128]{3,2,1,0:T(8,128)S(1)}, f32[7,8,8,128]{3,2,1,0:T(8,128)S(1)}, u32[]{:S(2)}, u32[]{:S(2)}) %collective-permute-start.1) | collective-permute-done | bytes 229408 | tf_op jit(solution)/shard_map/ppermute | solution.py:129
  12.5 1.6 %collective-permute-start.2 = (f32[10,32,128]{2,1,0:T(8,128)S(1)}, f32[10,32,128]{2,1,0:T(8,128)S(1)}, u32[]{:S(2)}, u32[]{:S(2)}) collective-permute-start(f32[10,32,128]{2,1,0:T(8,128)S(1)} %get-tuple-element.38), channel_id=1, source_target_pairs={{0,4},{4,8},{8,12},{12,16},{16,20},{20,24},{24,28},{28,0},{1,5},{5... | collective-permute-start | bytes 491528 | tf_op jit(solution)/shard_map/ppermute | solution.py:144
  14.2 3.9 %collective-permute-start.3 = (f32[10,32,128]{2,1,0:T(8,128)S(1)}, f32[10,32,128]{2,1,0:T(8,128)S(1)}, u32[]{:S(2)}, u32[]{:S(2)}) collective-permute-start(f32[10,32,128]{2,1,0:T(8,128)S(1)} %get-tuple-element.39), channel_id=1, source_target_pairs={{4,0},{8,4},{12,8},{16,12},{20,16},{24,20},{28,24},{0,28},{5,1},{9... | collective-permute-start | bytes 491528 | tf_op jit(solution)/shard_map/ppermute | solution.py:145
  18.2 2.5 %collective-permute-done.2 = f32[10,32,128]{2,1,0:T(8,128)S(1)} collective-permute-done((f32[10,32,128]{2,1,0:T(8,128)S(1)}, f32[10,32,128]{2,1,0:T(8,128)S(1)}, u32[]{:S(2)}, u32[]{:S(2)}) %collective-permute-start.2) | collective-permute-done | bytes 163872 | tf_op jit(solution)/shard_map/ppermute | solution.py:144
  20.7 0.5 %collective-permute-done.3 = f32[10,32,128]{2,1,0:T(8,128)S(1)} collective-permute-done((f32[10,32,128]{2,1,0:T(8,128)S(1)}, f32[10,32,128]{2,1,0:T(8,128)S(1)}, u32[]{:S(2)}, u32[]{:S(2)}) %collective-permute-start.3) | collective-permute-done | bytes 163872 | tf_op jit(solution)/shard_map/ppermute | solution.py:145
  22.0 0.6 %select_reduce_fusion.5 = (f32[]{:T(128)}, f32[512]{0:T(512)S(1)}) fusion(s32[512]{0:T(512)S(1)} %copy-done.4, s32[]{:T(128)S(6)} %mul.404, s32[512]{0:T(512)S(1)} %copy-done.5, s32[]{:T(128)S(6)} %mul.403, f32[512]{0:T(512)S(1)} %select_reduce_fusion.1, f32[512]{0:T(512)S(1)} %copy-done.7), kind=kLoop, calls=%fused_computation.328 | loop fusion | flops 13311 | bytes 10252 | tf_op jit(solution)/shard_map/reduce_sum | solution.py:199
  23.0 0.7 %and_select_fusion = f32[8,16]{1,0:T(8,128)S(1)} fusion(f32[]{:T(128)} %get-tuple-element.22, pred[16]{0:T(512)(128)(4,1)S(1)} %iota_compare_fusion.7, pred[8]{0:T(512)(128)(4,1)S(1)} %iota_compare_fusion.8), kind=kLoop, calls=%fused_computation.323 | loop fusion | flops 256 | bytes 540 | tf_op jit(solution)/shard_map/jit(_where)/select_n | solution.py:256
  23.8 0.8 %collective-permute-start.4 = (f32[129]{0:T(256)S(1)}, f32[129]{0:T(256)S(1)}, u32[]{:S(2)}, u32[]{:S(2)}) collective-permute-start(f32[129]{0:T(256)S(1)} %select_reduce_fusion.2), channel_id=1, source_target_pairs={{0,4},{4,0},{8,12},{12,8},{16,20},{20,16},{24,28},{28,24},{1,5},{5... | collective-permute-start | bytes 1556 | tf_op jit(solution)/shard_map/ppermute | solution.py:267
  25.6 1.8 %collective-permute-done.4 = f32[129]{0:T(256)S(1)} collective-permute-done((f32[129]{0:T(256)S(1)}, f32[129]{0:T(256)S(1)}, u32[]{:S(2)}, u32[]{:S(2)}) %collective-permute-start.4) | collective-permute-done | bytes 548 | tf_op jit(solution)/shard_map/ppermute | solution.py:267
  27.5 2.3 %collective-permute-start.5 = (f32[129]{0:T(256)S(1)}, f32[129]{0:T(256)S(1)}, u32[]{:S(2)}, u32[]{:S(2)}) collective-permute-start(f32[129]{0:T(256)S(1)} %add.244), channel_id=1, source_target_pairs={{0,1},{1,0},{2,3},{3,2},{4,5},{5,4},{6,7},{7,6},{8,9},{9,8},{10,11... | collective-permute-start | bytes 1556 | tf_op jit(solution)/shard_map/ppermute | solution.py:67
  30.4 0.3 collective-permute-done.5
  30.6 2.2 %collective-permute-start.6 = (f32[129]{0:T(256)S(1)}, f32[129]{0:T(256)S(1)}, u32[]{:S(2)}, u32[]{:S(2)}) collective-permute-start(f32[129]{0:T(256)S(1)} %add.249), channel_id=1, source_target_pairs={{0,2},{1,3},{2,0},{3,1},{4,6},{5,7},{6,4},{7,5},{8,10},{9,11},{10,... | collective-permute-start | bytes 1556 | tf_op jit(solution)/shard_map/ppermute | solution.py:67
  32.8 1.5 %collective-permute-done.6 = f32[129]{0:T(256)S(1)} collective-permute-done((f32[129]{0:T(256)S(1)}, f32[129]{0:T(256)S(1)}, u32[]{:S(2)}, u32[]{:S(2)}) %collective-permute-start.6) | collective-permute-done | bytes 548 | tf_op jit(solution)/shard_map/ppermute | solution.py:67
  34.3 0.9 %collective-permute-start.7 = (f32[129]{0:T(256)S(1)}, f32[129]{0:T(256)S(1)}, u32[]{:S(2)}, u32[]{:S(2)}) collective-permute-start(f32[129]{0:T(256)S(1)} %add.250), channel_id=1, source_target_pairs={{0,8},{4,12},{8,0},{12,4},{16,24},{20,28},{24,16},{28,20},{1,9},{5... | collective-permute-start | bytes 1556 | tf_op jit(solution)/shard_map/ppermute | solution.py:67
  35.2 2.7 %collective-permute-done.7 = f32[129]{0:T(256)S(1)} collective-permute-done((f32[129]{0:T(256)S(1)}, f32[129]{0:T(256)S(1)}, u32[]{:S(2)}, u32[]{:S(2)}) %collective-permute-start.7) | collective-permute-done | bytes 548 | tf_op jit(solution)/shard_map/ppermute | solution.py:67
  37.9 2.2 %collective-permute-start.8 = (f32[129]{0:T(256)S(1)}, f32[129]{0:T(256)S(1)}, u32[]{:S(2)}, u32[]{:S(2)}) collective-permute-start(f32[129]{0:T(256)S(1)} %add.251), channel_id=1, source_target_pairs={{0,16},{4,20},{8,24},{12,28},{16,0},{20,4},{24,8},{28,12},{1,17},{... | collective-permute-start | bytes 1556 | tf_op jit(solution)/shard_map/ppermute | solution.py:67
  40.2 2.2 %collective-permute-done.8 = f32[129]{0:T(256)S(1)} collective-permute-done((f32[129]{0:T(256)S(1)}, f32[129]{0:T(256)S(1)}, u32[]{:S(2)}, u32[]{:S(2)}) %collective-permute-start.8) | collective-permute-done | bytes 548 | tf_op jit(solution)/shard_map/ppermute | solution.py:67
  42.4 0.5 %slice.929 = f32[1]{0:T(128)} slice(f32[129]{0:T(256)S(1)} %add.252), slice={[0:1]} | slice | bytes 8 | tf_op jit(solution)/shard_map/slice | solution.py:307
  43.6 0.6 %fusion.121 = f32[64]{0:T(128)} fusion(f32[129]{0:T(256)S(1)} %add.252, f32[]{:T(128)} %bitcast.83), kind=kLoop, calls=%fused_computation.340 | loop fusion | flops 192 | bytes 772 | tf_op jit(solution)/shard_map/mul | solution.py:309
  44.2 0.9 %maximum_add_fusion = f32[4,8,16,128]{3,2,1,0:T(8,128)} fusion(f32[1,8,16,128]{3,2,1,0:T(8,128)S(1)} %fusion.11, f32[1,8,16,128]{3,2,1,0:T(8,128)S(1)} %fusion.28, f32[1,8,16,128]{3,2,1,0:T(8,128)S(1)} %fusion.37, f32[1,8,16,128]{3,2,1,0:T(8,128)S(1)} %fusion.49, f32[4,8,16]{2,1,0:T(8,128)S(1)} %get-tuple-element.94, f32[4,8,16]{2,1,0:T(8,128)S(1)} %get-tuple-element.93, ...), kind=kLoop, calls=%fused_computation.12 | loop fusion | flops 393216 | bytes 528640 | tf_op jit(solution)/shard_map/add | solution.py:318
  (137 shorter events, 5.6 us)
Async XLA Ops:
  0.6 1.8 %copy-start.1 = (f32[4,8,16,128]{3,2,1,0:T(8,128)S(1)}, f32[4,8,16,128]{3,2,1,0:T(8,128)}, u32[]{:S(2)}) copy-start(f32[4,8,16,128]{3,2,1,0:T(8,128)} %param.12) | copy-start | bytes 786436
  0.6 1.8 %copy-start.2 = (f32[4,8,16,128]{3,2,1,0:T(8,128)S(1)}, f32[4,8,16,128]{3,2,1,0:T(8,128)}, u32[]{:S(2)}) copy-start(f32[4,8,16,128]{3,2,1,0:T(8,128)} %param.11) | copy-start | bytes 786436
  2.5 1.0 %copy-start.3 = (s32[8,16]{1,0:T(8,128)S(1)}, s32[8,16]{1,0:T(8,128)}, u32[]{:S(2)}) copy-start(s32[8,16]{1,0:T(8,128)} %param.14) | copy-start | bytes 1540
  2.5 1.0 %copy-start.8 = (f32[64]{0:T(128)S(1)}, f32[64]{0:T(128)}, u32[]{:S(2)}) copy-start(f32[64]{0:T(128)} %param.13) | copy-start | bytes 772
  2.6 1.1 %copy-start.6 = (s32[8,16]{1,0:T(8,128)S(1)}, s32[8,16]{1,0:T(8,128)}, u32[]{:S(2)}) copy-start(s32[8,16]{1,0:T(8,128)} %param.15) | copy-start | bytes 1540
  2.6 1.1 %copy-start.9 = (f32[64]{0:T(128)S(1)}, f32[64]{0:T(128)}, u32[]{:S(2)}) copy-start(f32[64]{0:T(128)} %param.16) | copy-start | bytes 772
  4.1 3.9 %copy-start.4 = (s32[512]{0:T(512)S(1)}, s32[512]{0:T(512)}, u32[]{:S(2)}) copy-start(s32[512]{0:T(512)} %param.18) | copy-start | bytes 6148
  4.1 3.9 %copy-start.5 = (s32[512]{0:T(512)S(1)}, s32[512]{0:T(512)}, u32[]{:S(2)}) copy-start(s32[512]{0:T(512)} %param.17) | copy-start | bytes 6148
  4.2 7.9 %collective-permute-start = (f32[8,8,8,128]{3,2,1,0:T(8,128)S(1)}, f32[8,8,8,128]{3,2,1,0:T(8,128)S(1)}, u32[]{:S(2)}, u32[]{:S(2)}) collective-permute-start(f32[8,8,8,128]{3,2,1,0:T(8,128)S(1)} %pad_maximum_fusion.1), channel_id=1, source_target_pairs={{0,1},{1,2},{2,3},{4,5},{5,6},{6,7},{8,9},{9,10},{10,11},{12,13},{... | collective-permute-start | bytes 786440 | tf_op jit(solution)/shard_map/ppermute | solution.py:128
  6.6 5.5 %collective-permute-start.1 = (f32[7,8,8,128]{3,2,1,0:T(8,128)S(1)}, f32[7,8,8,128]{3,2,1,0:T(8,128)S(1)}, u32[]{:S(2)}, u32[]{:S(2)}) collective-permute-start(f32[7,8,8,128]{3,2,1,0:T(8,128)S(1)} %fusion.1), channel_id=1, source_target_pairs={{1,0},{2,1},{3,2},{5,4},{6,5},{7,6},{9,8},{10,9},{11,10},{13,12},{... | collective-permute-start | bytes 688136 | tf_op jit(solution)/shard_map/ppermute | solution.py:129
  12.4 1.7 %copy-start = (f32[9,8,32,128]{3,2,1,0:T(8,128)}, f32[9,8,32,128]{3,2,1,0:T(8,128)S(1)}, u32[]{:S(2)}) copy-start(f32[9,8,32,128]{3,2,1,0:T(8,128)S(1)} %maximum_maximum_fusion) | copy-start | bytes 3538948
  12.5 8.2 %collective-permute-start.2 = (f32[10,32,128]{2,1,0:T(8,128)S(1)}, f32[10,32,128]{2,1,0:T(8,128)S(1)}, u32[]{:S(2)}, u32[]{:S(2)}) collective-permute-start(f32[10,32,128]{2,1,0:T(8,128)S(1)} %get-tuple-element.38), channel_id=1, source_target_pairs={{0,4},{4,8},{8,12},{12,16},{16,20},{20,24},{24,28},{28,0},{1,5},{5... | collective-permute-start | bytes 491528 | tf_op jit(solution)/shard_map/ppermute | solution.py:144
  14.1 7.9 %copy-start.7 = (f32[512]{0:T(512)S(1)}, f32[512]{0:T(512)}, u32[]{:S(2)}) copy-start(f32[512]{0:T(512)} %param.19) | copy-start | bytes 6148
  14.2 7.1 %collective-permute-start.3 = (f32[10,32,128]{2,1,0:T(8,128)S(1)}, f32[10,32,128]{2,1,0:T(8,128)S(1)}, u32[]{:S(2)}, u32[]{:S(2)}) collective-permute-start(f32[10,32,128]{2,1,0:T(8,128)S(1)} %get-tuple-element.39), channel_id=1, source_target_pairs={{4,0},{8,4},{12,8},{16,12},{20,16},{24,20},{28,24},{0,28},{5,1},{9... | collective-permute-start | bytes 491528 | tf_op jit(solution)/shard_map/ppermute | solution.py:145
  21.3 3.5 %slice-start = ((f32[9,8,32,128]{3,2,1,0:T(8,128)}), f32[8,8,32,128]{3,2,1,0:T(8,128)S(1)}, s32[]{:S(2)}) async-start(f32[9,8,32,128]{3,2,1,0:T(8,128)} %copy-done), calls=%async_computation | async-start | bytes 2097152 | tf_op jit(solution)/shard_map/slice | solution.py:151
  23.8 3.6 %collective-permute-start.4 = (f32[129]{0:T(256)S(1)}, f32[129]{0:T(256)S(1)}, u32[]{:S(2)}, u32[]{:S(2)}) collective-permute-start(f32[129]{0:T(256)S(1)} %select_reduce_fusion.2), channel_id=1, source_target_pairs={{0,4},{4,0},{8,12},{12,8},{16,20},{20,16},{24,28},{28,24},{1,5},{5... | collective-permute-start | bytes 1556 | tf_op jit(solution)/shard_map/ppermute | solution.py:267
  27.5 3.1 %collective-permute-start.5 = (f32[129]{0:T(256)S(1)}, f32[129]{0:T(256)S(1)}, u32[]{:S(2)}, u32[]{:S(2)}) collective-permute-start(f32[129]{0:T(256)S(1)} %add.244), channel_id=1, source_target_pairs={{0,1},{1,0},{2,3},{3,2},{4,5},{5,4},{6,7},{7,6},{8,9},{9,8},{10,11... | collective-permute-start | bytes 1556 | tf_op jit(solution)/shard_map/ppermute | solution.py:67
  30.6 3.7 %collective-permute-start.6 = (f32[129]{0:T(256)S(1)}, f32[129]{0:T(256)S(1)}, u32[]{:S(2)}, u32[]{:S(2)}) collective-permute-start(f32[129]{0:T(256)S(1)} %add.249), channel_id=1, source_target_pairs={{0,2},{1,3},{2,0},{3,1},{4,6},{5,7},{6,4},{7,5},{8,10},{9,11},{10,... | collective-permute-start | bytes 1556 | tf_op jit(solution)/shard_map/ppermute | solution.py:67
  34.3 3.6 %collective-permute-start.7 = (f32[129]{0:T(256)S(1)}, f32[129]{0:T(256)S(1)}, u32[]{:S(2)}, u32[]{:S(2)}) collective-permute-start(f32[129]{0:T(256)S(1)} %add.250), channel_id=1, source_target_pairs={{0,8},{4,12},{8,0},{12,4},{16,24},{20,28},{24,16},{28,20},{1,9},{5... | collective-permute-start | bytes 1556 | tf_op jit(solution)/shard_map/ppermute | solution.py:67
  37.9 4.5 %collective-permute-start.8 = (f32[129]{0:T(256)S(1)}, f32[129]{0:T(256)S(1)}, u32[]{:S(2)}, u32[]{:S(2)}) collective-permute-start(f32[129]{0:T(256)S(1)} %add.251), channel_id=1, source_target_pairs={{0,16},{4,20},{8,24},{12,28},{16,0},{20,4},{24,8},{28,12},{1,17},{... | collective-permute-start | bytes 1556 | tf_op jit(solution)/shard_map/ppermute | solution.py:67

commit v21 on v19

--- a/solution.py
+++ b/solution.py
@@ -62,7 +62,7 @@
         if size & (size - 1):
             values = lax.psum(values, axis)
             continue
-        step = 2 if (skip_first and index == 0) else 1
+        step = 2 if (skip_first and axis == "ax") else 1
         while step < size:
             values = values + lax.ppermute(values, axis, [(i, i ^ step) for i in range(size)])
             step *= 2
@@ -263,8 +263,8 @@
         axis=(0, 1),
     )
 
-    size_az = lax.axis_size("az")
-    first_round = payload + lax.ppermute(payload, "az", [(i, i ^ 1) for i in range(size_az)])
+    size_ax_first = lax.axis_size("ax")
+    first_round = payload + lax.ppermute(payload, "ax", [(i, i ^ 1) for i in range(size_ax_first)])
     placed, _ = lax.optimization_barrier((placed, first_round))
     push_e = -step_dt * c(s_t, -1, -1, ea, ex) * placed
     r1a, r1x = na + 2, nx + 2

time: 46.5 us -> 47.8 us (1.028)
  waiting for transfers between devices: 15 us -> 16.6 us
    ppermute x4, waiting for transfers between devices: 7.21 us -> 10.6 us  [butterfly_sum(): lax.ppermute(values, axis, [(i, i ^ step) for i in range(size)])]
    ppermute x4, starting transfers between devices: 7.12 us -> 4.07 us  [butterfly_sum(): lax.ppermute(values, axis, [(i, i ^ step) for i in range(size)])]
    ppermute x1, starting transfers between devices: 0.78 us -> 3.54 us  [shards(): lax.ppermute(payload, 'ax', [(i, i ^ 1) for i in range(size_ax_first)])]
    ppermute x1, waiting for transfers between devices: 1.84 us -> 0.01 us  [shards(): lax.ppermute(payload, 'ax', [(i, i ^ 1) for i in range(size_ax_first)])]
  transfers between devices with their start and end apart: 9 -> 9, of which waited for: 8 -> 7; matrix products, arithmetic and copies ran while one was open for 6% -> 6% of each run, Pallas kernels for 0% -> 0%
where the time goes in v21:
time: 47.8 us; the launch traced here: 47.5 us
  starting transfers between devices  16.7 us (35%)
  waiting for transfers between devices  16.6 us (35%)
  other arithmetic  5.78 us (12%)
  local copies, waits for them, and re-layouts  5.22 us (11%)
  between operations  3.26 us (7%)
    ppermute x4, waiting for transfers between devices, butterfly_sum(): lax.ppermute(values, axis, [(i, i ^ step) for i in range(size)])  10.6 us
    ppermute x4, starting transfers between devices, butterfly_sum(): lax.ppermute(values, axis, [(i, i ^ step) for i in range(size)])  4.07 us
    ppermute x1, starting transfers between devices, shards(): from_above = lax.ppermute(sent_down, 'az', down)  3.86 us
    ppermute x1, starting transfers between devices, shards(): lax.ppermute(payload, 'ax', [(i, i ^ 1) for i in range(size_ax_first)])  3.54 us
    ppermute x1, waiting for transfers between devices, shards(): lax.ppermute(jnp.concatenate([sent_x[:5, :, :tile], sent_x[6:, :, :tile]]...  2.94 us
    ppermute x1, waiting for transfers between devices, shards(): from_below = lax.ppermute(sent_up, 'az', up)  2.48 us
    ppermute x1, starting transfers between devices, shards(): x_before = lax.ppermute(sent_x[:, :, length_x - tile:], 'ax', right)  2.37 us
    ppermute x1, starting transfers between devices, shards(): from_below = lax.ppermute(sent_up, 'az', up)  1.57 us
  transfers between devices with their start and end apart: 9, of which 7 were waited for; matrix products, arithmetic and copies ran while one was open for 6% of the time, Pallas kernels for 0%

profile of v21, /device:TPU:0, one launch (start us, length us, event | category | flops | bytes accessed | tf_op | source)
XLA Modules:
  0.0 47.5 jit_solution(2749823534972700262)
XLA Ops:
  0.7 1.2 %fusion.125 = (f32[1,8,16,1]{3,2,1,0:T(8,128)S(1)}, f32[1,8,16,1]{3,2,1,0:T(8,128)S(1)}, f32[1,8,16,1]{3,2,1,0:T(8,128)S(1)}, f32[1,8,16,1]{3,2,1,0:T(8,128)S(1)}, f32[1,8,16,1]{3,2,1,0:T(8,128)S(1)}) fusion(f32[4,8,16,128]{3,2,1,0:T(8,128)} %param.10), kind=kLoop, calls=%fused_computation.342 | loop fusion | bytes 5120 | tf_op jit(solution)/shard_map/slice | solution.py:105
  3.0 0.2 copy.133
  4.2 2.4 %collective-permute-start = (f32[8,8,8,128]{3,2,1,0:T(8,128)S(1)}, f32[8,8,8,128]{3,2,1,0:T(8,128)S(1)}, u32[]{:S(2)}, u32[]{:S(2)}) collective-permute-start(f32[8,8,8,128]{3,2,1,0:T(8,128)S(1)} %pad_maximum_fusion.1), channel_id=1, source_target_pairs={{0,1},{1,2},{2,3},{4,5},{5,6},{6,7},{8,9},{9,10},{10,11},{12,13},{... | collective-permute-start | bytes 786440 | tf_op jit(solution)/shard_map/ppermute | solution.py:128
  6.6 1.3 %collective-permute-start.1 = (f32[7,8,8,128]{3,2,1,0:T(8,128)S(1)}, f32[7,8,8,128]{3,2,1,0:T(8,128)S(1)}, u32[]{:S(2)}, u32[]{:S(2)}) collective-permute-start(f32[7,8,8,128]{3,2,1,0:T(8,128)S(1)} %fusion.1), channel_id=1, source_target_pairs={{1,0},{2,1},{3,2},{5,4},{6,5},{7,6},{9,8},{10,9},{11,10},{13,12},{... | collective-permute-start | bytes 688136 | tf_op jit(solution)/shard_map/ppermute | solution.py:129
  8.3 0.8 %slice_bitcast_fusion.9 = f32[8,16,128]{2,1,0:T(8,128)S(1)} fusion(f32[4,8,16,128]{3,2,1,0:T(8,128)} %param.10), kind=kLoop, calls=%fused_computation.168 | loop fusion | bytes 131072 | tf_op jit(solution)/shard_map/squeeze | solution.py:244
  9.1 2.9 %collective-permute-done.1 = f32[7,8,8,128]{3,2,1,0:T(8,128)S(1)} collective-permute-done((f32[7,8,8,128]{3,2,1,0:T(8,128)S(1)}, f32[7,8,8,128]{3,2,1,0:T(8,128)S(1)}, u32[]{:S(2)}, u32[]{:S(2)}) %collective-permute-start.1) | collective-permute-done | bytes 229408 | tf_op jit(solution)/shard_map/ppermute | solution.py:129
  12.5 1.6 %collective-permute-start.2 = (f32[10,32,128]{2,1,0:T(8,128)S(1)}, f32[10,32,128]{2,1,0:T(8,128)S(1)}, u32[]{:S(2)}, u32[]{:S(2)}) collective-permute-start(f32[10,32,128]{2,1,0:T(8,128)S(1)} %get-tuple-element.38), channel_id=1, source_target_pairs={{0,4},{4,8},{8,12},{12,16},{16,20},{20,24},{24,28},{28,0},{1,5},{5... | collective-permute-start | bytes 491528 | tf_op jit(solution)/shard_map/ppermute | solution.py:144
  14.2 3.9 %collective-permute-start.3 = (f32[10,32,128]{2,1,0:T(8,128)S(1)}, f32[10,32,128]{2,1,0:T(8,128)S(1)}, u32[]{:S(2)}, u32[]{:S(2)}) collective-permute-start(f32[10,32,128]{2,1,0:T(8,128)S(1)} %get-tuple-element.39), channel_id=1, source_target_pairs={{4,0},{8,4},{12,8},{16,12},{20,16},{24,20},{28,24},{0,28},{5,1},{9... | collective-permute-start | bytes 491528 | tf_op jit(solution)/shard_map/ppermute | solution.py:145
  18.2 2.5 %collective-permute-done.2 = f32[10,32,128]{2,1,0:T(8,128)S(1)} collective-permute-done((f32[10,32,128]{2,1,0:T(8,128)S(1)}, f32[10,32,128]{2,1,0:T(8,128)S(1)}, u32[]{:S(2)}, u32[]{:S(2)}) %collective-permute-start.2) | collective-permute-done | bytes 163872 | tf_op jit(solution)/shard_map/ppermute | solution.py:144
  20.7 0.5 %collective-permute-done.3 = f32[10,32,128]{2,1,0:T(8,128)S(1)} collective-permute-done((f32[10,32,128]{2,1,0:T(8,128)S(1)}, f32[10,32,128]{2,1,0:T(8,128)S(1)}, u32[]{:S(2)}, u32[]{:S(2)}) %collective-permute-start.3) | collective-permute-done | bytes 163872 | tf_op jit(solution)/shard_map/ppermute | solution.py:145
  22.0 0.6 %select_reduce_fusion.5 = (f32[]{:T(128)}, f32[512]{0:T(512)S(1)}) fusion(s32[512]{0:T(512)S(1)} %copy-done.4, s32[]{:T(128)S(6)} %mul.404, s32[512]{0:T(512)S(1)} %copy-done.5, s32[]{:T(128)S(6)} %mul.403, f32[512]{0:T(512)S(1)} %select_reduce_fusion.1, f32[512]{0:T(512)S(1)} %copy-done.7), kind=kLoop, calls=%fused_computation.328 | loop fusion | flops 13311 | bytes 10252 | tf_op jit(solution)/shard_map/reduce_sum | solution.py:199
  23.0 0.7 %and_select_fusion = f32[8,16]{1,0:T(8,128)S(1)} fusion(f32[]{:T(128)} %get-tuple-element.22, pred[16]{0:T(512)(128)(4,1)S(1)} %iota_compare_fusion.7, pred[8]{0:T(512)(128)(4,1)S(1)} %iota_compare_fusion.8), kind=kLoop, calls=%fused_computation.323 | loop fusion | flops 256 | bytes 540 | tf_op jit(solution)/shard_map/jit(_where)/select_n | solution.py:256
  23.8 3.5 %collective-permute-start.4 = (f32[129]{0:T(256)S(1)}, f32[129]{0:T(256)S(1)}, u32[]{:S(2)}, u32[]{:S(2)}) collective-permute-start(f32[129]{0:T(256)S(1)} %select_reduce_fusion.2), channel_id=1, source_target_pairs={{0,1},{1,0},{2,3},{3,2},{4,5},{5,4},{6,7},{7,6},{8,9},{9,8},{10,11... | collective-permute-start | bytes 1556 | tf_op jit(solution)/shard_map/ppermute | solution.py:267
  28.4 0.6 %collective-permute-start.5 = (f32[129]{0:T(256)S(1)}, f32[129]{0:T(256)S(1)}, u32[]{:S(2)}, u32[]{:S(2)}) collective-permute-start(f32[129]{0:T(256)S(1)} %add.244), channel_id=1, source_target_pairs={{0,4},{4,0},{8,12},{12,8},{16,20},{20,16},{24,28},{28,24},{1,5},{5... | collective-permute-start | bytes 1556 | tf_op jit(solution)/shard_map/ppermute | solution.py:67
  29.6 2.4 %collective-permute-done.5 = f32[129]{0:T(256)S(1)} collective-permute-done((f32[129]{0:T(256)S(1)}, f32[129]{0:T(256)S(1)}, u32[]{:S(2)}, u32[]{:S(2)}) %collective-permute-start.5) | collective-permute-done | bytes 548 | tf_op jit(solution)/shard_map/ppermute | solution.py:67
  32.0 0.7 %collective-permute-start.6 = (f32[129]{0:T(256)S(1)}, f32[129]{0:T(256)S(1)}, u32[]{:S(2)}, u32[]{:S(2)}) collective-permute-start(f32[129]{0:T(256)S(1)} %add.249), channel_id=1, source_target_pairs={{0,8},{4,12},{8,0},{12,4},{16,24},{20,28},{24,16},{28,20},{1,9},{5... | collective-permute-start | bytes 1556 | tf_op jit(solution)/shard_map/ppermute | solution.py:67
  32.8 2.8 %collective-permute-done.6 = f32[129]{0:T(256)S(1)} collective-permute-done((f32[129]{0:T(256)S(1)}, f32[129]{0:T(256)S(1)}, u32[]{:S(2)}, u32[]{:S(2)}) %collective-permute-start.6) | collective-permute-done | bytes 548 | tf_op jit(solution)/shard_map/ppermute | solution.py:67
  35.6 2.0 %collective-permute-start.7 = (f32[129]{0:T(256)S(1)}, f32[129]{0:T(256)S(1)}, u32[]{:S(2)}, u32[]{:S(2)}) collective-permute-start(f32[129]{0:T(256)S(1)} %add.250), channel_id=1, source_target_pairs={{0,16},{4,20},{8,24},{12,28},{16,0},{20,4},{24,8},{28,12},{1,17},{... | collective-permute-start | bytes 1556 | tf_op jit(solution)/shard_map/ppermute | solution.py:67
  37.6 2.5 %collective-permute-done.7 = f32[129]{0:T(256)S(1)} collective-permute-done((f32[129]{0:T(256)S(1)}, f32[129]{0:T(256)S(1)}, u32[]{:S(2)}, u32[]{:S(2)}) %collective-permute-start.7) | collective-permute-done | bytes 548 | tf_op jit(solution)/shard_map/ppermute | solution.py:67
  40.1 0.7 %collective-permute-start.8 = (f32[129]{0:T(256)S(1)}, f32[129]{0:T(256)S(1)}, u32[]{:S(2)}, u32[]{:S(2)}) collective-permute-start(f32[129]{0:T(256)S(1)} %add.251), channel_id=1, source_target_pairs={{0,2},{1,3},{2,0},{3,1},{4,6},{5,7},{6,4},{7,5},{8,10},{9,11},{10,... | collective-permute-start | bytes 1556 | tf_op jit(solution)/shard_map/ppermute | solution.py:67
  40.8 2.8 %collective-permute-done.8 = f32[129]{0:T(256)S(1)} collective-permute-done((f32[129]{0:T(256)S(1)}, f32[129]{0:T(256)S(1)}, u32[]{:S(2)}, u32[]{:S(2)}) %collective-permute-start.8) | collective-permute-done | bytes 548 | tf_op jit(solution)/shard_map/ppermute | solution.py:67
  43.7 0.5 %slice.929 = f32[1]{0:T(128)} slice(f32[129]{0:T(256)S(1)} %add.252), slice={[0:1]} | slice | bytes 8 | tf_op jit(solution)/shard_map/slice | solution.py:307
  44.8 0.6 %fusion.121 = f32[64]{0:T(128)} fusion(f32[129]{0:T(256)S(1)} %add.252, f32[]{:T(128)} %bitcast.83), kind=kLoop, calls=%fused_computation.340 | loop fusion | flops 192 | bytes 772 | tf_op jit(solution)/shard_map/mul | solution.py:309
  45.5 0.9 %maximum_add_fusion = f32[4,8,16,128]{3,2,1,0:T(8,128)} fusion(f32[1,8,16,128]{3,2,1,0:T(8,128)S(1)} %fusion.11, f32[1,8,16,128]{3,2,1,0:T(8,128)S(1)} %fusion.28, f32[1,8,16,128]{3,2,1,0:T(8,128)S(1)} %fusion.37, f32[1,8,16,128]{3,2,1,0:T(8,128)S(1)} %fusion.49, f32[4,8,16]{2,1,0:T(8,128)S(1)} %get-tuple-element.94, f32[4,8,16]{2,1,0:T(8,128)S(1)} %get-tuple-element.93, ...), kind=kLoop, calls=%fused_computation.12 | loop fusion | flops 393216 | bytes 528640 | tf_op jit(solution)/shard_map/add | solution.py:318
  (137 shorter events, 5.4 us)
Async XLA Ops:
  0.6 1.8 %copy-start.1 = (f32[4,8,16,128]{3,2,1,0:T(8,128)S(1)}, f32[4,8,16,128]{3,2,1,0:T(8,128)}, u32[]{:S(2)}) copy-start(f32[4,8,16,128]{3,2,1,0:T(8,128)} %param.12) | copy-start | bytes 786436
  0.6 1.8 %copy-start.2 = (f32[4,8,16,128]{3,2,1,0:T(8,128)S(1)}, f32[4,8,16,128]{3,2,1,0:T(8,128)}, u32[]{:S(2)}) copy-start(f32[4,8,16,128]{3,2,1,0:T(8,128)} %param.11) | copy-start | bytes 786436
  2.5 1.0 %copy-start.3 = (s32[8,16]{1,0:T(8,128)S(1)}, s32[8,16]{1,0:T(8,128)}, u32[]{:S(2)}) copy-start(s32[8,16]{1,0:T(8,128)} %param.14) | copy-start | bytes 1540
  2.5 1.0 %copy-start.8 = (f32[64]{0:T(128)S(1)}, f32[64]{0:T(128)}, u32[]{:S(2)}) copy-start(f32[64]{0:T(128)} %param.13) | copy-start | bytes 772
  2.6 1.1 %copy-start.6 = (s32[8,16]{1,0:T(8,128)S(1)}, s32[8,16]{1,0:T(8,128)}, u32[]{:S(2)}) copy-start(s32[8,16]{1,0:T(8,128)} %param.15) | copy-start | bytes 1540
  2.6 1.1 %copy-start.9 = (f32[64]{0:T(128)S(1)}, f32[64]{0:T(128)}, u32[]{:S(2)}) copy-start(f32[64]{0:T(128)} %param.16) | copy-start | bytes 772
  4.1 3.9 %copy-start.4 = (s32[512]{0:T(512)S(1)}, s32[512]{0:T(512)}, u32[]{:S(2)}) copy-start(s32[512]{0:T(512)} %param.18) | copy-start | bytes 6148
  4.1 3.9 %copy-start.5 = (s32[512]{0:T(512)S(1)}, s32[512]{0:T(512)}, u32[]{:S(2)}) copy-start(s32[512]{0:T(512)} %param.17) | copy-start | bytes 6148
  4.2 7.9 %collective-permute-start = (f32[8,8,8,128]{3,2,1,0:T(8,128)S(1)}, f32[8,8,8,128]{3,2,1,0:T(8,128)S(1)}, u32[]{:S(2)}, u32[]{:S(2)}) collective-permute-start(f32[8,8,8,128]{3,2,1,0:T(8,128)S(1)} %pad_maximum_fusion.1), channel_id=1, source_target_pairs={{0,1},{1,2},{2,3},{4,5},{5,6},{6,7},{8,9},{9,10},{10,11},{12,13},{... | collective-permute-start | bytes 786440 | tf_op jit(solution)/shard_map/ppermute | solution.py:128
  6.6 5.5 %collective-permute-start.1 = (f32[7,8,8,128]{3,2,1,0:T(8,128)S(1)}, f32[7,8,8,128]{3,2,1,0:T(8,128)S(1)}, u32[]{:S(2)}, u32[]{:S(2)}) collective-permute-start(f32[7,8,8,128]{3,2,1,0:T(8,128)S(1)} %fusion.1), channel_id=1, source_target_pairs={{1,0},{2,1},{3,2},{5,4},{6,5},{7,6},{9,8},{10,9},{11,10},{13,12},{... | collective-permute-start | bytes 688136 | tf_op jit(solution)/shard_map/ppermute | solution.py:129
  12.4 1.7 %copy-start = (f32[9,8,32,128]{3,2,1,0:T(8,128)}, f32[9,8,32,128]{3,2,1,0:T(8,128)S(1)}, u32[]{:S(2)}) copy-start(f32[9,8,32,128]{3,2,1,0:T(8,128)S(1)} %maximum_maximum_fusion) | copy-start | bytes 3538948
  12.5 8.2 %collective-permute-start.2 = (f32[10,32,128]{2,1,0:T(8,128)S(1)}, f32[10,32,128]{2,1,0:T(8,128)S(1)}, u32[]{:S(2)}, u32[]{:S(2)}) collective-permute-start(f32[10,32,128]{2,1,0:T(8,128)S(1)} %get-tuple-element.38), channel_id=1, source_target_pairs={{0,4},{4,8},{8,12},{12,16},{16,20},{20,24},{24,28},{28,0},{1,5},{5... | collective-permute-start | bytes 491528 | tf_op jit(solution)/shard_map/ppermute | solution.py:144
  14.1 7.9 %copy-start.7 = (f32[512]{0:T(512)S(1)}, f32[512]{0:T(512)}, u32[]{:S(2)}) copy-start(f32[512]{0:T(512)} %param.19) | copy-start | bytes 6148
  14.2 7.1 %collective-permute-start.3 = (f32[10,32,128]{2,1,0:T(8,128)S(1)}, f32[10,32,128]{2,1,0:T(8,128)S(1)}, u32[]{:S(2)}, u32[]{:S(2)}) collective-permute-start(f32[10,32,128]{2,1,0:T(8,128)S(1)} %get-tuple-element.39), channel_id=1, source_target_pairs={{4,0},{8,4},{12,8},{16,12},{20,16},{24,20},{28,24},{0,28},{5,1},{9... | collective-permute-start | bytes 491528 | tf_op jit(solution)/shard_map/ppermute | solution.py:145
  21.3 6.2 %slice-start = ((f32[9,8,32,128]{3,2,1,0:T(8,128)}), f32[8,8,32,128]{3,2,1,0:T(8,128)S(1)}, s32[]{:S(2)}) async-start(f32[9,8,32,128]{3,2,1,0:T(8,128)} %copy-done), calls=%async_computation | async-start | bytes 2097152 | tf_op jit(solution)/shard_map/slice | solution.py:151
  23.8 4.6 %collective-permute-start.4 = (f32[129]{0:T(256)S(1)}, f32[129]{0:T(256)S(1)}, u32[]{:S(2)}, u32[]{:S(2)}) collective-permute-start(f32[129]{0:T(256)S(1)} %select_reduce_fusion.2), channel_id=1, source_target_pairs={{0,1},{1,0},{2,3},{3,2},{4,5},{5,4},{6,7},{7,6},{8,9},{9,8},{10,11... | collective-permute-start | bytes 1556 | tf_op jit(solution)/shard_map/ppermute | solution.py:267
  28.4 3.6 %collective-permute-start.5 = (f32[129]{0:T(256)S(1)}, f32[129]{0:T(256)S(1)}, u32[]{:S(2)}, u32[]{:S(2)}) collective-permute-start(f32[129]{0:T(256)S(1)} %add.244), channel_id=1, source_target_pairs={{0,4},{4,0},{8,12},{12,8},{16,20},{20,16},{24,28},{28,24},{1,5},{5... | collective-permute-start | bytes 1556 | tf_op jit(solution)/shard_map/ppermute | solution.py:67
  32.0 3.6 %collective-permute-start.6 = (f32[129]{0:T(256)S(1)}, f32[129]{0:T(256)S(1)}, u32[]{:S(2)}, u32[]{:S(2)}) collective-permute-start(f32[129]{0:T(256)S(1)} %add.249), channel_id=1, source_target_pairs={{0,8},{4,12},{8,0},{12,4},{16,24},{20,28},{24,16},{28,20},{1,9},{5... | collective-permute-start | bytes 1556 | tf_op jit(solution)/shard_map/ppermute | solution.py:67
  35.6 4.5 %collective-permute-start.7 = (f32[129]{0:T(256)S(1)}, f32[129]{0:T(256)S(1)}, u32[]{:S(2)}, u32[]{:S(2)}) collective-permute-start(f32[129]{0:T(256)S(1)} %add.250), channel_id=1, source_target_pairs={{0,16},{4,20},{8,24},{12,28},{16,0},{20,4},{24,8},{28,12},{1,17},{... | collective-permute-start | bytes 1556 | tf_op jit(solution)/shard_map/ppermute | solution.py:67
  40.1 3.6 %collective-permute-start.8 = (f32[129]{0:T(256)S(1)}, f32[129]{0:T(256)S(1)}, u32[]{:S(2)}, u32[]{:S(2)}) collective-permute-start(f32[129]{0:T(256)S(1)} %add.251), channel_id=1, source_target_pairs={{0,2},{1,3},{2,0},{3,1},{4,6},{5,7},{6,4},{7,5},{8,10},{9,11},{10,... | collective-permute-start | bytes 1556 | tf_op jit(solution)/shard_map/ppermute | solution.py:67
